TPU v7x, 128 devices: a whole 4x4x4 slice. The times are simulated.
128 devices in a mesh: gx: 8 (over z, core), gy: 16 (over x, y).
Axes of the slice: x: 4, y: 4, z: 4, core: 2. Of those that a mesh axis runs over, the one named last changes fastest.
Arguments:
- pixel_adjoint: float32 [4, 32, 16384], P(None, None, ('gx', 'gy')), may hold values from -6 to 6
- pixel_owner: int32 [4, 16384, 1], P(None, ('gx', 'gy')), may hold values from 0 to 127; in each aligned block of 128 rows (0 to 127, 128 to 255, ..., all dimensions but the last counted through in order) at most 2 rows name the same one
- pixel_column: int32 [4, 16384], P(None, ('gx', 'gy')), may hold values from 0 to 1023
- pixel_level: int32 [4, 16384], P(None, ('gx', 'gy')), may hold values from 0 to 24
- wind_x: float32 [4, 64, 2048], P(None, 'gx', 'gy'), may hold values from -0.45 to 0.45
- wind_y: float32 [4, 64, 2048], P(None, 'gx', 'gy'), may hold values from -0.45 to 0.45
- diffusivity: float32 [39, 64, 2048], P(None, 'gx', 'gy'), may hold values from 0.1 to 10
- prior_emission: float32 [2, 64, 2048], P(None, 'gx', 'gy'), may hold values from 0.01 to 0.1
- region_map: int32 [64, 2048], P('gx', 'gy'), may hold values from 0 to 1023, as said below
Outputs:
- adjoint_out: float32 [2, 40, 64, 2048], P(None, None, 'gx', 'gy')
- emission_gradient: float32 [2, 1024], P(None, ('gx', 'gy'))
Inputs may be any that keep to these rules, and one draw needn't show every extreme that they name: `pixel_owner`: within the 128 entries of one device in one step no owner is named more than 2 times, a bound that some block reaches. `region_map`: constant on aligned blocks of 2 rows by 4 columns; every region covers exactly 16 such blocks.
All inputs are finite; a program needn't handle non-finite values.
Results may differ from a plain program's by a relative error of at most 0.00014.
Values sent between devices are 32-bit elements; how exact they have to be, the bound alone decides.
No kernel may reach another device: no remote copies, remote signals or barrier semaphores. Data moves between devices by JAX's collectives and lax.ppermute only.
A program may use at most 64 MiB of HBM per device.

v0:
```python
import functools

import jax
import jax.numpy as jnp
from jax import lax
from jax.experimental import pallas as pl
from jax.experimental.pallas import tpu as pltpu
from jax.sharding import PartitionSpec as P

HI = lax.Precision.HIGHEST
REG_DEV = 8


def _full(shape):
    nd = len(shape)
    return pl.BlockSpec(shape, lambda i, _n=nd: (0,) * _n)


def _fluxes(forced_ref, wx, wy, e_ref, w_ref, n_ref, s_ref):
    east = jnp.maximum(wx, 0.0)
    west = jnp.maximum(-wx, 0.0)
    north = jnp.maximum(wy, 0.0)
    south = jnp.maximum(-wy, 0.0)
    species, levels = forced_ref.shape[0], forced_ref.shape[1]
    rows, cols = wx.shape
    for s in range(species):

        def body(l, carry):
            f = forced_ref[s, l]
            e_ref[s, l] = (east * f)[0:1, :]
            w_ref[s, l] = (west * f)[rows - 1:rows, :]
            n_ref[s, l] = (north * f)[:, 0:1]
            s_ref[s, l] = (south * f)[:, cols - 1:cols]
            return carry

        lax.fori_loop(0, levels, body, 0, unroll=8)


def _init_kernel(diff_ref, forcing_ref, wx_ref, wy_ref,
                 ratio_ref, inv_ref, e_ref, w_ref, n_ref, s_ref):
    levels = ratio_ref.shape[0]
    zero = jnp.zeros(ratio_ref.shape[1:], jnp.float32)
    carried = zero
    for l in range(levels):
        below = diff_ref[l - 1] if l > 0 else zero
        above = diff_ref[l] if l < levels - 1 else zero
        inverse = 1.0 / (1.0 + below + above + below * carried)
        ratio = -above * inverse
        ratio_ref[l] = ratio
        inv_ref[l] = inverse
        carried = ratio
    k = wx_ref.shape[0] - 1
    _fluxes(forcing_ref, wx_ref[k], wy_ref[k], e_ref, w_ref, n_ref, s_ref)


def _step_kernel(k, first, *refs):
    last = k == 0
    if last:
        (forced_ref, he_ref, hw_ref, hn_ref, hs_ref, wx_ref, wy_ref, diff_ref,
         ratio_ref, inv_ref, prior_ref, ss_ref,
         adj_ref, ss_out_ref, red_ref) = refs
    else:
        (forced_ref, he_ref, hw_ref, hn_ref, hs_ref, wx_ref, wy_ref, diff_ref,
         ratio_ref, inv_ref, prior_ref, ss_ref, next_forcing_ref,
         adj_ref, e_ref, w_ref, n_ref, s_ref, ss_out_ref, red_ref) = refs
    species, levels, rows, cols = forced_ref.shape
    wx = wx_ref[k]
    wy = wy_ref[k]
    east = jnp.maximum(wx, 0.0)
    west = jnp.maximum(-wx, 0.0)
    north = jnp.maximum(wy, 0.0)
    south = jnp.maximum(-wy, 0.0)
    remain = 1.0 - (east + west + north + south)
    row = lax.broadcasted_iota(jnp.int32, (rows, cols), 0)
    col = lax.broadcasted_iota(jnp.int32, (rows, cols), 1)
    top_row = row == rows - 1
    bottom_row = row == 0
    last_col = col == cols - 1
    first_col = col == 0
    zero = jnp.zeros((rows, cols), jnp.float32)

    for s in range(species):

        def forward(l, reduced):
            f = forced_ref[s, l]
            from_east = jnp.where(
                top_row, jnp.broadcast_to(he_ref[s, l], (rows, cols)),
                pltpu.roll(east * f, rows - 1, 0))
            from_west = jnp.where(
                bottom_row, jnp.broadcast_to(hw_ref[s, l], (rows, cols)),
                pltpu.roll(west * f, 1, 0))
            from_north = jnp.where(
                last_col, jnp.broadcast_to(hn_ref[s, l], (rows, cols)),
                pltpu.roll(north * f, cols - 1, 1))
            from_south = jnp.where(
                first_col, jnp.broadcast_to(hs_ref[s, l], (rows, cols)),
                pltpu.roll(south * f, 1, 1))
            moved = f * remain
            moved = moved + from_east + from_west
            moved = moved + from_north + from_south
            below = jnp.where(l > 0, diff_ref[jnp.maximum(l - 1, 0)], zero)
            reduced = (moved + below * reduced) * inv_ref[l]
            red_ref[l] = reduced
            return reduced

        lax.fori_loop(0, levels, forward, zero, unroll=8)

        def backward(i, result):
            l = levels - 1 - i
            result = red_ref[l] - ratio_ref[l] * result
            adj_ref[s, l] = result
            return result

        lax.fori_loop(0, levels, backward, zero, unroll=8)
        if first:
            ss_out_ref[s] = prior_ref[s] * adj_ref[s, 0]
        else:
            ss_out_ref[s] = ss_ref[s] + prior_ref[s] * adj_ref[s, 0]

    if not last:
        for s in range(species):

            def add(l, carry):
                adj_ref[s, l] = adj_ref[s, l] + next_forcing_ref[s, l]
                return carry

            lax.fori_loop(0, levels, add, 0, unroll=8)
        _fluxes(adj_ref, wx_ref[k - 1], wy_ref[k - 1], e_ref, w_ref, n_ref, s_ref)


def _halo_shapes(species, levels, rows, cols):
    row_halo = jax.ShapeDtypeStruct((species, levels, 1, cols), jnp.float32)
    col_halo = jax.ShapeDtypeStruct((species, levels, rows, 1), jnp.float32)
    return [row_halo, row_halo, col_halo, col_halo]


def init_call(diffusivity, forcing, wind_x, wind_y):
    steps, species, levels, rows, cols = forcing.shape
    k = steps - 1
    plane = jax.ShapeDtypeStruct((levels, rows, cols), jnp.float32)
    halos = _halo_shapes(species, levels, rows, cols)
    return pl.pallas_call(
        _init_kernel,
        grid=(1,),
        in_specs=[
            _full(diffusivity.shape),
            pl.BlockSpec((None, species, levels, rows, cols), lambda i: (k, 0, 0, 0, 0)),
            _full(wind_x.shape),
            _full(wind_y.shape),
        ],
        out_specs=[_full(plane.shape), _full(plane.shape)] + [_full(h.shape) for h in halos],
        out_shape=[plane, plane] + halos,
    )(diffusivity, forcing, wind_x, wind_y)


def step_call(k, first, forced, halos, wind_x, wind_y, diffusivity, ratios, inverses,
              prior, surface_sum, forcing):
    species, levels, rows, cols = forced.shape
    last = k == 0
    state = jax.ShapeDtypeStruct((species, levels, rows, cols), jnp.float32)
    surf = jax.ShapeDtypeStruct(prior.shape, jnp.float32)
    in_specs = [_full(forced.shape)] + [_full(h.shape) for h in halos]
    args = [forced] + list(halos)
    in_specs += [_full(wind_x.shape), _full(wind_y.shape)]
    args += [wind_x, wind_y]
    in_specs += [_full(diffusivity.shape), _full(ratios.shape), _full(inverses.shape),
                 _full(prior.shape), _full(surface_sum.shape)]
    args += [diffusivity, ratios, inverses, prior, surface_sum]
    out_shape = [state]
    if not last:
        in_specs.append(
            pl.BlockSpec((None, species, levels, rows, cols), lambda i: (k - 1, 0, 0, 0, 0)))
        args.append(forcing)
        out_shape += _halo_shapes(species, levels, rows, cols)
    out_shape.append(surf)
    return pl.pallas_call(
        functools.partial(_step_kernel, k, first),
        grid=(1,),
        in_specs=in_specs,
        out_specs=[_full(o.shape) for o in out_shape],
        out_shape=out_shape,
        scratch_shapes=[pltpu.VMEM((levels, rows, cols), jnp.float32)],
    )(*args)


def exchange(halos):
    east, west, north, south = halos
    gx = lax.axis_size("gx")
    gy = lax.axis_size("gy")
    up_x = [(i, i + 1) for i in range(gx - 1)]
    down_x = [(i + 1, i) for i in range(gx - 1)]
    up_y = [(i, i + 1) for i in range(gy - 1)]
    down_y = [(i + 1, i) for i in range(gy - 1)]
    east = lax.ppermute(east, "gx", down_x)
    west = lax.ppermute(west, "gx", up_x)
    north = lax.ppermute(north, "gy", down_y)
    south = lax.ppermute(south, "gy", up_y)
    return [east, west, north, south]


def local(pixel_adjoint, pixel_owner, pixel_column, pixel_level, wind_x, wind_y,
          diffusivity, prior_emission, region_map):
    devices = lax.axis_size("gx") * lax.axis_size("gy")
    steps, rows, cols = wind_x.shape
    levels = diffusivity.shape[0] + 1
    species = prior_emission.shape[0]
    kernel = pixel_adjoint.shape[1] // species
    pixels = pixel_adjoint.shape[2]
    capacity = 2 * pixels // devices
    cells = rows * cols
    slots = devices * capacity

    owners = pixel_owner[:, :, 0]
    matches = (owners[:, :, None] == jnp.arange(devices, dtype=jnp.int32)).astype(jnp.int32)
    rank = jnp.sum(jnp.cumsum(matches, axis=1) * matches, axis=2) - 1
    position = owners * capacity + rank
    rows_out = jnp.concatenate(
        [pixel_adjoint, pixel_column.astype(jnp.float32)[:, None, :],
         pixel_level.astype(jnp.float32)[:, None, :]], axis=1)
    place = (position[:, :, None] == jnp.arange(slots, dtype=jnp.int32)).astype(jnp.float32)
    placed = jnp.einsum("kap,kpq->kaq", rows_out, place, precision=HI)
    received = lax.all_to_all(placed, ("gx", "gy"), 2, 2, tiled=True)

    payload = received[:, :species * kernel].reshape(steps, species, kernel, slots)
    column = jnp.round(received[:, species * kernel]).astype(jnp.int32)
    start = jnp.round(received[:, species * kernel + 1]).astype(jnp.int32)
    offset = jnp.arange(levels, dtype=jnp.int32)[None, :, None] - start[:, None, :]
    profile = jnp.zeros((steps, species, levels, slots), jnp.float32)
    for j in range(kernel):
        profile = profile + jnp.where((offset == j)[:, None], payload[:, :, j][:, :, None, :], 0.0)
    hits = (column[:, :, None] == jnp.arange(cells, dtype=jnp.int32)).astype(jnp.float32)
    forcing = jnp.einsum("ksq,kqc->ksc", profile.reshape(steps, species * levels, slots), hits,
                         precision=HI)
    forcing = forcing.reshape(steps, species, levels, rows, cols)

    ratios, inverses, *halos = init_call(diffusivity, forcing, wind_x, wind_y)
    forced = forcing[steps - 1]
    surface_sum = jnp.zeros(prior_emission.shape, jnp.float32)
    for k in reversed(range(steps)):
        halos = exchange(halos)
        outs = step_call(k, k == steps - 1, forced, halos, wind_x, wind_y, diffusivity,
                         ratios, inverses, prior_emission, surface_sum, forcing)
        if k > 0:
            forced, *halos, surface_sum = outs
        else:
            adjoint, surface_sum = outs

    nreg = REG_DEV * devices
    member = (region_map.reshape(-1)[:, None] == jnp.arange(nreg, dtype=jnp.int32)).astype(jnp.float32)
    partial = jnp.dot(surface_sum.reshape(species, cells), member, precision=HI)
    pieces = lax.all_to_all(partial.reshape(species, devices, nreg // devices), ("gx", "gy"), 1, 1,
                            tiled=True)
    gradient = jnp.sum(pieces, axis=1)
    return adjoint, gradient


def solution(mesh):
    in_specs = (
        P(None, None, ("gx", "gy")),
        P(None, ("gx", "gy"), None),
        P(None, ("gx", "gy")),
        P(None, ("gx", "gy")),
        P(None, "gx", "gy"),
        P(None, "gx", "gy"),
        P(None, "gx", "gy"),
        P(None, "gx", "gy"),
        P("gx", "gy"),
    )
    out_specs = (P(None, None, "gx", "gy"), P(None, ("gx", "gy")))
    return jax.shard_map(local, mesh=mesh, in_specs=in_specs, out_specs=out_specs, check_vma=False)
```

profile of v0, /device:TPU:1, one launch (start us, length us, event | category | flops | bytes accessed | tf_op | source)
XLA Modules:
  0.0 161.7 jit_solution(13557163371295229631)
XLA Ops:
  0.6 0.8 fusion.8
  1.5 0.3 reduce_window_sum.11
  1.7 0.9 select_reduce_fusion
  2.6 0.7 multiply_add_fusion.1
  3.3 0.7 convert_element_type.27
  4.0 0.7 convert_element_type.26
  4.7 1.2 fusion.6
  5.9 0.2 copy.47
  6.2 0.6 reshape.171
  6.8 21.9 %all_to_all.10 = f32[128,1,272]{2,1,0:T(1,128)S(1)} all-to-all(f32[128,1,272]{2,1,0:T(1,128)S(1)} %reshape.171), channel_id=1, replica_groups=mesh['gx'=8,'gy'=16] {'gx','gy'}, dimensions={0} | all-to-all | bytes 278528 | tf_op jit(solution)/shard_map/all_to_all | solution.py:222
  28.6 0.5 broadcast.234
  29.2 1.1 reduce
  30.3 0.4 reshape.172
  30.7 0.6 fusion.31
  31.3 0.2 copy.71
  31.5 0.1 fusion.32
  31.6 0.2 copy.72
  31.8 0.4 fusion.24
  32.2 0.2 copy.73
  32.6 0.8 add_add_fusion
  33.3 1.7 %fusion = f32[4,80,1024]{2,1,0:T(8,128)S(1)} fusion(f32[4,80,256]{2,1,0:T(8,128)S(1)} %bitcast.66, s32[4,256]{1,0:T(4,128)S(1)} %convert_bitcast_fusion), kind=kOutput, calls=%fused_computation.1 | convolution fusion | flops 1007681536 | bytes 1642496 | tf_op jit(solution)/shard_map/ksq,kqc->ksc/dot_general | solution.py:232
  35.0 1.3 copy.75
  36.4 3.1 %shard_map.104 = (f32[40,8,128]{2,1,0:T(8,128)}, f32[40,8,128]{2,1,0:T(8,128)}, f32[2,40,1,128]{3,2,1,0:T(1,128)}, f32[2,40,1,128]{3,2,1,0:T(1,128)}, f32[2,40,8,1]{3,2,1,0:T(8,128)}, /*index=5*/f32[2,40,8,1]{3,2,1,0:T(8,128)}) custom-call(f32[39,8,128]{2,1,0:T(8,128)} %refs_7_.7, f32[4,2,40,8,128]{4,3,2,1,0:T(8,128)} %bitcast.58, f32[4,8,128]{2,1,0:T(8,128)} %refs_5_.7, ...), custom_call_target="tpu_custom_call" | custom-call | tf_op jit(solution)/shard_map/pallas_call | solution.py:142
  39.4 2.6 %collective-permute-start = (f32[2,40,1,128]{3,2,1,0:T(1,128)}, f32[2,40,1,128]{3,2,1,0:T(1,128)S(1)}, u32[]{:S(2)}, u32[]{:S(2)}) collective-permute-start(f32[2,40,1,128]{3,2,1,0:T(1,128)} %get-tuple-element.28), channel_id=1, source_target_pairs={{16,0},{32,16},{48,32},{64,48},{80,64},{96,80},{112,96},{17,1},{33... | collective-permute-start | bytes 122888 | tf_op jit(solution)/shard_map/ppermute | solution.py:194
  42.0 3.0 %collective-permute-start.1 = (f32[2,40,1,128]{3,2,1,0:T(1,128)}, f32[2,40,1,128]{3,2,1,0:T(1,128)S(1)}, u32[]{:S(2)}, u32[]{:S(2)}) collective-permute-start(f32[2,40,1,128]{3,2,1,0:T(1,128)} %get-tuple-element.29), channel_id=1, source_target_pairs={{0,16},{16,32},{32,48},{48,64},{64,80},{80,96},{96,112},{1,17},{17... | collective-permute-start | bytes 122888 | tf_op jit(solution)/shard_map/ppermute | solution.py:195
  45.0 1.3 collective-permute-start.2
  46.3 4.0 %collective-permute-start.3 = (f32[2,40,8,1]{3,2,1,0:T(8,128)}, f32[2,40,8,1]{3,2,1,0:T(8,128)S(1)}, u32[]{:S(2)}, u32[]{:S(2)}) collective-permute-start(f32[2,40,8,1]{3,2,1,0:T(8,128)} %get-tuple-element.31), channel_id=1, source_target_pairs={{0,1},{1,2},{2,3},{3,4},{4,5},{5,6},{6,7},{7,8},{8,9},{9,10},{10,1... | collective-permute-start | bytes 7688 | tf_op jit(solution)/shard_map/ppermute | solution.py:197
  50.4 0.8 copy.74
  51.1 5.5 %collective-permute-done.2.refs_3_ = f32[2,40,8,1]{3,2,1,0:T(8,128)S(1)} collective-permute-done((f32[2,40,8,1]{3,2,1,0:T(8,128)}, f32[2,40,8,1]{3,2,1,0:T(8,128)S(1)}, u32[]{:S(2)}, u32[]{:S(2)}) %collective-permute-start.2) | collective-permute-done | bytes 2592 | tf_op jit(solution)/shard_map/ppermute | solution.py:196
  56.7 1.2 collective-permute-done.3.refs_4_
  58.0 0.7 broadcast_in_dim.301.refs_11_
  58.6 0.1 copy-done.4
  58.7 4.5 %shard_map.105 = (f32[2,40,8,128]{3,2,1,0:T(8,128)}, f32[2,40,1,128]{3,2,1,0:T(1,128)}, f32[2,40,1,128]{3,2,1,0:T(1,128)}, f32[2,40,8,1]{3,2,1,0:T(8,128)}, f32[...) custom-call(f32[2,40,8,128]{3,2,1,0:T(8,128)} %bitcast.67, f32[2,40,1,128]{3,2,1,0:T(1,128)} %copy-done.10, ...), custom_call_target="tpu_custom_call" | custom-call | tf_op jit(solution)/shard_map/pallas_call | solution.py:176
  63.2 2.5 %collective-permute-start.4 = (f32[2,40,1,128]{3,2,1,0:T(1,128)}, f32[2,40,1,128]{3,2,1,0:T(1,128)S(1)}, u32[]{:S(2)}, u32[]{:S(2)}) collective-permute-start(f32[2,40,1,128]{3,2,1,0:T(1,128)} %get-tuple-element.35), channel_id=1, source_target_pairs={{16,0},{32,16},{48,32},{64,48},{80,64},{96,80},{112,96},{17,1},{33... | collective-permute-start | bytes 122888 | tf_op jit(solution)/shard_map/ppermute | solution.py:194
  65.7 3.1 %collective-permute-start.5 = (f32[2,40,1,128]{3,2,1,0:T(1,128)}, f32[2,40,1,128]{3,2,1,0:T(1,128)S(1)}, u32[]{:S(2)}, u32[]{:S(2)}) collective-permute-start(f32[2,40,1,128]{3,2,1,0:T(1,128)} %get-tuple-element.36), channel_id=1, source_target_pairs={{0,16},{16,32},{32,48},{48,64},{64,80},{80,96},{96,112},{1,17},{17... | collective-permute-start | bytes 122888 | tf_op jit(solution)/shard_map/ppermute | solution.py:195
  68.8 1.3 collective-permute-start.6
  70.1 4.6 %collective-permute-start.7 = (f32[2,40,8,1]{3,2,1,0:T(8,128)}, f32[2,40,8,1]{3,2,1,0:T(8,128)S(1)}, u32[]{:S(2)}, u32[]{:S(2)}) collective-permute-start(f32[2,40,8,1]{3,2,1,0:T(8,128)} %get-tuple-element.38), channel_id=1, source_target_pairs={{0,1},{1,2},{2,3},{3,4},{4,5},{5,6},{6,7},{7,8},{8,9},{9,10},{10,1... | collective-permute-start | bytes 7688 | tf_op jit(solution)/shard_map/ppermute | solution.py:197
  74.7 5.8 %collective-permute-done.6.refs_3_ = f32[2,40,8,1]{3,2,1,0:T(8,128)S(1)} collective-permute-done((f32[2,40,8,1]{3,2,1,0:T(8,128)}, f32[2,40,8,1]{3,2,1,0:T(8,128)S(1)}, u32[]{:S(2)}, u32[]{:S(2)}) %collective-permute-start.6) | collective-permute-done | bytes 2592 | tf_op jit(solution)/shard_map/ppermute | solution.py:196
  80.5 1.9 %collective-permute-done.7.refs_4_ = f32[2,40,8,1]{3,2,1,0:T(8,128)S(1)} collective-permute-done((f32[2,40,8,1]{3,2,1,0:T(8,128)}, f32[2,40,8,1]{3,2,1,0:T(8,128)S(1)}, u32[]{:S(2)}, u32[]{:S(2)}) %collective-permute-start.7) | collective-permute-done | bytes 2592 | tf_op jit(solution)/shard_map/ppermute | solution.py:197
  82.4 0.7 copy-done.7
  83.1 0.0 copy-done.13
  83.1 4.6 %shard_map.106 = (f32[2,40,8,128]{3,2,1,0:T(8,128)}, f32[2,40,1,128]{3,2,1,0:T(1,128)}, f32[2,40,1,128]{3,2,1,0:T(1,128)}, f32[2,40,8,1]{3,2,1,0:T(8,128)}, f32[...) custom-call(f32[2,40,8,128]{3,2,1,0:T(8,128)} %get-tuple-element.34.refs_0_, f32[2,40,1,128]{3,2,1,0:T(1,128)} %copy-done.13, ...), custom_call_target="tpu_custom_call" | custom-call | tf_op jit(solution)/shard_map/pallas_call | solution.py:176
  87.7 2.1 %collective-permute-start.8 = (f32[2,40,1,128]{3,2,1,0:T(1,128)}, f32[2,40,1,128]{3,2,1,0:T(1,128)S(1)}, u32[]{:S(2)}, u32[]{:S(2)}) collective-permute-start(f32[2,40,1,128]{3,2,1,0:T(1,128)} %get-tuple-element.41), channel_id=1, source_target_pairs={{16,0},{32,16},{48,32},{64,48},{80,64},{96,80},{112,96},{17,1},{33... | collective-permute-start | bytes 122888 | tf_op jit(solution)/shard_map/ppermute | solution.py:194
  89.8 3.4 %collective-permute-start.9 = (f32[2,40,1,128]{3,2,1,0:T(1,128)}, f32[2,40,1,128]{3,2,1,0:T(1,128)S(1)}, u32[]{:S(2)}, u32[]{:S(2)}) collective-permute-start(f32[2,40,1,128]{3,2,1,0:T(1,128)} %get-tuple-element.42), channel_id=1, source_target_pairs={{0,16},{16,32},{32,48},{48,64},{64,80},{80,96},{96,112},{1,17},{17... | collective-permute-start | bytes 122888 | tf_op jit(solution)/shard_map/ppermute | solution.py:195
  93.3 1.3 collective-permute-start.10
  94.6 4.5 %collective-permute-start.11 = (f32[2,40,8,1]{3,2,1,0:T(8,128)}, f32[2,40,8,1]{3,2,1,0:T(8,128)S(1)}, u32[]{:S(2)}, u32[]{:S(2)}) collective-permute-start(f32[2,40,8,1]{3,2,1,0:T(8,128)} %get-tuple-element.44), channel_id=1, source_target_pairs={{0,1},{1,2},{2,3},{3,4},{4,5},{5,6},{6,7},{7,8},{8,9},{9,10},{10,1... | collective-permute-start | bytes 7688 | tf_op jit(solution)/shard_map/ppermute | solution.py:197
  99.0 5.6 %collective-permute-done.10.refs_3_ = f32[2,40,8,1]{3,2,1,0:T(8,128)S(1)} collective-permute-done((f32[2,40,8,1]{3,2,1,0:T(8,128)}, f32[2,40,8,1]{3,2,1,0:T(8,128)S(1)}, u32[]{:S(2)}, u32[]{:S(2)}) %collective-permute-start.10) | collective-permute-done | bytes 2592 | tf_op jit(solution)/shard_map/ppermute | solution.py:196
  104.6 1.9 %collective-permute-done.11.refs_4_ = f32[2,40,8,1]{3,2,1,0:T(8,128)S(1)} collective-permute-done((f32[2,40,8,1]{3,2,1,0:T(8,128)}, f32[2,40,8,1]{3,2,1,0:T(8,128)S(1)}, u32[]{:S(2)}, u32[]{:S(2)}) %collective-permute-start.11) | collective-permute-done | bytes 2592 | tf_op jit(solution)/shard_map/ppermute | solution.py:197
  106.5 0.7 copy-done.6
  107.2 0.0 copy-done.11
  107.2 4.6 %shard_map.107 = (f32[2,40,8,128]{3,2,1,0:T(8,128)}, f32[2,40,1,128]{3,2,1,0:T(1,128)}, f32[2,40,1,128]{3,2,1,0:T(1,128)}, f32[2,40,8,1]{3,2,1,0:T(8,128)}, f32[...) custom-call(f32[2,40,8,128]{3,2,1,0:T(8,128)} %get-tuple-element.40.refs_0_, f32[2,40,1,128]{3,2,1,0:T(1,128)} %copy-done.11, ...), custom_call_target="tpu_custom_call" | custom-call | tf_op jit(solution)/shard_map/pallas_call | solution.py:176
  111.8 2.0 %collective-permute-start.12 = (f32[2,40,1,128]{3,2,1,0:T(1,128)}, f32[2,40,1,128]{3,2,1,0:T(1,128)S(1)}, u32[]{:S(2)}, u32[]{:S(2)}) collective-permute-start(f32[2,40,1,128]{3,2,1,0:T(1,128)} %get-tuple-element.47), channel_id=1, source_target_pairs={{16,0},{32,16},{48,32},{64,48},{80,64},{96,80},{112,96},{17,1},{33... | collective-permute-start | bytes 122888 | tf_op jit(solution)/shard_map/ppermute | solution.py:194
  113.8 3.6 %collective-permute-start.13 = (f32[2,40,1,128]{3,2,1,0:T(1,128)}, f32[2,40,1,128]{3,2,1,0:T(1,128)S(1)}, u32[]{:S(2)}, u32[]{:S(2)}) collective-permute-start(f32[2,40,1,128]{3,2,1,0:T(1,128)} %get-tuple-element.48), channel_id=1, source_target_pairs={{0,16},{16,32},{32,48},{48,64},{64,80},{80,96},{96,112},{1,17},{17... | collective-permute-start | bytes 122888 | tf_op jit(solution)/shard_map/ppermute | solution.py:195
  117.4 1.3 collective-permute-start.14
  118.7 4.4 %collective-permute-start.15 = (f32[2,40,8,1]{3,2,1,0:T(8,128)}, f32[2,40,8,1]{3,2,1,0:T(8,128)S(1)}, u32[]{:S(2)}, u32[]{:S(2)}) collective-permute-start(f32[2,40,8,1]{3,2,1,0:T(8,128)} %get-tuple-element.50), channel_id=1, source_target_pairs={{0,1},{1,2},{2,3},{3,4},{4,5},{5,6},{6,7},{7,8},{8,9},{9,10},{10,1... | collective-permute-start | bytes 7688 | tf_op jit(solution)/shard_map/ppermute | solution.py:197
  123.0 5.5 %collective-permute-done.14.refs_3_ = f32[2,40,8,1]{3,2,1,0:T(8,128)S(1)} collective-permute-done((f32[2,40,8,1]{3,2,1,0:T(8,128)}, f32[2,40,8,1]{3,2,1,0:T(8,128)S(1)}, u32[]{:S(2)}, u32[]{:S(2)}) %collective-permute-start.14) | collective-permute-done | bytes 2592 | tf_op jit(solution)/shard_map/ppermute | solution.py:196
  128.6 1.9 %collective-permute-done.15.refs_4_ = f32[2,40,8,1]{3,2,1,0:T(8,128)S(1)} collective-permute-done((f32[2,40,8,1]{3,2,1,0:T(8,128)}, f32[2,40,8,1]{3,2,1,0:T(8,128)S(1)}, u32[]{:S(2)}, u32[]{:S(2)}) %collective-permute-start.15) | collective-permute-done | bytes 2592 | tf_op jit(solution)/shard_map/ppermute | solution.py:197
  130.5 0.7 copy-done.1
  131.2 3.4 %shard_map.108 = (f32[2,40,8,128]{3,2,1,0:T(8,128)}, f32[2,8,128]{2,1,0:T(8,128)}) custom-call(f32[2,40,8,128]{3,2,1,0:T(8,128)} %get-tuple-element.46.refs_0_, f32[2,40,1,128]{3,2,1,0:T(1,128)} %copy-done.8, f32[2,40,1,128]{3,2,1,0:T(1,128)} %copy-done.9, f32[2,40,8,1]{3,2,1,0:T(8,128)} %copy-done, f32[2,40,8,1]{3,2,1,0:T(8,128)} %copy-done.1, ...), custom_call_target="tpu_custom_call" | custom-call | tf_op jit(solution)/shard_map/pallas_call | solution.py:176
  134.6 0.7 reshape.169
  135.3 1.9 %fusion.1 = f32[2,128,8]{1,0,2:T(2,128)S(1)} fusion(f32[2,1024,1]{1,0,2:T(2,128)S(1)} %reshape.169, s32[128,8]{0,1:T(8,128)S(1)} %multiply_add_fusion, s32[1024]{0:T(1024)S(1)} %bitcast.75), kind=kOutput, calls=%fused_computation.2 | convolution fusion | flops 26214400 | bytes 24576 | tf_op jit(solution)/shard_map/dot_general | solution.py:250
  137.2 0.2 copy.51
  137.3 23.6 %all_to_all.11 = f32[2,128,8]{2,0,1:T(2,128)S(1)} all-to-all(f32[2,128,8]{2,0,1:T(2,128)S(1)} %copy.51), channel_id=1, replica_groups=mesh['gx'=8,'gy'=16] {'gx','gy'}, dimensions={1} | all-to-all | bytes 16384 | tf_op jit(solution)/shard_map/all_to_all | solution.py:251
  161.0 0.7 reduce_sum.19
  (49 shorter events, 0.2 us)
Async XLA Ops:
  39.4 18.5 %collective-permute-start = (f32[2,40,1,128]{3,2,1,0:T(1,128)}, f32[2,40,1,128]{3,2,1,0:T(1,128)S(1)}, u32[]{:S(2)}, u32[]{:S(2)}) collective-permute-start(f32[2,40,1,128]{3,2,1,0:T(1,128)} %get-tuple-element.28), channel_id=1, source_target_pairs={{16,0},{32,16},{48,32},{64,48},{80,64},{96,80},{112,96},{17,1},{33... | collective-permute-start | bytes 122888 | tf_op jit(solution)/shard_map/ppermute | solution.py:194
  42.0 15.9 %collective-permute-start.1 = (f32[2,40,1,128]{3,2,1,0:T(1,128)}, f32[2,40,1,128]{3,2,1,0:T(1,128)S(1)}, u32[]{:S(2)}, u32[]{:S(2)}) collective-permute-start(f32[2,40,1,128]{3,2,1,0:T(1,128)} %get-tuple-element.29), channel_id=1, source_target_pairs={{0,16},{16,32},{32,48},{48,64},{64,80},{80,96},{96,112},{1,17},{17... | collective-permute-start | bytes 122888 | tf_op jit(solution)/shard_map/ppermute | solution.py:195
  45.0 11.7 %collective-permute-start.2 = (f32[2,40,8,1]{3,2,1,0:T(8,128)}, f32[2,40,8,1]{3,2,1,0:T(8,128)S(1)}, u32[]{:S(2)}, u32[]{:S(2)}) collective-permute-start(f32[2,40,8,1]{3,2,1,0:T(8,128)} %get-tuple-element.30), channel_id=1, source_target_pairs={{1,0},{2,1},{3,2},{4,3},{5,4},{6,5},{7,6},{8,7},{9,8},{10,9},{11,1... | collective-permute-start | bytes 7688 | tf_op jit(solution)/shard_map/ppermute | solution.py:196
  46.3 11.6 %collective-permute-start.3 = (f32[2,40,8,1]{3,2,1,0:T(8,128)}, f32[2,40,8,1]{3,2,1,0:T(8,128)S(1)}, u32[]{:S(2)}, u32[]{:S(2)}) collective-permute-start(f32[2,40,8,1]{3,2,1,0:T(8,128)} %get-tuple-element.31), channel_id=1, source_target_pairs={{0,1},{1,2},{2,3},{3,4},{4,5},{5,6},{6,7},{7,8},{8,9},{9,10},{10,1... | collective-permute-start | bytes 7688 | tf_op jit(solution)/shard_map/ppermute | solution.py:197
  56.7 1.9 %copy-start.2 = (f32[2,40,8,1]{3,2,1,0:T(8,128)}, f32[2,40,8,1]{3,2,1,0:T(8,128)S(1)}, u32[]{:S(2)}) copy-start(f32[2,40,8,1]{3,2,1,0:T(8,128)S(1)} %collective-permute-done.2.refs_3_) | copy-start | bytes 7684
  57.9 0.7 copy-start.4
  57.9 0.7 copy-start.10
  57.9 0.7 copy-start.12
  63.2 19.2 %collective-permute-start.4 = (f32[2,40,1,128]{3,2,1,0:T(1,128)}, f32[2,40,1,128]{3,2,1,0:T(1,128)S(1)}, u32[]{:S(2)}, u32[]{:S(2)}) collective-permute-start(f32[2,40,1,128]{3,2,1,0:T(1,128)} %get-tuple-element.35), channel_id=1, source_target_pairs={{16,0},{32,16},{48,32},{64,48},{80,64},{96,80},{112,96},{17,1},{33... | collective-permute-start | bytes 122888 | tf_op jit(solution)/shard_map/ppermute | solution.py:194
  65.7 16.7 %collective-permute-start.5 = (f32[2,40,1,128]{3,2,1,0:T(1,128)}, f32[2,40,1,128]{3,2,1,0:T(1,128)S(1)}, u32[]{:S(2)}, u32[]{:S(2)}) collective-permute-start(f32[2,40,1,128]{3,2,1,0:T(1,128)} %get-tuple-element.36), channel_id=1, source_target_pairs={{0,16},{16,32},{32,48},{48,64},{64,80},{80,96},{96,112},{1,17},{17... | collective-permute-start | bytes 122888 | tf_op jit(solution)/shard_map/ppermute | solution.py:195
  68.8 11.7 %collective-permute-start.6 = (f32[2,40,8,1]{3,2,1,0:T(8,128)}, f32[2,40,8,1]{3,2,1,0:T(8,128)S(1)}, u32[]{:S(2)}, u32[]{:S(2)}) collective-permute-start(f32[2,40,8,1]{3,2,1,0:T(8,128)} %get-tuple-element.37), channel_id=1, source_target_pairs={{1,0},{2,1},{3,2},{4,3},{5,4},{6,5},{7,6},{8,7},{9,8},{10,9},{11,1... | collective-permute-start | bytes 7688 | tf_op jit(solution)/shard_map/ppermute | solution.py:196
  70.1 12.3 %collective-permute-start.7 = (f32[2,40,8,1]{3,2,1,0:T(8,128)}, f32[2,40,8,1]{3,2,1,0:T(8,128)S(1)}, u32[]{:S(2)}, u32[]{:S(2)}) collective-permute-start(f32[2,40,8,1]{3,2,1,0:T(8,128)} %get-tuple-element.38), channel_id=1, source_target_pairs={{0,1},{1,2},{2,3},{3,4},{4,5},{5,6},{6,7},{7,8},{8,9},{9,10},{10,1... | collective-permute-start | bytes 7688 | tf_op jit(solution)/shard_map/ppermute | solution.py:197
  80.5 1.9 %copy-start.5 = (f32[2,40,8,1]{3,2,1,0:T(8,128)}, f32[2,40,8,1]{3,2,1,0:T(8,128)S(1)}, u32[]{:S(2)}) copy-start(f32[2,40,8,1]{3,2,1,0:T(8,128)S(1)} %collective-permute-done.6.refs_3_) | copy-start | bytes 7684
  82.4 0.7 copy-start.7
  82.4 0.7 copy-start.13
  82.4 0.7 copy-start.15
  87.7 18.8 %collective-permute-start.8 = (f32[2,40,1,128]{3,2,1,0:T(1,128)}, f32[2,40,1,128]{3,2,1,0:T(1,128)S(1)}, u32[]{:S(2)}, u32[]{:S(2)}) collective-permute-start(f32[2,40,1,128]{3,2,1,0:T(1,128)} %get-tuple-element.41), channel_id=1, source_target_pairs={{16,0},{32,16},{48,32},{64,48},{80,64},{96,80},{112,96},{17,1},{33... | collective-permute-start | bytes 122888 | tf_op jit(solution)/shard_map/ppermute | solution.py:194
  89.8 16.7 %collective-permute-start.9 = (f32[2,40,1,128]{3,2,1,0:T(1,128)}, f32[2,40,1,128]{3,2,1,0:T(1,128)S(1)}, u32[]{:S(2)}, u32[]{:S(2)}) collective-permute-start(f32[2,40,1,128]{3,2,1,0:T(1,128)} %get-tuple-element.42), channel_id=1, source_target_pairs={{0,16},{16,32},{32,48},{48,64},{64,80},{80,96},{96,112},{1,17},{17... | collective-permute-start | bytes 122888 | tf_op jit(solution)/shard_map/ppermute | solution.py:195
  93.3 11.3 %collective-permute-start.10 = (f32[2,40,8,1]{3,2,1,0:T(8,128)}, f32[2,40,8,1]{3,2,1,0:T(8,128)S(1)}, u32[]{:S(2)}, u32[]{:S(2)}) collective-permute-start(f32[2,40,8,1]{3,2,1,0:T(8,128)} %get-tuple-element.43), channel_id=1, source_target_pairs={{1,0},{2,1},{3,2},{4,3},{5,4},{6,5},{7,6},{8,7},{9,8},{10,9},{11,1... | collective-permute-start | bytes 7688 | tf_op jit(solution)/shard_map/ppermute | solution.py:196
  94.6 11.9 %collective-permute-start.11 = (f32[2,40,8,1]{3,2,1,0:T(8,128)}, f32[2,40,8,1]{3,2,1,0:T(8,128)S(1)}, u32[]{:S(2)}, u32[]{:S(2)}) collective-permute-start(f32[2,40,8,1]{3,2,1,0:T(8,128)} %get-tuple-element.44), channel_id=1, source_target_pairs={{0,1},{1,2},{2,3},{3,4},{4,5},{5,6},{6,7},{7,8},{8,9},{9,10},{10,1... | collective-permute-start | bytes 7688 | tf_op jit(solution)/shard_map/ppermute | solution.py:197
  104.6 1.9 %copy-start.3 = (f32[2,40,8,1]{3,2,1,0:T(8,128)}, f32[2,40,8,1]{3,2,1,0:T(8,128)S(1)}, u32[]{:S(2)}) copy-start(f32[2,40,8,1]{3,2,1,0:T(8,128)S(1)} %collective-permute-done.10.refs_3_) | copy-start | bytes 7684
  106.5 0.7 copy-start.6
  106.5 0.7 copy-start.11
  106.5 0.7 copy-start.14
  111.8 23.5 %copy-start.16 = (s32[8,128]{1,0:T(8,128)S(1)}, s32[8,128]{1,0:T(8,128)}, u32[]{:S(2)}) copy-start(s32[8,128]{1,0:T(8,128)} %param.17) | copy-start | bytes 12292
  111.8 18.7 %collective-permute-start.12 = (f32[2,40,1,128]{3,2,1,0:T(1,128)}, f32[2,40,1,128]{3,2,1,0:T(1,128)S(1)}, u32[]{:S(2)}, u32[]{:S(2)}) collective-permute-start(f32[2,40,1,128]{3,2,1,0:T(1,128)} %get-tuple-element.47), channel_id=1, source_target_pairs={{16,0},{32,16},{48,32},{64,48},{80,64},{96,80},{112,96},{17,1},{33... | collective-permute-start | bytes 122888 | tf_op jit(solution)/shard_map/ppermute | solution.py:194
  113.8 16.7 %collective-permute-start.13 = (f32[2,40,1,128]{3,2,1,0:T(1,128)}, f32[2,40,1,128]{3,2,1,0:T(1,128)S(1)}, u32[]{:S(2)}, u32[]{:S(2)}) collective-permute-start(f32[2,40,1,128]{3,2,1,0:T(1,128)} %get-tuple-element.48), channel_id=1, source_target_pairs={{0,16},{16,32},{32,48},{48,64},{64,80},{80,96},{96,112},{1,17},{17... | collective-permute-start | bytes 122888 | tf_op jit(solution)/shard_map/ppermute | solution.py:195
  117.4 11.2 %collective-permute-start.14 = (f32[2,40,8,1]{3,2,1,0:T(8,128)}, f32[2,40,8,1]{3,2,1,0:T(8,128)S(1)}, u32[]{:S(2)}, u32[]{:S(2)}) collective-permute-start(f32[2,40,8,1]{3,2,1,0:T(8,128)} %get-tuple-element.49), channel_id=1, source_target_pairs={{1,0},{2,1},{3,2},{4,3},{5,4},{6,5},{7,6},{8,7},{9,8},{10,9},{11,1... | collective-permute-start | bytes 7688 | tf_op jit(solution)/shard_map/ppermute | solution.py:196
  118.7 11.8 %collective-permute-start.15 = (f32[2,40,8,1]{3,2,1,0:T(8,128)}, f32[2,40,8,1]{3,2,1,0:T(8,128)S(1)}, u32[]{:S(2)}, u32[]{:S(2)}) collective-permute-start(f32[2,40,8,1]{3,2,1,0:T(8,128)} %get-tuple-element.50), channel_id=1, source_target_pairs={{0,1},{1,2},{2,3},{3,4},{4,5},{5,6},{6,7},{7,8},{8,9},{9,10},{10,1... | collective-permute-start | bytes 7688 | tf_op jit(solution)/shard_map/ppermute | solution.py:197
  128.6 1.9 %copy-start = (f32[2,40,8,1]{3,2,1,0:T(8,128)}, f32[2,40,8,1]{3,2,1,0:T(8,128)S(1)}, u32[]{:S(2)}) copy-start(f32[2,40,8,1]{3,2,1,0:T(8,128)S(1)} %collective-permute-done.14.refs_3_) | copy-start | bytes 7684
  130.4 0.7 copy-start.1
  130.4 0.7 copy-start.8
  130.5 0.7 copy-start.9
where the time goes:
time: 163 us; the launch traced here: 162 us
  blocking collectives  45.5 us (28%)
  starting transfers between devices  44.9 us (28%)
  waiting for transfers between devices  29.3 us (18%)
  Pallas kernels  20.1 us (12%)
  local copies, waits for them, and re-layouts  9.1 us (6%)
  other arithmetic  7.03 us (4%)
  matrix products  4.77 us (3%)
    all_to_all x1, blocking collectives, local(): lax.all_to_all(partial.reshape(species, devices, nreg // devices), ('gx',...  23.6 us
    ppermute x4, waiting for transfers between devices, exchange(): north = lax.ppermute(north, 'gy', down_y)  22.4 us
    all_to_all x1, blocking collectives, local(): received = lax.all_to_all(placed, ('gx', 'gy'), 2, 2, tiled=True)  21.9 us
    ppermute x4, starting transfers between devices, exchange(): south = lax.ppermute(south, 'gy', up_y)  17.5 us
    pallas_call x4, Pallas kernels, step_call(): pl.pallas_call(functools.partial(_step_kernel, k, first), grid=(1,), in_s...  17.1 us
    ppermute x4, starting transfers between devices, exchange(): west = lax.ppermute(west, 'gx', up_x)  13 us
    ppermute x4, starting transfers between devices, exchange(): east = lax.ppermute(east, 'gx', down_x)  9.2 us
    ppermute x4, waiting for transfers between devices, exchange(): south = lax.ppermute(south, 'gy', up_y)  6.82 us
  transfers between devices with their start and end apart: 16, of which 8 were waited for; matrix products, arithmetic and copies ran while one was open for 1% of the time, Pallas kernels for 0%

commit v1 on v0

v1 whole, which is shorter than its diff:
```python
import functools

import jax
import jax.numpy as jnp
from jax import lax
from jax.experimental import pallas as pl
from jax.experimental.pallas import tpu as pltpu
from jax.sharding import PartitionSpec as P

HI = lax.Precision.HIGHEST
REG_DEV = 8


def _full(shape):
    nd = len(shape)
    return pl.BlockSpec(shape, lambda i, _n=nd: (0,) * _n)


def _step_kernel(k, first, last, *refs):
    refs = list(refs)
    forced_ref = refs.pop(0)
    mask_ref, wx_ref, wy_ref, diff_ref, prior_ref = refs[:5]
    refs = refs[5:]
    if not first:
        ratio_in, inv_in, ss_ref = refs[:3]
        refs = refs[3:]
    if not last:
        next_forcing_ref = refs.pop(0)
    if first:
        ratio_ref, inv_ref = refs[:2]
        refs = refs[2:]
    else:
        ratio_ref, inv_ref = ratio_in, inv_in
    out_ref, ss_out_ref, red_ref = refs

    species, levels, rows, lanes = out_ref.shape
    zero = jnp.zeros((rows, lanes), jnp.float32)

    if first:
        carried = zero
        for l in range(levels):
            below = diff_ref[l - 1] if l > 0 else zero
            above = diff_ref[l] if l < levels - 1 else zero
            inverse = 1.0 / (1.0 + below + above + below * carried)
            ratio = -above * inverse
            ratio_ref[l] = ratio
            inv_ref[l] = inverse
            carried = ratio

    inside = mask_ref[...] > 0.5
    wx = wx_ref[k]
    wy = wy_ref[k]
    east = jnp.maximum(wx, 0.0)
    west = jnp.maximum(-wx, 0.0)
    north = jnp.maximum(wy, 0.0)
    south = jnp.maximum(-wy, 0.0)
    remain = 1.0 - (east + west + north + south)

    for s in range(species):

        def forward(l, reduced):
            f = forced_ref[s, l]
            if first:
                f = jnp.where(inside, f, 0.0)
            from_east = pltpu.roll(east * f, rows - 1, 0)
            from_west = pltpu.roll(west * f, 1, 0)
            from_north = pltpu.roll(north * f, lanes - 1, 1)
            from_south = pltpu.roll(south * f, 1, 1)
            moved = f * remain
            moved = moved + from_east + from_west
            moved = moved + from_north + from_south
            below = jnp.where(l > 0, diff_ref[jnp.maximum(l - 1, 0)], zero)
            reduced = (moved + below * reduced) * inv_ref[l]
            red_ref[l] = reduced
            return reduced

        lax.fori_loop(0, levels, forward, zero, unroll=4)

        def backward(i, result):
            l = levels - 1 - i
            result = red_ref[l] - ratio_ref[l] * result
            if last:
                out_ref[s, l] = result
            else:
                out_ref[s, l] = jnp.where(inside, result + next_forcing_ref[s, l], 0.0)
            return result

        surface = lax.fori_loop(0, levels, backward, zero, unroll=4)
        if first:
            ss_out_ref[s] = prior_ref[s] * surface
        else:
            ss_out_ref[s] = ss_ref[s] + prior_ref[s] * surface


def step_call(k, steps, forced, mask, wind_x, wind_y, diffusivity, prior, ratios, inverses,
              surface_sum, forcing):
    first = k == steps - 1
    last = k == 0
    species, levels, rows, lanes = forcing.shape[1:]
    state = jax.ShapeDtypeStruct((species, levels, rows, lanes), jnp.float32)
    plane = jax.ShapeDtypeStruct((levels, rows, lanes), jnp.float32)
    surf = jax.ShapeDtypeStruct(prior.shape, jnp.float32)
    block = (None, species, levels, rows, lanes)
    if first:
        in_specs = [pl.BlockSpec(block, lambda i: (k, 0, 0, 0, 0))]
        args = [forcing]
    else:
        in_specs = [_full(forced.shape)]
        args = [forced]
    for a in (mask, wind_x, wind_y, diffusivity, prior):
        in_specs.append(_full(a.shape))
        args.append(a)
    if not first:
        for a in (ratios, inverses, surface_sum):
            in_specs.append(_full(a.shape))
            args.append(a)
    if not last:
        in_specs.append(pl.BlockSpec(block, lambda i: (k - 1, 0, 0, 0, 0)))
        args.append(forcing)
    out_shape = [plane, plane] if first else []
    out_shape += [state, surf]
    return pl.pallas_call(
        functools.partial(_step_kernel, k, first, last),
        grid=(1,),
        in_specs=in_specs,
        out_specs=[_full(o.shape) for o in out_shape],
        out_shape=out_shape,
        scratch_shapes=[pltpu.VMEM((levels, rows, lanes), jnp.float32)],
    )(*args)


def extend(chans, halo, lanes):
    gx = lax.axis_size("gx")
    gy = lax.axis_size("gy")
    up_x = [(i, i + 1) for i in range(gx - 1)]
    down_x = [(i + 1, i) for i in range(gx - 1)]
    up_y = [(i, i + 1) for i in range(gy - 1)]
    down_y = [(i + 1, i) for i in range(gy - 1)]
    channels, rows, cols = chans.shape
    top = lax.ppermute(jnp.swapaxes(chans[:, rows - halo:], 0, 1), "gx", up_x)
    bottom = lax.ppermute(jnp.swapaxes(chans[:, :halo], 0, 1), "gx", down_x)
    ext = jnp.concatenate([jnp.swapaxes(top, 0, 1), chans, jnp.swapaxes(bottom, 0, 1)], axis=1)
    left = lax.ppermute(jnp.transpose(ext[:, :, cols - halo:], (2, 1, 0)), "gy", up_y)
    right = lax.ppermute(jnp.transpose(ext[:, :, :halo], (2, 1, 0)), "gy", down_y)
    gap = jnp.zeros((channels, rows + 2 * halo, lanes - cols - 2 * halo), jnp.float32)
    return jnp.concatenate(
        [ext, jnp.transpose(right, (2, 1, 0)), gap, jnp.transpose(left, (2, 1, 0))], axis=2)


def local(pixel_adjoint, pixel_owner, pixel_column, pixel_level, wind_x, wind_y,
          diffusivity, prior_emission, region_map):
    gx_n = lax.axis_size("gx")
    gy_n = lax.axis_size("gy")
    devices = gx_n * gy_n
    steps, rows, cols = wind_x.shape
    levels = diffusivity.shape[0] + 1
    species = prior_emission.shape[0]
    kernel = pixel_adjoint.shape[1] // species
    pixels = pixel_adjoint.shape[2]
    capacity = 2 * pixels // devices
    cells = rows * cols
    slots = devices * capacity
    halo = steps
    lanes = 2 * cols
    ext_rows = rows + 2 * halo

    owners = pixel_owner[:, :, 0]
    matches = (owners[:, :, None] == jnp.arange(devices, dtype=jnp.int32)).astype(jnp.int32)
    rank = jnp.sum(jnp.cumsum(matches, axis=1) * matches, axis=2) - 1
    position = owners * capacity + rank
    rows_out = jnp.concatenate(
        [pixel_adjoint, pixel_column.astype(jnp.float32)[:, None, :],
         pixel_level.astype(jnp.float32)[:, None, :]], axis=1)
    place = (position[:, :, None] == jnp.arange(slots, dtype=jnp.int32)).astype(jnp.float32)
    placed = jnp.einsum("kap,kpq->kaq", rows_out, place, precision=HI)
    received = lax.all_to_all(placed, ("gx", "gy"), 2, 2, tiled=True)

    payload = received[:, :species * kernel].reshape(steps, species, kernel, slots)
    column = jnp.round(received[:, species * kernel]).astype(jnp.int32)
    start = jnp.round(received[:, species * kernel + 1]).astype(jnp.int32)
    offset = jnp.arange(levels, dtype=jnp.int32)[None, :, None] - start[:, None, :]
    profile = jnp.zeros((steps, species, levels, slots), jnp.float32)
    for j in range(kernel):
        profile = profile + jnp.where((offset == j)[:, None], payload[:, :, j][:, :, None, :], 0.0)
    hits = (column[:, :, None] == jnp.arange(cells, dtype=jnp.int32)).astype(jnp.float32)
    forcing = jnp.einsum("ksq,kqc->ksc", profile.reshape(steps, species * levels, slots), hits,
                         precision=HI)

    chans = jnp.concatenate(
        [forcing.reshape(steps * species * levels, rows, cols), wind_x, wind_y, diffusivity],
        axis=0)
    ext = extend(chans, halo, lanes)
    n_f = steps * species * levels
    forcing_ext = ext[:n_f].reshape(steps, species, levels, ext_rows, lanes)
    wx_ext = ext[n_f:n_f + steps]
    wy_ext = ext[n_f + steps:n_f + 2 * steps]
    diff_ext = ext[n_f + 2 * steps:]

    gxi = lax.axis_index("gx")
    gyi = lax.axis_index("gy")
    r = jnp.arange(ext_rows, dtype=jnp.int32)[:, None]
    c = jnp.arange(lanes, dtype=jnp.int32)[None, :]
    grow = gxi * rows + r - halo
    ccol = jnp.where(c < cols + halo, c, c - lanes)
    gcol = gyi * cols + ccol
    inside = ((grow >= 0) & (grow < gx_n * rows) & (gcol >= 0) & (gcol < gy_n * cols)
              & ((c < cols + halo) | (c >= lanes - halo)))
    mask = inside.astype(jnp.float32)
    prior_ext = jnp.pad(prior_emission, ((0, 0), (halo, halo), (0, lanes - cols)))

    forced = None
    ratios = inverses = surface_sum = None
    for k in reversed(range(steps)):
        outs = step_call(k, steps, forced, mask, wx_ext, wy_ext, diff_ext, prior_ext, ratios,
                         inverses, surface_sum, forcing_ext)
        if k == steps - 1:
            ratios, inverses, forced, surface_sum = outs
        else:
            forced, surface_sum = outs
    adjoint = forced[:, :, halo:halo + rows, :cols]
    surface_sum = surface_sum[:, halo:halo + rows, :cols]

    nreg = REG_DEV * devices
    member = (region_map.reshape(-1)[:, None] == jnp.arange(nreg, dtype=jnp.int32)).astype(jnp.float32)
    partial = jnp.dot(surface_sum.reshape(species, cells), member, precision=HI)
    pieces = lax.all_to_all(partial.reshape(species, devices, nreg // devices), ("gx", "gy"), 1, 1,
                            tiled=True)
    gradient = jnp.sum(pieces, axis=1)
    return adjoint, gradient


def solution(mesh):
    in_specs = (
        P(None, None, ("gx", "gy")),
        P(None, ("gx", "gy"), None),
        P(None, ("gx", "gy")),
        P(None, ("gx", "gy")),
        P(None, "gx", "gy"),
        P(None, "gx", "gy"),
        P(None, "gx", "gy"),
        P(None, "gx", "gy"),
        P("gx", "gy"),
    )
    out_specs = (P(None, None, "gx", "gy"), P(None, ("gx", "gy")))
    return jax.shard_map(local, mesh=mesh, in_specs=in_specs, out_specs=out_specs, check_vma=False)
```

time: 163 us -> 129 us (0.79)
  starting transfers between devices: 44.9 us -> 17.4 us
  blocking collectives: 45.5 us -> 21.9 us
  local copies, waits for them, and re-layouts: 9.1 us -> 30 us
  waiting for transfers between devices: 29.3 us -> 18 us
  other arithmetic: 7.03 us -> 11.9 us
  Pallas kernels: 20.1 us -> 23.9 us
    ppermute x16 -> x4, starting transfers between devices: 44.9 us -> 10.4 us  [the longest x1 3.99 us: extend(): lax.ppermute(jnp.transpose(ext[:, :, cols - halo:], (2, 1, 0)), 'gy', up_y)]
    all_to_all x1 -> x0, blocking collectives: 23.6 us -> none  [local(): lax.all_to_all(partial.reshape(species, devices, nreg // devices), ('gx',...]
    ppermute x16 -> x4, waiting for transfers between devices: 29.3 us -> 9.82 us  [the longest x1 5.52 us: extend(): top = lax.ppermute(jnp.swapaxes(chans[:, rows - halo:], 0, 1), 'gx', up_x)]
    transpose x0 -> x4, local copies, waits for them, and re-layouts: none -> 11.1 us  [the longest x2 6.6 us: extend(): jnp.transpose(ext[:, :, :halo], (2, 1, 0))]
    all_to_all x0 -> x1, waiting for transfers between devices: none -> 8.19 us  [local(): lax.all_to_all(partial.reshape(species, devices, nreg // devices), ('gx',...]
    slice x0 -> x5, local copies, waits for them, and re-layouts: none -> 6.99 us  [the longest x1 2.88 us: local(): forcing_ext = ext[:n_f].reshape(steps, species, levels, ext_rows, lanes)]
    all_to_all x0 -> x1, starting transfers between devices: none -> 6.96 us  [local(): lax.all_to_all(partial.reshape(species, devices, nreg // devices), ('gx',...]
    ppermute x0 -> x2, local copies, waits for them, and re-layouts: none -> 6.28 us  [the longest x1 3.16 us: extend(): lax.ppermute(jnp.transpose(ext[:, :, :halo], (2, 1, 0)), 'gy', down_y)]
  transfers between devices with their start and end apart: 16 -> 5, of which waited for: 8 -> 3; matrix products, arithmetic and copies ran while one was open for 1% -> 7% of each run, Pallas kernels for 0% -> 0%
where the time goes in v1:
time: 129 us
  local copies, waits for them, and re-layouts  30 us (23%)
  Pallas kernels  23.9 us (19%)
  blocking collectives  21.9 us (17%)
  waiting for transfers between devices  18 us (14%)
  starting transfers between devices  17.4 us (13%)
  other arithmetic  11.9 us (9%)
  matrix products  4.78 us (4%)
    pallas_call x4, Pallas kernels, step_call(): pl.pallas_call(functools.partial(_step_kernel, k, first, last), grid=(1,)...  23.9 us
    all_to_all x1, blocking collectives, local(): received = lax.all_to_all(placed, ('gx', 'gy'), 2, 2, tiled=True)  21.9 us
    all_to_all x1, waiting for transfers between devices, local(): lax.all_to_all(partial.reshape(species, devices, nreg // devices), ('gx',...  8.19 us
    all_to_all x1, starting transfers between devices, local(): lax.all_to_all(partial.reshape(species, devices, nreg // devices), ('gx',...  6.96 us
    transpose x2, local copies, waits for them, and re-layouts, extend(): jnp.transpose(ext[:, :, :halo], (2, 1, 0))  6.6 us
    ppermute x1, waiting for transfers between devices, extend(): top = lax.ppermute(jnp.swapaxes(chans[:, rows - halo:], 0, 1), 'gx', up_x)  5.52 us
    ppermute x1, waiting for transfers between devices, extend(): bottom = lax.ppermute(jnp.swapaxes(chans[:, :halo], 0, 1), 'gx', down_x)  4.29 us
    ppermute x1, starting transfers between devices, extend(): lax.ppermute(jnp.transpose(ext[:, :, cols - halo:], (2, 1, 0)), 'gy', up_y)  3.99 us
  transfers between devices with their start and end apart: 5, of which 3 were waited for; matrix products, arithmetic and copies ran while one was open for 7% of the time, Pallas kernels for 0%

profile of v1, /device:TPU:1, one launch (start us, length us, event | category | flops | bytes accessed | tf_op | source)
XLA Modules:
  0.0 128.9 jit_solution(927487754317880032)
XLA Ops:
  0.6 0.8 fusion.8
  1.5 0.3 reduce_window_sum.11
  1.7 0.9 select_reduce_fusion
  2.6 0.7 multiply_add_fusion.1
  3.3 0.7 convert_element_type.31
  4.0 0.7 convert_element_type.32
  4.7 1.2 fusion.6
  5.9 0.2 copy.59
  6.2 0.6 reshape.213
  6.8 21.9 %all_to_all.10 = f32[128,1,272]{2,1,0:T(1,128)S(1)} all-to-all(f32[128,1,272]{2,1,0:T(1,128)S(1)} %reshape.213), channel_id=1, replica_groups=mesh['gx'=8,'gy'=16] {'gx','gy'}, dimensions={0} | all-to-all | bytes 278528 | tf_op jit(solution)/shard_map/all_to_all | solution.py:176
  28.6 0.5 broadcast.329
  29.2 1.1 reduce
  30.3 0.4 reshape.214
  30.7 0.6 fusion.35
  31.3 0.2 copy.87
  31.5 0.1 fusion.36
  31.6 0.2 copy.88
  31.8 0.4 fusion.24
  32.2 0.2 copy.89
  32.6 0.8 add_add_fusion
  33.3 1.7 %fusion = f32[4,80,1024]{2,1,0:T(8,128)S(1)} fusion(f32[4,80,256]{2,1,0:T(8,128)S(1)} %bitcast.80, s32[4,256]{1,0:T(4,128)S(1)} %convert_bitcast_fusion), kind=kOutput, calls=%fused_computation.2 | convolution fusion | flops 1007681536 | bytes 1642496 | tf_op jit(solution)/shard_map/ksq,kqc->ksc/dot_general | solution.py:186
  35.1 0.0 copy-start.1
  35.1 0.0 copy-start.2
  35.1 0.0 copy-start
  35.1 0.3 copy.90
  35.4 0.0 copy-start.3
  35.4 0.1 constant_dynamic-update-slice_fusion.3
  35.5 0.3 copy-done.1
  35.8 0.0 copy-done.2
  35.8 0.2 copy-done
  36.0 1.4 %slice_bitcast_fusion.3 = (f32[4,367,128]{2,0,1:T(4,128)}, f32[4,367,128]{2,0,1:T(4,128)}) fusion(f32[367,8,128]{2,1,0:T(8,128)S(1)} %constant_dynamic-update-slice_fusion), kind=kLoop, calls=%fused_computation.12 | loop fusion | bytes 3006464 | tf_op jit(solution)/shard_map/transpose | solution.py:140
  37.4 3.0 %collective-permute-start = (f32[4,367,128]{2,0,1:T(4,128)}, f32[4,367,128]{2,0,1:T(4,128)S(1)}, u32[]{:S(2)}, u32[]{:S(2)}) collective-permute-start(f32[4,367,128]{2,0,1:T(4,128)} %get-tuple-element.34), channel_id=1, source_target_pairs={{0,16},{16,32},{32,48},{48,64},{64,80},{80,96},{96,112},{1,17},{17... | collective-permute-start | bytes 2254856 | tf_op jit(solution)/shard_map/ppermute | solution.py:140
  40.4 1.9 %collective-permute-start.1 = (f32[4,367,128]{2,0,1:T(4,128)}, f32[4,367,128]{2,0,1:T(4,128)S(1)}, u32[]{:S(2)}, u32[]{:S(2)}) collective-permute-start(f32[4,367,128]{2,0,1:T(4,128)} %get-tuple-element.35), channel_id=1, source_target_pairs={{16,0},{32,16},{48,32},{64,48},{80,64},{96,80},{112,96},{17,1},{33... | collective-permute-start | bytes 2254856 | tf_op jit(solution)/shard_map/ppermute | solution.py:141
  42.4 0.0 copy-done.3
  42.4 0.6 pad.4.refs_5_
  43.0 0.1 pad.9.clone
  43.1 0.7 and_convert_fusion.refs_1_
  43.8 5.5 %collective-permute-done = f32[4,367,128]{2,0,1:T(4,128)S(1)} collective-permute-done((f32[4,367,128]{2,0,1:T(4,128)}, f32[4,367,128]{2,0,1:T(4,128)S(1)}, u32[]{:S(2)}, u32[]{:S(2)}) %collective-permute-start) | collective-permute-done | bytes 751648 | tf_op jit(solution)/shard_map/ppermute | solution.py:140
  49.3 4.3 %collective-permute-done.1 = f32[4,367,128]{2,0,1:T(4,128)S(1)} collective-permute-done((f32[4,367,128]{2,0,1:T(4,128)}, f32[4,367,128]{2,0,1:T(4,128)S(1)}, u32[]{:S(2)}, u32[]{:S(2)}) %collective-permute-start.1) | collective-permute-done | bytes 751648 | tf_op jit(solution)/shard_map/ppermute | solution.py:141
  53.6 0.6 pad_maximum_fusion.1
  54.2 3.4 %slice_bitcast_fusion.1 = (f32[4,16,367]{0,1,2:T(8,128)}, f32[4,16,367]{0,1,2:T(8,128)}) fusion(f32[367,16,128]{2,1,0:T(8,128)S(1)} %pad_maximum_fusion.1), kind=kLoop, calls=%fused_computation.6 | loop fusion | bytes 375808 | tf_op jit(solution)/shard_map/transpose | solution.py:144
  57.6 3.2 %copy.63 = f32[4,16,367]{2,1,0:T(8,128)S(1)} copy(f32[4,16,367]{0,1,2:T(8,128)} %get-tuple-element.32) | data formatting | bytes 187904 | tf_op jit(solution)/shard_map/transpose | solution.py:144
  60.8 1.5 %collective-permute-start.2 = (f32[4,16,367]{2,1,0:T(8,128)S(1)}, f32[4,16,367]{2,1,0:T(8,128)S(1)}, u32[]{:S(2)}, u32[]{:S(2)}) collective-permute-start(f32[4,16,367]{2,1,0:T(8,128)S(1)} %copy.63), channel_id=1, source_target_pairs={{1,0},{2,1},{3,2},{4,3},{5,4},{6,5},{7,6},{8,7},{9,8},{10,9},{11,1... | collective-permute-start | bytes 281864 | tf_op jit(solution)/shard_map/ppermute | solution.py:144
  62.3 3.2 %copy.65 = f32[4,16,367]{2,1,0:T(8,128)S(1)} copy(f32[4,16,367]{0,1,2:T(8,128)} %get-tuple-element.33) | data formatting | bytes 187904 | tf_op jit(solution)/shard_map/transpose | solution.py:143
  65.4 4.0 %collective-permute-start.3 = (f32[4,16,367]{2,1,0:T(8,128)S(1)}, f32[4,16,367]{2,1,0:T(8,128)S(1)}, u32[]{:S(2)}, u32[]{:S(2)}) collective-permute-start(f32[4,16,367]{2,1,0:T(8,128)S(1)} %copy.65), channel_id=1, source_target_pairs={{0,1},{1,2},{2,3},{3,4},{4,5},{5,6},{6,7},{7,8},{8,9},{9,10},{10,1... | collective-permute-start | bytes 281864 | tf_op jit(solution)/shard_map/ppermute | solution.py:143
  69.4 0.0 collective-permute-done.2
  69.4 3.2 %copy.64 = f32[4,16,367]{0,1,2:T(8,128)} copy(f32[4,16,367]{2,1,0:T(8,128)S(1)} %collective-permute-done.2) | data formatting | bytes 187904 | tf_op jit(solution)/shard_map/ppermute | solution.py:144
  72.6 0.0 collective-permute-done.3
  72.6 3.1 %copy.66 = f32[4,16,367]{0,1,2:T(8,128)} copy(f32[4,16,367]{2,1,0:T(8,128)S(1)} %collective-permute-done.3) | data formatting | bytes 187904 | tf_op jit(solution)/shard_map/ppermute | solution.py:143
  75.7 3.6 %pad_maximum_fusion = f32[367,16,256]{2,1,0:T(8,128)S(1)} fusion(f32[367,16,4]{2,1,0:T(8,128)} %bitcast.70, f32[367,16,4]{2,1,0:T(8,128)} %bitcast.69, f32[367,4,128]{2,1,0:T(4,128)S(1)} %bitcast.78, f32[367,8,128]{2,1,0:T(8,128)S(1)} %constant_dynamic-update-slice_fusion, f32[367,4,128]{2,1,0:T(4,128)S(1)} %bitcast.76, f32[256]{0:T(256)S(1)} %pad.9.clone), kind=kLoop, calls=%fused_computation | loop fusion | flops 7516160 | bytes 9208320 | tf_op jit(solution)/shard_map/concatenate | solution.py:146
  79.4 2.9 %slice.139 = f32[320,16,256]{2,1,0:T(8,128)} slice(f32[367,16,256]{2,1,0:T(8,128)S(1)} %pad_maximum_fusion), slice={[0:320], [0:16], [0:256]} | slice | bytes 10485760 | tf_op jit(solution)/shard_map/slice | solution.py:194
  82.2 0.9 slice.142.refs_4_
  83.1 0.6 fusion.34
  83.8 6.4 %shard_map.104 = (f32[40,16,256]{2,1,0:T(8,128)}, f32[40,16,256]{2,1,0:T(8,128)}, f32[2,40,16,256]{3,2,1,0:T(8,128)}, f32[2,16,256]{2,1,0:T(8,128)}) custom-call(f32[4,2,40,16,256]{4,3,2,1,0:T(8,128)} %bitcast.65, f32[16,256]{1,0:T(8,128)} %and_convert_fusion.refs_1_, f32[4,16,256]{2,1,0:T(8,128)} %get-tuple-element.31.refs_2_, ...), custom_call_target="tpu_custom_call" | custom-call | tf_op jit(solution)/shard_map/pallas_call | solution.py:122
  90.2 6.0 %shard_map.105 = (f32[2,40,16,256]{3,2,1,0:T(8,128)}, f32[2,16,256]{2,1,0:T(8,128)}) custom-call(f32[2,40,16,256]{3,2,1,0:T(8,128)} %get-tuple-element.12.refs_0_, f32[16,256]{1,0:T(8,128)} %and_convert_fusion.refs_1_, f32[4,16,256]{2,1,0:T(8,128)} %get-tuple-element.31.refs_2_, f32[4,16,256]{2,1,0:T(8,128)} %get-tuple-element.30.refs_3_, ...), custom_call_target="tpu_custom_call" | custom-call | tf_op jit(solution)/shard_map/pallas_call | solution.py:122
  96.2 6.0 %shard_map.106 = (f32[2,40,16,256]{3,2,1,0:T(8,128)}, f32[2,16,256]{2,1,0:T(8,128)}) custom-call(f32[2,40,16,256]{3,2,1,0:T(8,128)} %get-tuple-element.16.refs_0_, f32[16,256]{1,0:T(8,128)} %and_convert_fusion.refs_1_, f32[4,16,256]{2,1,0:T(8,128)} %get-tuple-element.31.refs_2_, f32[4,16,256]{2,1,0:T(8,128)} %get-tuple-element.30.refs_3_, ...), custom_call_target="tpu_custom_call" | custom-call | tf_op jit(solution)/shard_map/pallas_call | solution.py:122
  102.2 5.5 %shard_map.107 = (f32[2,40,16,256]{3,2,1,0:T(8,128)}, f32[2,16,256]{2,1,0:T(8,128)}) custom-call(f32[2,40,16,256]{3,2,1,0:T(8,128)} %get-tuple-element.18.refs_0_, f32[16,256]{1,0:T(8,128)} %and_convert_fusion.refs_1_, f32[4,16,256]{2,1,0:T(8,128)} %get-tuple-element.31.refs_2_, f32[4,16,256]{2,1,0:T(8,128)} %get-tuple-element.30.refs_3_, ...), custom_call_target="tpu_custom_call" | custom-call | tf_op jit(solution)/shard_map/pallas_call | solution.py:122
  107.7 0.7 slice.115
  108.4 1.9 %fusion.1 = f32[2,128,8]{1,0,2:T(2,128)S(1)} fusion(f32[2,1024,1]{1,0,2:T(2,128)S(1)} %reshape.211, s32[128,8]{0,1:T(8,128)S(1)} %multiply_add_fusion, s32[1024]{0:T(1024)S(1)} %bitcast.88), kind=kOutput, calls=%fused_computation.3 | convolution fusion | flops 26214400 | bytes 24576 | tf_op jit(solution)/shard_map/dot_general | solution.py:225
  110.3 0.8 copy.67
  111.1 7.0 %all-to-all-start.1 = ((f32[2,128,8]{2,0,1:T(2,128)}), f32[2,128,8]{2,0,1:T(2,128)S(1)}, u32[]{:S(2)}, u32[]{:S(2)}) async-start(f32[2,128,8]{2,0,1:T(2,128)} %copy.67), calls=%async_computation.1 | async-start | bytes 262144 | tf_op jit(solution)/shard_map/all_to_all | solution.py:226
  118.1 1.9 %slice.114 = f32[2,40,8,128]{3,2,1,0:T(8,128)} slice(f32[2,40,16,256]{3,2,1,0:T(8,128)} %get-tuple-element.20), slice={[0:2], [0:40], [4:12], [0:128]} | slice | bytes 655360 | tf_op jit(solution)/shard_map/slice | solution.py:220
  120.0 8.2 %all-to-all-done.1 = f32[2,128,8]{2,0,1:T(2,128)S(1)} async-done(((f32[2,128,8]{2,0,1:T(2,128)}), f32[2,128,8]{2,0,1:T(2,128)S(1)}, u32[]{:S(2)}, u32[]{:S(2)}) %all-to-all-start.1) | async-done | bytes 8224 | tf_op jit(solution)/shard_map/all_to_all | solution.py:226
  128.2 0.7 reduce_sum.19
  (22 shorter events, 0.2 us)
Async XLA Ops:
  35.1 0.7 copy-start.1
  35.1 0.7 copy-start.2
  35.1 0.9 copy-start
  35.4 7.0 %copy-start.3 = (f32[2,8,128]{2,1,0:T(8,128)S(1)}, f32[2,8,128]{2,1,0:T(8,128)}, u32[]{:S(2)}) copy-start(f32[2,8,128]{2,1,0:T(8,128)} %param.16) | copy-start | bytes 24580
  37.4 11.9 %collective-permute-start = (f32[4,367,128]{2,0,1:T(4,128)}, f32[4,367,128]{2,0,1:T(4,128)S(1)}, u32[]{:S(2)}, u32[]{:S(2)}) collective-permute-start(f32[4,367,128]{2,0,1:T(4,128)} %get-tuple-element.34), channel_id=1, source_target_pairs={{0,16},{16,32},{32,48},{48,64},{64,80},{80,96},{96,112},{1,17},{17... | collective-permute-start | bytes 2254856 | tf_op jit(solution)/shard_map/ppermute | solution.py:140
  40.4 13.1 %collective-permute-start.1 = (f32[4,367,128]{2,0,1:T(4,128)}, f32[4,367,128]{2,0,1:T(4,128)S(1)}, u32[]{:S(2)}, u32[]{:S(2)}) collective-permute-start(f32[4,367,128]{2,0,1:T(4,128)} %get-tuple-element.35), channel_id=1, source_target_pairs={{16,0},{32,16},{48,32},{64,48},{80,64},{96,80},{112,96},{17,1},{33... | collective-permute-start | bytes 2254856 | tf_op jit(solution)/shard_map/ppermute | solution.py:141
  60.8 8.6 %collective-permute-start.2 = (f32[4,16,367]{2,1,0:T(8,128)S(1)}, f32[4,16,367]{2,1,0:T(8,128)S(1)}, u32[]{:S(2)}, u32[]{:S(2)}) collective-permute-start(f32[4,16,367]{2,1,0:T(8,128)S(1)} %copy.63), channel_id=1, source_target_pairs={{1,0},{2,1},{3,2},{4,3},{5,4},{6,5},{7,6},{8,7},{9,8},{10,9},{11,1... | collective-permute-start | bytes 281864 | tf_op jit(solution)/shard_map/ppermute | solution.py:144
  65.4 7.2 %collective-permute-start.3 = (f32[4,16,367]{2,1,0:T(8,128)S(1)}, f32[4,16,367]{2,1,0:T(8,128)S(1)}, u32[]{:S(2)}, u32[]{:S(2)}) collective-permute-start(f32[4,16,367]{2,1,0:T(8,128)S(1)} %copy.65), channel_id=1, source_target_pairs={{0,1},{1,2},{2,3},{3,4},{4,5},{5,6},{6,7},{7,8},{8,9},{9,10},{10,1... | collective-permute-start | bytes 281864 | tf_op jit(solution)/shard_map/ppermute | solution.py:143
  102.2 6.2 %copy-start.4 = (s32[8,128]{1,0:T(8,128)S(1)}, s32[8,128]{1,0:T(8,128)}, u32[]{:S(2)}) copy-start(s32[8,128]{1,0:T(8,128)} %param.17) | copy-start | bytes 12292
  111.1 17.0 %all-to-all-start.1 = ((f32[2,128,8]{2,0,1:T(2,128)}), f32[2,128,8]{2,0,1:T(2,128)S(1)}, u32[]{:S(2)}, u32[]{:S(2)}) async-start(f32[2,128,8]{2,0,1:T(2,128)} %copy.67), calls=%async_computation.1 | async-start | bytes 262144 | tf_op jit(solution)/shard_map/all_to_all | solution.py:226

commit v2 on v1

--- a/solution.py
+++ b/solution.py
@@ -18,23 +18,33 @@
 
 def _step_kernel(k, first, last, *refs):
     refs = list(refs)
-    forced_ref = refs.pop(0)
+    if first:
+        own_ref, xh_ref, yh_ref = refs[:3]
+        refs = refs[3:]
+    else:
+        forced_ref = refs.pop(0)
     mask_ref, wx_ref, wy_ref, diff_ref, prior_ref = refs[:5]
     refs = refs[5:]
     if not first:
         ratio_in, inv_in, ss_ref = refs[:3]
         refs = refs[3:]
     if not last:
-        next_forcing_ref = refs.pop(0)
+        nown_ref, nxh_ref, nyh_ref = refs[:3]
+        refs = refs[3:]
     if first:
         ratio_ref, inv_ref = refs[:2]
         refs = refs[2:]
     else:
         ratio_ref, inv_ref = ratio_in, inv_in
-    out_ref, ss_out_ref, red_ref = refs
-
-    species, levels, rows, lanes = out_ref.shape
+    out_ref, ss_out_ref, red_ref = refs[:3]
+    if first:
+        forced_ref = refs[3]
+
+    species, levels = ss_out_ref.shape[0], red_ref.shape[0]
+    rows, lanes = red_ref.shape[1:]
+    tr, tc = ss_out_ref.shape[1:]
     zero = jnp.zeros((rows, lanes), jnp.float32)
+    inside = mask_ref[...] > 0.5
 
     if first:
         carried = zero
@@ -46,8 +56,17 @@
             ratio_ref[l] = ratio
             inv_ref[l] = inverse
             carried = ratio
-
-    inside = mask_ref[...] > 0.5
+        for s in range(species):
+
+            def assemble(l, carry):
+                forced_ref[s, l, :tr, :tc] = own_ref[s, l]
+                forced_ref[s, l, tr:, :tc] = xh_ref[s, l]
+                forced_ref[s, l, :, tc:] = yh_ref[s, l]
+                forced_ref[s, l] = jnp.where(inside, forced_ref[s, l], 0.0)
+                return carry
+
+            lax.fori_loop(0, levels, assemble, 0, unroll=4)
+
     wx = wx_ref[k]
     wy = wy_ref[k]
     east = jnp.maximum(wx, 0.0)
@@ -60,8 +79,6 @@
 
         def forward(l, reduced):
             f = forced_ref[s, l]
-            if first:
-                f = jnp.where(inside, f, 0.0)
             from_east = pltpu.roll(east * f, rows - 1, 0)
             from_west = pltpu.roll(west * f, 1, 0)
             from_north = pltpu.roll(north * f, lanes - 1, 1)
@@ -80,33 +97,45 @@
             l = levels - 1 - i
             result = red_ref[l] - ratio_ref[l] * result
             if last:
-                out_ref[s, l] = result
+                out_ref[s, l] = result[:tr, :tc]
             else:
-                out_ref[s, l] = jnp.where(inside, result + next_forcing_ref[s, l], 0.0)
+                out_ref[s, l, :tr, :tc] = jnp.where(
+                    inside[:tr, :tc], result[:tr, :tc] + nown_ref[s, l], 0.0)
+                out_ref[s, l, tr:, :tc] = jnp.where(
+                    inside[tr:, :tc], result[tr:, :tc] + nxh_ref[s, l], 0.0)
+                out_ref[s, l, :, tc:] = jnp.where(
+                    inside[:, tc:], result[:, tc:] + nyh_ref[s, l], 0.0)
             return result
 
         surface = lax.fori_loop(0, levels, backward, zero, unroll=4)
         if first:
-            ss_out_ref[s] = prior_ref[s] * surface
+            ss_out_ref[s] = prior_ref[s] * surface[:tr, :tc]
         else:
-            ss_out_ref[s] = ss_ref[s] + prior_ref[s] * surface
+            ss_out_ref[s] = ss_ref[s] + prior_ref[s] * surface[:tr, :tc]
 
 
 def step_call(k, steps, forced, mask, wind_x, wind_y, diffusivity, prior, ratios, inverses,
-              surface_sum, forcing):
+              surface_sum, own, xh, yh):
     first = k == steps - 1
     last = k == 0
-    species, levels, rows, lanes = forcing.shape[1:]
-    state = jax.ShapeDtypeStruct((species, levels, rows, lanes), jnp.float32)
-    plane = jax.ShapeDtypeStruct((levels, rows, lanes), jnp.float32)
+    species, levels, rows, cols = own.shape[1:]
+    rows_e, lanes = mask.shape
+    ext = jax.ShapeDtypeStruct((species, levels, rows_e, lanes), jnp.float32)
+    tile = jax.ShapeDtypeStruct((species, levels, rows, cols), jnp.float32)
+    plane = jax.ShapeDtypeStruct((levels, rows_e, lanes), jnp.float32)
     surf = jax.ShapeDtypeStruct(prior.shape, jnp.float32)
-    block = (None, species, levels, rows, lanes)
-    if first:
-        in_specs = [pl.BlockSpec(block, lambda i: (k, 0, 0, 0, 0))]
-        args = [forcing]
+
+    def blocks(step):
+        return [pl.BlockSpec((None,) + a.shape[1:], lambda i, _s=step: (_s, 0, 0, 0, 0))
+                for a in (own, xh, yh)]
+
+    in_specs, args = [], []
+    if first:
+        in_specs += blocks(k)
+        args += [own, xh, yh]
     else:
-        in_specs = [_full(forced.shape)]
-        args = [forced]
+        in_specs.append(_full(forced.shape))
+        args.append(forced)
     for a in (mask, wind_x, wind_y, diffusivity, prior):
         in_specs.append(_full(a.shape))
         args.append(a)
@@ -115,36 +144,43 @@
             in_specs.append(_full(a.shape))
             args.append(a)
     if not last:
-        in_specs.append(pl.BlockSpec(block, lambda i: (k - 1, 0, 0, 0, 0)))
-        args.append(forcing)
+        in_specs += blocks(k - 1)
+        args += [own, xh, yh]
     out_shape = [plane, plane] if first else []
-    out_shape += [state, surf]
+    out_shape += [tile if last else ext, surf]
+    scratch = [pltpu.VMEM((levels, rows_e, lanes), jnp.float32)]
+    if first:
+        scratch.append(pltpu.VMEM((species, levels, rows_e, lanes), jnp.float32))
     return pl.pallas_call(
         functools.partial(_step_kernel, k, first, last),
         grid=(1,),
         in_specs=in_specs,
         out_specs=[_full(o.shape) for o in out_shape],
         out_shape=out_shape,
-        scratch_shapes=[pltpu.VMEM((levels, rows, lanes), jnp.float32)],
+        scratch_shapes=scratch,
     )(*args)
 
 
-def extend(chans, halo, lanes):
-    gx = lax.axis_size("gx")
-    gy = lax.axis_size("gy")
-    up_x = [(i, i + 1) for i in range(gx - 1)]
-    down_x = [(i + 1, i) for i in range(gx - 1)]
-    up_y = [(i, i + 1) for i in range(gy - 1)]
-    down_y = [(i + 1, i) for i in range(gy - 1)]
-    channels, rows, cols = chans.shape
-    top = lax.ppermute(jnp.swapaxes(chans[:, rows - halo:], 0, 1), "gx", up_x)
-    bottom = lax.ppermute(jnp.swapaxes(chans[:, :halo], 0, 1), "gx", down_x)
-    ext = jnp.concatenate([jnp.swapaxes(top, 0, 1), chans, jnp.swapaxes(bottom, 0, 1)], axis=1)
-    left = lax.ppermute(jnp.transpose(ext[:, :, cols - halo:], (2, 1, 0)), "gy", up_y)
-    right = lax.ppermute(jnp.transpose(ext[:, :, :halo], (2, 1, 0)), "gy", down_y)
-    gap = jnp.zeros((channels, rows + 2 * halo, lanes - cols - 2 * halo), jnp.float32)
-    return jnp.concatenate(
-        [ext, jnp.transpose(right, (2, 1, 0)), gap, jnp.transpose(left, (2, 1, 0))], axis=2)
+def _pairs(axis):
+    n = lax.axis_size(axis)
+    return [(i, i + 1) for i in range(n - 1)], [(i + 1, i) for i in range(n - 1)]
+
+
+def extend(tile, halo):
+    up_x, down_x = _pairs("gx")
+    up_y, down_y = _pairs("gy")
+    rows, cols = tile.shape[-2:]
+    below = lax.ppermute(tile[..., :halo, :], "gx", down_x)
+    above = lax.ppermute(tile[..., rows - halo:, :], "gx", up_x)
+    xh = jnp.concatenate([below, jnp.zeros_like(below)[..., :rows - 2 * halo, :], above], axis=-2)
+    tall = jnp.concatenate([tile, xh], axis=-2)
+    right = lax.ppermute(jnp.swapaxes(tall[..., :halo], -1, -3), "gy", down_y)
+    left = lax.ppermute(jnp.swapaxes(tall[..., cols - halo:], -1, -3), "gy", up_y)
+    right = jnp.swapaxes(right, -1, -3)
+    left = jnp.swapaxes(left, -1, -3)
+    gap = jnp.zeros(right.shape[:-1] + (cols - 2 * halo,), jnp.float32)
+    yh = jnp.concatenate([right, gap, left], axis=-1)
+    return xh, yh
 
 
 def local(pixel_adjoint, pixel_owner, pixel_column, pixel_level, wind_x, wind_y,
@@ -162,7 +198,7 @@
     slots = devices * capacity
     halo = steps
     lanes = 2 * cols
-    ext_rows = rows + 2 * halo
+    ext_rows = 2 * rows
 
     owners = pixel_owner[:, :, 0]
     matches = (owners[:, :, None] == jnp.arange(devices, dtype=jnp.int32)).astype(jnp.int32)
@@ -186,39 +222,36 @@
     forcing = jnp.einsum("ksq,kqc->ksc", profile.reshape(steps, species * levels, slots), hits,
                          precision=HI)
 
-    chans = jnp.concatenate(
-        [forcing.reshape(steps * species * levels, rows, cols), wind_x, wind_y, diffusivity],
-        axis=0)
-    ext = extend(chans, halo, lanes)
-    n_f = steps * species * levels
-    forcing_ext = ext[:n_f].reshape(steps, species, levels, ext_rows, lanes)
-    wx_ext = ext[n_f:n_f + steps]
-    wy_ext = ext[n_f + steps:n_f + 2 * steps]
-    diff_ext = ext[n_f + 2 * steps:]
+    own = forcing.reshape(steps, species, levels, rows, cols)
+    xh, yh = extend(own, halo)
+    statics = jnp.concatenate([wind_x, wind_y, diffusivity], axis=0)
+    sxh, syh = extend(statics, halo)
+    statics = jnp.concatenate([jnp.concatenate([statics, sxh], axis=1), syh], axis=2)
+    wx_ext = statics[:steps]
+    wy_ext = statics[steps:2 * steps]
+    diff_ext = statics[2 * steps:]
 
     gxi = lax.axis_index("gx")
     gyi = lax.axis_index("gy")
     r = jnp.arange(ext_rows, dtype=jnp.int32)[:, None]
     c = jnp.arange(lanes, dtype=jnp.int32)[None, :]
-    grow = gxi * rows + r - halo
+    grow = gxi * rows + jnp.where(r < rows + halo, r, r - ext_rows)
     ccol = jnp.where(c < cols + halo, c, c - lanes)
     gcol = gyi * cols + ccol
     inside = ((grow >= 0) & (grow < gx_n * rows) & (gcol >= 0) & (gcol < gy_n * cols)
               & ((c < cols + halo) | (c >= lanes - halo)))
     mask = inside.astype(jnp.float32)
-    prior_ext = jnp.pad(prior_emission, ((0, 0), (halo, halo), (0, lanes - cols)))
 
     forced = None
     ratios = inverses = surface_sum = None
     for k in reversed(range(steps)):
-        outs = step_call(k, steps, forced, mask, wx_ext, wy_ext, diff_ext, prior_ext, ratios,
-                         inverses, surface_sum, forcing_ext)
+        outs = step_call(k, steps, forced, mask, wx_ext, wy_ext, diff_ext, prior_emission,
+                         ratios, inverses, surface_sum, own, xh, yh)
         if k == steps - 1:
             ratios, inverses, forced, surface_sum = outs
         else:
             forced, surface_sum = outs
-    adjoint = forced[:, :, halo:halo + rows, :cols]
-    surface_sum = surface_sum[:, halo:halo + rows, :cols]
+    adjoint = forced
 
     nreg = REG_DEV * devices
     member = (region_map.reshape(-1)[:, None] == jnp.arange(nreg, dtype=jnp.int32)).astype(jnp.float32)

time: 129 us -> 137 us (1.062)
  starting transfers between devices: 17.4 us -> 34.9 us
  local copies, waits for them, and re-layouts: 30 us -> 19.8 us
  waiting for transfers between devices: 18 us -> 11.6 us
  other arithmetic: 11.9 us -> 15.9 us
  blocking collectives: 21.9 us -> 24.2 us
    ppermute x4 -> x8, starting transfers between devices: 10.4 us -> 23.4 us  [the longest x2 9.68 us: extend(): lax.ppermute(jnp.swapaxes(tall[..., cols - halo:], -1, -3), 'gy', up_y)]
    slice x5 -> x4, local copies, waits for them, and re-layouts: 6.99 us -> 1.77 us  [the longest x1 0.88 us: local(): diff_ext = statics[2 * steps:]]
    all_to_all x1, waiting for transfers between devices: 8.19 us -> 3.16 us  [local(): received = lax.all_to_all(placed, ('gx', 'gy'), 2, 2, tiled=True)]
    all_to_all x1, starting transfers between devices: 6.96 us -> 11.5 us  [local(): received = lax.all_to_all(placed, ('gx', 'gy'), 2, 2, tiled=True)]
    transpose x4, local copies, waits for them, and re-layouts: 11.1 us -> 7.18 us  [the longest x3 5.36 us: extend(): right = lax.ppermute(jnp.swapaxes(tall[..., :halo], -1, -3), 'gy', down_y)]
    concatenate x2 -> x5, other arithmetic: 4.22 us -> 8.08 us  [the longest x1 3.99 us: extend(): yh = jnp.concatenate([right, gap, left], axis=-1)]
    all_to_all x1, blocking collectives: 21.9 us -> 24.2 us  [local(): lax.all_to_all(partial.reshape(species, devices, nreg // devices), ('gx',...]
    ppermute x4 -> x8, waiting for transfers between devices: 9.82 us -> 8.42 us  [the longest x2 6.63 us: extend(): right = lax.ppermute(jnp.swapaxes(tall[..., :halo], -1, -3), 'gy', down_y)]
  transfers between devices with their start and end apart: 5 -> 9, of which waited for: 3 -> 5; matrix products, arithmetic and copies ran while one was open for 7% -> 7% of each run, Pallas kernels for 0% -> 0%
where the time goes in v2:
time: 137 us; the launch traced here: 136 us
  starting transfers between devices  34.9 us (25%)
  blocking collectives  24.2 us (18%)
  Pallas kernels  23.6 us (17%)
  local copies, waits for them, and re-layouts  19.8 us (14%)
  other arithmetic  15.9 us (12%)
  waiting for transfers between devices  11.6 us (8%)
  matrix products  4.78 us (3%)
    all_to_all x1, blocking collectives, local(): lax.all_to_all(partial.reshape(species, devices, nreg // devices), ('gx',...  24.2 us
    pallas_call x4, Pallas kernels, step_call(): pl.pallas_call(functools.partial(_step_kernel, k, first, last), grid=(1,)...  23.6 us
    all_to_all x1, starting transfers between devices, local(): received = lax.all_to_all(placed, ('gx', 'gy'), 2, 2, tiled=True)  11.5 us
    ppermute x2, starting transfers between devices, extend(): lax.ppermute(jnp.swapaxes(tall[..., cols - halo:], -1, -3), 'gy', up_y)  9.68 us
    ppermute x2, waiting for transfers between devices, extend(): right = lax.ppermute(jnp.swapaxes(tall[..., :halo], -1, -3), 'gy', down_y)  6.63 us
    ppermute x2, starting transfers between devices, extend(): below = lax.ppermute(tile[..., :halo, :], 'gx', down_x)  5.59 us
    ppermute x2, starting transfers between devices, extend(): above = lax.ppermute(tile[..., rows - halo:, :], 'gx', up_x)  5.56 us
    transpose x3, local copies, waits for them, and re-layouts, extend(): right = lax.ppermute(jnp.swapaxes(tall[..., :halo], -1, -3), 'gy', down_y)  5.36 us
  transfers between devices with their start and end apart: 9, of which 5 were waited for; matrix products, arithmetic and copies ran while one was open for 7% of the time, Pallas kernels for 0%

profile of v2, /device:TPU:1, one launch (start us, length us, event | category | flops | bytes accessed | tf_op | source)
XLA Modules:
  0.0 135.7 jit_solution(8289448334508001946)
XLA Ops:
  0.7 0.9 fusion.8
  1.5 0.3 reduce_window_sum.11
  1.8 0.9 select_reduce_fusion
  2.7 0.7 multiply_add_fusion.1
  3.4 0.7 convert_element_type.29
  4.1 0.7 convert_element_type.30
  4.8 1.2 fusion.6
  6.0 0.2 copy.59
  6.2 1.3 reshape.217
  7.5 11.5 %all-to-all-start = ((f32[128,1,272]{2,1,0:T(1,128)}), f32[128,1,272]{2,1,0:T(1,128)S(1)}, u32[]{:S(2)}, u32[]{:S(2)}) async-start(f32[128,1,272]{2,1,0:T(1,128)} %reshape.217), calls=%async_computation | async-start | bytes 393216 | tf_op jit(solution)/shard_map/all_to_all | solution.py:212
  19.1 3.0 %collective-permute-start.4 = (f32[47,4,128]{2,1,0:T(4,128)S(1)}, f32[47,4,128]{2,1,0:T(4,128)S(1)}, u32[]{:S(2)}, u32[]{:S(2)}) collective-permute-start(f32[47,4,128]{2,1,0:T(4,128)S(1)} %get-tuple-element.40), channel_id=1, source_target_pairs={{16,0},{32,16},{48,32},{64,48},{80,64},{96,80},{112,96},{17,1},{33... | collective-permute-start | bytes 288776 | tf_op jit(solution)/shard_map/ppermute | solution.py:173
  22.1 2.6 %collective-permute-start.5 = (f32[47,4,128]{2,1,0:T(4,128)S(1)}, f32[47,4,128]{2,1,0:T(4,128)S(1)}, u32[]{:S(2)}, u32[]{:S(2)}) collective-permute-start(f32[47,4,128]{2,1,0:T(4,128)S(1)} %get-tuple-element.41), channel_id=1, source_target_pairs={{0,16},{16,32},{32,48},{48,64},{64,80},{80,96},{96,112},{1,17},{17... | collective-permute-start | bytes 288776 | tf_op jit(solution)/shard_map/ppermute | solution.py:174
  24.8 0.7 and_convert_fusion.refs_3_.refs_1_
  25.4 0.7 collective-permute-done.4
  26.1 0.2 collective-permute-done.5
  26.4 0.1 pad_maximum_fusion.4
  26.4 3.2 %all-to-all-done = f32[128,1,272]{2,1,0:T(1,128)S(1)} async-done(((f32[128,1,272]{2,1,0:T(1,128)}), f32[128,1,272]{2,1,0:T(1,128)S(1)}, u32[]{:S(2)}, u32[]{:S(2)}) %all-to-all-start) | async-done | bytes 139296 | tf_op jit(solution)/shard_map/all_to_all | solution.py:212
  29.6 0.5 broadcast.339
  30.1 1.1 reduce
  31.2 0.4 reshape.218
  31.7 0.6 fusion.37
  32.3 0.2 copy.87
  32.5 0.1 fusion.39
  32.6 0.2 copy.88
  32.8 0.4 fusion.24
  33.1 0.2 copy.89
  33.5 0.8 add_add_fusion
  34.3 1.7 %fusion = f32[4,80,1024]{2,1,0:T(8,128)S(1)} fusion(f32[4,80,256]{2,1,0:T(8,128)S(1)} %bitcast.77, s32[4,256]{1,0:T(4,128)S(1)} %convert_bitcast_fusion), kind=kOutput, calls=%fused_computation.1 | convolution fusion | flops 1007681536 | bytes 1642496 | tf_op jit(solution)/shard_map/ksq,kqc->ksc/dot_general | solution.py:222
  36.0 0.3 copy.90
  36.3 0.2 fusion.35
  36.5 2.6 %collective-permute-start = (f32[4,2,40,4,128]{4,3,2,1,0:T(4,128)S(1)}, f32[4,2,40,4,128]{4,3,2,1,0:T(4,128)S(1)}, u32[]{:S(2)}, u32[]{:S(2)}) collective-permute-start(f32[4,2,40,4,128]{4,3,2,1,0:T(4,128)S(1)} %get-tuple-element.32), channel_id=1, source_target_pairs={{16,0},{32,16},{48,32},{64,48},{80,64},{96,80},{112,96},{17,1},{33... | collective-permute-start | bytes 1966088 | tf_op jit(solution)/shard_map/ppermute | solution.py:173
  39.1 3.0 %collective-permute-start.1 = (f32[4,2,40,4,128]{4,3,2,1,0:T(4,128)S(1)}, f32[4,2,40,4,128]{4,3,2,1,0:T(4,128)}, u32[]{:S(2)}, u32[]{:S(2)}) collective-permute-start(f32[4,2,40,4,128]{4,3,2,1,0:T(4,128)S(1)} %get-tuple-element.33), channel_id=1, source_target_pairs={{0,16},{16,32},{32,48},{48,64},{64,80},{80,96},{96,112},{1,17},{17... | collective-permute-start | bytes 1966088 | tf_op jit(solution)/shard_map/ppermute | solution.py:174
  42.1 0.2 slice_bitcast_fusion.3
  42.3 1.3 collective-permute-start.6
  43.6 4.0 %collective-permute-start.7 = (f32[4,16,47]{0,1,2:T(8,128)S(1)}, f32[4,16,47]{0,1,2:T(8,128)S(1)}, u32[]{:S(2)}, u32[]{:S(2)}) collective-permute-start(f32[4,16,47]{0,1,2:T(8,128)S(1)} %get-tuple-element.39), channel_id=1, source_target_pairs={{0,1},{1,2},{2,3},{3,4},{4,5},{5,6},{6,7},{7,8},{8,9},{9,10},{10,1... | collective-permute-start | bytes 36104 | tf_op jit(solution)/shard_map/ppermute | solution.py:178
  47.6 0.1 pad.10.clone
  47.7 0.1 pad.4.clone
  47.7 6.6 %collective-permute-done.6 = f32[4,16,47]{0,1,2:T(8,128)S(1)} collective-permute-done((f32[4,16,47]{0,1,2:T(8,128)S(1)}, f32[4,16,47]{0,1,2:T(8,128)S(1)}, u32[]{:S(2)}, u32[]{:S(2)}) %collective-permute-start.6) | collective-permute-done | bytes 12064 | tf_op jit(solution)/shard_map/ppermute | solution.py:177
  54.4 0.9 collective-permute-done.7
  55.2 0.2 pad_maximum_fusion.3
  55.4 0.9 slice.149.refs_6_.refs_4_
  56.3 0.7 fusion.36
  57.0 0.0 collective-permute-done
  57.0 0.0 collective-permute-done.1
  57.0 1.5 %pad_maximum_fusion = f32[4,2,40,16,128]{4,3,2,1,0:T(8,128)S(1)} fusion(f32[4,2,40,4,128]{4,3,2,1,0:T(4,128)} %collective-permute-done.1, f32[4,2,40,4,128]{4,3,2,1,0:T(4,128)S(1)} %collective-permute-done, f32[4,2,40,8,128]{4,3,2,1,0:T(8,128)S(1)} %bitcast.66), kind=kLoop, calls=%fused_computation.6 | loop fusion | flops 1310720 | bytes 5242880 | tf_op jit(solution)/shard_map/concatenate | solution.py:176
  58.4 2.4 %slice_bitcast_fusion.1 = (f32[4,2,4,16,40]{2,3,4,1,0:T(8,128)}, f32[4,2,4,16,40]{2,3,4,1,0:T(8,128)S(1)}) fusion(f32[4,2,40,16,128]{4,3,2,1,0:T(8,128)S(1)} %pad_maximum_fusion), kind=kLoop, calls=%fused_computation.5 | loop fusion | bytes 327680 | tf_op jit(solution)/shard_map/transpose | solution.py:177
  60.8 2.8 %copy.63 = f32[4,2,4,16,40]{4,3,2,1,0:T(8,128)S(1)} copy(f32[4,2,4,16,40]{2,3,4,1,0:T(8,128)} %get-tuple-element.30) | data formatting | bytes 163840 | tf_op jit(solution)/shard_map/transpose | solution.py:177
  63.6 1.3 collective-permute-start.2
  64.9 1.8 %copy.65 = f32[4,2,4,16,40]{4,3,2,1,0:T(8,128)} copy(f32[4,2,4,16,40]{2,3,4,1,0:T(8,128)S(1)} %get-tuple-element.31) | data formatting | bytes 163840 | tf_op jit(solution)/shard_map/transpose | solution.py:178
  66.7 5.7 %collective-permute-start.3 = (f32[4,2,4,16,40]{4,3,2,1,0:T(8,128)}, f32[4,2,4,16,40]{4,3,2,1,0:T(8,128)}, u32[]{:S(2)}, u32[]{:S(2)}) collective-permute-start(f32[4,2,4,16,40]{4,3,2,1,0:T(8,128)} %copy.65), channel_id=1, source_target_pairs={{0,1},{1,2},{2,3},{3,4},{4,5},{5,6},{6,7},{7,8},{8,9},{9,10},{10,1... | collective-permute-start | bytes 245768 | tf_op jit(solution)/shard_map/ppermute | solution.py:178
  72.4 2.4 %pad_maximum_fusion.2.refs_1_.refs_9_.refs_10_ = f32[4,2,40,8,128]{4,3,2,1,0:T(8,128)} fusion(f32[4,2,40,4,128]{4,3,2,1,0:T(4,128)} %collective-permute-done.1, f32[4,2,40,4,128]{4,3,2,1,0:T(4,128)S(1)} %collective-permute-done), kind=kLoop, calls=%fused_computation.11 | loop fusion | flops 327680 | bytes 2621440 | tf_op jit(solution)/shard_map/concatenate | solution.py:175
  74.8 0.0 collective-permute-done.2
  74.8 2.1 %copy.64 = f32[4,2,4,16,40]{2,3,4,1,0:T(8,128)S(1)} copy(f32[4,2,4,16,40]{4,3,2,1,0:T(8,128)} %collective-permute-done.2) | data formatting | bytes 163840 | tf_op jit(solution)/shard_map/ppermute | solution.py:177
  77.0 3.5 %copy.66 = f32[4,2,4,16,40]{2,3,4,1,0:T(8,128)} copy(f32[4,2,4,16,40]{4,3,2,1,0:T(8,128)} %collective-permute-done.3) | data formatting | bytes 163840 | tf_op jit(solution)/shard_map/ppermute | solution.py:178
  80.5 4.0 %pad_maximum_fusion.1.refs_2_.refs_10_.refs_11_ = f32[4,2,40,16,128]{4,3,2,1,0:T(8,128)} fusion(f32[4,2,40,16,4]{4,3,2,1,0:T(8,128)} %bitcast.72, f32[4,2,40,16,4]{4,3,2,1,0:T(8,128)S(1)} %bitcast.71, f32[128]{0:T(128)S(1)} %pad.10.clone), kind=kLoop, calls=%fused_computation.7 | loop fusion | flops 1310720 | bytes 2785792 | tf_op jit(solution)/shard_map/concatenate | solution.py:182
  84.5 6.6 %shard_map.104 = (f32[40,16,256]{2,1,0:T(8,128)}, f32[40,16,256]{2,1,0:T(8,128)}, f32[2,40,16,256]{3,2,1,0:T(8,128)}, f32[2,8,128]{2,1,0:T(8,128)}) custom-call(f32[4,2,40,8,128]{4,3,2,1,0:T(8,128)} %bitcast.67, f32[4,2,40,8,128]{4,3,2,1,0:T(8,128)} %pad_maximum_fusion.2.refs_1_.refs_9_.refs_10_, ...), custom_call_target="tpu_custom_call" | custom-call | tf_op jit(solution)/shard_map/pallas_call | solution.py:154
  91.1 6.0 %shard_map.105 = (f32[2,40,16,256]{3,2,1,0:T(8,128)}, f32[2,8,128]{2,1,0:T(8,128)}) custom-call(f32[2,40,16,256]{3,2,1,0:T(8,128)} %get-tuple-element.12.refs_0_, f32[16,256]{1,0:T(8,128)} %and_convert_fusion.refs_3_.refs_1_, f32[4,16,256]{2,1,0:T(8,128)} %get-tuple-element.35.refs_4_.refs_2_, f32[4,16,256]{2,1,0:T(8,128)} %get-tuple-element.34.refs_5_.refs_3_, ...), custom_call_target="tpu_custom_call" | custom-call | tf_op jit(solution)/shard_map/pallas_call | solution.py:154
  97.0 5.9 %shard_map.106 = (f32[2,40,16,256]{3,2,1,0:T(8,128)}, f32[2,8,128]{2,1,0:T(8,128)}) custom-call(f32[2,40,16,256]{3,2,1,0:T(8,128)} %get-tuple-element.16.refs_0_, f32[16,256]{1,0:T(8,128)} %and_convert_fusion.refs_3_.refs_1_, f32[4,16,256]{2,1,0:T(8,128)} %get-tuple-element.35.refs_4_.refs_2_, f32[4,16,256]{2,1,0:T(8,128)} %get-tuple-element.34.refs_5_.refs_3_, ...), custom_call_target="tpu_custom_call" | custom-call | tf_op jit(solution)/shard_map/pallas_call | solution.py:154
  103.0 5.1 %shard_map.107 = (f32[2,40,8,128]{3,2,1,0:T(8,128)}, f32[2,8,128]{2,1,0:T(8,128)}) custom-call(f32[2,40,16,256]{3,2,1,0:T(8,128)} %get-tuple-element.18.refs_0_, f32[16,256]{1,0:T(8,128)} %and_convert_fusion.refs_3_.refs_1_, f32[4,16,256]{2,1,0:T(8,128)} %get-tuple-element.35.refs_4_.refs_2_, f32[4,16,256]{2,1,0:T(8,128)} %get-tuple-element.34.refs_5_.refs_3_, ...), custom_call_target="tpu_custom_call" | custom-call | tf_op jit(solution)/shard_map/pallas_call | solution.py:154
  108.1 0.7 reshape.215
  108.8 1.9 %fusion.1 = f32[2,128,8]{1,0,2:T(2,128)S(1)} fusion(f32[2,1024,1]{1,0,2:T(2,128)S(1)} %reshape.215, s32[128,8]{0,1:T(8,128)S(1)} %multiply_add_fusion, s32[1024]{0:T(1024)S(1)} %bitcast.87), kind=kOutput, calls=%fused_computation.2 | convolution fusion | flops 26214400 | bytes 24576 | tf_op jit(solution)/shard_map/dot_general | solution.py:258
  110.6 0.2 copy.67
  110.8 24.2 %all_to_all.10 = f32[2,128,8]{2,0,1:T(2,128)S(1)} all-to-all(f32[2,128,8]{2,0,1:T(2,128)S(1)} %copy.67), channel_id=1, replica_groups=mesh['gx'=8,'gy'=16] {'gx','gy'}, dimensions={1} | all-to-all | bytes 16384 | tf_op jit(solution)/shard_map/all_to_all | solution.py:259
  135.0 0.7 reduce_sum.19
  (31 shorter events, 0.2 us)
Async XLA Ops:
  0.6 18.4 %copy-start.2 = (f32[4,8,128]{2,1,0:T(8,128)S(1)}, f32[4,8,128]{2,1,0:T(8,128)}, u32[]{:S(2)}) copy-start(f32[4,8,128]{2,1,0:T(8,128)} %param.13) | copy-start | bytes 49156
  0.6 18.4 %copy-start.3 = (f32[4,8,128]{2,1,0:T(8,128)S(1)}, f32[4,8,128]{2,1,0:T(8,128)}, u32[]{:S(2)}) copy-start(f32[4,8,128]{2,1,0:T(8,128)} %param.14) | copy-start | bytes 49156
  0.7 18.4 %copy-start.1 = (f32[39,8,128]{2,1,0:T(8,128)S(1)}, f32[39,8,128]{2,1,0:T(8,128)}, u32[]{:S(2)}) copy-start(f32[39,8,128]{2,1,0:T(8,128)} %param.15) | copy-start | bytes 479236
  7.5 22.1 %all-to-all-start = ((f32[128,1,272]{2,1,0:T(1,128)}), f32[128,1,272]{2,1,0:T(1,128)S(1)}, u32[]{:S(2)}, u32[]{:S(2)}) async-start(f32[128,1,272]{2,1,0:T(1,128)} %reshape.217), calls=%async_computation | async-start | bytes 393216 | tf_op jit(solution)/shard_map/all_to_all | solution.py:212
  19.1 7.0 %collective-permute-start.4 = (f32[47,4,128]{2,1,0:T(4,128)S(1)}, f32[47,4,128]{2,1,0:T(4,128)S(1)}, u32[]{:S(2)}, u32[]{:S(2)}) collective-permute-start(f32[47,4,128]{2,1,0:T(4,128)S(1)} %get-tuple-element.40), channel_id=1, source_target_pairs={{16,0},{32,16},{48,32},{64,48},{80,64},{96,80},{112,96},{17,1},{33... | collective-permute-start | bytes 288776 | tf_op jit(solution)/shard_map/ppermute | solution.py:173
  22.1 4.3 %collective-permute-start.5 = (f32[47,4,128]{2,1,0:T(4,128)S(1)}, f32[47,4,128]{2,1,0:T(4,128)S(1)}, u32[]{:S(2)}, u32[]{:S(2)}) collective-permute-start(f32[47,4,128]{2,1,0:T(4,128)S(1)} %get-tuple-element.41), channel_id=1, source_target_pairs={{0,16},{16,32},{32,48},{48,64},{64,80},{80,96},{96,112},{1,17},{17... | collective-permute-start | bytes 288776 | tf_op jit(solution)/shard_map/ppermute | solution.py:174
  36.3 20.7 %copy-start = (f32[40,8,8,128]{3,2,1,0:T(8,128)}, f32[40,8,8,128]{3,2,1,0:T(8,128)S(1)}, u32[]{:S(2)}) copy-start(f32[40,8,8,128]{3,2,1,0:T(8,128)S(1)} %copy.90) | copy-start | bytes 3932164
  36.5 20.5 %collective-permute-start = (f32[4,2,40,4,128]{4,3,2,1,0:T(4,128)S(1)}, f32[4,2,40,4,128]{4,3,2,1,0:T(4,128)S(1)}, u32[]{:S(2)}, u32[]{:S(2)}) collective-permute-start(f32[4,2,40,4,128]{4,3,2,1,0:T(4,128)S(1)} %get-tuple-element.32), channel_id=1, source_target_pairs={{16,0},{32,16},{48,32},{64,48},{80,64},{96,80},{112,96},{17,1},{33... | collective-permute-start | bytes 1966088 | tf_op jit(solution)/shard_map/ppermute | solution.py:173
  39.1 17.8 %collective-permute-start.1 = (f32[4,2,40,4,128]{4,3,2,1,0:T(4,128)S(1)}, f32[4,2,40,4,128]{4,3,2,1,0:T(4,128)}, u32[]{:S(2)}, u32[]{:S(2)}) collective-permute-start(f32[4,2,40,4,128]{4,3,2,1,0:T(4,128)S(1)} %get-tuple-element.33), channel_id=1, source_target_pairs={{0,16},{16,32},{32,48},{48,64},{64,80},{80,96},{96,112},{1,17},{17... | collective-permute-start | bytes 1966088 | tf_op jit(solution)/shard_map/ppermute | solution.py:174
  42.3 12.1 %collective-permute-start.6 = (f32[4,16,47]{0,1,2:T(8,128)S(1)}, f32[4,16,47]{0,1,2:T(8,128)S(1)}, u32[]{:S(2)}, u32[]{:S(2)}) collective-permute-start(f32[4,16,47]{0,1,2:T(8,128)S(1)} %get-tuple-element.38), channel_id=1, source_target_pairs={{1,0},{2,1},{3,2},{4,3},{5,4},{6,5},{7,6},{8,7},{9,8},{10,9},{11,1... | collective-permute-start | bytes 36104 | tf_op jit(solution)/shard_map/ppermute | solution.py:177
  43.6 11.7 %collective-permute-start.7 = (f32[4,16,47]{0,1,2:T(8,128)S(1)}, f32[4,16,47]{0,1,2:T(8,128)S(1)}, u32[]{:S(2)}, u32[]{:S(2)}) collective-permute-start(f32[4,16,47]{0,1,2:T(8,128)S(1)} %get-tuple-element.39), channel_id=1, source_target_pairs={{0,1},{1,2},{2,3},{3,4},{4,5},{5,6},{6,7},{7,8},{8,9},{9,10},{10,1... | collective-permute-start | bytes 36104 | tf_op jit(solution)/shard_map/ppermute | solution.py:178
  63.6 11.2 %collective-permute-start.2 = (f32[4,2,4,16,40]{4,3,2,1,0:T(8,128)S(1)}, f32[4,2,4,16,40]{4,3,2,1,0:T(8,128)}, u32[]{:S(2)}, u32[]{:S(2)}) collective-permute-start(f32[4,2,4,16,40]{4,3,2,1,0:T(8,128)S(1)} %copy.63), channel_id=1, source_target_pairs={{1,0},{2,1},{3,2},{4,3},{5,4},{6,5},{7,6},{8,7},{9,8},{10,9},{11,1... | collective-permute-start | bytes 245768 | tf_op jit(solution)/shard_map/ppermute | solution.py:177
  66.7 10.2 %collective-permute-start.3 = (f32[4,2,4,16,40]{4,3,2,1,0:T(8,128)}, f32[4,2,4,16,40]{4,3,2,1,0:T(8,128)}, u32[]{:S(2)}, u32[]{:S(2)}) collective-permute-start(f32[4,2,4,16,40]{4,3,2,1,0:T(8,128)} %copy.65), channel_id=1, source_target_pairs={{0,1},{1,2},{2,3},{3,4},{4,5},{5,6},{6,7},{7,8},{8,9},{9,10},{10,1... | collective-permute-start | bytes 245768 | tf_op jit(solution)/shard_map/ppermute | solution.py:178
  103.0 5.8 %copy-start.4 = (s32[8,128]{1,0:T(8,128)S(1)}, s32[8,128]{1,0:T(8,128)}, u32[]{:S(2)}) copy-start(s32[8,128]{1,0:T(8,128)} %param.17) | copy-start | bytes 12292

commit v3 on v2

--- a/solution.py
+++ b/solution.py
@@ -16,15 +16,15 @@
     return pl.BlockSpec(shape, lambda i, _n=nd: (0,) * _n)
 
 
-def _step_kernel(k, first, last, *refs):
+def _step_kernel(k, steps, first, last, *refs):
     refs = list(refs)
     if first:
         own_ref, xh_ref, yh_ref = refs[:3]
         refs = refs[3:]
     else:
         forced_ref = refs.pop(0)
-    mask_ref, wx_ref, wy_ref, diff_ref, prior_ref = refs[:5]
-    refs = refs[5:]
+    mask_ref, se_ref, prior_ref = refs[:3]
+    refs = refs[3:]
     if not first:
         ratio_in, inv_in, ss_ref = refs[:3]
         refs = refs[3:]
@@ -43,14 +43,15 @@
     species, levels = ss_out_ref.shape[0], red_ref.shape[0]
     rows, lanes = red_ref.shape[1:]
     tr, tc = ss_out_ref.shape[1:]
+    d0 = 2 * steps
     zero = jnp.zeros((rows, lanes), jnp.float32)
     inside = mask_ref[...] > 0.5
 
     if first:
         carried = zero
         for l in range(levels):
-            below = diff_ref[l - 1] if l > 0 else zero
-            above = diff_ref[l] if l < levels - 1 else zero
+            below = se_ref[d0 + l - 1] if l > 0 else zero
+            above = se_ref[d0 + l] if l < levels - 1 else zero
             inverse = 1.0 / (1.0 + below + above + below * carried)
             ratio = -above * inverse
             ratio_ref[l] = ratio
@@ -59,16 +60,17 @@
         for s in range(species):
 
             def assemble(l, carry):
-                forced_ref[s, l, :tr, :tc] = own_ref[s, l]
-                forced_ref[s, l, tr:, :tc] = xh_ref[s, l]
-                forced_ref[s, l, :, tc:] = yh_ref[s, l]
+                c = s * levels + l
+                forced_ref[s, l, :tr, :tc] = own_ref[c]
+                forced_ref[s, l, tr:, :tc] = xh_ref[c]
+                forced_ref[s, l, :, tc:] = yh_ref[c]
                 forced_ref[s, l] = jnp.where(inside, forced_ref[s, l], 0.0)
                 return carry
 
             lax.fori_loop(0, levels, assemble, 0, unroll=4)
 
-    wx = wx_ref[k]
-    wy = wy_ref[k]
+    wx = se_ref[k]
+    wy = se_ref[steps + k]
     east = jnp.maximum(wx, 0.0)
     west = jnp.maximum(-wx, 0.0)
     north = jnp.maximum(wy, 0.0)
@@ -86,7 +88,7 @@
             moved = f * remain
             moved = moved + from_east + from_west
             moved = moved + from_north + from_south
-            below = jnp.where(l > 0, diff_ref[jnp.maximum(l - 1, 0)], zero)
+            below = jnp.where(l > 0, se_ref[d0 + jnp.maximum(l - 1, 0)], zero)
             reduced = (moved + below * reduced) * inv_ref[l]
             red_ref[l] = reduced
             return reduced
@@ -95,16 +97,17 @@
 
         def backward(i, result):
             l = levels - 1 - i
+            c = s * levels + l
             result = red_ref[l] - ratio_ref[l] * result
             if last:
                 out_ref[s, l] = result[:tr, :tc]
             else:
                 out_ref[s, l, :tr, :tc] = jnp.where(
-                    inside[:tr, :tc], result[:tr, :tc] + nown_ref[s, l], 0.0)
+                    inside[:tr, :tc], result[:tr, :tc] + nown_ref[c], 0.0)
                 out_ref[s, l, tr:, :tc] = jnp.where(
-                    inside[tr:, :tc], result[tr:, :tc] + nxh_ref[s, l], 0.0)
+                    inside[tr:, :tc], result[tr:, :tc] + nxh_ref[c], 0.0)
                 out_ref[s, l, :, tc:] = jnp.where(
-                    inside[:, tc:], result[:, tc:] + nyh_ref[s, l], 0.0)
+                    inside[:, tc:], result[:, tc:] + nyh_ref[c], 0.0)
             return result
 
         surface = lax.fori_loop(0, levels, backward, zero, unroll=4)
@@ -114,29 +117,30 @@
             ss_out_ref[s] = ss_ref[s] + prior_ref[s] * surface[:tr, :tc]
 
 
-def step_call(k, steps, forced, mask, wind_x, wind_y, diffusivity, prior, ratios, inverses,
-              surface_sum, own, xh, yh):
+def step_call(k, steps, species, levels, forced, mask, statics, prior, ratios, inverses,
+              surface_sum, chans, xh, yh):
     first = k == steps - 1
     last = k == 0
-    species, levels, rows, cols = own.shape[1:]
+    rows, cols = chans.shape[1:]
     rows_e, lanes = mask.shape
+    planes = species * levels
     ext = jax.ShapeDtypeStruct((species, levels, rows_e, lanes), jnp.float32)
     tile = jax.ShapeDtypeStruct((species, levels, rows, cols), jnp.float32)
     plane = jax.ShapeDtypeStruct((levels, rows_e, lanes), jnp.float32)
     surf = jax.ShapeDtypeStruct(prior.shape, jnp.float32)
 
     def blocks(step):
-        return [pl.BlockSpec((None,) + a.shape[1:], lambda i, _s=step: (_s, 0, 0, 0, 0))
-                for a in (own, xh, yh)]
+        return [pl.BlockSpec((planes,) + a.shape[1:], lambda i, _s=step: (_s, 0, 0))
+                for a in (chans, xh, yh)]
 
     in_specs, args = [], []
     if first:
         in_specs += blocks(k)
-        args += [own, xh, yh]
+        args += [chans, xh, yh]
     else:
         in_specs.append(_full(forced.shape))
         args.append(forced)
-    for a in (mask, wind_x, wind_y, diffusivity, prior):
+    for a in (mask, statics, prior):
         in_specs.append(_full(a.shape))
         args.append(a)
     if not first:
@@ -145,14 +149,14 @@
             args.append(a)
     if not last:
         in_specs += blocks(k - 1)
-        args += [own, xh, yh]
+        args += [chans, xh, yh]
     out_shape = [plane, plane] if first else []
     out_shape += [tile if last else ext, surf]
     scratch = [pltpu.VMEM((levels, rows_e, lanes), jnp.float32)]
     if first:
         scratch.append(pltpu.VMEM((species, levels, rows_e, lanes), jnp.float32))
     return pl.pallas_call(
-        functools.partial(_step_kernel, k, first, last),
+        functools.partial(_step_kernel, k, steps, first, last),
         grid=(1,),
         in_specs=in_specs,
         out_specs=[_full(o.shape) for o in out_shape],
@@ -166,21 +170,110 @@
     return [(i, i + 1) for i in range(n - 1)], [(i + 1, i) for i in range(n - 1)]
 
 
-def extend(tile, halo):
+def _whole(shapes):
+    return [pl.BlockSpec(memory_space=pltpu.VMEM) for _ in shapes]
+
+
+def _xpack_kernel(chans_ref, lo_ref, hi_ref):
+    rows = chans_ref.shape[1]
+    half = rows // 2
+    row = lax.broadcasted_iota(jnp.int32, chans_ref.shape[1:], 0)
+
+    def body(i, carry):
+        a = chans_ref[2 * i]
+        b = chans_ref[2 * i + 1]
+        lo_ref[i] = jnp.where(row < half, a, pltpu.roll(b, half, 0))
+        hi_ref[i] = jnp.where(row < half, pltpu.roll(a, half, 0), b)
+        return carry
+
+    lax.fori_loop(0, lo_ref.shape[0], body, 0, unroll=4)
+
+
+def _ypack_kernel(chans_ref, below_ref, above_ref, xh_ref, right_ref, left_ref):
+    rows, cols = chans_ref.shape[1:]
+    half = rows // 2
+    group = cols // half
+    row = lax.broadcasted_iota(jnp.int32, (rows, cols), 0)
+    lane = lax.broadcasted_iota(jnp.int32, (rows, cols), 1)
+    zero = jnp.zeros((rows, cols), jnp.float32)
+
+    def body(g, carry):
+        acc = [zero, zero, zero, zero]
+        for q2 in range(group // 2):
+            i = g * (group // 2) + q2
+            b = below_ref[i]
+            a = above_ref[i]
+            xh0 = jnp.where(row < half, b, pltpu.roll(a, half, 0))
+            xh1 = jnp.where(row < half, pltpu.roll(b, half, 0), a)
+            xh_ref[2 * i] = xh0
+            xh_ref[2 * i + 1] = xh1
+            for off, top, bot in ((0, chans_ref[2 * i], xh0), (1, chans_ref[2 * i + 1], xh1)):
+                q = 2 * q2 + off
+                sel = (lane >= half * q) & (lane < half * q + half)
+                rs = (half * q) % cols
+                ls = (half * q + half) % cols
+                acc[0] = jnp.where(sel, pltpu.roll(top, rs, 1) if rs else top, acc[0])
+                acc[1] = jnp.where(sel, pltpu.roll(bot, rs, 1) if rs else bot, acc[1])
+                acc[2] = jnp.where(sel, pltpu.roll(top, ls, 1) if ls else top, acc[2])
+                acc[3] = jnp.where(sel, pltpu.roll(bot, ls, 1) if ls else bot, acc[3])
+        right_ref[g, :rows] = acc[0]
+        right_ref[g, rows:] = acc[1]
+        left_ref[g, :rows] = acc[2]
+        left_ref[g, rows:] = acc[3]
+        return carry
+
+    lax.fori_loop(0, right_ref.shape[0], body, 0)
+
+
+def _yunpack_kernel(first_static, chans_ref, xh_ref, right_ref, left_ref, yh_ref, se_ref):
+    rows, cols = chans_ref.shape[1:]
+    half = rows // 2
+    group = cols // half
+    lane = lax.broadcasted_iota(jnp.int32, (2 * rows, cols), 1)
+
+    def body(g, carry):
+        r = right_ref[g]
+        l = left_ref[g]
+        for q in range(group):
+            rs = (cols - half * q) % cols
+            ls = (cols - half - half * q) % cols
+            yh = jnp.where(lane < half, pltpu.roll(r, rs, 1) if rs else r,
+                           jnp.where(lane >= cols - half, pltpu.roll(l, ls, 1) if ls else l, 0.0))
+            yh_ref[g * group + q] = yh
+        return carry
+
+    lax.fori_loop(0, right_ref.shape[0], body, 0)
+    for c in range(se_ref.shape[0]):
+        se_ref[c, :rows, :cols] = chans_ref[first_static + c]
+        se_ref[c, rows:, :cols] = xh_ref[first_static + c]
+        se_ref[c, :, cols:] = yh_ref[first_static + c]
+
+
+def extend(chans, first_static, n_statics):
     up_x, down_x = _pairs("gx")
     up_y, down_y = _pairs("gy")
-    rows, cols = tile.shape[-2:]
-    below = lax.ppermute(tile[..., :halo, :], "gx", down_x)
-    above = lax.ppermute(tile[..., rows - halo:, :], "gx", up_x)
-    xh = jnp.concatenate([below, jnp.zeros_like(below)[..., :rows - 2 * halo, :], above], axis=-2)
-    tall = jnp.concatenate([tile, xh], axis=-2)
-    right = lax.ppermute(jnp.swapaxes(tall[..., :halo], -1, -3), "gy", down_y)
-    left = lax.ppermute(jnp.swapaxes(tall[..., cols - halo:], -1, -3), "gy", up_y)
-    right = jnp.swapaxes(right, -1, -3)
-    left = jnp.swapaxes(left, -1, -3)
-    gap = jnp.zeros(right.shape[:-1] + (cols - 2 * halo,), jnp.float32)
-    yh = jnp.concatenate([right, gap, left], axis=-1)
-    return xh, yh
+    channels, rows, cols = chans.shape
+    halo = rows // 2
+    group = cols // halo
+    pairs = jax.ShapeDtypeStruct((channels // 2, rows, cols), jnp.float32)
+    lo, hi = pl.pallas_call(
+        _xpack_kernel, out_shape=[pairs, pairs],
+        in_specs=_whole([chans]), out_specs=_whole([0, 0]))(chans)
+    below = lax.ppermute(lo, "gx", down_x)
+    above = lax.ppermute(hi, "gx", up_x)
+    packed = jax.ShapeDtypeStruct((channels // group, 2 * rows, cols), jnp.float32)
+    xh, right, left = pl.pallas_call(
+        _ypack_kernel,
+        out_shape=[jax.ShapeDtypeStruct(chans.shape, jnp.float32), packed, packed],
+        in_specs=_whole([0, 0, 0]), out_specs=_whole([0, 0, 0]))(chans, below, above)
+    right = lax.ppermute(right, "gy", down_y)
+    left = lax.ppermute(left, "gy", up_y)
+    yh, statics = pl.pallas_call(
+        functools.partial(_yunpack_kernel, first_static),
+        out_shape=[jax.ShapeDtypeStruct((channels, 2 * rows, cols), jnp.float32),
+                   jax.ShapeDtypeStruct((n_statics, 2 * rows, 2 * cols), jnp.float32)],
+        in_specs=_whole([0, 0, 0, 0]), out_specs=_whole([0, 0]))(chans, xh, right, left)
+    return xh, yh, statics
 
 
 def local(pixel_adjoint, pixel_owner, pixel_column, pixel_level, wind_x, wind_y,
@@ -196,7 +289,8 @@
     capacity = 2 * pixels // devices
     cells = rows * cols
     slots = devices * capacity
-    halo = steps
+    halo = rows // 2
+    assert steps <= halo
     lanes = 2 * cols
     ext_rows = 2 * rows
 
@@ -222,14 +316,14 @@
     forcing = jnp.einsum("ksq,kqc->ksc", profile.reshape(steps, species * levels, slots), hits,
                          precision=HI)
 
-    own = forcing.reshape(steps, species, levels, rows, cols)
-    xh, yh = extend(own, halo)
-    statics = jnp.concatenate([wind_x, wind_y, diffusivity], axis=0)
-    sxh, syh = extend(statics, halo)
-    statics = jnp.concatenate([jnp.concatenate([statics, sxh], axis=1), syh], axis=2)
-    wx_ext = statics[:steps]
-    wy_ext = statics[steps:2 * steps]
-    diff_ext = statics[2 * steps:]
+    n_f = steps * species * levels
+    n_s = 2 * steps + levels - 1
+    group = cols // halo
+    channels = -(-(n_f + n_s) // group) * group
+    chans = jnp.concatenate(
+        [forcing.reshape(n_f, rows, cols), wind_x, wind_y, diffusivity,
+         jnp.zeros((channels - n_f - n_s, rows, cols), jnp.float32)], axis=0)
+    xh, yh, statics = extend(chans, n_f, n_s)
 
     gxi = lax.axis_index("gx")
     gyi = lax.axis_index("gy")
@@ -245,8 +339,8 @@
     forced = None
     ratios = inverses = surface_sum = None
     for k in reversed(range(steps)):
-        outs = step_call(k, steps, forced, mask, wx_ext, wy_ext, diff_ext, prior_emission,
-                         ratios, inverses, surface_sum, own, xh, yh)
+        outs = step_call(k, steps, species, levels, forced, mask, statics, prior_emission,
+                         ratios, inverses, surface_sum, chans, xh, yh)
         if k == steps - 1:
             ratios, inverses, forced, surface_sum = outs
         else:

time: 137 us -> 123 us (0.90)
  starting transfers between devices: 34.9 us -> 10.8 us
  blocking collectives: 24.2 us -> 42.1 us
  Pallas kernels: 23.6 us -> 38 us
  local copies, waits for them, and re-layouts: 19.8 us -> 7.96 us
  other arithmetic: 15.9 us -> 7.73 us
    all_to_all x0 -> x1, blocking collectives: none -> 21.9 us  [local(): received = lax.all_to_all(placed, ('gx', 'gy'), 2, 2, tiled=True)]
    pallas_call x4 -> x7, Pallas kernels: 23.6 us -> 38 us  [the longest x4 23.5 us: step_call(): pl.pallas_call(functools.partial(_step_kernel, k, steps, first, last), gr...]
    ppermute x8 -> x4, starting transfers between devices: 23.4 us -> 10.8 us  [the longest x1 3.99 us: extend(): left = lax.ppermute(left, 'gy', up_y)]
    all_to_all x1 -> x0, starting transfers between devices: 11.5 us -> none  [local(): received = lax.all_to_all(placed, ('gx', 'gy'), 2, 2, tiled=True)]
    concatenate x5 -> x0, other arithmetic: 8.08 us -> none  [the longest x1 3.99 us: extend(): yh = jnp.concatenate([right, gap, left], axis=-1)]
    transpose x4 -> x0, local copies, waits for them, and re-layouts: 7.18 us -> none  [the longest x3 5.36 us: extend(): right = lax.ppermute(jnp.swapaxes(tall[..., :halo], -1, -3), 'gy', down_y)]
    ppermute x2 -> x0, local copies, waits for them, and re-layouts: 5.67 us -> none  [the longest x1 3.54 us: extend(): lax.ppermute(jnp.swapaxes(tall[..., cols - halo:], -1, -3), 'gy', up_y)]
    all_to_all x1, blocking collectives: 24.2 us -> 20.2 us  [local(): lax.all_to_all(partial.reshape(species, devices, nreg // devices), ('gx',...]
  transfers between devices with their start and end apart: 9 -> 4, of which waited for: 5 -> 4; matrix products, arithmetic and copies ran while one was open for 7% -> 1% of each run, Pallas kernels for 0% -> 0%
where the time goes in v3:
time: 123 us
  blocking collectives  42.1 us (34%)
  Pallas kernels  38 us (31%)
  starting transfers between devices  10.8 us (9%)
  waiting for transfers between devices  10.4 us (8%)
  local copies, waits for them, and re-layouts  7.96 us (6%)
  other arithmetic  7.73 us (6%)
  matrix products  4.78 us (4%)
    pallas_call x4, Pallas kernels, step_call(): pl.pallas_call(functools.partial(_step_kernel, k, steps, first, last), gr...  23.5 us
    all_to_all x1, blocking collectives, local(): received = lax.all_to_all(placed, ('gx', 'gy'), 2, 2, tiled=True)  21.9 us
    all_to_all x1, blocking collectives, local(): lax.all_to_all(partial.reshape(species, devices, nreg // devices), ('gx',...  20.2 us
    ppermute x1, waiting for transfers between devices, extend(): below = lax.ppermute(lo, 'gx', down_x)  7.21 us
    pallas_call x1, Pallas kernels, extend(): pl.pallas_call(functools.partial(_yunpack_kernel, first_static), out_shap...  6.18 us
    unnamed x36, local copies, waits for them, and re-layouts  5.63 us
    pallas_call x1, Pallas kernels, extend(): pl.pallas_call(_ypack_kernel, out_shape=[jax.ShapeDtypeStruct(chans.shape...  5.34 us
    ppermute x1, starting transfers between devices, extend(): left = lax.ppermute(left, 'gy', up_y)  3.99 us
  transfers between devices with their start and end apart: 4, of which 4 were waited for; matrix products, arithmetic and copies ran while one was open for 1% of the time, Pallas kernels for 0%

profile of v3, /device:TPU:1, one launch (start us, length us, event | category | flops | bytes accessed | tf_op | source)
XLA Modules:
  0.0 122.6 jit_solution(17444609137089217490)
XLA Ops:
  0.6 0.8 fusion.8
  1.5 0.3 reduce_window_sum.11
  1.7 0.9 select_reduce_fusion
  2.6 0.7 multiply_add_fusion.1
  3.3 0.7 convert_element_type.29
  4.0 0.7 convert_element_type.30
  4.7 1.2 fusion.6
  5.9 0.2 copy.47
  6.2 0.6 reshape.217
  6.8 21.9 %all_to_all.10 = f32[128,1,272]{2,1,0:T(1,128)S(1)} all-to-all(f32[128,1,272]{2,1,0:T(1,128)S(1)} %reshape.217), channel_id=1, replica_groups=mesh['gx'=8,'gy'=16] {'gx','gy'}, dimensions={0} | all-to-all | bytes 278528 | tf_op jit(solution)/shard_map/all_to_all | solution.py:306
  28.6 0.5 broadcast.335
  29.2 1.1 reduce
  30.3 0.4 reshape.218
  30.7 0.6 fusion.35
  31.3 0.2 copy.71
  31.5 0.1 fusion.36
  31.6 0.2 copy.72
  31.8 0.4 fusion.24
  32.2 0.2 copy.73
  32.6 0.8 add_add_fusion
  33.3 1.7 %fusion = f32[4,80,1024]{2,1,0:T(8,128)S(1)} fusion(f32[4,80,256]{2,1,0:T(8,128)S(1)} %bitcast.57, s32[4,256]{1,0:T(4,128)S(1)} %convert_bitcast_fusion), kind=kOutput, calls=%fused_computation.1 | convolution fusion | flops 1007681536 | bytes 1642496 | tf_op jit(solution)/shard_map/ksq,kqc->ksc/dot_general | solution.py:316
  35.1 0.3 copy.74
  35.3 0.0 copy-start.6
  35.3 0.0 copy-start.7
  35.4 0.0 copy-start.3
  35.4 0.1 constant_dynamic-update-slice_fusion.3
  35.5 0.6 copy-done.6
  36.1 0.0 copy-done.7
  36.1 0.2 copy-done.3
  36.3 0.0 copy-start
  36.3 1.1 copy-done
  37.5 2.9 %shard_map.104 = (f32[192,8,128]{2,1,0:T(8,128)}, f32[192,8,128]{2,1,0:T(8,128)}) custom-call(f32[384,8,128]{2,1,0:T(8,128)} %copy-done), custom_call_target="tpu_custom_call" | custom-call | tf_op jit(solution)/shard_map/pallas_call | solution.py:259
  40.4 2.6 %collective-permute-start = (f32[192,8,128]{2,1,0:T(8,128)}, f32[192,8,128]{2,1,0:T(8,128)S(1)}, u32[]{:S(2)}, u32[]{:S(2)}) collective-permute-start(f32[192,8,128]{2,1,0:T(8,128)} %get-tuple-element.19), channel_id=1, source_target_pairs={{16,0},{32,16},{48,32},{64,48},{80,64},{96,80},{112,96},{17,1},{33... | collective-permute-start | bytes 2359304 | tf_op jit(solution)/shard_map/ppermute | solution.py:262
  43.0 3.0 %collective-permute-start.1 = (f32[192,8,128]{2,1,0:T(8,128)}, f32[192,8,128]{2,1,0:T(8,128)S(1)}, u32[]{:S(2)}, u32[]{:S(2)}) collective-permute-start(f32[192,8,128]{2,1,0:T(8,128)} %get-tuple-element.20), channel_id=1, source_target_pairs={{0,16},{16,32},{32,48},{48,64},{64,80},{80,96},{96,112},{1,17},{17... | collective-permute-start | bytes 2359304 | tf_op jit(solution)/shard_map/ppermute | solution.py:263
  46.0 0.7 and_convert_fusion.refs_3_.refs_1_
  46.7 7.2 %collective-permute-done.below_ref = f32[192,8,128]{2,1,0:T(8,128)S(1)} collective-permute-done((f32[192,8,128]{2,1,0:T(8,128)}, f32[192,8,128]{2,1,0:T(8,128)S(1)}, u32[]{:S(2)}, u32[]{:S(2)}) %collective-permute-start) | collective-permute-done | bytes 786464 | tf_op jit(solution)/shard_map/ppermute | solution.py:262
  53.9 0.0 copy-start.1
  53.9 1.3 %collective-permute-done.1.above_ref = f32[192,8,128]{2,1,0:T(8,128)S(1)} collective-permute-done((f32[192,8,128]{2,1,0:T(8,128)}, f32[192,8,128]{2,1,0:T(8,128)S(1)}, u32[]{:S(2)}, u32[]{:S(2)}) %collective-permute-start.1) | collective-permute-done | bytes 786464 | tf_op jit(solution)/shard_map/ppermute | solution.py:263
  55.2 0.0 copy-done.1
  55.2 0.0 copy-start.2
  55.2 0.9 copy-done.2
  56.1 5.3 %shard_map.105 = (f32[384,8,128]{2,1,0:T(8,128)}, f32[12,16,128]{2,1,0:T(8,128)}, f32[12,16,128]{2,1,0:T(8,128)}) custom-call(f32[384,8,128]{2,1,0:T(8,128)} %copy-done, f32[192,8,128]{2,1,0:T(8,128)} %copy-done.1, f32[192,8,128]{2,1,0:T(8,128)} %copy-done.2), custom_call_target="tpu_custom_call" | custom-call | tf_op jit(solution)/shard_map/pallas_call | solution.py:265
  61.4 1.3 %collective-permute-start.2 = (f32[12,16,128]{2,1,0:T(8,128)}, f32[12,16,128]{2,1,0:T(8,128)S(1)}, u32[]{:S(2)}, u32[]{:S(2)}) collective-permute-start(f32[12,16,128]{2,1,0:T(8,128)} %get-tuple-element.22), channel_id=1, source_target_pairs={{1,0},{2,1},{3,2},{4,3},{5,4},{6,5},{7,6},{8,7},{9,8},{10,9},{11,1... | collective-permute-start | bytes 294920 | tf_op jit(solution)/shard_map/ppermute | solution.py:269
  62.7 4.0 %collective-permute-start.3 = (f32[12,16,128]{2,1,0:T(8,128)}, f32[12,16,128]{2,1,0:T(8,128)S(1)}, u32[]{:S(2)}, u32[]{:S(2)}) collective-permute-start(f32[12,16,128]{2,1,0:T(8,128)} %get-tuple-element.23), channel_id=1, source_target_pairs={{0,1},{1,2},{2,3},{3,4},{4,5},{5,6},{6,7},{7,8},{8,9},{9,10},{10,1... | collective-permute-start | bytes 294920 | tf_op jit(solution)/shard_map/ppermute | solution.py:270
  66.7 0.3 collective-permute-done.2.right_ref
  67.0 0.0 copy-start.4
  67.0 1.7 %collective-permute-done.3.left_ref = f32[12,16,128]{2,1,0:T(8,128)S(1)} collective-permute-done((f32[12,16,128]{2,1,0:T(8,128)}, f32[12,16,128]{2,1,0:T(8,128)S(1)}, u32[]{:S(2)}, u32[]{:S(2)}) %collective-permute-start.3) | collective-permute-done | bytes 98336 | tf_op jit(solution)/shard_map/ppermute | solution.py:270
  68.7 0.0 copy-start.5
  68.7 0.0 copy-done.4
  68.7 0.6 copy-done.5
  69.3 6.2 %shard_map.106 = (f32[384,16,128]{2,1,0:T(8,128)}, f32[47,16,256]{2,1,0:T(8,128)}) custom-call(f32[384,8,128]{2,1,0:T(8,128)} %copy-done, f32[384,8,128]{2,1,0:T(8,128)} %get-tuple-element.21.xh_ref.refs_1_.refs_7_.refs_8_, f32[12,16,128]{2,1,0:T(8,128)} %copy-done.4, f32[12,16,128]{2,1,0:T(8,128)} %copy-done.5), custom_call_target="tpu_custom_call" | custom-call | tf_op jit(solution)/shard_map/pallas_call | solution.py:271
  75.5 6.5 %shard_map.107 = (f32[40,16,256]{2,1,0:T(8,128)}, f32[40,16,256]{2,1,0:T(8,128)}, f32[2,40,16,256]{3,2,1,0:T(8,128)}, f32[2,8,128]{2,1,0:T(8,128)}) custom-call(f32[384,8,128]{2,1,0:T(8,128)} %copy-done, f32[384,8,128]{2,1,0:T(8,128)} %get-tuple-element.21.xh_ref.refs_1_.refs_7_.refs_8_, f32[384,16,128]{2,1,0:T(8,128)} %get-tuple-element.24.refs_2_.refs_8_.refs_9_, ...), custom_call_target="tpu_custom_call" | custom-call | tf_op jit(solution)/shard_map/pallas_call | solution.py:158
  82.0 6.0 %shard_map.108 = (f32[2,40,16,256]{3,2,1,0:T(8,128)}, f32[2,8,128]{2,1,0:T(8,128)}) custom-call(f32[2,40,16,256]{3,2,1,0:T(8,128)} %get-tuple-element.26.refs_0_, f32[16,256]{1,0:T(8,128)} %and_convert_fusion.refs_3_.refs_1_, f32[47,16,256]{2,1,0:T(8,128)} %get-tuple-element.25.refs_4_.refs_2_, f32[2,8,128]{2,1,0:T(8,128)} %refs_3_.5, ...), custom_call_target="tpu_custom_call" | custom-call | tf_op jit(solution)/shard_map/pallas_call | solution.py:158
  88.0 5.9 %shard_map.109 = (f32[2,40,16,256]{3,2,1,0:T(8,128)}, f32[2,8,128]{2,1,0:T(8,128)}) custom-call(f32[2,40,16,256]{3,2,1,0:T(8,128)} %get-tuple-element.30.refs_0_, f32[16,256]{1,0:T(8,128)} %and_convert_fusion.refs_3_.refs_1_, f32[47,16,256]{2,1,0:T(8,128)} %get-tuple-element.25.refs_4_.refs_2_, f32[2,8,128]{2,1,0:T(8,128)} %refs_3_.5, ...), custom_call_target="tpu_custom_call" | custom-call | tf_op jit(solution)/shard_map/pallas_call | solution.py:158
  94.0 0.0 copy-start.8
  94.0 5.1 %shard_map.110 = (f32[2,40,8,128]{3,2,1,0:T(8,128)}, f32[2,8,128]{2,1,0:T(8,128)}) custom-call(f32[2,40,16,256]{3,2,1,0:T(8,128)} %get-tuple-element.32.refs_0_, f32[16,256]{1,0:T(8,128)} %and_convert_fusion.refs_3_.refs_1_, f32[47,16,256]{2,1,0:T(8,128)} %get-tuple-element.25.refs_4_.refs_2_, f32[2,8,128]{2,1,0:T(8,128)} %refs_3_.5, ...), custom_call_target="tpu_custom_call" | custom-call | tf_op jit(solution)/shard_map/pallas_call | solution.py:158
  99.0 0.7 reshape.215
  99.7 0.0 copy-done.8
  99.7 1.9 %fusion.1 = f32[2,128,8]{1,0,2:T(2,128)S(1)} fusion(f32[2,1024,1]{1,0,2:T(2,128)S(1)} %reshape.215, s32[128,8]{0,1:T(8,128)S(1)} %multiply_add_fusion, s32[1024]{0:T(1024)S(1)} %bitcast.65), kind=kOutput, calls=%fused_computation.2 | convolution fusion | flops 26214400 | bytes 24576 | tf_op jit(solution)/shard_map/dot_general | solution.py:352
  101.6 0.2 copy.51
  101.8 20.2 %all_to_all.11 = f32[2,128,8]{2,0,1:T(2,128)S(1)} all-to-all(f32[2,128,8]{2,0,1:T(2,128)S(1)} %copy.51), channel_id=1, replica_groups=mesh['gx'=8,'gy'=16] {'gx','gy'}, dimensions={1} | all-to-all | bytes 16384 | tf_op jit(solution)/shard_map/all_to_all | solution.py:353
  121.9 0.7 reduce_sum.19
  (19 shorter events, 0.2 us)
Async XLA Ops:
  35.3 0.7 copy-start.6
  35.3 0.7 copy-start.7
  35.4 0.9 copy-start.3
  36.3 1.2 copy-start
  40.4 13.5 %collective-permute-start = (f32[192,8,128]{2,1,0:T(8,128)}, f32[192,8,128]{2,1,0:T(8,128)S(1)}, u32[]{:S(2)}, u32[]{:S(2)}) collective-permute-start(f32[192,8,128]{2,1,0:T(8,128)} %get-tuple-element.19), channel_id=1, source_target_pairs={{16,0},{32,16},{48,32},{64,48},{80,64},{96,80},{112,96},{17,1},{33... | collective-permute-start | bytes 2359304 | tf_op jit(solution)/shard_map/ppermute | solution.py:262
  43.0 12.2 %collective-permute-start.1 = (f32[192,8,128]{2,1,0:T(8,128)}, f32[192,8,128]{2,1,0:T(8,128)S(1)}, u32[]{:S(2)}, u32[]{:S(2)}) collective-permute-start(f32[192,8,128]{2,1,0:T(8,128)} %get-tuple-element.20), channel_id=1, source_target_pairs={{0,16},{16,32},{32,48},{48,64},{64,80},{80,96},{96,112},{1,17},{17... | collective-permute-start | bytes 2359304 | tf_op jit(solution)/shard_map/ppermute | solution.py:263
  53.9 1.3 %copy-start.1 = (f32[192,8,128]{2,1,0:T(8,128)}, f32[192,8,128]{2,1,0:T(8,128)S(1)}, u32[]{:S(2)}) copy-start(f32[192,8,128]{2,1,0:T(8,128)S(1)} %collective-permute-done.below_ref) | copy-start | bytes 2359300
  55.2 0.9 copy-start.2
  61.4 5.6 %collective-permute-start.2 = (f32[12,16,128]{2,1,0:T(8,128)}, f32[12,16,128]{2,1,0:T(8,128)S(1)}, u32[]{:S(2)}, u32[]{:S(2)}) collective-permute-start(f32[12,16,128]{2,1,0:T(8,128)} %get-tuple-element.22), channel_id=1, source_target_pairs={{1,0},{2,1},{3,2},{4,3},{5,4},{6,5},{7,6},{8,7},{9,8},{10,9},{11,1... | collective-permute-start | bytes 294920 | tf_op jit(solution)/shard_map/ppermute | solution.py:269
  62.7 5.9 %collective-permute-start.3 = (f32[12,16,128]{2,1,0:T(8,128)}, f32[12,16,128]{2,1,0:T(8,128)S(1)}, u32[]{:S(2)}, u32[]{:S(2)}) collective-permute-start(f32[12,16,128]{2,1,0:T(8,128)} %get-tuple-element.23), channel_id=1, source_target_pairs={{0,1},{1,2},{2,3},{3,4},{4,5},{5,6},{6,7},{7,8},{8,9},{9,10},{10,1... | collective-permute-start | bytes 294920 | tf_op jit(solution)/shard_map/ppermute | solution.py:270
  67.0 1.7 %copy-start.4 = (f32[12,16,128]{2,1,0:T(8,128)}, f32[12,16,128]{2,1,0:T(8,128)S(1)}, u32[]{:S(2)}) copy-start(f32[12,16,128]{2,1,0:T(8,128)S(1)} %collective-permute-done.2.right_ref) | copy-start | bytes 294916
  68.7 0.6 copy-start.5
  94.0 5.8 %copy-start.8 = (s32[8,128]{1,0:T(8,128)S(1)}, s32[8,128]{1,0:T(8,128)}, u32[]{:S(2)}) copy-start(s32[8,128]{1,0:T(8,128)} %param.17) | copy-start | bytes 12292

commit v4 on v3

--- a/solution.py
+++ b/solution.py
@@ -350,8 +350,9 @@
     nreg = REG_DEV * devices
     member = (region_map.reshape(-1)[:, None] == jnp.arange(nreg, dtype=jnp.int32)).astype(jnp.float32)
     partial = jnp.dot(surface_sum.reshape(species, cells), member, precision=HI)
-    pieces = lax.all_to_all(partial.reshape(species, devices, nreg // devices), ("gx", "gy"), 1, 1,
-                            tiled=True)
+    per_dev = nreg // devices
+    pieces = lax.all_to_all(partial.reshape(species, gx_n, gy_n, per_dev), "gy", 2, 2, tiled=True)
+    pieces = lax.all_to_all(jnp.sum(pieces, axis=2), "gx", 1, 1, tiled=True)
     gradient = jnp.sum(pieces, axis=1)
     return adjoint, gradient
 

time: 123 us -> 134 us (1.089)
  matrix products: 4.78 us -> 10.4 us
  blocking collectives: 42.1 us -> 46.2 us
    dot_general x1, matrix products: 1.87 us -> 7.47 us  [local(): partial = jnp.dot(surface_sum.reshape(species, cells), member, precision=HI)]
    all_to_all x1 -> x2, blocking collectives: 20.2 us -> 24.3 us  [the longest x1 12.7 us: local(): lax.all_to_all(partial.reshape(species, gx_n, gy_n, per_dev), 'gy', 2, 2,...]
    unnamed x36 -> x38, local copies, waits for them, and re-layouts: 5.63 us -> 5.84 us
where the time goes in v4:
time: 134 us; the launch traced here: 133 us
  blocking collectives  46.2 us (34%)
  Pallas kernels  37.9 us (28%)
  starting transfers between devices  11 us (8%)
  matrix products  10.4 us (8%)
  waiting for transfers between devices  10.2 us (8%)
  other arithmetic  8.3 us (6%)
  local copies, waits for them, and re-layouts  8.14 us (6%)
    pallas_call x4, Pallas kernels, step_call(): pl.pallas_call(functools.partial(_step_kernel, k, steps, first, last), gr...  23.5 us
    all_to_all x1, blocking collectives, local(): received = lax.all_to_all(placed, ('gx', 'gy'), 2, 2, tiled=True)  21.9 us
    all_to_all x1, blocking collectives, local(): lax.all_to_all(partial.reshape(species, gx_n, gy_n, per_dev), 'gy', 2, 2,...  12.7 us
    all_to_all x1, blocking collectives, local(): pieces = lax.all_to_all(jnp.sum(pieces, axis=2), 'gx', 1, 1, tiled=True)  11.7 us
    dot_general x1, matrix products, local(): partial = jnp.dot(surface_sum.reshape(species, cells), member, precision=HI)  7.47 us
    ppermute x1, waiting for transfers between devices, extend(): below = lax.ppermute(lo, 'gx', down_x)  7.21 us
    pallas_call x1, Pallas kernels, extend(): pl.pallas_call(functools.partial(_yunpack_kernel, first_static), out_shap...  6.16 us
    unnamed x38, local copies, waits for them, and re-layouts  5.84 us
  transfers between devices with their start and end apart: 4, of which 4 were waited for; matrix products, arithmetic and copies ran while one was open for 1% of the time, Pallas kernels for 0%

profile of v4, /device:TPU:1, one launch (start us, length us, event | category | flops | bytes accessed | tf_op | source)
XLA Modules:
  0.0 133.1 jit_solution(9609260408830202138)
XLA Ops:
  0.6 0.8 fusion.8
  1.5 0.3 reduce_window_sum.11
  1.7 0.9 select_reduce_fusion
  2.6 0.7 multiply_add_fusion.1
  3.3 0.7 convert_element_type.29
  4.0 0.7 convert_element_type.30
  4.7 1.2 fusion.6
  5.9 0.2 copy.47
  6.2 0.6 reshape.221
  6.8 21.9 %all_to_all.15 = f32[128,1,272]{2,1,0:T(1,128)S(1)} all-to-all(f32[128,1,272]{2,1,0:T(1,128)S(1)} %reshape.221), channel_id=1, replica_groups=mesh['gx'=8,'gy'=16] {'gx','gy'}, dimensions={0} | all-to-all | bytes 278528 | tf_op jit(solution)/shard_map/all_to_all | solution.py:306
  28.6 0.5 broadcast.339
  29.2 1.1 reduce
  30.3 0.4 reshape.222
  30.7 0.6 fusion.36
  31.3 0.2 copy.73
  31.5 0.1 fusion.37
  31.6 0.2 copy.72
  31.8 0.4 fusion.24
  32.2 0.2 copy.74
  32.6 0.8 add_add_fusion
  33.3 1.7 %fusion = f32[4,80,1024]{2,1,0:T(8,128)S(1)} fusion(f32[4,80,256]{2,1,0:T(8,128)S(1)} %bitcast.62, s32[4,256]{1,0:T(4,128)S(1)} %convert_bitcast_fusion), kind=kOutput, calls=%fused_computation.1 | convolution fusion | flops 1007681536 | bytes 1642496 | tf_op jit(solution)/shard_map/ksq,kqc->ksc/dot_general | solution.py:316
  35.1 0.3 copy.76
  35.3 0.0 copy-start.6
  35.3 0.0 copy-start.7
  35.4 0.0 copy-start.3
  35.4 0.1 constant_dynamic-update-slice_fusion.3
  35.5 0.6 copy-done.6
  36.0 0.0 copy-done.7
  36.1 0.2 copy-done.3
  36.3 0.0 copy-start
  36.3 1.1 copy-done
  37.5 2.9 %shard_map.104 = (f32[192,8,128]{2,1,0:T(8,128)}, f32[192,8,128]{2,1,0:T(8,128)}) custom-call(f32[384,8,128]{2,1,0:T(8,128)} %copy-done), custom_call_target="tpu_custom_call" | custom-call | tf_op jit(solution)/shard_map/pallas_call | solution.py:259
  40.4 2.6 %collective-permute-start = (f32[192,8,128]{2,1,0:T(8,128)}, f32[192,8,128]{2,1,0:T(8,128)S(1)}, u32[]{:S(2)}, u32[]{:S(2)}) collective-permute-start(f32[192,8,128]{2,1,0:T(8,128)} %get-tuple-element.19), channel_id=1, source_target_pairs={{16,0},{32,16},{48,32},{64,48},{80,64},{96,80},{112,96},{17,1},{33... | collective-permute-start | bytes 2359304 | tf_op jit(solution)/shard_map/ppermute | solution.py:262
  43.0 3.0 %collective-permute-start.1 = (f32[192,8,128]{2,1,0:T(8,128)}, f32[192,8,128]{2,1,0:T(8,128)S(1)}, u32[]{:S(2)}, u32[]{:S(2)}) collective-permute-start(f32[192,8,128]{2,1,0:T(8,128)} %get-tuple-element.20), channel_id=1, source_target_pairs={{0,16},{16,32},{32,48},{48,64},{64,80},{80,96},{96,112},{1,17},{17... | collective-permute-start | bytes 2359304 | tf_op jit(solution)/shard_map/ppermute | solution.py:263
  46.0 0.7 and_convert_fusion.refs_3_.refs_1_
  46.7 7.2 %collective-permute-done.below_ref = f32[192,8,128]{2,1,0:T(8,128)S(1)} collective-permute-done((f32[192,8,128]{2,1,0:T(8,128)}, f32[192,8,128]{2,1,0:T(8,128)S(1)}, u32[]{:S(2)}, u32[]{:S(2)}) %collective-permute-start) | collective-permute-done | bytes 786464 | tf_op jit(solution)/shard_map/ppermute | solution.py:262
  53.9 0.0 copy-start.1
  53.9 1.3 collective-permute-done.1.above_ref
  55.2 0.0 copy-done.1
  55.2 0.0 copy-start.2
  55.2 0.9 copy-done.2
  56.1 5.3 %shard_map.105 = (f32[384,8,128]{2,1,0:T(8,128)}, f32[12,16,128]{2,1,0:T(8,128)}, f32[12,16,128]{2,1,0:T(8,128)}) custom-call(f32[384,8,128]{2,1,0:T(8,128)} %copy-done, f32[192,8,128]{2,1,0:T(8,128)} %copy-done.1, f32[192,8,128]{2,1,0:T(8,128)} %copy-done.2), custom_call_target="tpu_custom_call" | custom-call | tf_op jit(solution)/shard_map/pallas_call | solution.py:265
  61.4 1.3 collective-permute-start.2
  62.7 4.2 %collective-permute-start.3 = (f32[12,16,128]{2,1,0:T(8,128)}, f32[12,16,128]{2,1,0:T(8,128)S(1)}, u32[]{:S(2)}, u32[]{:S(2)}) collective-permute-start(f32[12,16,128]{2,1,0:T(8,128)} %get-tuple-element.23), channel_id=1, source_target_pairs={{0,1},{1,2},{2,3},{3,4},{4,5},{5,6},{6,7},{7,8},{8,9},{9,10},{10,1... | collective-permute-start | bytes 294920 | tf_op jit(solution)/shard_map/ppermute | solution.py:270
  66.9 0.1 collective-permute-done.2.right_ref
  67.0 0.0 copy-start.4
  67.0 1.7 %collective-permute-done.3.left_ref = f32[12,16,128]{2,1,0:T(8,128)S(1)} collective-permute-done((f32[12,16,128]{2,1,0:T(8,128)}, f32[12,16,128]{2,1,0:T(8,128)S(1)}, u32[]{:S(2)}, u32[]{:S(2)}) %collective-permute-start.3) | collective-permute-done | bytes 98336 | tf_op jit(solution)/shard_map/ppermute | solution.py:270
  68.7 0.0 copy-done.4
  68.7 0.6 copy-done.5
  69.3 6.2 %shard_map.106 = (f32[384,16,128]{2,1,0:T(8,128)}, f32[47,16,256]{2,1,0:T(8,128)}) custom-call(f32[384,8,128]{2,1,0:T(8,128)} %copy-done, f32[384,8,128]{2,1,0:T(8,128)} %get-tuple-element.21.xh_ref.refs_1_.refs_7_.refs_8_, f32[12,16,128]{2,1,0:T(8,128)} %copy-done.4, f32[12,16,128]{2,1,0:T(8,128)} %copy-done.5), custom_call_target="tpu_custom_call" | custom-call | tf_op jit(solution)/shard_map/pallas_call | solution.py:271
  75.4 6.5 %shard_map.107 = (f32[40,16,256]{2,1,0:T(8,128)}, f32[40,16,256]{2,1,0:T(8,128)}, f32[2,40,16,256]{3,2,1,0:T(8,128)}, f32[2,8,128]{2,1,0:T(8,128)}) custom-call(f32[384,8,128]{2,1,0:T(8,128)} %copy-done, f32[384,8,128]{2,1,0:T(8,128)} %get-tuple-element.21.xh_ref.refs_1_.refs_7_.refs_8_, f32[384,16,128]{2,1,0:T(8,128)} %get-tuple-element.24.refs_2_.refs_8_.refs_9_, ...), custom_call_target="tpu_custom_call" | custom-call | tf_op jit(solution)/shard_map/pallas_call | solution.py:158
  81.9 6.0 %shard_map.108 = (f32[2,40,16,256]{3,2,1,0:T(8,128)}, f32[2,8,128]{2,1,0:T(8,128)}) custom-call(f32[2,40,16,256]{3,2,1,0:T(8,128)} %get-tuple-element.26.refs_0_, f32[16,256]{1,0:T(8,128)} %and_convert_fusion.refs_3_.refs_1_, f32[47,16,256]{2,1,0:T(8,128)} %get-tuple-element.25.refs_4_.refs_2_, f32[2,8,128]{2,1,0:T(8,128)} %refs_3_.5, ...), custom_call_target="tpu_custom_call" | custom-call | tf_op jit(solution)/shard_map/pallas_call | solution.py:158
  88.0 5.9 %shard_map.109 = (f32[2,40,16,256]{3,2,1,0:T(8,128)}, f32[2,8,128]{2,1,0:T(8,128)}) custom-call(f32[2,40,16,256]{3,2,1,0:T(8,128)} %get-tuple-element.30.refs_0_, f32[16,256]{1,0:T(8,128)} %and_convert_fusion.refs_3_.refs_1_, f32[47,16,256]{2,1,0:T(8,128)} %get-tuple-element.25.refs_4_.refs_2_, f32[2,8,128]{2,1,0:T(8,128)} %refs_3_.5, ...), custom_call_target="tpu_custom_call" | custom-call | tf_op jit(solution)/shard_map/pallas_call | solution.py:158
  93.9 5.1 %shard_map.110 = (f32[2,40,8,128]{3,2,1,0:T(8,128)}, f32[2,8,128]{2,1,0:T(8,128)}) custom-call(f32[2,40,16,256]{3,2,1,0:T(8,128)} %get-tuple-element.32.refs_0_, f32[16,256]{1,0:T(8,128)} %and_convert_fusion.refs_3_.refs_1_, f32[47,16,256]{2,1,0:T(8,128)} %get-tuple-element.25.refs_4_.refs_2_, f32[2,8,128]{2,1,0:T(8,128)} %refs_3_.5, ...), custom_call_target="tpu_custom_call" | custom-call | tf_op jit(solution)/shard_map/pallas_call | solution.py:158
  98.9 0.7 reshape.219
  99.6 0.0 copy-done.8
  99.7 7.5 %fusion.1 = f32[2,8,16,8]{2,0,3,1:T(2,128)S(1)} fusion(s32[8,16,8]{1,2,0:T(8,128)S(1)} %multiply_add_fusion, s32[1024]{0:T(1024)S(1)} %bitcast.71, f32[2,1024,1,1]{1,0,2,3:T(2,128)S(1)} %reshape.219), kind=kOutput, calls=%fused_computation.2 | convolution fusion | flops 26214400 | bytes 24576 | tf_op jit(solution)/shard_map/dot_general | solution.py:352
  107.1 0.1 copy.51
  107.3 0.1 reshape.223
  107.4 12.7 %all_to_all.16 = f32[16,1,128]{2,1,0:T(1,128)S(1)} all-to-all(f32[16,1,128]{2,1,0:T(1,128)S(1)} %reshape.223), channel_id=1, replica_groups=mesh['gx'=8,'gy'=16] {'gy'}, dimensions={0} | all-to-all | bytes 16384 | tf_op jit(solution)/shard_map/all_to_all | solution.py:354
  120.0 0.7 reduce.1
  120.7 0.1 reshape.224
  120.9 11.7 %all_to_all.17 = f32[2,8,8]{2,0,1:T(2,128)S(1)} all-to-all(f32[2,8,8]{2,0,1:T(2,128)S(1)} %copy.53), channel_id=1, replica_groups=mesh['gx'=8,'gy'=16] {'gx'}, dimensions={1} | all-to-all | bytes 1024 | tf_op jit(solution)/shard_map/all_to_all | solution.py:355
  132.5 0.6 reduce_sum.29
  (23 shorter events, 0.2 us)
Async XLA Ops:
  35.3 0.7 copy-start.6
  35.3 0.7 copy-start.7
  35.4 0.9 copy-start.3
  36.3 1.2 copy-start
  40.4 13.5 %collective-permute-start = (f32[192,8,128]{2,1,0:T(8,128)}, f32[192,8,128]{2,1,0:T(8,128)S(1)}, u32[]{:S(2)}, u32[]{:S(2)}) collective-permute-start(f32[192,8,128]{2,1,0:T(8,128)} %get-tuple-element.19), channel_id=1, source_target_pairs={{16,0},{32,16},{48,32},{64,48},{80,64},{96,80},{112,96},{17,1},{33... | collective-permute-start | bytes 2359304 | tf_op jit(solution)/shard_map/ppermute | solution.py:262
  43.0 12.2 %collective-permute-start.1 = (f32[192,8,128]{2,1,0:T(8,128)}, f32[192,8,128]{2,1,0:T(8,128)S(1)}, u32[]{:S(2)}, u32[]{:S(2)}) collective-permute-start(f32[192,8,128]{2,1,0:T(8,128)} %get-tuple-element.20), channel_id=1, source_target_pairs={{0,16},{16,32},{32,48},{48,64},{64,80},{80,96},{96,112},{1,17},{17... | collective-permute-start | bytes 2359304 | tf_op jit(solution)/shard_map/ppermute | solution.py:263
  53.9 1.3 copy-start.1
  55.2 0.9 copy-start.2
  61.4 5.6 %collective-permute-start.2 = (f32[12,16,128]{2,1,0:T(8,128)}, f32[12,16,128]{2,1,0:T(8,128)S(1)}, u32[]{:S(2)}, u32[]{:S(2)}) collective-permute-start(f32[12,16,128]{2,1,0:T(8,128)} %get-tuple-element.22), channel_id=1, source_target_pairs={{1,0},{2,1},{3,2},{4,3},{5,4},{6,5},{7,6},{8,7},{9,8},{10,9},{11,1... | collective-permute-start | bytes 294920 | tf_op jit(solution)/shard_map/ppermute | solution.py:269
  62.7 5.9 %collective-permute-start.3 = (f32[12,16,128]{2,1,0:T(8,128)}, f32[12,16,128]{2,1,0:T(8,128)S(1)}, u32[]{:S(2)}, u32[]{:S(2)}) collective-permute-start(f32[12,16,128]{2,1,0:T(8,128)} %get-tuple-element.23), channel_id=1, source_target_pairs={{0,1},{1,2},{2,3},{3,4},{4,5},{5,6},{6,7},{7,8},{8,9},{9,10},{10,1... | collective-permute-start | bytes 294920 | tf_op jit(solution)/shard_map/ppermute | solution.py:270
  67.0 1.7 %copy-start.4 = (f32[12,16,128]{2,1,0:T(8,128)}, f32[12,16,128]{2,1,0:T(8,128)S(1)}, u32[]{:S(2)}) copy-start(f32[12,16,128]{2,1,0:T(8,128)S(1)} %collective-permute-done.2.right_ref) | copy-start | bytes 294916
  68.7 0.6 copy-start.5
  93.9 5.8 %copy-start.8 = (s32[8,128]{1,0:T(8,128)S(1)}, s32[8,128]{1,0:T(8,128)}, u32[]{:S(2)}) copy-start(s32[8,128]{1,0:T(8,128)} %param.17) | copy-start | bytes 12292

commit v5 on v3

--- a/solution.py
+++ b/solution.py
@@ -76,6 +76,12 @@
     north = jnp.maximum(wy, 0.0)
     south = jnp.maximum(-wy, 0.0)
     remain = 1.0 - (east + west + north + south)
+
+    if last:
+        _last_step(species, levels, tr, tc, forced_ref, east, west, north, south, remain,
+                   se_ref, d0, inv_ref, ratio_ref, red_ref, out_ref, ss_ref, ss_out_ref,
+                   prior_ref)
+        return
 
     for s in range(species):
 
@@ -99,15 +105,12 @@
             l = levels - 1 - i
             c = s * levels + l
             result = red_ref[l] - ratio_ref[l] * result
-            if last:
-                out_ref[s, l] = result[:tr, :tc]
-            else:
-                out_ref[s, l, :tr, :tc] = jnp.where(
-                    inside[:tr, :tc], result[:tr, :tc] + nown_ref[c], 0.0)
-                out_ref[s, l, tr:, :tc] = jnp.where(
-                    inside[tr:, :tc], result[tr:, :tc] + nxh_ref[c], 0.0)
-                out_ref[s, l, :, tc:] = jnp.where(
-                    inside[:, tc:], result[:, tc:] + nyh_ref[c], 0.0)
+            out_ref[s, l, :tr, :tc] = jnp.where(
+                inside[:tr, :tc], result[:tr, :tc] + nown_ref[c], 0.0)
+            out_ref[s, l, tr:, :tc] = jnp.where(
+                inside[tr:, :tc], result[tr:, :tc] + nxh_ref[c], 0.0)
+            out_ref[s, l, :, tc:] = jnp.where(
+                inside[:, tc:], result[:, tc:] + nyh_ref[c], 0.0)
             return result
 
         surface = lax.fori_loop(0, levels, backward, zero, unroll=4)
@@ -115,6 +118,54 @@
             ss_out_ref[s] = prior_ref[s] * surface[:tr, :tc]
         else:
             ss_out_ref[s] = ss_ref[s] + prior_ref[s] * surface[:tr, :tc]
+
+
+def _last_step(species, levels, tr, tc, forced_ref, east, west, north, south, remain, se_ref,
+               d0, inv_ref, ratio_ref, red_ref, out_ref, ss_ref, ss_out_ref, prior_ref):
+    row = lax.broadcasted_iota(jnp.int32, (tr, tc), 0)
+    lane = lax.broadcasted_iota(jnp.int32, (tr, tc), 1)
+    last_row = row == tr - 1
+    first_row = row == 0
+    last_lane = lane == tc - 1
+    first_lane = lane == 0
+    e_a, e_b = east[:tr, :tc], east[tr:, :tc]
+    w_a, w_b = west[:tr, :tc], west[tr:, :tc]
+    n_a, n_c = north[:tr, :tc], north[:tr, tc:]
+    s_a, s_c = south[:tr, :tc], south[:tr, tc:]
+    rem = remain[:tr, :tc]
+    zero = jnp.zeros((tr, tc), jnp.float32)
+    for s in range(species):
+
+        def forward(l, reduced):
+            f_a = forced_ref[s, l, :tr, :tc]
+            f_b = forced_ref[s, l, tr:, :tc]
+            f_c = forced_ref[s, l, :tr, tc:]
+            from_east = jnp.where(last_row, pltpu.roll(e_b * f_b, tr - 1, 0),
+                                  pltpu.roll(e_a * f_a, tr - 1, 0))
+            from_west = jnp.where(first_row, pltpu.roll(w_b * f_b, 1, 0),
+                                  pltpu.roll(w_a * f_a, 1, 0))
+            from_north = jnp.where(last_lane, pltpu.roll(n_c * f_c, tc - 1, 1),
+                                   pltpu.roll(n_a * f_a, tc - 1, 1))
+            from_south = jnp.where(first_lane, pltpu.roll(s_c * f_c, 1, 1),
+                                   pltpu.roll(s_a * f_a, 1, 1))
+            moved = f_a * rem
+            moved = moved + from_east + from_west
+            moved = moved + from_north + from_south
+            below = jnp.where(l > 0, se_ref[d0 + jnp.maximum(l - 1, 0), :tr, :tc], zero)
+            reduced = (moved + below * reduced) * inv_ref[l, :tr, :tc]
+            red_ref[l, :tr, :tc] = reduced
+            return reduced
+
+        lax.fori_loop(0, levels, forward, zero, unroll=4)
+
+        def backward(i, result):
+            l = levels - 1 - i
+            result = red_ref[l, :tr, :tc] - ratio_ref[l, :tr, :tc] * result
+            out_ref[s, l] = result
+            return result
+
+        surface = lax.fori_loop(0, levels, backward, zero, unroll=4)
+        ss_out_ref[s] = ss_ref[s] + prior_ref[s] * surface
 
 
 def step_call(k, steps, species, levels, forced, mask, statics, prior, ratios, inverses,

time: 123 us -> 123 us (level)
  no operation moved by 1% of the time
where the time goes in v5:
time: 123 us; the launch traced here: 122 us
  blocking collectives  42.1 us (34%)
  Pallas kernels  37.6 us (31%)
  starting transfers between devices  10.8 us (9%)
  waiting for transfers between devices  10.4 us (8%)
  local copies, waits for them, and re-layouts  7.96 us (6%)
  other arithmetic  7.73 us (6%)
  matrix products  4.78 us (4%)
    pallas_call x4, Pallas kernels, step_call(): pl.pallas_call(functools.partial(_step_kernel, k, steps, first, last), gr...  23.1 us
    all_to_all x1, blocking collectives, local(): received = lax.all_to_all(placed, ('gx', 'gy'), 2, 2, tiled=True)  21.9 us
    all_to_all x1, blocking collectives, local(): lax.all_to_all(partial.reshape(species, devices, nreg // devices), ('gx',...  20.2 us
    ppermute x1, waiting for transfers between devices, extend(): below = lax.ppermute(lo, 'gx', down_x)  7.21 us
    pallas_call x1, Pallas kernels, extend(): pl.pallas_call(functools.partial(_yunpack_kernel, first_static), out_shap...  6.18 us
    unnamed x36, local copies, waits for them, and re-layouts  5.63 us
    pallas_call x1, Pallas kernels, extend(): pl.pallas_call(_ypack_kernel, out_shape=[jax.ShapeDtypeStruct(chans.shape...  5.34 us
    ppermute x1, starting transfers between devices, extend(): left = lax.ppermute(left, 'gy', up_y)  3.99 us
  transfers between devices with their start and end apart: 4, of which 4 were waited for; matrix products, arithmetic and copies ran while one was open for 1% of the time, Pallas kernels for 0%

profile of v5, /device:TPU:1, one launch (start us, length us, event | category | flops | bytes accessed | tf_op | source)
XLA Modules:
  0.0 122.3 jit_solution(10216961372902237763)
XLA Ops:
  0.6 0.8 fusion.8
  1.5 0.3 reduce_window_sum.11
  1.7 0.9 select_reduce_fusion
  2.6 0.7 multiply_add_fusion.1
  3.3 0.7 convert_element_type.29
  4.0 0.7 convert_element_type.30
  4.7 1.2 fusion.6
  5.9 0.2 copy.47
  6.2 0.6 reshape.217
  6.8 21.9 %all_to_all.10 = f32[128,1,272]{2,1,0:T(1,128)S(1)} all-to-all(f32[128,1,272]{2,1,0:T(1,128)S(1)} %reshape.217), channel_id=1, replica_groups=mesh['gx'=8,'gy'=16] {'gx','gy'}, dimensions={0} | all-to-all | bytes 278528 | tf_op jit(solution)/shard_map/all_to_all | solution.py:357
  28.6 0.5 broadcast.335
  29.2 1.1 reduce
  30.3 0.4 reshape.218
  30.7 0.6 fusion.35
  31.3 0.2 copy.71
  31.5 0.1 fusion.36
  31.6 0.2 copy.72
  31.8 0.4 fusion.24
  32.2 0.2 copy.73
  32.6 0.8 add_add_fusion
  33.3 1.7 %fusion = f32[4,80,1024]{2,1,0:T(8,128)S(1)} fusion(f32[4,80,256]{2,1,0:T(8,128)S(1)} %bitcast.57, s32[4,256]{1,0:T(4,128)S(1)} %convert_bitcast_fusion), kind=kOutput, calls=%fused_computation.1 | convolution fusion | flops 1007681536 | bytes 1642496 | tf_op jit(solution)/shard_map/ksq,kqc->ksc/dot_general | solution.py:367
  35.1 0.3 copy.74
  35.3 0.0 copy-start.6
  35.3 0.0 copy-start.7
  35.4 0.0 copy-start.3
  35.4 0.1 constant_dynamic-update-slice_fusion.3
  35.5 0.6 copy-done.6
  36.1 0.0 copy-done.7
  36.1 0.2 copy-done.3
  36.3 0.0 copy-start
  36.3 1.1 copy-done
  37.5 2.9 %shard_map.104 = (f32[192,8,128]{2,1,0:T(8,128)}, f32[192,8,128]{2,1,0:T(8,128)}) custom-call(f32[384,8,128]{2,1,0:T(8,128)} %copy-done), custom_call_target="tpu_custom_call" | custom-call | tf_op jit(solution)/shard_map/pallas_call | solution.py:310
  40.4 2.6 %collective-permute-start = (f32[192,8,128]{2,1,0:T(8,128)}, f32[192,8,128]{2,1,0:T(8,128)S(1)}, u32[]{:S(2)}, u32[]{:S(2)}) collective-permute-start(f32[192,8,128]{2,1,0:T(8,128)} %get-tuple-element.19), channel_id=1, source_target_pairs={{16,0},{32,16},{48,32},{64,48},{80,64},{96,80},{112,96},{17,1},{33... | collective-permute-start | bytes 2359304 | tf_op jit(solution)/shard_map/ppermute | solution.py:313
  43.0 3.0 %collective-permute-start.1 = (f32[192,8,128]{2,1,0:T(8,128)}, f32[192,8,128]{2,1,0:T(8,128)S(1)}, u32[]{:S(2)}, u32[]{:S(2)}) collective-permute-start(f32[192,8,128]{2,1,0:T(8,128)} %get-tuple-element.20), channel_id=1, source_target_pairs={{0,16},{16,32},{32,48},{48,64},{64,80},{80,96},{96,112},{1,17},{17... | collective-permute-start | bytes 2359304 | tf_op jit(solution)/shard_map/ppermute | solution.py:314
  46.0 0.7 and_convert_fusion.refs_3_.refs_1_
  46.7 7.2 %collective-permute-done.below_ref = f32[192,8,128]{2,1,0:T(8,128)S(1)} collective-permute-done((f32[192,8,128]{2,1,0:T(8,128)}, f32[192,8,128]{2,1,0:T(8,128)S(1)}, u32[]{:S(2)}, u32[]{:S(2)}) %collective-permute-start) | collective-permute-done | bytes 786464 | tf_op jit(solution)/shard_map/ppermute | solution.py:313
  53.9 0.0 copy-start.1
  53.9 1.3 %collective-permute-done.1.above_ref = f32[192,8,128]{2,1,0:T(8,128)S(1)} collective-permute-done((f32[192,8,128]{2,1,0:T(8,128)}, f32[192,8,128]{2,1,0:T(8,128)S(1)}, u32[]{:S(2)}, u32[]{:S(2)}) %collective-permute-start.1) | collective-permute-done | bytes 786464 | tf_op jit(solution)/shard_map/ppermute | solution.py:314
  55.2 0.0 copy-done.1
  55.2 0.0 copy-start.2
  55.2 0.9 copy-done.2
  56.1 5.3 %shard_map.105 = (f32[384,8,128]{2,1,0:T(8,128)}, f32[12,16,128]{2,1,0:T(8,128)}, f32[12,16,128]{2,1,0:T(8,128)}) custom-call(f32[384,8,128]{2,1,0:T(8,128)} %copy-done, f32[192,8,128]{2,1,0:T(8,128)} %copy-done.1, f32[192,8,128]{2,1,0:T(8,128)} %copy-done.2), custom_call_target="tpu_custom_call" | custom-call | tf_op jit(solution)/shard_map/pallas_call | solution.py:316
  61.4 1.3 %collective-permute-start.2 = (f32[12,16,128]{2,1,0:T(8,128)}, f32[12,16,128]{2,1,0:T(8,128)S(1)}, u32[]{:S(2)}, u32[]{:S(2)}) collective-permute-start(f32[12,16,128]{2,1,0:T(8,128)} %get-tuple-element.22), channel_id=1, source_target_pairs={{1,0},{2,1},{3,2},{4,3},{5,4},{6,5},{7,6},{8,7},{9,8},{10,9},{11,1... | collective-permute-start | bytes 294920 | tf_op jit(solution)/shard_map/ppermute | solution.py:320
  62.7 4.0 %collective-permute-start.3 = (f32[12,16,128]{2,1,0:T(8,128)}, f32[12,16,128]{2,1,0:T(8,128)S(1)}, u32[]{:S(2)}, u32[]{:S(2)}) collective-permute-start(f32[12,16,128]{2,1,0:T(8,128)} %get-tuple-element.23), channel_id=1, source_target_pairs={{0,1},{1,2},{2,3},{3,4},{4,5},{5,6},{6,7},{7,8},{8,9},{9,10},{10,1... | collective-permute-start | bytes 294920 | tf_op jit(solution)/shard_map/ppermute | solution.py:321
  66.7 0.3 collective-permute-done.2.right_ref
  67.0 0.0 copy-start.4
  67.0 1.7 %collective-permute-done.3.left_ref = f32[12,16,128]{2,1,0:T(8,128)S(1)} collective-permute-done((f32[12,16,128]{2,1,0:T(8,128)}, f32[12,16,128]{2,1,0:T(8,128)S(1)}, u32[]{:S(2)}, u32[]{:S(2)}) %collective-permute-start.3) | collective-permute-done | bytes 98336 | tf_op jit(solution)/shard_map/ppermute | solution.py:321
  68.7 0.0 copy-start.5
  68.7 0.0 copy-done.4
  68.7 0.6 copy-done.5
  69.3 6.2 %shard_map.106 = (f32[384,16,128]{2,1,0:T(8,128)}, f32[47,16,256]{2,1,0:T(8,128)}) custom-call(f32[384,8,128]{2,1,0:T(8,128)} %copy-done, f32[384,8,128]{2,1,0:T(8,128)} %get-tuple-element.21.xh_ref.refs_1_.refs_7_.refs_8_, f32[12,16,128]{2,1,0:T(8,128)} %copy-done.4, f32[12,16,128]{2,1,0:T(8,128)} %copy-done.5), custom_call_target="tpu_custom_call" | custom-call | tf_op jit(solution)/shard_map/pallas_call | solution.py:322
  75.5 6.5 %shard_map.107 = (f32[40,16,256]{2,1,0:T(8,128)}, f32[40,16,256]{2,1,0:T(8,128)}, f32[2,40,16,256]{3,2,1,0:T(8,128)}, f32[2,8,128]{2,1,0:T(8,128)}) custom-call(f32[384,8,128]{2,1,0:T(8,128)} %copy-done, f32[384,8,128]{2,1,0:T(8,128)} %get-tuple-element.21.xh_ref.refs_1_.refs_7_.refs_8_, f32[384,16,128]{2,1,0:T(8,128)} %get-tuple-element.24.refs_2_.refs_8_.refs_9_, ...), custom_call_target="tpu_custom_call" | custom-call | tf_op jit(solution)/shard_map/pallas_call | solution.py:209
  82.0 6.0 %shard_map.108 = (f32[2,40,16,256]{3,2,1,0:T(8,128)}, f32[2,8,128]{2,1,0:T(8,128)}) custom-call(f32[2,40,16,256]{3,2,1,0:T(8,128)} %get-tuple-element.26.refs_0_, f32[16,256]{1,0:T(8,128)} %and_convert_fusion.refs_3_.refs_1_, f32[47,16,256]{2,1,0:T(8,128)} %get-tuple-element.25.refs_4_.refs_2_, f32[2,8,128]{2,1,0:T(8,128)} %refs_3_.5, ...), custom_call_target="tpu_custom_call" | custom-call | tf_op jit(solution)/shard_map/pallas_call | solution.py:209
  88.0 5.9 %shard_map.109 = (f32[2,40,16,256]{3,2,1,0:T(8,128)}, f32[2,8,128]{2,1,0:T(8,128)}) custom-call(f32[2,40,16,256]{3,2,1,0:T(8,128)} %get-tuple-element.30.refs_0_, f32[16,256]{1,0:T(8,128)} %and_convert_fusion.refs_3_.refs_1_, f32[47,16,256]{2,1,0:T(8,128)} %get-tuple-element.25.refs_4_.refs_2_, f32[2,8,128]{2,1,0:T(8,128)} %refs_3_.5, ...), custom_call_target="tpu_custom_call" | custom-call | tf_op jit(solution)/shard_map/pallas_call | solution.py:209
  94.0 0.0 copy-start.8
  94.0 4.7 %shard_map.110 = (f32[2,40,8,128]{3,2,1,0:T(8,128)}, f32[2,8,128]{2,1,0:T(8,128)}) custom-call(f32[2,40,16,256]{3,2,1,0:T(8,128)} %get-tuple-element.32.refs_0_, f32[16,256]{1,0:T(8,128)} %and_convert_fusion.refs_3_.refs_1_, f32[47,16,256]{2,1,0:T(8,128)} %get-tuple-element.25.refs_4_.refs_2_, f32[2,8,128]{2,1,0:T(8,128)} %refs_3_.5, ...), custom_call_target="tpu_custom_call" | custom-call | tf_op jit(solution)/shard_map/pallas_call | solution.py:209
  98.6 0.7 reshape.215
  99.3 0.0 copy-done.8
  99.4 1.9 %fusion.1 = f32[2,128,8]{1,0,2:T(2,128)S(1)} fusion(f32[2,1024,1]{1,0,2:T(2,128)S(1)} %reshape.215, s32[128,8]{0,1:T(8,128)S(1)} %multiply_add_fusion, s32[1024]{0:T(1024)S(1)} %bitcast.65), kind=kOutput, calls=%fused_computation.2 | convolution fusion | flops 26214400 | bytes 24576 | tf_op jit(solution)/shard_map/dot_general | solution.py:403
  101.2 0.2 copy.51
  101.4 20.2 %all_to_all.11 = f32[2,128,8]{2,0,1:T(2,128)S(1)} all-to-all(f32[2,128,8]{2,0,1:T(2,128)S(1)} %copy.51), channel_id=1, replica_groups=mesh['gx'=8,'gy'=16] {'gx','gy'}, dimensions={1} | all-to-all | bytes 16384 | tf_op jit(solution)/shard_map/all_to_all | solution.py:404
  121.6 0.7 reduce_sum.19
  (19 shorter events, 0.2 us)
Async XLA Ops:
  35.3 0.7 copy-start.6
  35.3 0.7 copy-start.7
  35.4 0.9 copy-start.3
  36.3 1.2 copy-start
  40.4 13.5 %collective-permute-start = (f32[192,8,128]{2,1,0:T(8,128)}, f32[192,8,128]{2,1,0:T(8,128)S(1)}, u32[]{:S(2)}, u32[]{:S(2)}) collective-permute-start(f32[192,8,128]{2,1,0:T(8,128)} %get-tuple-element.19), channel_id=1, source_target_pairs={{16,0},{32,16},{48,32},{64,48},{80,64},{96,80},{112,96},{17,1},{33... | collective-permute-start | bytes 2359304 | tf_op jit(solution)/shard_map/ppermute | solution.py:313
  43.0 12.2 %collective-permute-start.1 = (f32[192,8,128]{2,1,0:T(8,128)}, f32[192,8,128]{2,1,0:T(8,128)S(1)}, u32[]{:S(2)}, u32[]{:S(2)}) collective-permute-start(f32[192,8,128]{2,1,0:T(8,128)} %get-tuple-element.20), channel_id=1, source_target_pairs={{0,16},{16,32},{32,48},{48,64},{64,80},{80,96},{96,112},{1,17},{17... | collective-permute-start | bytes 2359304 | tf_op jit(solution)/shard_map/ppermute | solution.py:314
  53.9 1.3 %copy-start.1 = (f32[192,8,128]{2,1,0:T(8,128)}, f32[192,8,128]{2,1,0:T(8,128)S(1)}, u32[]{:S(2)}) copy-start(f32[192,8,128]{2,1,0:T(8,128)S(1)} %collective-permute-done.below_ref) | copy-start | bytes 2359300
  55.2 0.9 copy-start.2
  61.4 5.6 %collective-permute-start.2 = (f32[12,16,128]{2,1,0:T(8,128)}, f32[12,16,128]{2,1,0:T(8,128)S(1)}, u32[]{:S(2)}, u32[]{:S(2)}) collective-permute-start(f32[12,16,128]{2,1,0:T(8,128)} %get-tuple-element.22), channel_id=1, source_target_pairs={{1,0},{2,1},{3,2},{4,3},{5,4},{6,5},{7,6},{8,7},{9,8},{10,9},{11,1... | collective-permute-start | bytes 294920 | tf_op jit(solution)/shard_map/ppermute | solution.py:320
  62.7 5.9 %collective-permute-start.3 = (f32[12,16,128]{2,1,0:T(8,128)}, f32[12,16,128]{2,1,0:T(8,128)S(1)}, u32[]{:S(2)}, u32[]{:S(2)}) collective-permute-start(f32[12,16,128]{2,1,0:T(8,128)} %get-tuple-element.23), channel_id=1, source_target_pairs={{0,1},{1,2},{2,3},{3,4},{4,5},{5,6},{6,7},{7,8},{8,9},{9,10},{10,1... | collective-permute-start | bytes 294920 | tf_op jit(solution)/shard_map/ppermute | solution.py:321
  67.0 1.7 %copy-start.4 = (f32[12,16,128]{2,1,0:T(8,128)}, f32[12,16,128]{2,1,0:T(8,128)S(1)}, u32[]{:S(2)}) copy-start(f32[12,16,128]{2,1,0:T(8,128)S(1)} %collective-permute-done.2.right_ref) | copy-start | bytes 294916
  68.7 0.6 copy-start.5
  94.0 5.4 %copy-start.8 = (s32[8,128]{1,0:T(8,128)S(1)}, s32[8,128]{1,0:T(8,128)}, u32[]{:S(2)}) copy-start(s32[8,128]{1,0:T(8,128)} %param.17) | copy-start | bytes 12292

commit v6 on v5

v6 whole, which is shorter than its diff:
```python
import functools

import jax
import jax.numpy as jnp
from jax import lax
from jax.experimental import pallas as pl
from jax.experimental.pallas import tpu as pltpu
from jax.sharding import PartitionSpec as P

HI = lax.Precision.HIGHEST
REG_DEV = 8


def _full(shape):
    nd = len(shape)
    return pl.BlockSpec(shape, lambda i, _n=nd: (0,) * _n)


def _unpack(r, l, q, cols, half):
    lane = lax.broadcasted_iota(jnp.int32, r.shape, 1)
    rs = (cols - half * q) % cols
    ls = (cols - half - half * q) % cols
    return jnp.where(lane < half, pltpu.roll(r, rs, 1) if rs else r,
                     jnp.where(lane >= cols - half, pltpu.roll(l, ls, 1) if ls else l, 0.0))


def _steps_kernel(steps, species, levels, first_static, n_statics,
                  right_ref, left_ref, mask_ref, prior_ref, chans_hbm, xh_hbm,
                  adj_ref, ss_ref,
                  own_buf, xhb_buf, yh_buf, st_own, st_xh, se_ref, state_ref, red_ref,
                  ratio_ref, inv_ref, sems):
    planes = species * levels
    rows, lanes = mask_ref.shape
    tr, tc = adj_ref.shape[2:]
    half = tr // 2
    group = tc // half
    d0 = 2 * steps

    statics_o = pltpu.make_async_copy(chans_hbm.at[pl.ds(first_static, n_statics)], st_own,
                                      sems.at[0])
    statics_x = pltpu.make_async_copy(xh_hbm.at[pl.ds(first_static, n_statics)], st_xh,
                                      sems.at[1])
    statics_o.start()
    statics_x.start()
    loads = {}
    for k in reversed(range(steps)):
        co = pltpu.make_async_copy(chans_hbm.at[pl.ds(k * planes, planes)], own_buf.at[k],
                                   sems.at[2 + 2 * k])
        cx = pltpu.make_async_copy(xh_hbm.at[pl.ds(k * planes, planes)], xhb_buf.at[k],
                                   sems.at[3 + 2 * k])
        co.start()
        cx.start()
        loads[k] = (co, cx)

    n_fgroups = first_static // group

    def unpack_group(g, carry):
        r = right_ref[g]
        l = left_ref[g]
        for q in range(group):
            yh_buf[g * group + q] = _unpack(r, l, q, tc, half)
        return carry

    lax.fori_loop(0, n_fgroups, unpack_group, 0)
    for c in range(n_statics):
        ch = first_static + c
        se_ref[c, :, tc:] = _unpack(right_ref[ch // group], left_ref[ch // group], ch % group,
                                    tc, half)
    statics_o.wait()
    statics_x.wait()

    def assemble_static(c, carry):
        se_ref[c, :tr, :tc] = st_own[c]
        se_ref[c, tr:, :tc] = st_xh[c]
        return carry

    lax.fori_loop(0, n_statics, assemble_static, 0)

    zero = jnp.zeros((rows, lanes), jnp.float32)
    inside = mask_ref[...] > 0.5
    carried = zero
    for l in range(levels):
        below = se_ref[d0 + l - 1] if l > 0 else zero
        above = se_ref[d0 + l] if l < levels - 1 else zero
        inverse = 1.0 / (1.0 + below + above + below * carried)
        ratio = -above * inverse
        ratio_ref[l] = ratio
        inv_ref[l] = inverse
        carried = ratio

    for k in reversed(range(steps)):
        first = k == steps - 1
        last = k == 0
        if first:
            loads[k][0].wait()
            loads[k][1].wait()
            for s in range(species):

                def assemble(l, carry, s=s, k=k):
                    c = s * levels + l
                    state_ref[s, l, :tr, :tc] = own_buf[k, c]
                    state_ref[s, l, tr:, :tc] = xhb_buf[k, c]
                    state_ref[s, l, :, tc:] = yh_buf[k * planes + c]
                    state_ref[s, l] = jnp.where(inside, state_ref[s, l], 0.0)
                    return carry

                lax.fori_loop(0, levels, assemble, 0, unroll=4)
        if not last:
            loads[k - 1][0].wait()
            loads[k - 1][1].wait()

        wx = se_ref[k]
        wy = se_ref[steps + k]
        east = jnp.maximum(wx, 0.0)
        west = jnp.maximum(-wx, 0.0)
        north = jnp.maximum(wy, 0.0)
        south = jnp.maximum(-wy, 0.0)
        remain = 1.0 - (east + west + north + south)
        if last:
            _last_step(species, levels, tr, tc, state_ref, east, west, north, south, remain,
                       se_ref, d0, inv_ref, ratio_ref, red_ref, adj_ref, ss_ref, prior_ref)
            continue

        for s in range(species):

            def forward(l, reduced, s=s):
                f = state_ref[s, l]
                from_east = pltpu.roll(east * f, rows - 1, 0)
                from_west = pltpu.roll(west * f, 1, 0)
                from_north = pltpu.roll(north * f, lanes - 1, 1)
                from_south = pltpu.roll(south * f, 1, 1)
                moved = f * remain
                moved = moved + from_east + from_west
                moved = moved + from_north + from_south
                below = jnp.where(l > 0, se_ref[d0 + jnp.maximum(l - 1, 0)], zero)
                reduced = (moved + below * reduced) * inv_ref[l]
                red_ref[l] = reduced
                return reduced

            lax.fori_loop(0, levels, forward, zero, unroll=4)

            def backward(i, result, s=s, k=k):
                l = levels - 1 - i
                c = s * levels + l
                result = red_ref[l] - ratio_ref[l] * result
                state_ref[s, l, :tr, :tc] = jnp.where(
                    inside[:tr, :tc], result[:tr, :tc] + own_buf[k - 1, c], 0.0)
                state_ref[s, l, tr:, :tc] = jnp.where(
                    inside[tr:, :tc], result[tr:, :tc] + xhb_buf[k - 1, c], 0.0)
                state_ref[s, l, :, tc:] = jnp.where(
                    inside[:, tc:], result[:, tc:] + yh_buf[(k - 1) * planes + c], 0.0)
                return result

            surface = lax.fori_loop(0, levels, backward, zero, unroll=4)
            if first:
                ss_ref[s] = prior_ref[s] * surface[:tr, :tc]
            else:
                ss_ref[s] = ss_ref[s] + prior_ref[s] * surface[:tr, :tc]


def _last_step(species, levels, tr, tc, forced_ref, east, west, north, south, remain, se_ref,
               d0, inv_ref, ratio_ref, red_ref, out_ref, ss_ref, prior_ref):
    row = lax.broadcasted_iota(jnp.int32, (tr, tc), 0)
    lane = lax.broadcasted_iota(jnp.int32, (tr, tc), 1)
    last_row = row == tr - 1
    first_row = row == 0
    last_lane = lane == tc - 1
    first_lane = lane == 0
    e_a, e_b = east[:tr, :tc], east[tr:, :tc]
    w_a, w_b = west[:tr, :tc], west[tr:, :tc]
    n_a, n_c = north[:tr, :tc], north[:tr, tc:]
    s_a, s_c = south[:tr, :tc], south[:tr, tc:]
    rem = remain[:tr, :tc]
    zero = jnp.zeros((tr, tc), jnp.float32)
    for s in range(species):

        def forward(l, reduced, s=s):
            f_a = forced_ref[s, l, :tr, :tc]
            f_b = forced_ref[s, l, tr:, :tc]
            f_c = forced_ref[s, l, :tr, tc:]
            from_east = jnp.where(last_row, pltpu.roll(e_b * f_b, tr - 1, 0),
                                  pltpu.roll(e_a * f_a, tr - 1, 0))
            from_west = jnp.where(first_row, pltpu.roll(w_b * f_b, 1, 0),
                                  pltpu.roll(w_a * f_a, 1, 0))
            from_north = jnp.where(last_lane, pltpu.roll(n_c * f_c, tc - 1, 1),
                                   pltpu.roll(n_a * f_a, tc - 1, 1))
            from_south = jnp.where(first_lane, pltpu.roll(s_c * f_c, 1, 1),
                                   pltpu.roll(s_a * f_a, 1, 1))
            moved = f_a * rem
            moved = moved + from_east + from_west
            moved = moved + from_north + from_south
            below = jnp.where(l > 0, se_ref[d0 + jnp.maximum(l - 1, 0), :tr, :tc], zero)
            reduced = (moved + below * reduced) * inv_ref[l, :tr, :tc]
            red_ref[l, :tr, :tc] = reduced
            return reduced

        lax.fori_loop(0, levels, forward, zero, unroll=4)

        def backward(i, result, s=s):
            l = levels - 1 - i
            result = red_ref[l, :tr, :tc] - ratio_ref[l, :tr, :tc] * result
            out_ref[s, l] = result
            return result

        surface = lax.fori_loop(0, levels, backward, zero, unroll=4)
        ss_ref[s] = ss_ref[s] + prior_ref[s] * surface


def steps_call(steps, species, levels, first_static, n_statics, right, left, mask, prior,
               chans, xh):
    channels, tr, tc = chans.shape
    rows, lanes = mask.shape
    planes = species * levels
    vmem = pl.BlockSpec(memory_space=pltpu.VMEM)
    anyspace = pl.BlockSpec(memory_space=pl.ANY)
    return pl.pallas_call(
        functools.partial(_steps_kernel, steps, species, levels, first_static, n_statics),
        in_specs=[vmem, vmem, vmem, vmem, anyspace, anyspace],
        out_specs=[vmem, vmem],
        out_shape=[jax.ShapeDtypeStruct((species, levels, tr, tc), jnp.float32),
                   jax.ShapeDtypeStruct(prior.shape, jnp.float32)],
        scratch_shapes=[
            pltpu.VMEM((steps, planes, tr, tc), jnp.float32),
            pltpu.VMEM((steps, planes, tr, tc), jnp.float32),
            pltpu.VMEM((first_static, rows, tc), jnp.float32),
            pltpu.VMEM((n_statics, tr, tc), jnp.float32),
            pltpu.VMEM((n_statics, tr, tc), jnp.float32),
            pltpu.VMEM((n_statics, rows, lanes), jnp.float32),
            pltpu.VMEM((species, levels, rows, lanes), jnp.float32),
            pltpu.VMEM((levels, rows, lanes), jnp.float32),
            pltpu.VMEM((levels, rows, lanes), jnp.float32),
            pltpu.VMEM((levels, rows, lanes), jnp.float32),
            pltpu.SemaphoreType.DMA((2 + 2 * steps,)),
        ],
        compiler_params=pltpu.CompilerParams(vmem_limit_bytes=48 * 1024 * 1024),
    )(right, left, mask, prior, chans, xh)


def _pairs(axis):
    n = lax.axis_size(axis)
    return [(i, i + 1) for i in range(n - 1)], [(i + 1, i) for i in range(n - 1)]


def _whole(shapes):
    return [pl.BlockSpec(memory_space=pltpu.VMEM) for _ in shapes]


def _xpack_kernel(chans_ref, lo_ref, hi_ref):
    rows = chans_ref.shape[1]
    half = rows // 2
    row = lax.broadcasted_iota(jnp.int32, chans_ref.shape[1:], 0)

    def body(i, carry):
        a = chans_ref[2 * i]
        b = chans_ref[2 * i + 1]
        lo_ref[i] = jnp.where(row < half, a, pltpu.roll(b, half, 0))
        hi_ref[i] = jnp.where(row < half, pltpu.roll(a, half, 0), b)
        return carry

    lax.fori_loop(0, lo_ref.shape[0], body, 0, unroll=4)


def _ypack_kernel(chans_ref, below_ref, above_ref, xh_ref, right_ref, left_ref):
    rows, cols = chans_ref.shape[1:]
    half = rows // 2
    group = cols // half
    row = lax.broadcasted_iota(jnp.int32, (rows, cols), 0)
    lane = lax.broadcasted_iota(jnp.int32, (rows, cols), 1)
    zero = jnp.zeros((rows, cols), jnp.float32)

    def body(g, carry):
        acc = [zero, zero, zero, zero]
        for q2 in range(group // 2):
            i = g * (group // 2) + q2
            b = below_ref[i]
            a = above_ref[i]
            xh0 = jnp.where(row < half, b, pltpu.roll(a, half, 0))
            xh1 = jnp.where(row < half, pltpu.roll(b, half, 0), a)
            xh_ref[2 * i] = xh0
            xh_ref[2 * i + 1] = xh1
            for off, top, bot in ((0, chans_ref[2 * i], xh0), (1, chans_ref[2 * i + 1], xh1)):
                q = 2 * q2 + off
                sel = (lane >= half * q) & (lane < half * q + half)
                rs = (half * q) % cols
                ls = (half * q + half) % cols
                acc[0] = jnp.where(sel, pltpu.roll(top, rs, 1) if rs else top, acc[0])
                acc[1] = jnp.where(sel, pltpu.roll(bot, rs, 1) if rs else bot, acc[1])
                acc[2] = jnp.where(sel, pltpu.roll(top, ls, 1) if ls else top, acc[2])
                acc[3] = jnp.where(sel, pltpu.roll(bot, ls, 1) if ls else bot, acc[3])
        right_ref[g, :rows] = acc[0]
        right_ref[g, rows:] = acc[1]
        left_ref[g, :rows] = acc[2]
        left_ref[g, rows:] = acc[3]
        return carry

    lax.fori_loop(0, right_ref.shape[0], body, 0)


def extend(chans, first_static, n_statics):
    up_x, down_x = _pairs("gx")
    up_y, down_y = _pairs("gy")
    channels, rows, cols = chans.shape
    halo = rows // 2
    group = cols // halo
    pairs = jax.ShapeDtypeStruct((channels // 2, rows, cols), jnp.float32)
    lo, hi = pl.pallas_call(
        _xpack_kernel, out_shape=[pairs, pairs],
        in_specs=_whole([chans]), out_specs=_whole([0, 0]))(chans)
    below = lax.ppermute(lo, "gx", down_x)
    above = lax.ppermute(hi, "gx", up_x)
    packed = jax.ShapeDtypeStruct((channels // group, 2 * rows, cols), jnp.float32)
    xh, right, left = pl.pallas_call(
        _ypack_kernel,
        out_shape=[jax.ShapeDtypeStruct(chans.shape, jnp.float32), packed, packed],
        in_specs=_whole([0, 0, 0]), out_specs=_whole([0, 0, 0]))(chans, below, above)
    right = lax.ppermute(right, "gy", down_y)
    left = lax.ppermute(left, "gy", up_y)
    return xh, right, left


def local(pixel_adjoint, pixel_owner, pixel_column, pixel_level, wind_x, wind_y,
          diffusivity, prior_emission, region_map):
    gx_n = lax.axis_size("gx")
    gy_n = lax.axis_size("gy")
    devices = gx_n * gy_n
    steps, rows, cols = wind_x.shape
    levels = diffusivity.shape[0] + 1
    species = prior_emission.shape[0]
    kernel = pixel_adjoint.shape[1] // species
    pixels = pixel_adjoint.shape[2]
    capacity = 2 * pixels // devices
    cells = rows * cols
    slots = devices * capacity
    halo = rows // 2
    assert steps <= halo
    lanes = 2 * cols
    ext_rows = 2 * rows

    owners = pixel_owner[:, :, 0]
    matches = (owners[:, :, None] == jnp.arange(devices, dtype=jnp.int32)).astype(jnp.int32)
    rank = jnp.sum(jnp.cumsum(matches, axis=1) * matches, axis=2) - 1
    position = owners * capacity + rank
    rows_out = jnp.concatenate(
        [pixel_adjoint, pixel_column.astype(jnp.float32)[:, None, :],
         pixel_level.astype(jnp.float32)[:, None, :]], axis=1)
    place = (position[:, :, None] == jnp.arange(slots, dtype=jnp.int32)).astype(jnp.float32)
    placed = jnp.einsum("kap,kpq->kaq", rows_out, place, precision=HI)
    received = lax.all_to_all(placed, ("gx", "gy"), 2, 2, tiled=True)

    payload = received[:, :species * kernel].reshape(steps, species, kernel, slots)
    column = jnp.round(received[:, species * kernel]).astype(jnp.int32)
    start = jnp.round(received[:, species * kernel + 1]).astype(jnp.int32)
    offset = jnp.arange(levels, dtype=jnp.int32)[None, :, None] - start[:, None, :]
    profile = jnp.zeros((steps, species, levels, slots), jnp.float32)
    for j in range(kernel):
        profile = profile + jnp.where((offset == j)[:, None], payload[:, :, j][:, :, None, :], 0.0)
    hits = (column[:, :, None] == jnp.arange(cells, dtype=jnp.int32)).astype(jnp.float32)
    forcing = jnp.einsum("ksq,kqc->ksc", profile.reshape(steps, species * levels, slots), hits,
                         precision=HI)

    n_f = steps * species * levels
    n_s = 2 * steps + levels - 1
    group = cols // halo
    channels = -(-(n_f + n_s) // group) * group
    chans = jnp.concatenate(
        [forcing.reshape(n_f, rows, cols), wind_x, wind_y, diffusivity,
         jnp.zeros((channels - n_f - n_s, rows, cols), jnp.float32)], axis=0)
    xh, right, left = extend(chans, n_f, n_s)

    gxi = lax.axis_index("gx")
    gyi = lax.axis_index("gy")
    r = jnp.arange(ext_rows, dtype=jnp.int32)[:, None]
    c = jnp.arange(lanes, dtype=jnp.int32)[None, :]
    grow = gxi * rows + jnp.where(r < rows + halo, r, r - ext_rows)
    ccol = jnp.where(c < cols + halo, c, c - lanes)
    gcol = gyi * cols + ccol
    inside = ((grow >= 0) & (grow < gx_n * rows) & (gcol >= 0) & (gcol < gy_n * cols)
              & ((c < cols + halo) | (c >= lanes - halo)))
    mask = inside.astype(jnp.float32)

    adjoint, surface_sum = steps_call(steps, species, levels, n_f, n_s, right, left, mask,
                                      prior_emission, chans, xh)

    nreg = REG_DEV * devices
    member = (region_map.reshape(-1)[:, None] == jnp.arange(nreg, dtype=jnp.int32)).astype(jnp.float32)
    partial = jnp.dot(surface_sum.reshape(species, cells), member, precision=HI)
    pieces = lax.all_to_all(partial.reshape(species, devices, nreg // devices), ("gx", "gy"), 1, 1,
                            tiled=True)
    gradient = jnp.sum(pieces, axis=1)
    return adjoint, gradient


def solution(mesh):
    in_specs = (
        P(None, None, ("gx", "gy")),
        P(None, ("gx", "gy"), None),
        P(None, ("gx", "gy")),
        P(None, ("gx", "gy")),
        P(None, "gx", "gy"),
        P(None, "gx", "gy"),
        P(None, "gx", "gy"),
        P(None, "gx", "gy"),
        P("gx", "gy"),
    )
    out_specs = (P(None, None, "gx", "gy"), P(None, ("gx", "gy")))
    return jax.shard_map(local, mesh=mesh, in_specs=in_specs, out_specs=out_specs, check_vma=False)
```

time: 123 us -> 108 us (0.88)
  Pallas kernels: 37.6 us -> 22.9 us
    pallas_call x5 -> x1, Pallas kernels: 29.3 us -> 14.7 us  [steps_call(): pl.pallas_call(functools.partial(_steps_kernel, steps, species, levels, f...]
    unnamed x36 -> x38, local copies, waits for them, and re-layouts: 5.63 us -> 6.39 us
  transfers between devices with their start and end apart: 4 -> 4, of which waited for: 4 -> 4; matrix products, arithmetic and copies ran while one was open for 1% -> 0% of each run, Pallas kernels for 0% -> 0%
where the time goes in v6:
time: 108 us
  blocking collectives  42.1 us (39%)
  Pallas kernels  22.9 us (21%)
  waiting for transfers between devices  11 us (10%)
  starting transfers between devices  10.8 us (10%)
  local copies, waits for them, and re-layouts  8.02 us (7%)
  other arithmetic  7.13 us (7%)
  matrix products  4.77 us (4%)
    all_to_all x1, blocking collectives, local(): received = lax.all_to_all(placed, ('gx', 'gy'), 2, 2, tiled=True)  21.9 us
    all_to_all x1, blocking collectives, local(): lax.all_to_all(partial.reshape(species, devices, nreg // devices), ('gx',...  20.2 us
    pallas_call x1, Pallas kernels, steps_call(): pl.pallas_call(functools.partial(_steps_kernel, steps, species, levels, f...  14.7 us
    ppermute x1, waiting for transfers between devices, extend(): below = lax.ppermute(lo, 'gx', down_x)  7.81 us
    unnamed x38, local copies, waits for them, and re-layouts  6.39 us
    pallas_call x1, Pallas kernels, extend(): pl.pallas_call(_ypack_kernel, out_shape=[jax.ShapeDtypeStruct(chans.shape...  5.32 us
    ppermute x1, starting transfers between devices, extend(): left = lax.ppermute(left, 'gy', up_y)  3.99 us
    ppermute x1, starting transfers between devices, extend(): above = lax.ppermute(hi, 'gx', up_x)  2.95 us
  transfers between devices with their start and end apart: 4, of which 4 were waited for; matrix products, arithmetic and copies ran while one was open for 0% of the time, Pallas kernels for 0%

profile of v6, /device:TPU:1, one launch (start us, length us, event | category | flops | bytes accessed | tf_op | source)
XLA Modules:
  0.0 107.6 jit_solution(15982614079914140183)
XLA Ops:
  0.6 0.8 fusion.8
  1.5 0.3 reduce_window_sum.11
  1.7 0.9 select_reduce_fusion
  2.6 0.7 multiply_add_fusion.1
  3.3 0.7 convert_element_type.29
  4.0 0.7 convert_element_type.30
  4.7 1.2 %fusion.6 = f32[4,34,256]{2,1,0:T(8,128)S(1)} fusion(s32[4,128]{1,0:T(4,128)S(1)} %bitcast.62, f32[4,1,128]{2,1,0:T(1,128)S(1)} %bitcast.64, f32[4,1,128]{2,1,0:T(1,128)S(1)} %bitcast.63, f32[4,32,128]{2,1,0:T(8,128)} %param.9), kind=kOutput, calls=%fused_computation.8 | convolution fusion | flops 53643264 | bytes 210944 | tf_op jit(solution)/shard_map/kap,kpq->kaq/dot_general | solution.py:347
  5.9 0.2 copy.47
  6.2 0.6 reshape.217
  6.8 21.9 %all_to_all.10 = f32[128,1,272]{2,1,0:T(1,128)S(1)} all-to-all(f32[128,1,272]{2,1,0:T(1,128)S(1)} %reshape.217), channel_id=1, replica_groups=mesh['gx'=8,'gy'=16] {'gx','gy'}, dimensions={0} | all-to-all | bytes 278528 | tf_op jit(solution)/shard_map/all_to_all | solution.py:348
  28.6 0.5 broadcast.335
  29.2 1.1 %reduce = f32[128,272]{1,0:T(8,128)S(1)} reduce(f32[128,1,272]{2,1,0:T(1,128)S(1)} %all_to_all.10, f32[]{:T(128)} %broadcast.335), dimensions={1}, to_apply=%all_to_all.6.reduce_sub_computation | reduce | bytes 278532 | tf_op jit(solution)/shard_map/all_to_all | solution.py:348
  30.3 0.4 reshape.218
  30.7 0.6 fusion.35
  31.3 0.2 copy.71
  31.5 0.1 fusion.36
  31.6 0.2 copy.72
  31.8 0.4 fusion.24
  32.2 0.2 copy.73
  32.6 0.8 add_add_fusion
  33.3 1.7 %fusion = f32[4,80,1024]{2,1,0:T(8,128)S(1)} fusion(f32[4,80,256]{2,1,0:T(8,128)S(1)} %bitcast.57, s32[4,256]{1,0:T(4,128)S(1)} %convert_bitcast_fusion), kind=kOutput, calls=%fused_computation.1 | convolution fusion | flops 1007681536 | bytes 1642496 | tf_op jit(solution)/shard_map/ksq,kqc->ksc/dot_general | solution.py:358
  35.0 0.3 copy.74
  35.3 0.0 copy-start.7
  35.3 0.0 copy-start.8
  35.3 0.0 copy-start.6
  35.4 0.1 constant_dynamic-update-slice_fusion.3
  35.4 0.6 copy-done.7
  36.0 0.0 copy-done.8
  36.1 0.2 copy-done.6
  36.3 0.0 copy-start
  36.3 1.2 %copy-done = f32[384,8,128]{2,1,0:T(8,128)} copy-done((f32[384,8,128]{2,1,0:T(8,128)}, f32[384,8,128]{2,1,0:T(8,128)S(1)}, u32[]{:S(2)}) %copy-start) | copy-done | bytes 1572888
  37.5 2.9 %shard_map.104 = (f32[192,8,128]{2,1,0:T(8,128)}, f32[192,8,128]{2,1,0:T(8,128)}) custom-call(f32[384,8,128]{2,1,0:T(8,128)} %copy-done), custom_call_target="tpu_custom_call" | custom-call | tf_op jit(solution)/shard_map/pallas_call | solution.py:306
  40.4 2.6 %collective-permute-start = (f32[192,8,128]{2,1,0:T(8,128)}, f32[192,8,128]{2,1,0:T(8,128)S(1)}, u32[]{:S(2)}, u32[]{:S(2)}) collective-permute-start(f32[192,8,128]{2,1,0:T(8,128)} %get-tuple-element.9), channel_id=1, source_target_pairs={{16,0},{32,16},{48,32},{64,48},{80,64},{96,80},{112,96},{17,1},{33... | collective-permute-start | bytes 2359304 | tf_op jit(solution)/shard_map/ppermute | solution.py:309
  43.0 3.0 %collective-permute-start.1 = (f32[192,8,128]{2,1,0:T(8,128)}, f32[192,8,128]{2,1,0:T(8,128)S(1)}, u32[]{:S(2)}, u32[]{:S(2)}) collective-permute-start(f32[192,8,128]{2,1,0:T(8,128)} %get-tuple-element.10), channel_id=1, source_target_pairs={{0,16},{16,32},{32,48},{48,64},{64,80},{80,96},{96,112},{1,17},{17... | collective-permute-start | bytes 2359304 | tf_op jit(solution)/shard_map/ppermute | solution.py:310
  46.0 0.1 and_convert_fusion.mask_ref
  46.1 0.0 copy-start.1
  46.1 0.0 copy-start.3
  46.1 7.8 %collective-permute-done.below_ref = f32[192,8,128]{2,1,0:T(8,128)S(1)} collective-permute-done((f32[192,8,128]{2,1,0:T(8,128)}, f32[192,8,128]{2,1,0:T(8,128)S(1)}, u32[]{:S(2)}, u32[]{:S(2)}) %collective-permute-start) | collective-permute-done | bytes 786464 | tf_op jit(solution)/shard_map/ppermute | solution.py:309
  53.9 0.0 copy-start.4
  53.9 1.3 %collective-permute-done.1.above_ref = f32[192,8,128]{2,1,0:T(8,128)S(1)} collective-permute-done((f32[192,8,128]{2,1,0:T(8,128)}, f32[192,8,128]{2,1,0:T(8,128)S(1)}, u32[]{:S(2)}, u32[]{:S(2)}) %collective-permute-start.1) | collective-permute-done | bytes 786464 | tf_op jit(solution)/shard_map/ppermute | solution.py:310
  55.2 0.0 copy-done.4
  55.2 0.0 copy-start.5
  55.2 0.9 copy-done.5
  56.0 5.3 %shard_map.105 = (f32[384,8,128]{2,1,0:T(8,128)}, f32[12,16,128]{2,1,0:T(8,128)}, f32[12,16,128]{2,1,0:T(8,128)}) custom-call(f32[384,8,128]{2,1,0:T(8,128)} %copy-done, f32[192,8,128]{2,1,0:T(8,128)} %copy-done.4, f32[192,8,128]{2,1,0:T(8,128)} %copy-done.5), custom_call_target="tpu_custom_call" | custom-call | tf_op jit(solution)/shard_map/pallas_call | solution.py:312
  61.4 1.3 %collective-permute-start.2 = (f32[12,16,128]{2,1,0:T(8,128)}, f32[12,16,128]{2,1,0:T(8,128)S(1)}, u32[]{:S(2)}, u32[]{:S(2)}) collective-permute-start(f32[12,16,128]{2,1,0:T(8,128)} %get-tuple-element.11), channel_id=1, source_target_pairs={{1,0},{2,1},{3,2},{4,3},{5,4},{6,5},{7,6},{8,7},{9,8},{10,9},{11,1... | collective-permute-start | bytes 294920 | tf_op jit(solution)/shard_map/ppermute | solution.py:316
  62.7 4.0 %collective-permute-start.3 = (f32[12,16,128]{2,1,0:T(8,128)}, f32[12,16,128]{2,1,0:T(8,128)S(1)}, u32[]{:S(2)}, u32[]{:S(2)}) collective-permute-start(f32[12,16,128]{2,1,0:T(8,128)} %get-tuple-element.12), channel_id=1, source_target_pairs={{0,1},{1,2},{2,3},{3,4},{4,5},{5,6},{6,7},{7,8},{8,9},{9,10},{10,1... | collective-permute-start | bytes 294920 | tf_op jit(solution)/shard_map/ppermute | solution.py:317
  66.7 0.3 collective-permute-done.2.right_ref
  66.9 1.7 %collective-permute-done.3.left_ref = f32[12,16,128]{2,1,0:T(8,128)S(1)} collective-permute-done((f32[12,16,128]{2,1,0:T(8,128)}, f32[12,16,128]{2,1,0:T(8,128)S(1)}, u32[]{:S(2)}, u32[]{:S(2)}) %collective-permute-start.3) | collective-permute-done | bytes 98336 | tf_op jit(solution)/shard_map/ppermute | solution.py:317
  68.6 0.0 copy-done.1
  68.6 0.0 copy-done.3
  68.6 0.0 copy-start.2
  68.6 1.4 %copy-done.2 = f32[384,8,128]{2,1,0:T(8,128)S(1)} copy-done((f32[384,8,128]{2,1,0:T(8,128)S(1)}, f32[384,8,128]{2,1,0:T(8,128)}, u32[]{:S(2)}) %copy-start.2) | copy-done | bytes 1572888
  70.0 0.0 copy-start.9
  70.0 14.7 %shard_map.106 = (f32[2,40,8,128]{3,2,1,0:T(8,128)}, f32[2,8,128]{2,1,0:T(8,128)S(1)}) custom-call(f32[12,16,128]{2,1,0:T(8,128)S(1)} %collective-permute-done.2.right_ref, f32[12,16,128]{2,1,0:T(8,128)S(1)} %collective-permute-done.3.left_ref, f32[16,256]{1,0:T(8,128)S(1)} %and_convert_fusion.mask_ref, f32[2,8,128]{2,1,0:T(8,128)S(1)} %copy-done.3, ...), custom_call_target="tpu_custom_call" | custom-call | tf_op jit(solution)/shard_map/pallas_call | solution.py:216
  84.7 0.0 copy-done.9
  84.7 1.9 %fusion.1 = f32[2,128,8]{1,0,2:T(2,128)S(1)} fusion(f32[2,1024,1]{1,0,2:T(2,128)S(1)} %reshape.215, s32[128,8]{0,1:T(8,128)S(1)} %multiply_add_fusion, s32[1024]{0:T(1024)S(1)} %bitcast.65), kind=kOutput, calls=%fused_computation.2 | convolution fusion | flops 26214400 | bytes 24576 | tf_op jit(solution)/shard_map/dot_general | solution.py:386
  86.6 0.2 copy.51
  86.7 20.2 %all_to_all.11 = f32[2,128,8]{2,0,1:T(2,128)S(1)} all-to-all(f32[2,128,8]{2,0,1:T(2,128)S(1)} %copy.51), channel_id=1, replica_groups=mesh['gx'=8,'gy'=16] {'gx','gy'}, dimensions={1} | all-to-all | bytes 16384 | tf_op jit(solution)/shard_map/all_to_all | solution.py:387
  106.9 0.7 reduce_sum.19
  (20 shorter events, 0.2 us)
Async XLA Ops:
  35.3 0.7 copy-start.7
  35.3 0.7 copy-start.8
  35.3 0.9 copy-start.6
  36.3 1.2 %copy-start = (f32[384,8,128]{2,1,0:T(8,128)}, f32[384,8,128]{2,1,0:T(8,128)S(1)}, u32[]{:S(2)}) copy-start(f32[384,8,128]{2,1,0:T(8,128)S(1)} %broadcast_dynamic-update-slice_fusion.chans_ref.chans_hbm) | copy-start | bytes 4718596
  40.4 13.5 %collective-permute-start = (f32[192,8,128]{2,1,0:T(8,128)}, f32[192,8,128]{2,1,0:T(8,128)S(1)}, u32[]{:S(2)}, u32[]{:S(2)}) collective-permute-start(f32[192,8,128]{2,1,0:T(8,128)} %get-tuple-element.9), channel_id=1, source_target_pairs={{16,0},{32,16},{48,32},{64,48},{80,64},{96,80},{112,96},{17,1},{33... | collective-permute-start | bytes 2359304 | tf_op jit(solution)/shard_map/ppermute | solution.py:309
  43.0 12.2 %collective-permute-start.1 = (f32[192,8,128]{2,1,0:T(8,128)}, f32[192,8,128]{2,1,0:T(8,128)S(1)}, u32[]{:S(2)}, u32[]{:S(2)}) collective-permute-start(f32[192,8,128]{2,1,0:T(8,128)} %get-tuple-element.10), channel_id=1, source_target_pairs={{0,16},{16,32},{32,48},{48,64},{64,80},{80,96},{96,112},{1,17},{17... | collective-permute-start | bytes 2359304 | tf_op jit(solution)/shard_map/ppermute | solution.py:310
  46.1 22.5 %copy-start.1 = (f32[384,8,128]{2,1,0:T(8,128)S(1)}, f32[384,8,128]{2,1,0:T(8,128)}, u32[]{:S(2)}) copy-start(f32[384,8,128]{2,1,0:T(8,128)} %copy-done) | copy-start | bytes 4718596
  46.1 22.5 %copy-start.3 = (f32[2,8,128]{2,1,0:T(8,128)S(1)}, f32[2,8,128]{2,1,0:T(8,128)}, u32[]{:S(2)}) copy-start(f32[2,8,128]{2,1,0:T(8,128)} %prior_ref.1) | copy-start | bytes 24580
  53.9 1.3 %copy-start.4 = (f32[192,8,128]{2,1,0:T(8,128)}, f32[192,8,128]{2,1,0:T(8,128)S(1)}, u32[]{:S(2)}) copy-start(f32[192,8,128]{2,1,0:T(8,128)S(1)} %collective-permute-done.below_ref) | copy-start | bytes 2359300
  55.2 0.9 copy-start.5
  61.4 5.6 %collective-permute-start.2 = (f32[12,16,128]{2,1,0:T(8,128)}, f32[12,16,128]{2,1,0:T(8,128)S(1)}, u32[]{:S(2)}, u32[]{:S(2)}) collective-permute-start(f32[12,16,128]{2,1,0:T(8,128)} %get-tuple-element.11), channel_id=1, source_target_pairs={{1,0},{2,1},{3,2},{4,3},{5,4},{6,5},{7,6},{8,7},{9,8},{10,9},{11,1... | collective-permute-start | bytes 294920 | tf_op jit(solution)/shard_map/ppermute | solution.py:316
  62.7 5.9 %collective-permute-start.3 = (f32[12,16,128]{2,1,0:T(8,128)}, f32[12,16,128]{2,1,0:T(8,128)S(1)}, u32[]{:S(2)}, u32[]{:S(2)}) collective-permute-start(f32[12,16,128]{2,1,0:T(8,128)} %get-tuple-element.12), channel_id=1, source_target_pairs={{0,1},{1,2},{2,3},{3,4},{4,5},{5,6},{6,7},{7,8},{8,9},{9,10},{10,1... | collective-permute-start | bytes 294920 | tf_op jit(solution)/shard_map/ppermute | solution.py:317
  68.6 1.4 %copy-start.2 = (f32[384,8,128]{2,1,0:T(8,128)S(1)}, f32[384,8,128]{2,1,0:T(8,128)}, u32[]{:S(2)}) copy-start(f32[384,8,128]{2,1,0:T(8,128)} %get-tuple-element.13.xh_hbm) | copy-start | bytes 4718596
  70.0 14.7 %copy-start.9 = (s32[8,128]{1,0:T(8,128)S(1)}, s32[8,128]{1,0:T(8,128)}, u32[]{:S(2)}) copy-start(s32[8,128]{1,0:T(8,128)} %param.17) | copy-start | bytes 12292

commit v7 on v6

--- a/solution.py
+++ b/solution.py
@@ -24,11 +24,93 @@
                      jnp.where(lane >= cols - half, pltpu.roll(l, ls, 1) if ls else l, 0.0))
 
 
-def _steps_kernel(steps, species, levels, first_static, n_statics,
-                  right_ref, left_ref, mask_ref, prior_ref, chans_hbm, xh_hbm,
-                  adj_ref, ss_ref,
-                  own_buf, xhb_buf, yh_buf, st_own, st_xh, se_ref, state_ref, red_ref,
-                  ratio_ref, inv_ref, sems):
+def _exact_dot(a, b):
+    dims = (((1,), (1,)), ((), ()))
+    hi = a.astype(jnp.bfloat16)
+    rest = a - hi.astype(jnp.float32)
+    mid = rest.astype(jnp.bfloat16)
+    lo = (rest - mid.astype(jnp.float32)).astype(jnp.bfloat16)
+    out = lax.dot_general(hi, b, dims, preferred_element_type=jnp.float32)
+    out = out + lax.dot_general(mid, b, dims, preferred_element_type=jnp.float32)
+    return out + lax.dot_general(lo, b, dims, preferred_element_type=jnp.float32)
+
+
+def _forcing_kernel(species, kernel, levels, own_ref, below_ref, above_ref,
+                    tall_ref, right_ref, left_ref, lown_ref, lnb_ref):
+    steps, _, slots = own_ref.shape
+    tr2, tc = tall_ref.shape[2:]
+    tr = tr2 // 2
+    half = tr // 2
+    group = tc // half
+    n_pay = species * kernel
+    lane_t = lax.broadcasted_iota(jnp.int32, (tc, slots), 0)
+    row_i = lax.broadcasted_iota(jnp.int32, (tr, slots), 0)
+    lev_i = lax.broadcasted_iota(jnp.int32, (levels, slots), 0)
+    lane16 = lax.broadcasted_iota(jnp.int32, (tr2, tc), 1)
+    right_ref[...] = jnp.zeros(right_ref.shape, jnp.float32)
+    left_ref[...] = jnp.zeros(left_ref.shape, jnp.float32)
+    for k in range(steps):
+        hts = []
+        for src, ref in enumerate((own_ref, below_ref, above_ref)):
+            blk = ref[k]
+            col = blk[n_pay:n_pay + 1].astype(jnp.int32)
+            lev = blk[n_pay + 1:n_pay + 2].astype(jnp.int32)
+            row_q = col // tc
+            lane_q = col % tc
+            if src == 1:
+                row_q = jnp.where(row_q < half, row_q, -1)
+            elif src == 2:
+                row_q = jnp.where(row_q >= half, row_q, -1)
+            rmask = row_i == row_q
+            hts.append((lane_t == lane_q).astype(jnp.bfloat16))
+            offset = lev_i - lev
+            dst = lown_ref if src == 0 else lnb_ref
+            c0 = 0 if src < 2 else slots
+            for s in range(species):
+                prof = jnp.zeros((levels, slots), jnp.float32)
+                for j in range(kernel):
+                    prof = prof + jnp.where(offset == j, blk[s * kernel + j:s * kernel + j + 1], 0.0)
+                for l in range(levels):
+                    c = s * levels + l
+                    dst[c * tr:(c + 1) * tr, c0:c0 + slots] = jnp.where(
+                        rmask, jnp.broadcast_to(prof[l:l + 1], (tr, slots)), 0.0)
+        own = _exact_dot(lown_ref[...], hts[0])
+        xh = _exact_dot(lnb_ref[...], jnp.concatenate([hts[1], hts[2]], axis=1))
+        planes = own.shape[0] // tr
+        tall_ref[k, :, :tr, :] = own.reshape(planes, tr, tc)
+        tall_ref[k, :, tr:, :] = xh.reshape(planes, tr, tc)
+        for c in range(planes):
+            g, q = divmod(k * planes + c, group)
+            plane = tall_ref[k, c]
+            sel = (lane16 >= half * q) & (lane16 < half * q + half)
+            rs = (half * q) % tc
+            ls = (half * q + half) % tc
+            right_ref[g] = jnp.where(sel, pltpu.roll(plane, rs, 1) if rs else plane, right_ref[g])
+            left_ref[g] = jnp.where(sel, pltpu.roll(plane, ls, 1) if ls else plane, left_ref[g])
+
+
+def forcing_call(species, kernel, levels, own, below, above, cols):
+    steps, _, slots = own.shape
+    tr = 8
+    planes = species * levels
+    group = cols // (tr // 2)
+    packed = jax.ShapeDtypeStruct((steps * planes // group, 2 * tr, cols), jnp.float32)
+    vmem = pl.BlockSpec(memory_space=pltpu.VMEM)
+    return pl.pallas_call(
+        functools.partial(_forcing_kernel, species, kernel, levels),
+        in_specs=[vmem, vmem, vmem],
+        out_specs=[vmem, vmem, vmem],
+        out_shape=[jax.ShapeDtypeStruct((steps, planes, 2 * tr, cols), jnp.float32), packed,
+                   packed],
+        scratch_shapes=[pltpu.VMEM((planes * tr, slots), jnp.float32),
+                        pltpu.VMEM((planes * tr, 2 * slots), jnp.float32)],
+    )(own, below, above)
+
+
+def _steps_kernel(steps, species, levels, n_statics,
+                  right_ref, left_ref, sright_ref, sleft_ref, st_own, st_xh, mask_ref, prior_ref,
+                  tall_hbm, adj_ref, ss_ref,
+                  tall_buf, yh_buf, se_ref, state_ref, red_ref, ratio_ref, inv_ref, sems):
     planes = species * levels
     rows, lanes = mask_ref.shape
     tr, tc = adj_ref.shape[2:]
@@ -36,23 +118,13 @@
     group = tc // half
     d0 = 2 * steps
 
-    statics_o = pltpu.make_async_copy(chans_hbm.at[pl.ds(first_static, n_statics)], st_own,
-                                      sems.at[0])
-    statics_x = pltpu.make_async_copy(xh_hbm.at[pl.ds(first_static, n_statics)], st_xh,
-                                      sems.at[1])
-    statics_o.start()
-    statics_x.start()
     loads = {}
     for k in reversed(range(steps)):
-        co = pltpu.make_async_copy(chans_hbm.at[pl.ds(k * planes, planes)], own_buf.at[k],
-                                   sems.at[2 + 2 * k])
-        cx = pltpu.make_async_copy(xh_hbm.at[pl.ds(k * planes, planes)], xhb_buf.at[k],
-                                   sems.at[3 + 2 * k])
-        co.start()
-        cx.start()
-        loads[k] = (co, cx)
-
-    n_fgroups = first_static // group
+        copy = pltpu.make_async_copy(tall_hbm.at[k], tall_buf.at[k], sems.at[k])
+        copy.start()
+        loads[k] = copy
+
+    n_fgroups = right_ref.shape[0]
 
     def unpack_group(g, carry):
         r = right_ref[g]
@@ -63,11 +135,8 @@
 
     lax.fori_loop(0, n_fgroups, unpack_group, 0)
     for c in range(n_statics):
-        ch = first_static + c
-        se_ref[c, :, tc:] = _unpack(right_ref[ch // group], left_ref[ch // group], ch % group,
+        se_ref[c, :, tc:] = _unpack(sright_ref[c // group], sleft_ref[c // group], c % group,
                                     tc, half)
-    statics_o.wait()
-    statics_x.wait()
 
     def assemble_static(c, carry):
         se_ref[c, :tr, :tc] = st_own[c]
@@ -92,22 +161,19 @@
         first = k == steps - 1
         last = k == 0
         if first:
-            loads[k][0].wait()
-            loads[k][1].wait()
+            loads[k].wait()
             for s in range(species):
 
                 def assemble(l, carry, s=s, k=k):
                     c = s * levels + l
-                    state_ref[s, l, :tr, :tc] = own_buf[k, c]
-                    state_ref[s, l, tr:, :tc] = xhb_buf[k, c]
+                    state_ref[s, l, :, :tc] = tall_buf[k, c]
                     state_ref[s, l, :, tc:] = yh_buf[k * planes + c]
                     state_ref[s, l] = jnp.where(inside, state_ref[s, l], 0.0)
                     return carry
 
                 lax.fori_loop(0, levels, assemble, 0, unroll=4)
         if not last:
-            loads[k - 1][0].wait()
-            loads[k - 1][1].wait()
+            loads[k - 1].wait()
 
         wx = se_ref[k]
         wy = se_ref[steps + k]
@@ -143,10 +209,8 @@
                 l = levels - 1 - i
                 c = s * levels + l
                 result = red_ref[l] - ratio_ref[l] * result
-                state_ref[s, l, :tr, :tc] = jnp.where(
-                    inside[:tr, :tc], result[:tr, :tc] + own_buf[k - 1, c], 0.0)
-                state_ref[s, l, tr:, :tc] = jnp.where(
-                    inside[tr:, :tc], result[tr:, :tc] + xhb_buf[k - 1, c], 0.0)
+                state_ref[s, l, :, :tc] = jnp.where(
+                    inside[:, :tc], result[:, :tc] + tall_buf[k - 1, c], 0.0)
                 state_ref[s, l, :, tc:] = jnp.where(
                     inside[:, tc:], result[:, tc:] + yh_buf[(k - 1) * planes + c], 0.0)
                 return result
@@ -206,34 +270,31 @@
         ss_ref[s] = ss_ref[s] + prior_ref[s] * surface
 
 
-def steps_call(steps, species, levels, first_static, n_statics, right, left, mask, prior,
-               chans, xh):
-    channels, tr, tc = chans.shape
-    rows, lanes = mask.shape
-    planes = species * levels
+def steps_call(steps, species, levels, n_statics, right, left, sright, sleft, st_own, st_xh,
+               mask, prior, tall):
+    _, planes, rows, tc = tall.shape
+    tr = rows // 2
+    lanes = mask.shape[1]
     vmem = pl.BlockSpec(memory_space=pltpu.VMEM)
     anyspace = pl.BlockSpec(memory_space=pl.ANY)
     return pl.pallas_call(
-        functools.partial(_steps_kernel, steps, species, levels, first_static, n_statics),
-        in_specs=[vmem, vmem, vmem, vmem, anyspace, anyspace],
+        functools.partial(_steps_kernel, steps, species, levels, n_statics),
+        in_specs=[vmem] * 8 + [anyspace],
         out_specs=[vmem, vmem],
         out_shape=[jax.ShapeDtypeStruct((species, levels, tr, tc), jnp.float32),
                    jax.ShapeDtypeStruct(prior.shape, jnp.float32)],
         scratch_shapes=[
-            pltpu.VMEM((steps, planes, tr, tc), jnp.float32),
-            pltpu.VMEM((steps, planes, tr, tc), jnp.float32),
-            pltpu.VMEM((first_static, rows, tc), jnp.float32),
-            pltpu.VMEM((n_statics, tr, tc), jnp.float32),
-            pltpu.VMEM((n_statics, tr, tc), jnp.float32),
+            pltpu.VMEM((steps, planes, rows, tc), jnp.float32),
+            pltpu.VMEM((steps * planes, rows, tc), jnp.float32),
             pltpu.VMEM((n_statics, rows, lanes), jnp.float32),
             pltpu.VMEM((species, levels, rows, lanes), jnp.float32),
             pltpu.VMEM((levels, rows, lanes), jnp.float32),
             pltpu.VMEM((levels, rows, lanes), jnp.float32),
             pltpu.VMEM((levels, rows, lanes), jnp.float32),
-            pltpu.SemaphoreType.DMA((2 + 2 * steps,)),
+            pltpu.SemaphoreType.DMA((steps,)),
         ],
         compiler_params=pltpu.CompilerParams(vmem_limit_bytes=48 * 1024 * 1024),
-    )(right, left, mask, prior, chans, xh)
+    )(right, left, sright, sleft, st_own, st_xh, mask, prior, tall)
 
 
 def _pairs(axis):
@@ -347,25 +408,20 @@
     placed = jnp.einsum("kap,kpq->kaq", rows_out, place, precision=HI)
     received = lax.all_to_all(placed, ("gx", "gy"), 2, 2, tiled=True)
 
-    payload = received[:, :species * kernel].reshape(steps, species, kernel, slots)
-    column = jnp.round(received[:, species * kernel]).astype(jnp.int32)
-    start = jnp.round(received[:, species * kernel + 1]).astype(jnp.int32)
-    offset = jnp.arange(levels, dtype=jnp.int32)[None, :, None] - start[:, None, :]
-    profile = jnp.zeros((steps, species, levels, slots), jnp.float32)
-    for j in range(kernel):
-        profile = profile + jnp.where((offset == j)[:, None], payload[:, :, j][:, :, None, :], 0.0)
-    hits = (column[:, :, None] == jnp.arange(cells, dtype=jnp.int32)).astype(jnp.float32)
-    forcing = jnp.einsum("ksq,kqc->ksc", profile.reshape(steps, species * levels, slots), hits,
-                         precision=HI)
-
-    n_f = steps * species * levels
+    up_x, down_x = _pairs("gx")
+    below = lax.ppermute(received, "gx", down_x)
+    above = lax.ppermute(received, "gx", up_x)
+    tall, right, left = forcing_call(species, kernel, levels, received, below, above, cols)
+    up_y, down_y = _pairs("gy")
+    right = lax.ppermute(right, "gy", down_y)
+    left = lax.ppermute(left, "gy", up_y)
+
     n_s = 2 * steps + levels - 1
     group = cols // halo
-    channels = -(-(n_f + n_s) // group) * group
-    chans = jnp.concatenate(
-        [forcing.reshape(n_f, rows, cols), wind_x, wind_y, diffusivity,
-         jnp.zeros((channels - n_f - n_s, rows, cols), jnp.float32)], axis=0)
-    xh, right, left = extend(chans, n_f, n_s)
+    n_pad = -(-n_s // group) * group
+    statics = jnp.concatenate(
+        [wind_x, wind_y, diffusivity, jnp.zeros((n_pad - n_s, rows, cols), jnp.float32)], axis=0)
+    st_xh, sright, sleft = extend(statics, 0, n_s)
 
     gxi = lax.axis_index("gx")
     gyi = lax.axis_index("gy")
@@ -378,8 +434,8 @@
               & ((c < cols + halo) | (c >= lanes - halo)))
     mask = inside.astype(jnp.float32)
 
-    adjoint, surface_sum = steps_call(steps, species, levels, n_f, n_s, right, left, mask,
-                                      prior_emission, chans, xh)
+    adjoint, surface_sum = steps_call(steps, species, levels, n_s, right, left, sright, sleft,
+                                      statics, st_xh, mask, prior_emission, tall)
 
     nreg = REG_DEV * devices
     member = (region_map.reshape(-1)[:, None] == jnp.arange(nreg, dtype=jnp.int32)).astype(jnp.float32)

time: 108 us -> 107 us (level)
  starting transfers between devices: 10.8 us -> 33.3 us
  blocking collectives: 42.1 us -> 23.2 us
  waiting for transfers between devices: 11 us -> 3.79 us
  Pallas kernels: 22.9 us -> 26.8 us
  matrix products: 4.77 us -> 3.06 us
    all_to_all x1 -> x0, blocking collectives: 21.9 us -> none  [local(): received = lax.all_to_all(placed, ('gx', 'gy'), 2, 2, tiled=True)]
    all_to_all x0 -> x1, starting transfers between devices: none -> 11.5 us  [local(): received = lax.all_to_all(placed, ('gx', 'gy'), 2, 2, tiled=True)]
    ppermute x0 -> x4, starting transfers between devices: none -> 11 us  [the longest x1 4.17 us: local(): left = lax.ppermute(left, 'gy', up_y)]
    pallas_call x1 -> x2, Pallas kernels: 14.7 us -> 22.9 us  [the longest x1 14 us: steps_call(): pl.pallas_call(functools.partial(_steps_kernel, steps, species, levels, n...]
    ppermute x1, waiting for transfers between devices: 7.81 us -> 0.01 us  [extend(): below = lax.ppermute(lo, 'gx', down_x)]
    pallas_call x1, Pallas kernels: 5.32 us -> 2.1 us  [extend(): pl.pallas_call(_ypack_kernel, out_shape=[jax.ShapeDtypeStruct(chans.shape...]
    all_to_all x1, blocking collectives: 20.2 us -> 23.2 us  [local(): lax.all_to_all(partial.reshape(species, devices, nreg // devices), ('gx',...]
    all_to_all x0 -> x1, waiting for transfers between devices: none -> 2.21 us  [local(): received = lax.all_to_all(placed, ('gx', 'gy'), 2, 2, tiled=True)]
  transfers between devices with their start and end apart: 4 -> 9, of which waited for: 4 -> 3; matrix products, arithmetic and copies ran while one was open for 0% -> 3% of each run, Pallas kernels for 0% -> 12%
where the time goes in v7:
time: 107 us; the launch traced here: 106 us
  starting transfers between devices  33.3 us (31%)
  Pallas kernels  26.8 us (25%)
  blocking collectives  23.2 us (22%)
  local copies, waits for them, and re-layouts  8.26 us (8%)
  other arithmetic  6.87 us (6%)
  waiting for transfers between devices  3.79 us (4%)
  matrix products  3.06 us (3%)
    all_to_all x1, blocking collectives, local(): lax.all_to_all(partial.reshape(species, devices, nreg // devices), ('gx',...  23.2 us
    pallas_call x1, Pallas kernels, steps_call(): pl.pallas_call(functools.partial(_steps_kernel, steps, species, levels, n...  14 us
    all_to_all x1, starting transfers between devices, local(): received = lax.all_to_all(placed, ('gx', 'gy'), 2, 2, tiled=True)  11.5 us
    pallas_call x1, Pallas kernels, forcing_call(): pl.pallas_call(functools.partial(_forcing_kernel, species, kernel, levels...  8.86 us
    unnamed x28, local copies, waits for them, and re-layouts  7.03 us
    ppermute x1, starting transfers between devices, local(): left = lax.ppermute(left, 'gy', up_y)  4.17 us
    ppermute x1, starting transfers between devices, extend(): left = lax.ppermute(left, 'gy', up_y)  3.99 us
    ppermute x1, starting transfers between devices, extend(): below = lax.ppermute(lo, 'gx', down_x)  2.96 us
  transfers between devices with their start and end apart: 9, of which 3 were waited for; matrix products, arithmetic and copies ran while one was open for 3% of the time, Pallas kernels for 12%

profile of v7, /device:TPU:1, one launch (start us, length us, event | category | flops | bytes accessed | tf_op | source)
XLA Modules:
  0.0 106.3 jit_solution(8843459176218949187)
XLA Ops:
  0.6 0.0 copy-start.11
  0.6 0.0 copy-start.10
  0.7 0.0 copy-start.7
  0.7 0.9 fusion.6
  1.5 0.3 reduce_window_sum.11
  1.8 0.9 select_reduce_fusion
  2.7 0.7 multiply_add_fusion.1
  3.4 0.7 convert_element_type.14
  4.1 0.7 convert_element_type.15
  4.8 1.2 %fusion.4 = f32[4,34,256]{2,1,0:T(8,128)S(1)} fusion(s32[4,128]{1,0:T(4,128)S(1)} %bitcast.14, f32[4,1,128]{2,1,0:T(1,128)S(1)} %bitcast.16, f32[4,1,128]{2,1,0:T(1,128)S(1)} %bitcast.15, f32[4,32,128]{2,1,0:T(8,128)} %param.9), kind=kOutput, calls=%fused_computation.5 | convolution fusion | flops 53643264 | bytes 210944 | tf_op jit(solution)/shard_map/kap,kpq->kaq/dot_general | solution.py:408
  6.0 0.0 copy-start.3
  6.0 0.2 copy.18
  6.2 1.3 %reshape.87 = f32[128,1,272]{2,1,0:T(1,128)} reshape(f32[256,4,34]{2,1,0:T(4,128)S(1)} %bitcast.9) | data formatting | bytes 278528
  7.5 11.5 %all-to-all-start = ((f32[128,1,272]{2,1,0:T(1,128)}), f32[128,1,272]{2,1,0:T(1,128)S(1)}, u32[]{:S(2)}, u32[]{:S(2)}) async-start(f32[128,1,272]{2,1,0:T(1,128)} %reshape.87), calls=%async_computation | async-start | bytes 393216 | tf_op jit(solution)/shard_map/all_to_all | solution.py:409
  19.0 0.1 pad.3.clone
  19.1 0.0 copy-done.11
  19.1 0.0 copy-done.10
  19.1 0.0 copy-done.7
  19.1 0.8 maximum_maximum_fusion.chans_ref.st_own
  19.9 1.8 %shard_map.105 = (f32[32,8,128]{2,1,0:T(8,128)}, f32[32,8,128]{2,1,0:T(8,128)}) custom-call(f32[64,8,128]{2,1,0:T(8,128)} %maximum_maximum_fusion.chans_ref.st_own), custom_call_target="tpu_custom_call" | custom-call | tf_op jit(solution)/shard_map/pallas_call | solution.py:367
  21.7 3.0 %collective-permute-start.4 = (f32[32,8,128]{2,1,0:T(8,128)}, f32[32,8,128]{2,1,0:T(8,128)S(1)}, u32[]{:S(2)}, u32[]{:S(2)}) collective-permute-start(f32[32,8,128]{2,1,0:T(8,128)} %get-tuple-element.14), channel_id=1, source_target_pairs={{16,0},{32,16},{48,32},{64,48},{80,64},{96,80},{112,96},{17,1},{33... | collective-permute-start | bytes 393224 | tf_op jit(solution)/shard_map/ppermute | solution.py:370
  24.7 2.6 %collective-permute-start.5 = (f32[32,8,128]{2,1,0:T(8,128)}, f32[32,8,128]{2,1,0:T(8,128)S(1)}, u32[]{:S(2)}, u32[]{:S(2)}) collective-permute-start(f32[32,8,128]{2,1,0:T(8,128)} %get-tuple-element.15), channel_id=1, source_target_pairs={{0,16},{16,32},{32,48},{48,64},{64,80},{80,96},{96,112},{1,17},{17... | collective-permute-start | bytes 393224 | tf_op jit(solution)/shard_map/ppermute | solution.py:371
  27.4 2.2 %all-to-all-done = f32[128,1,272]{2,1,0:T(1,128)S(1)} async-done(((f32[128,1,272]{2,1,0:T(1,128)}), f32[128,1,272]{2,1,0:T(1,128)S(1)}, u32[]{:S(2)}, u32[]{:S(2)}) %all-to-all-start) | async-done | bytes 139296 | tf_op jit(solution)/shard_map/all_to_all | solution.py:409
  29.6 0.5 broadcast.143
  30.1 1.1 %reduce = f32[128,272]{1,0:T(8,128)S(1)} reduce(f32[128,1,272]{2,1,0:T(1,128)S(1)} %all-to-all-done, f32[]{:T(128)} %broadcast.143), dimensions={1}, to_apply=%all_to_all.6.reduce_sub_computation | reduce | bytes 278532 | tf_op jit(solution)/shard_map/all_to_all | solution.py:409
  31.2 0.4 reshape.88
  31.7 0.0 copy-start.12
  31.7 0.2 copy.21.own_ref
  31.9 0.0 copy-start.4
  31.9 2.6 %collective-permute-start = (f32[4,34,256]{2,1,0:T(8,128)S(1)}, f32[4,34,256]{2,1,0:T(8,128)S(1)}, u32[]{:S(2)}, u32[]{:S(2)}) collective-permute-start(f32[4,34,256]{2,1,0:T(8,128)S(1)} %copy.21.own_ref), channel_id=1, source_target_pairs={{16,0},{32,16},{48,32},{64,48},{80,64},{96,80},{112,96},{17,1},{33... | collective-permute-start | bytes 417800 | tf_op jit(solution)/shard_map/ppermute | solution.py:412
  34.5 3.0 %collective-permute-start.1 = (f32[4,34,256]{2,1,0:T(8,128)S(1)}, f32[4,34,256]{2,1,0:T(8,128)S(1)}, u32[]{:S(2)}, u32[]{:S(2)}) collective-permute-start(f32[4,34,256]{2,1,0:T(8,128)S(1)} %copy.21.own_ref), channel_id=1, source_target_pairs={{0,16},{16,32},{32,48},{48,64},{64,80},{80,96},{96,112},{1,17},{17... | collective-permute-start | bytes 417800 | tf_op jit(solution)/shard_map/ppermute | solution.py:413
  37.5 0.1 and_convert_fusion.mask_ref
  37.6 0.0 collective-permute-done.4.below_ref
  37.6 0.0 copy-start.8
  37.6 0.0 collective-permute-done.5.above_ref
  37.6 0.6 copy-done.8
  38.2 0.0 copy-start.9
  38.2 0.6 copy-done.9
  38.9 2.1 %shard_map.106 = (f32[64,8,128]{2,1,0:T(8,128)}, f32[2,16,128]{2,1,0:T(8,128)}, f32[2,16,128]{2,1,0:T(8,128)}) custom-call(f32[64,8,128]{2,1,0:T(8,128)} %maximum_maximum_fusion.chans_ref.st_own, f32[32,8,128]{2,1,0:T(8,128)} %copy-done.8, f32[32,8,128]{2,1,0:T(8,128)} %copy-done.9), custom_call_target="tpu_custom_call" | custom-call | tf_op jit(solution)/shard_map/pallas_call | solution.py:373
  41.0 1.3 %collective-permute-start.6 = (f32[2,16,128]{2,1,0:T(8,128)}, f32[2,16,128]{2,1,0:T(8,128)S(1)}, u32[]{:S(2)}, u32[]{:S(2)}) collective-permute-start(f32[2,16,128]{2,1,0:T(8,128)} %get-tuple-element.16), channel_id=1, source_target_pairs={{1,0},{2,1},{3,2},{4,3},{5,4},{6,5},{7,6},{8,7},{9,8},{10,9},{11,1... | collective-permute-start | bytes 49160 | tf_op jit(solution)/shard_map/ppermute | solution.py:377
  42.3 4.0 %collective-permute-start.7 = (f32[2,16,128]{2,1,0:T(8,128)}, f32[2,16,128]{2,1,0:T(8,128)S(1)}, u32[]{:S(2)}, u32[]{:S(2)}) collective-permute-start(f32[2,16,128]{2,1,0:T(8,128)} %get-tuple-element.17), channel_id=1, source_target_pairs={{0,1},{1,2},{2,3},{3,4},{4,5},{5,6},{6,7},{7,8},{8,9},{9,10},{10,1... | collective-permute-start | bytes 49160 | tf_op jit(solution)/shard_map/ppermute | solution.py:378
  46.3 0.0 collective-permute-done.below_ref
  46.3 0.0 copy-start.5
  46.3 0.0 collective-permute-done.1.above_ref
  46.3 0.0 copy-done.4
  46.3 0.6 copy-done.5
  46.9 0.7 copy-done.6
  47.6 8.9 %shard_map.104 = (f32[4,80,16,128]{3,2,1,0:T(8,128)}, f32[10,16,128]{2,1,0:T(8,128)}, f32[10,16,128]{2,1,0:T(8,128)}) custom-call(f32[4,34,256]{2,1,0:T(8,128)} %copy-done.4, f32[4,34,256]{2,1,0:T(8,128)} %copy-done.5, f32[4,34,256]{2,1,0:T(8,128)} %copy-done.6), custom_call_target="tpu_custom_call" | custom-call | tf_op jit(solution)/shard_map/pallas_call | solution.py:99
  56.5 1.3 %collective-permute-start.2 = (f32[10,16,128]{2,1,0:T(8,128)}, f32[10,16,128]{2,1,0:T(8,128)S(1)}, u32[]{:S(2)}, u32[]{:S(2)}) collective-permute-start(f32[10,16,128]{2,1,0:T(8,128)} %get-tuple-element.12), channel_id=1, source_target_pairs={{1,0},{2,1},{3,2},{4,3},{5,4},{6,5},{7,6},{8,7},{9,8},{10,9},{11,1... | collective-permute-start | bytes 245768 | tf_op jit(solution)/shard_map/ppermute | solution.py:416
  57.8 4.2 %collective-permute-start.3 = (f32[10,16,128]{2,1,0:T(8,128)}, f32[10,16,128]{2,1,0:T(8,128)S(1)}, u32[]{:S(2)}, u32[]{:S(2)}) collective-permute-start(f32[10,16,128]{2,1,0:T(8,128)} %get-tuple-element.13), channel_id=1, source_target_pairs={{0,1},{1,2},{2,3},{3,4},{4,5},{5,6},{6,7},{7,8},{8,9},{9,10},{10,1... | collective-permute-start | bytes 245768 | tf_op jit(solution)/shard_map/ppermute | solution.py:417
  61.9 0.0 collective-permute-done.6.sright_ref
  62.0 0.0 collective-permute-done.7.sleft_ref
  62.0 0.6 collective-permute-done.2.right_ref
  62.6 0.9 collective-permute-done.3.left_ref
  63.5 0.0 copy-done.3
  63.5 0.0 copy-done
  63.5 1.7 %copy-done.1 = f32[4,80,16,128]{3,2,1,0:T(8,128)S(1)} copy-done((f32[4,80,16,128]{3,2,1,0:T(8,128)S(1)}, f32[4,80,16,128]{3,2,1,0:T(8,128)}, u32[]{:S(2)}) %copy-start.1) | copy-done | bytes 2621464
  65.3 0.9 copy-done.2
  66.2 14.0 %shard_map.107 = (f32[2,40,8,128]{3,2,1,0:T(8,128)}, f32[2,8,128]{2,1,0:T(8,128)S(1)}) custom-call(f32[10,16,128]{2,1,0:T(8,128)S(1)} %collective-permute-done.2.right_ref, f32[10,16,128]{2,1,0:T(8,128)S(1)} %collective-permute-done.3.left_ref, f32[2,16,128]{2,1,0:T(8,128)S(1)} %collective-permute-done.6.sright_ref, ...), custom_call_target="tpu_custom_call" | custom-call | tf_op jit(solution)/shard_map/pallas_call | solution.py:280
  80.3 0.0 copy-done.12
  80.3 1.9 %fusion = f32[2,128,8]{1,0,2:T(2,128)S(1)} fusion(f32[2,1024,1]{1,0,2:T(2,128)S(1)} %reshape.85, s32[128,8]{0,1:T(8,128)S(1)} %multiply_add_fusion, s32[1024]{0:T(1024)S(1)} %bitcast.17), kind=kOutput, calls=%fused_computation | convolution fusion | flops 26214400 | bytes 24576 | tf_op jit(solution)/shard_map/dot_general | solution.py:442
  82.2 0.2 copy.22
  82.3 23.2 %all_to_all.10 = f32[2,128,8]{2,0,1:T(2,128)S(1)} all-to-all(f32[2,128,8]{2,0,1:T(2,128)S(1)} %copy.22), channel_id=1, replica_groups=mesh['gx'=8,'gy'=16] {'gx','gy'}, dimensions={1} | all-to-all | bytes 16384 | tf_op jit(solution)/shard_map/all_to_all | solution.py:443
  105.6 0.7 reduce_sum.19
  (11 shorter events, 0.1 us)
Async XLA Ops:
  0.6 18.5 %copy-start.11 = (f32[4,8,128]{2,1,0:T(8,128)S(1)}, f32[4,8,128]{2,1,0:T(8,128)}, u32[]{:S(2)}) copy-start(f32[4,8,128]{2,1,0:T(8,128)} %param.13) | copy-start | bytes 49156
  0.6 18.5 %copy-start.10 = (f32[4,8,128]{2,1,0:T(8,128)S(1)}, f32[4,8,128]{2,1,0:T(8,128)}, u32[]{:S(2)}) copy-start(f32[4,8,128]{2,1,0:T(8,128)} %param.14) | copy-start | bytes 49156
  0.7 18.5 %copy-start.7 = (f32[39,8,128]{2,1,0:T(8,128)S(1)}, f32[39,8,128]{2,1,0:T(8,128)}, u32[]{:S(2)}) copy-start(f32[39,8,128]{2,1,0:T(8,128)} %param.15) | copy-start | bytes 479236
  6.0 57.6 %copy-start.3 = (f32[2,8,128]{2,1,0:T(8,128)S(1)}, f32[2,8,128]{2,1,0:T(8,128)}, u32[]{:S(2)}) copy-start(f32[2,8,128]{2,1,0:T(8,128)} %prior_ref.1) | copy-start | bytes 24580
  7.5 22.1 %all-to-all-start = ((f32[128,1,272]{2,1,0:T(1,128)}), f32[128,1,272]{2,1,0:T(1,128)S(1)}, u32[]{:S(2)}, u32[]{:S(2)}) async-start(f32[128,1,272]{2,1,0:T(1,128)} %reshape.87), calls=%async_computation | async-start | bytes 393216 | tf_op jit(solution)/shard_map/all_to_all | solution.py:409
  19.9 43.6 %copy-start = (f32[64,8,128]{2,1,0:T(8,128)S(1)}, f32[64,8,128]{2,1,0:T(8,128)}, u32[]{:S(2)}) copy-start(f32[64,8,128]{2,1,0:T(8,128)} %maximum_maximum_fusion.chans_ref.st_own) | copy-start | bytes 786436
  21.7 15.8 %collective-permute-start.4 = (f32[32,8,128]{2,1,0:T(8,128)}, f32[32,8,128]{2,1,0:T(8,128)S(1)}, u32[]{:S(2)}, u32[]{:S(2)}) collective-permute-start(f32[32,8,128]{2,1,0:T(8,128)} %get-tuple-element.14), channel_id=1, source_target_pairs={{16,0},{32,16},{48,32},{64,48},{80,64},{96,80},{112,96},{17,1},{33... | collective-permute-start | bytes 393224 | tf_op jit(solution)/shard_map/ppermute | solution.py:370
  24.7 12.9 %collective-permute-start.5 = (f32[32,8,128]{2,1,0:T(8,128)}, f32[32,8,128]{2,1,0:T(8,128)S(1)}, u32[]{:S(2)}, u32[]{:S(2)}) collective-permute-start(f32[32,8,128]{2,1,0:T(8,128)} %get-tuple-element.15), channel_id=1, source_target_pairs={{0,16},{16,32},{32,48},{48,64},{64,80},{80,96},{96,112},{1,17},{17... | collective-permute-start | bytes 393224 | tf_op jit(solution)/shard_map/ppermute | solution.py:371
  31.7 48.6 %copy-start.12 = (s32[8,128]{1,0:T(8,128)S(1)}, s32[8,128]{1,0:T(8,128)}, u32[]{:S(2)}) copy-start(s32[8,128]{1,0:T(8,128)} %param.17) | copy-start | bytes 12292
  31.9 14.4 %copy-start.4 = (f32[4,34,256]{2,1,0:T(8,128)}, f32[4,34,256]{2,1,0:T(8,128)S(1)}, u32[]{:S(2)}) copy-start(f32[4,34,256]{2,1,0:T(8,128)S(1)} %copy.21.own_ref) | copy-start | bytes 417796
  31.9 14.3 %collective-permute-start = (f32[4,34,256]{2,1,0:T(8,128)S(1)}, f32[4,34,256]{2,1,0:T(8,128)S(1)}, u32[]{:S(2)}, u32[]{:S(2)}) collective-permute-start(f32[4,34,256]{2,1,0:T(8,128)S(1)} %copy.21.own_ref), channel_id=1, source_target_pairs={{16,0},{32,16},{48,32},{64,48},{80,64},{96,80},{112,96},{17,1},{33... | collective-permute-start | bytes 417800 | tf_op jit(solution)/shard_map/ppermute | solution.py:412
  34.5 11.8 %collective-permute-start.1 = (f32[4,34,256]{2,1,0:T(8,128)S(1)}, f32[4,34,256]{2,1,0:T(8,128)S(1)}, u32[]{:S(2)}, u32[]{:S(2)}) collective-permute-start(f32[4,34,256]{2,1,0:T(8,128)S(1)} %copy.21.own_ref), channel_id=1, source_target_pairs={{0,16},{16,32},{32,48},{48,64},{64,80},{80,96},{96,112},{1,17},{17... | collective-permute-start | bytes 417800 | tf_op jit(solution)/shard_map/ppermute | solution.py:413
  37.6 0.7 copy-start.8
  38.2 0.6 copy-start.9
  41.0 21.0 %collective-permute-start.6 = (f32[2,16,128]{2,1,0:T(8,128)}, f32[2,16,128]{2,1,0:T(8,128)S(1)}, u32[]{:S(2)}, u32[]{:S(2)}) collective-permute-start(f32[2,16,128]{2,1,0:T(8,128)} %get-tuple-element.16), channel_id=1, source_target_pairs={{1,0},{2,1},{3,2},{4,3},{5,4},{6,5},{7,6},{8,7},{9,8},{10,9},{11,1... | collective-permute-start | bytes 49160 | tf_op jit(solution)/shard_map/ppermute | solution.py:377
  42.3 19.7 %collective-permute-start.7 = (f32[2,16,128]{2,1,0:T(8,128)}, f32[2,16,128]{2,1,0:T(8,128)S(1)}, u32[]{:S(2)}, u32[]{:S(2)}) collective-permute-start(f32[2,16,128]{2,1,0:T(8,128)} %get-tuple-element.17), channel_id=1, source_target_pairs={{0,1},{1,2},{2,3},{3,4},{4,5},{5,6},{6,7},{7,8},{8,9},{9,10},{10,1... | collective-permute-start | bytes 49160 | tf_op jit(solution)/shard_map/ppermute | solution.py:378
  46.3 0.7 copy-start.5
  46.9 0.7 copy-start.6
  56.5 6.1 %collective-permute-start.2 = (f32[10,16,128]{2,1,0:T(8,128)}, f32[10,16,128]{2,1,0:T(8,128)S(1)}, u32[]{:S(2)}, u32[]{:S(2)}) collective-permute-start(f32[10,16,128]{2,1,0:T(8,128)} %get-tuple-element.12), channel_id=1, source_target_pairs={{1,0},{2,1},{3,2},{4,3},{5,4},{6,5},{7,6},{8,7},{9,8},{10,9},{11,1... | collective-permute-start | bytes 245768 | tf_op jit(solution)/shard_map/ppermute | solution.py:416
  57.8 5.8 %collective-permute-start.3 = (f32[10,16,128]{2,1,0:T(8,128)}, f32[10,16,128]{2,1,0:T(8,128)S(1)}, u32[]{:S(2)}, u32[]{:S(2)}) collective-permute-start(f32[10,16,128]{2,1,0:T(8,128)} %get-tuple-element.13), channel_id=1, source_target_pairs={{0,1},{1,2},{2,3},{3,4},{4,5},{5,6},{6,7},{7,8},{8,9},{9,10},{10,1... | collective-permute-start | bytes 245768 | tf_op jit(solution)/shard_map/ppermute | solution.py:417
  63.5 1.7 %copy-start.1 = (f32[4,80,16,128]{3,2,1,0:T(8,128)S(1)}, f32[4,80,16,128]{3,2,1,0:T(8,128)}, u32[]{:S(2)}) copy-start(f32[4,80,16,128]{3,2,1,0:T(8,128)} %get-tuple-element.19.tall_hbm) | copy-start | bytes 7864324
  65.3 0.9 copy-start.2

commit v8 on v7

--- a/solution.py
+++ b/solution.py
@@ -24,15 +24,41 @@
                      jnp.where(lane >= cols - half, pltpu.roll(l, ls, 1) if ls else l, 0.0))
 
 
+def _pack_kernel(capacity, adj_ref, owner_ref, col_ref, lev_ref, out_ref, rows_ref):
+    steps, n_pay, pixels = adj_ref.shape
+    slots = out_ref.shape[2]
+    row = lax.broadcasted_iota(jnp.int32, (pixels, pixels), 0)
+    lane = lax.broadcasted_iota(jnp.int32, (pixels, pixels), 1)
+    slot = lax.broadcasted_iota(jnp.int32, (pixels, slots), 1).astype(jnp.float32)
+    for k in range(steps):
+        owner = jnp.broadcast_to(owner_ref[k].astype(jnp.float32), (pixels, pixels))
+        same = (owner == jnp.transpose(owner)) & (lane < row)
+        rank = jnp.sum(jnp.where(same, 1.0, 0.0), axis=1, keepdims=True)
+        position = owner[:, :1] * capacity + rank
+        place = jnp.where(position == slot, 1.0, 0.0)
+        rows_ref[:n_pay] = adj_ref[k]
+        rows_ref[n_pay:n_pay + 1] = col_ref[k:k + 1].astype(jnp.float32)
+        rows_ref[n_pay + 1:n_pay + 2] = lev_ref[k:k + 1].astype(jnp.float32)
+        out_ref[k] = lax.dot_general(rows_ref[...], place, (((1,), (0,)), ((), ())),
+                                     precision=lax.Precision.HIGHEST,
+                                     preferred_element_type=jnp.float32)
+
+
+def pack_call(capacity, slots, pixel_adjoint, pixel_owner, pixel_column, pixel_level):
+    steps, n_pay, pixels = pixel_adjoint.shape
+    vmem = pl.BlockSpec(memory_space=pltpu.VMEM)
+    return pl.pallas_call(
+        functools.partial(_pack_kernel, capacity),
+        in_specs=[vmem] * 4,
+        out_specs=vmem,
+        out_shape=jax.ShapeDtypeStruct((steps, n_pay + 2, slots), jnp.float32),
+        scratch_shapes=[pltpu.VMEM((n_pay + 2, pixels), jnp.float32)],
+    )(pixel_adjoint, pixel_owner, pixel_column, pixel_level)
+
+
 def _exact_dot(a, b):
-    dims = (((1,), (1,)), ((), ()))
-    hi = a.astype(jnp.bfloat16)
-    rest = a - hi.astype(jnp.float32)
-    mid = rest.astype(jnp.bfloat16)
-    lo = (rest - mid.astype(jnp.float32)).astype(jnp.bfloat16)
-    out = lax.dot_general(hi, b, dims, preferred_element_type=jnp.float32)
-    out = out + lax.dot_general(mid, b, dims, preferred_element_type=jnp.float32)
-    return out + lax.dot_general(lo, b, dims, preferred_element_type=jnp.float32)
+    return lax.dot_general(a, b.astype(jnp.float32), (((1,), (1,)), ((), ())),
+                           precision=lax.Precision.HIGHEST, preferred_element_type=jnp.float32)
 
 
 def _forcing_kernel(species, kernel, levels, own_ref, below_ref, above_ref,
@@ -397,15 +423,7 @@
     lanes = 2 * cols
     ext_rows = 2 * rows
 
-    owners = pixel_owner[:, :, 0]
-    matches = (owners[:, :, None] == jnp.arange(devices, dtype=jnp.int32)).astype(jnp.int32)
-    rank = jnp.sum(jnp.cumsum(matches, axis=1) * matches, axis=2) - 1
-    position = owners * capacity + rank
-    rows_out = jnp.concatenate(
-        [pixel_adjoint, pixel_column.astype(jnp.float32)[:, None, :],
-         pixel_level.astype(jnp.float32)[:, None, :]], axis=1)
-    place = (position[:, :, None] == jnp.arange(slots, dtype=jnp.int32)).astype(jnp.float32)
-    placed = jnp.einsum("kap,kpq->kaq", rows_out, place, precision=HI)
+    placed = pack_call(capacity, slots, pixel_adjoint, pixel_owner, pixel_column, pixel_level)
     received = lax.all_to_all(placed, ("gx", "gy"), 2, 2, tiled=True)
 
     up_x, down_x = _pairs("gx")

time: 107 us -> 111 us (1.037)
  Pallas kernels: 26.8 us -> 32.4 us
  other arithmetic: 6.87 us -> 3.51 us
  local copies, waits for them, and re-layouts: 8.26 us -> 10.8 us
  matrix products: 3.06 us -> 1.87 us
    pallas_call x1, Pallas kernels: 8.86 us -> 12 us  [forcing_call(): pl.pallas_call(functools.partial(_forcing_kernel, species, kernel, levels...]
    pallas_call x0 -> x1, Pallas kernels: none -> 2.45 us  [pack_call(): pl.pallas_call(functools.partial(_pack_kernel, capacity), in_specs=[vmem]...]
    convert_element_type x3 -> x0, other arithmetic: 2.22 us -> none  [the longest x1 0.85 us: local(): (owners[:, :, None] == jnp.arange(devices, dtype=jnp.int32)).astype(jnp.i...]
    unnamed x28 -> x25, local copies, waits for them, and re-layouts: 7.03 us -> 8.6 us
    dot_general x1 -> x0, matrix products: 1.19 us -> none  [local(): placed = jnp.einsum('kap,kpq->kaq', rows_out, place, precision=HI)]
    pallas_call x0 -> x1, local copies, waits for them, and re-layouts: none -> 1.17 us  [pack_call(): pl.pallas_call(functools.partial(_pack_kernel, capacity), in_specs=[vmem]...]
  transfers between devices with their start and end apart: 9 -> 9, of which waited for: 3 -> 3; matrix products, arithmetic and copies ran while one was open for 3% -> 4% of each run, Pallas kernels for 12% -> 14%
where the time goes in v8:
time: 111 us; the launch traced here: 110 us
  starting transfers between devices  33.3 us (30%)
  Pallas kernels  32.4 us (29%)
  blocking collectives  23.9 us (22%)
  local copies, waits for them, and re-layouts  10.8 us (10%)
  other arithmetic  3.51 us (3%)
  waiting for transfers between devices  3.26 us (3%)
  matrix products  1.87 us (2%)
    all_to_all x1, blocking collectives, local(): lax.all_to_all(partial.reshape(species, devices, nreg // devices), ('gx',...  23.9 us
    pallas_call x1, Pallas kernels, steps_call(): pl.pallas_call(functools.partial(_steps_kernel, steps, species, levels, n...  14 us
    pallas_call x1, Pallas kernels, forcing_call(): pl.pallas_call(functools.partial(_forcing_kernel, species, kernel, levels...  12 us
    all_to_all x1, starting transfers between devices, local(): received = lax.all_to_all(placed, ('gx', 'gy'), 2, 2, tiled=True)  11.5 us
    unnamed x25, local copies, waits for them, and re-layouts  8.6 us
    ppermute x1, starting transfers between devices, extend(): left = lax.ppermute(left, 'gy', up_y)  4.17 us
    ppermute x1, starting transfers between devices, local(): left = lax.ppermute(left, 'gy', up_y)  3.99 us
    ppermute x1, starting transfers between devices, extend(): below = lax.ppermute(lo, 'gx', down_x)  2.96 us
  transfers between devices with their start and end apart: 9, of which 3 were waited for; matrix products, arithmetic and copies ran while one was open for 4% of the time, Pallas kernels for 14%

profile of v8, /device:TPU:1, one launch (start us, length us, event | category | flops | bytes accessed | tf_op | source)
XLA Modules:
  0.0 109.9 jit_solution(12921621575123638233)
XLA Ops:
  0.6 0.0 copy-start.7
  0.6 1.6 %copy.20.owner_ref = s32[4,128,1]{2,1,0:T(8,128)} copy(s32[4,128,1]{1,2,0:T(1,128)} %param.10) | data formatting | bytes 4096 | tf_op args[1]
  2.2 2.4 %shard_map.104 = f32[4,34,256]{2,1,0:T(8,128)} custom-call(f32[4,32,128]{2,1,0:T(8,128)} %adj_ref.1, s32[4,128,1]{2,1,0:T(8,128)} %copy.20.owner_ref, s32[4,128]{1,0:T(4,128)} %col_ref.1, s32[4,128]{1,0:T(4,128)} %lev_ref.1), custom_call_target="tpu_custom_call" | custom-call | tf_op jit(solution)/shard_map/pallas_call | solution.py:50
  4.7 0.0 copy-start.3
  4.7 1.2 %copy.21 = f32[4,34,256]{1,0,2:T(4,128)S(1)} copy(f32[4,34,256]{2,1,0:T(8,128)} %shard_map.104) | data formatting | bytes 278528 | tf_op jit(solution)/shard_map/pallas_call | solution.py:50
  5.8 1.3 %reshape.78 = f32[128,1,272]{2,1,0:T(1,128)} reshape(f32[256,4,34]{2,1,0:T(4,128)S(1)} %bitcast.4) | data formatting | bytes 278528
  7.1 11.5 %all-to-all-start = ((f32[128,1,272]{2,1,0:T(1,128)}), f32[128,1,272]{2,1,0:T(1,128)S(1)}, u32[]{:S(2)}, u32[]{:S(2)}) async-start(f32[128,1,272]{2,1,0:T(1,128)} %reshape.78), calls=%async_computation | async-start | bytes 393216 | tf_op jit(solution)/shard_map/all_to_all | solution.py:427
  18.6 0.1 pad.3.clone
  18.7 0.0 copy-done.7
  18.7 1.6 %maximum_maximum_fusion.chans_ref.st_own = f32[64,8,128]{2,1,0:T(8,128)} fusion(f32[39,8,128]{2,1,0:T(8,128)S(1)} %copy-done.7, f32[4,8,128]{2,1,0:T(8,128)} %param.14, f32[4,8,128]{2,1,0:T(8,128)} %param.13, f32[64]{0:T(128)S(1)} %pad.3.clone), kind=kLoop, calls=%fused_computation.4 | loop fusion | flops 196608 | bytes 454912 | tf_op jit(solution)/shard_map/concatenate | solution.py:440
  20.3 0.0 copy-start
  20.3 1.8 %shard_map.106 = (f32[32,8,128]{2,1,0:T(8,128)}, f32[32,8,128]{2,1,0:T(8,128)}) custom-call(f32[64,8,128]{2,1,0:T(8,128)} %maximum_maximum_fusion.chans_ref.st_own), custom_call_target="tpu_custom_call" | custom-call | tf_op jit(solution)/shard_map/pallas_call | solution.py:393
  22.0 3.0 %collective-permute-start.4 = (f32[32,8,128]{2,1,0:T(8,128)}, f32[32,8,128]{2,1,0:T(8,128)S(1)}, u32[]{:S(2)}, u32[]{:S(2)}) collective-permute-start(f32[32,8,128]{2,1,0:T(8,128)} %get-tuple-element.14), channel_id=1, source_target_pairs={{16,0},{32,16},{48,32},{64,48},{80,64},{96,80},{112,96},{17,1},{33... | collective-permute-start | bytes 393224 | tf_op jit(solution)/shard_map/ppermute | solution.py:396
  25.0 2.6 %collective-permute-start.5 = (f32[32,8,128]{2,1,0:T(8,128)}, f32[32,8,128]{2,1,0:T(8,128)S(1)}, u32[]{:S(2)}, u32[]{:S(2)}) collective-permute-start(f32[32,8,128]{2,1,0:T(8,128)} %get-tuple-element.15), channel_id=1, source_target_pairs={{0,16},{16,32},{32,48},{48,64},{64,80},{80,96},{96,112},{1,17},{17... | collective-permute-start | bytes 393224 | tf_op jit(solution)/shard_map/ppermute | solution.py:397
  27.7 1.5 %all-to-all-done = f32[128,1,272]{2,1,0:T(1,128)S(1)} async-done(((f32[128,1,272]{2,1,0:T(1,128)}), f32[128,1,272]{2,1,0:T(1,128)S(1)}, u32[]{:S(2)}, u32[]{:S(2)}) %all-to-all-start) | async-done | bytes 139296 | tf_op jit(solution)/shard_map/all_to_all | solution.py:427
  29.2 0.5 broadcast.123
  29.7 1.1 %reduce = f32[128,272]{1,0:T(8,128)S(1)} reduce(f32[128,1,272]{2,1,0:T(1,128)S(1)} %all-to-all-done, f32[]{:T(128)} %broadcast.123), dimensions={1}, to_apply=%all_to_all.6.reduce_sub_computation | reduce | bytes 278532 | tf_op jit(solution)/shard_map/all_to_all | solution.py:427
  30.8 0.4 reshape.79
  31.3 0.0 copy-start.10
  31.3 0.2 copy.24.own_ref
  31.5 0.0 copy-start.4
  31.5 2.6 %collective-permute-start = (f32[4,34,256]{2,1,0:T(8,128)S(1)}, f32[4,34,256]{2,1,0:T(8,128)S(1)}, u32[]{:S(2)}, u32[]{:S(2)}) collective-permute-start(f32[4,34,256]{2,1,0:T(8,128)S(1)} %copy.24.own_ref), channel_id=1, source_target_pairs={{16,0},{32,16},{48,32},{64,48},{80,64},{96,80},{112,96},{17,1},{33... | collective-permute-start | bytes 417800 | tf_op jit(solution)/shard_map/ppermute | solution.py:430
  34.1 3.0 %collective-permute-start.1 = (f32[4,34,256]{2,1,0:T(8,128)S(1)}, f32[4,34,256]{2,1,0:T(8,128)S(1)}, u32[]{:S(2)}, u32[]{:S(2)}) collective-permute-start(f32[4,34,256]{2,1,0:T(8,128)S(1)} %copy.24.own_ref), channel_id=1, source_target_pairs={{0,16},{16,32},{32,48},{48,64},{64,80},{80,96},{96,112},{1,17},{17... | collective-permute-start | bytes 417800 | tf_op jit(solution)/shard_map/ppermute | solution.py:431
  37.1 0.1 and_convert_fusion.mask_ref
  37.2 0.0 collective-permute-done.4.below_ref
  37.2 0.0 copy-start.8
  37.2 0.0 collective-permute-done.5.above_ref
  37.2 0.6 copy-done.8
  37.8 0.0 copy-start.9
  37.8 0.7 copy-done.9
  38.5 2.1 %shard_map.107 = (f32[64,8,128]{2,1,0:T(8,128)}, f32[2,16,128]{2,1,0:T(8,128)}, f32[2,16,128]{2,1,0:T(8,128)}) custom-call(f32[64,8,128]{2,1,0:T(8,128)} %maximum_maximum_fusion.chans_ref.st_own, f32[32,8,128]{2,1,0:T(8,128)} %copy-done.8, f32[32,8,128]{2,1,0:T(8,128)} %copy-done.9), custom_call_target="tpu_custom_call" | custom-call | tf_op jit(solution)/shard_map/pallas_call | solution.py:399
  40.6 1.3 %collective-permute-start.6 = (f32[2,16,128]{2,1,0:T(8,128)}, f32[2,16,128]{2,1,0:T(8,128)S(1)}, u32[]{:S(2)}, u32[]{:S(2)}) collective-permute-start(f32[2,16,128]{2,1,0:T(8,128)} %get-tuple-element.16), channel_id=1, source_target_pairs={{1,0},{2,1},{3,2},{4,3},{5,4},{6,5},{7,6},{8,7},{9,8},{10,9},{11,1... | collective-permute-start | bytes 49160 | tf_op jit(solution)/shard_map/ppermute | solution.py:403
  41.9 4.2 %collective-permute-start.7 = (f32[2,16,128]{2,1,0:T(8,128)}, f32[2,16,128]{2,1,0:T(8,128)S(1)}, u32[]{:S(2)}, u32[]{:S(2)}) collective-permute-start(f32[2,16,128]{2,1,0:T(8,128)} %get-tuple-element.17), channel_id=1, source_target_pairs={{0,1},{1,2},{2,3},{3,4},{4,5},{5,6},{6,7},{7,8},{8,9},{9,10},{10,1... | collective-permute-start | bytes 49160 | tf_op jit(solution)/shard_map/ppermute | solution.py:404
  46.0 0.0 collective-permute-done.below_ref
  46.0 0.0 copy-start.5
  46.1 0.0 collective-permute-done.1.above_ref
  46.1 0.0 copy-done.4
  46.1 0.6 copy-done.5
  46.7 0.0 copy-start.6
  46.7 0.7 copy-done.6
  47.4 12.0 %shard_map.105 = (f32[4,80,16,128]{3,2,1,0:T(8,128)}, f32[10,16,128]{2,1,0:T(8,128)}, f32[10,16,128]{2,1,0:T(8,128)}) custom-call(f32[4,34,256]{2,1,0:T(8,128)} %copy-done.4, f32[4,34,256]{2,1,0:T(8,128)} %copy-done.5, f32[4,34,256]{2,1,0:T(8,128)} %copy-done.6), custom_call_target="tpu_custom_call" | custom-call | tf_op jit(solution)/shard_map/pallas_call | solution.py:125
  59.4 1.3 %collective-permute-start.2 = (f32[10,16,128]{2,1,0:T(8,128)}, f32[10,16,128]{2,1,0:T(8,128)S(1)}, u32[]{:S(2)}, u32[]{:S(2)}) collective-permute-start(f32[10,16,128]{2,1,0:T(8,128)} %get-tuple-element.12), channel_id=1, source_target_pairs={{1,0},{2,1},{3,2},{4,3},{5,4},{6,5},{7,6},{8,7},{9,8},{10,9},{11,1... | collective-permute-start | bytes 245768 | tf_op jit(solution)/shard_map/ppermute | solution.py:434
  60.7 4.0 %collective-permute-start.3 = (f32[10,16,128]{2,1,0:T(8,128)}, f32[10,16,128]{2,1,0:T(8,128)S(1)}, u32[]{:S(2)}, u32[]{:S(2)}) collective-permute-start(f32[10,16,128]{2,1,0:T(8,128)} %get-tuple-element.13), channel_id=1, source_target_pairs={{0,1},{1,2},{2,3},{3,4},{4,5},{5,6},{6,7},{7,8},{8,9},{9,10},{10,1... | collective-permute-start | bytes 245768 | tf_op jit(solution)/shard_map/ppermute | solution.py:435
  64.7 0.0 collective-permute-done.6.sright_ref
  64.7 0.0 collective-permute-done.7.sleft_ref
  64.7 0.8 collective-permute-done.2.right_ref
  65.6 0.9 collective-permute-done.3.left_ref
  66.5 0.0 copy-done.3
  66.5 0.0 copy-done
  66.5 0.0 copy-start.1
  66.5 1.7 %copy-done.1 = f32[4,80,16,128]{3,2,1,0:T(8,128)S(1)} copy-done((f32[4,80,16,128]{3,2,1,0:T(8,128)S(1)}, f32[4,80,16,128]{3,2,1,0:T(8,128)}, u32[]{:S(2)}) %copy-start.1) | copy-done | bytes 2621464
  68.2 0.0 copy-start.2
  68.2 0.9 copy-done.2
  69.2 14.0 %shard_map.108 = (f32[2,40,8,128]{3,2,1,0:T(8,128)}, f32[2,8,128]{2,1,0:T(8,128)S(1)}) custom-call(f32[10,16,128]{2,1,0:T(8,128)S(1)} %collective-permute-done.2.right_ref, f32[10,16,128]{2,1,0:T(8,128)S(1)} %collective-permute-done.3.left_ref, f32[2,16,128]{2,1,0:T(8,128)S(1)} %collective-permute-done.6.sright_ref, ...), custom_call_target="tpu_custom_call" | custom-call | tf_op jit(solution)/shard_map/pallas_call | solution.py:306
  83.2 0.0 copy-done.10
  83.3 1.9 %fusion = f32[2,128,8]{1,0,2:T(2,128)S(1)} fusion(f32[2,1024,1]{1,0,2:T(2,128)S(1)} %reshape.76, s32[128,8]{0,1:T(8,128)S(1)} %multiply_add_fusion, s32[1024]{0:T(1024)S(1)} %bitcast.6), kind=kOutput, calls=%fused_computation | convolution fusion | flops 26214400 | bytes 24576 | tf_op jit(solution)/shard_map/dot_general | solution.py:460
  85.1 0.2 copy.25
  85.3 23.9 %all_to_all.10 = f32[2,128,8]{2,0,1:T(2,128)S(1)} all-to-all(f32[2,128,8]{2,0,1:T(2,128)S(1)} %copy.25), channel_id=1, replica_groups=mesh['gx'=8,'gy'=16] {'gx','gy'}, dimensions={1} | all-to-all | bytes 16384 | tf_op jit(solution)/shard_map/all_to_all | solution.py:461
  109.2 0.7 reduce_sum.9
  (6 shorter events, 0.0 us)
Async XLA Ops:
  0.6 18.1 %copy-start.7 = (f32[39,8,128]{2,1,0:T(8,128)S(1)}, f32[39,8,128]{2,1,0:T(8,128)}, u32[]{:S(2)}) copy-start(f32[39,8,128]{2,1,0:T(8,128)} %param.15) | copy-start | bytes 479236
  4.7 61.8 %copy-start.3 = (f32[2,8,128]{2,1,0:T(8,128)S(1)}, f32[2,8,128]{2,1,0:T(8,128)}, u32[]{:S(2)}) copy-start(f32[2,8,128]{2,1,0:T(8,128)} %prior_ref.1) | copy-start | bytes 24580
  7.1 22.1 %all-to-all-start = ((f32[128,1,272]{2,1,0:T(1,128)}), f32[128,1,272]{2,1,0:T(1,128)S(1)}, u32[]{:S(2)}, u32[]{:S(2)}) async-start(f32[128,1,272]{2,1,0:T(1,128)} %reshape.78), calls=%async_computation | async-start | bytes 393216 | tf_op jit(solution)/shard_map/all_to_all | solution.py:427
  20.3 46.2 %copy-start = (f32[64,8,128]{2,1,0:T(8,128)S(1)}, f32[64,8,128]{2,1,0:T(8,128)}, u32[]{:S(2)}) copy-start(f32[64,8,128]{2,1,0:T(8,128)} %maximum_maximum_fusion.chans_ref.st_own) | copy-start | bytes 786436
  22.0 15.1 %collective-permute-start.4 = (f32[32,8,128]{2,1,0:T(8,128)}, f32[32,8,128]{2,1,0:T(8,128)S(1)}, u32[]{:S(2)}, u32[]{:S(2)}) collective-permute-start(f32[32,8,128]{2,1,0:T(8,128)} %get-tuple-element.14), channel_id=1, source_target_pairs={{16,0},{32,16},{48,32},{64,48},{80,64},{96,80},{112,96},{17,1},{33... | collective-permute-start | bytes 393224 | tf_op jit(solution)/shard_map/ppermute | solution.py:396
  25.0 12.2 %collective-permute-start.5 = (f32[32,8,128]{2,1,0:T(8,128)}, f32[32,8,128]{2,1,0:T(8,128)S(1)}, u32[]{:S(2)}, u32[]{:S(2)}) collective-permute-start(f32[32,8,128]{2,1,0:T(8,128)} %get-tuple-element.15), channel_id=1, source_target_pairs={{0,16},{16,32},{32,48},{48,64},{64,80},{80,96},{96,112},{1,17},{17... | collective-permute-start | bytes 393224 | tf_op jit(solution)/shard_map/ppermute | solution.py:397
  31.3 52.0 %copy-start.10 = (s32[8,128]{1,0:T(8,128)S(1)}, s32[8,128]{1,0:T(8,128)}, u32[]{:S(2)}) copy-start(s32[8,128]{1,0:T(8,128)} %param.17) | copy-start | bytes 12292
  31.5 14.6 %copy-start.4 = (f32[4,34,256]{2,1,0:T(8,128)}, f32[4,34,256]{2,1,0:T(8,128)S(1)}, u32[]{:S(2)}) copy-start(f32[4,34,256]{2,1,0:T(8,128)S(1)} %copy.24.own_ref) | copy-start | bytes 417796
  31.5 14.5 %collective-permute-start = (f32[4,34,256]{2,1,0:T(8,128)S(1)}, f32[4,34,256]{2,1,0:T(8,128)S(1)}, u32[]{:S(2)}, u32[]{:S(2)}) collective-permute-start(f32[4,34,256]{2,1,0:T(8,128)S(1)} %copy.24.own_ref), channel_id=1, source_target_pairs={{16,0},{32,16},{48,32},{64,48},{80,64},{96,80},{112,96},{17,1},{33... | collective-permute-start | bytes 417800 | tf_op jit(solution)/shard_map/ppermute | solution.py:430
  34.1 11.9 %collective-permute-start.1 = (f32[4,34,256]{2,1,0:T(8,128)S(1)}, f32[4,34,256]{2,1,0:T(8,128)S(1)}, u32[]{:S(2)}, u32[]{:S(2)}) collective-permute-start(f32[4,34,256]{2,1,0:T(8,128)S(1)} %copy.24.own_ref), channel_id=1, source_target_pairs={{0,16},{16,32},{32,48},{48,64},{64,80},{80,96},{96,112},{1,17},{17... | collective-permute-start | bytes 417800 | tf_op jit(solution)/shard_map/ppermute | solution.py:431
  37.2 0.6 copy-start.8
  37.8 0.7 copy-start.9
  40.6 24.1 %collective-permute-start.6 = (f32[2,16,128]{2,1,0:T(8,128)}, f32[2,16,128]{2,1,0:T(8,128)S(1)}, u32[]{:S(2)}, u32[]{:S(2)}) collective-permute-start(f32[2,16,128]{2,1,0:T(8,128)} %get-tuple-element.16), channel_id=1, source_target_pairs={{1,0},{2,1},{3,2},{4,3},{5,4},{6,5},{7,6},{8,7},{9,8},{10,9},{11,1... | collective-permute-start | bytes 49160 | tf_op jit(solution)/shard_map/ppermute | solution.py:403
  41.9 22.9 %collective-permute-start.7 = (f32[2,16,128]{2,1,0:T(8,128)}, f32[2,16,128]{2,1,0:T(8,128)S(1)}, u32[]{:S(2)}, u32[]{:S(2)}) collective-permute-start(f32[2,16,128]{2,1,0:T(8,128)} %get-tuple-element.17), channel_id=1, source_target_pairs={{0,1},{1,2},{2,3},{3,4},{4,5},{5,6},{6,7},{7,8},{8,9},{9,10},{10,1... | collective-permute-start | bytes 49160 | tf_op jit(solution)/shard_map/ppermute | solution.py:404
  46.0 0.7 copy-start.5
  46.7 0.7 copy-start.6
  59.4 6.1 %collective-permute-start.2 = (f32[10,16,128]{2,1,0:T(8,128)}, f32[10,16,128]{2,1,0:T(8,128)S(1)}, u32[]{:S(2)}, u32[]{:S(2)}) collective-permute-start(f32[10,16,128]{2,1,0:T(8,128)} %get-tuple-element.12), channel_id=1, source_target_pairs={{1,0},{2,1},{3,2},{4,3},{5,4},{6,5},{7,6},{8,7},{9,8},{10,9},{11,1... | collective-permute-start | bytes 245768 | tf_op jit(solution)/shard_map/ppermute | solution.py:434
  60.7 5.8 %collective-permute-start.3 = (f32[10,16,128]{2,1,0:T(8,128)}, f32[10,16,128]{2,1,0:T(8,128)S(1)}, u32[]{:S(2)}, u32[]{:S(2)}) collective-permute-start(f32[10,16,128]{2,1,0:T(8,128)} %get-tuple-element.13), channel_id=1, source_target_pairs={{0,1},{1,2},{2,3},{3,4},{4,5},{5,6},{6,7},{7,8},{8,9},{9,10},{10,1... | collective-permute-start | bytes 245768 | tf_op jit(solution)/shard_map/ppermute | solution.py:435
  66.5 1.7 %copy-start.1 = (f32[4,80,16,128]{3,2,1,0:T(8,128)S(1)}, f32[4,80,16,128]{3,2,1,0:T(8,128)}, u32[]{:S(2)}) copy-start(f32[4,80,16,128]{3,2,1,0:T(8,128)} %get-tuple-element.19.tall_hbm) | copy-start | bytes 7864324
  68.2 0.9 copy-start.2

commit v9 on v8

--- a/solution.py
+++ b/solution.py
@@ -57,8 +57,14 @@
 
 
 def _exact_dot(a, b):
-    return lax.dot_general(a, b.astype(jnp.float32), (((1,), (1,)), ((), ())),
-                           precision=lax.Precision.HIGHEST, preferred_element_type=jnp.float32)
+    dims = (((1,), (1,)), ((), ()))
+    hi = a.astype(jnp.bfloat16)
+    rest = a - hi.astype(jnp.float32)
+    mid = rest.astype(jnp.bfloat16)
+    lo = (rest - mid.astype(jnp.float32)).astype(jnp.bfloat16)
+    out = lax.dot_general(hi, b, dims, preferred_element_type=jnp.float32)
+    out = out + lax.dot_general(mid, b, dims, preferred_element_type=jnp.float32)
+    return out + lax.dot_general(lo, b, dims, preferred_element_type=jnp.float32)
 
 
 def _forcing_kernel(species, kernel, levels, own_ref, below_ref, above_ref,
@@ -213,9 +219,11 @@
                        se_ref, d0, inv_ref, ratio_ref, red_ref, adj_ref, ss_ref, prior_ref)
             continue
 
-        for s in range(species):
-
-            def forward(l, reduced, s=s):
+        def forward(l, reduced):
+            below = jnp.where(l > 0, se_ref[d0 + jnp.maximum(l - 1, 0)], zero)
+            inverse = inv_ref[l]
+            out = []
+            for s in range(species):
                 f = state_ref[s, l]
                 from_east = pltpu.roll(east * f, rows - 1, 0)
                 from_west = pltpu.roll(west * f, 1, 0)
@@ -224,28 +232,33 @@
                 moved = f * remain
                 moved = moved + from_east + from_west
                 moved = moved + from_north + from_south
-                below = jnp.where(l > 0, se_ref[d0 + jnp.maximum(l - 1, 0)], zero)
-                reduced = (moved + below * reduced) * inv_ref[l]
-                red_ref[l] = reduced
-                return reduced
-
-            lax.fori_loop(0, levels, forward, zero, unroll=4)
-
-            def backward(i, result, s=s, k=k):
-                l = levels - 1 - i
+                r = (moved + below * reduced[s]) * inverse
+                red_ref[s, l] = r
+                out.append(r)
+            return tuple(out)
+
+        lax.fori_loop(0, levels, forward, (zero,) * species, unroll=4)
+
+        def backward(i, result, k=k):
+            l = levels - 1 - i
+            ratio = ratio_ref[l]
+            out = []
+            for s in range(species):
                 c = s * levels + l
-                result = red_ref[l] - ratio_ref[l] * result
+                r = red_ref[s, l] - ratio * result[s]
                 state_ref[s, l, :, :tc] = jnp.where(
-                    inside[:, :tc], result[:, :tc] + tall_buf[k - 1, c], 0.0)
+                    inside[:, :tc], r[:, :tc] + tall_buf[k - 1, c], 0.0)
                 state_ref[s, l, :, tc:] = jnp.where(
-                    inside[:, tc:], result[:, tc:] + yh_buf[(k - 1) * planes + c], 0.0)
-                return result
-
-            surface = lax.fori_loop(0, levels, backward, zero, unroll=4)
+                    inside[:, tc:], r[:, tc:] + yh_buf[(k - 1) * planes + c], 0.0)
+                out.append(r)
+            return tuple(out)
+
+        surface = lax.fori_loop(0, levels, backward, (zero,) * species, unroll=4)
+        for s in range(species):
             if first:
-                ss_ref[s] = prior_ref[s] * surface[:tr, :tc]
+                ss_ref[s] = prior_ref[s] * surface[s][:tr, :tc]
             else:
-                ss_ref[s] = ss_ref[s] + prior_ref[s] * surface[:tr, :tc]
+                ss_ref[s] = ss_ref[s] + prior_ref[s] * surface[s][:tr, :tc]
 
 
 def _last_step(species, levels, tr, tc, forced_ref, east, west, north, south, remain, se_ref,
@@ -262,9 +275,11 @@
     s_a, s_c = south[:tr, :tc], south[:tr, tc:]
     rem = remain[:tr, :tc]
     zero = jnp.zeros((tr, tc), jnp.float32)
-    for s in range(species):
-
-        def forward(l, reduced, s=s):
+    def forward(l, reduced):
+        below = jnp.where(l > 0, se_ref[d0 + jnp.maximum(l - 1, 0), :tr, :tc], zero)
+        inverse = inv_ref[l, :tr, :tc]
+        out = []
+        for s in range(species):
             f_a = forced_ref[s, l, :tr, :tc]
             f_b = forced_ref[s, l, tr:, :tc]
             f_c = forced_ref[s, l, :tr, tc:]
@@ -279,21 +294,26 @@
             moved = f_a * rem
             moved = moved + from_east + from_west
             moved = moved + from_north + from_south
-            below = jnp.where(l > 0, se_ref[d0 + jnp.maximum(l - 1, 0), :tr, :tc], zero)
-            reduced = (moved + below * reduced) * inv_ref[l, :tr, :tc]
-            red_ref[l, :tr, :tc] = reduced
-            return reduced
-
-        lax.fori_loop(0, levels, forward, zero, unroll=4)
-
-        def backward(i, result, s=s):
-            l = levels - 1 - i
-            result = red_ref[l, :tr, :tc] - ratio_ref[l, :tr, :tc] * result
-            out_ref[s, l] = result
-            return result
-
-        surface = lax.fori_loop(0, levels, backward, zero, unroll=4)
-        ss_ref[s] = ss_ref[s] + prior_ref[s] * surface
+            r = (moved + below * reduced[s]) * inverse
+            red_ref[s, l, :tr, :tc] = r
+            out.append(r)
+        return tuple(out)
+
+    lax.fori_loop(0, levels, forward, (zero,) * species, unroll=4)
+
+    def backward(i, result):
+        l = levels - 1 - i
+        ratio = ratio_ref[l, :tr, :tc]
+        out = []
+        for s in range(species):
+            r = red_ref[s, l, :tr, :tc] - ratio * result[s]
+            out_ref[s, l] = r
+            out.append(r)
+        return tuple(out)
+
+    surface = lax.fori_loop(0, levels, backward, (zero,) * species, unroll=4)
+    for s in range(species):
+        ss_ref[s] = ss_ref[s] + prior_ref[s] * surface[s]
 
 
 def steps_call(steps, species, levels, n_statics, right, left, sright, sleft, st_own, st_xh,
@@ -314,7 +334,7 @@
             pltpu.VMEM((steps * planes, rows, tc), jnp.float32),
             pltpu.VMEM((n_statics, rows, lanes), jnp.float32),
             pltpu.VMEM((species, levels, rows, lanes), jnp.float32),
-            pltpu.VMEM((levels, rows, lanes), jnp.float32),
+            pltpu.VMEM((species, levels, rows, lanes), jnp.float32),
             pltpu.VMEM((levels, rows, lanes), jnp.float32),
             pltpu.VMEM((levels, rows, lanes), jnp.float32),
             pltpu.SemaphoreType.DMA((steps,)),

time: 111 us -> 104 us (0.937)
  Pallas kernels: 32.4 us -> 26 us
    pallas_call x1, Pallas kernels: 14 us -> 10.9 us  [steps_call(): pl.pallas_call(functools.partial(_steps_kernel, steps, species, levels, n...]
    pallas_call x1, Pallas kernels: 12 us -> 8.86 us  [forcing_call(): pl.pallas_call(functools.partial(_forcing_kernel, species, kernel, levels...]
  transfers between devices with their start and end apart: 9 -> 9, of which waited for: 3 -> 3; matrix products, arithmetic and copies ran while one was open for 4% -> 4% of each run, Pallas kernels for 14% -> 12%
where the time goes in v9:
time: 104 us; the launch traced here: 103 us
  starting transfers between devices  33.3 us (32%)
  Pallas kernels  26 us (25%)
  blocking collectives  23.9 us (23%)
  local copies, waits for them, and re-layouts  10.8 us (10%)
  other arithmetic  3.51 us (3%)
  waiting for transfers between devices  3.08 us (3%)
  matrix products  1.87 us (2%)
    all_to_all x1, blocking collectives, local(): lax.all_to_all(partial.reshape(species, devices, nreg // devices), ('gx',...  23.9 us
    all_to_all x1, starting transfers between devices, local(): received = lax.all_to_all(placed, ('gx', 'gy'), 2, 2, tiled=True)  11.5 us
    pallas_call x1, Pallas kernels, steps_call(): pl.pallas_call(functools.partial(_steps_kernel, steps, species, levels, n...  10.9 us
    pallas_call x1, Pallas kernels, forcing_call(): pl.pallas_call(functools.partial(_forcing_kernel, species, kernel, levels...  8.86 us
    unnamed x25, local copies, waits for them, and re-layouts  8.6 us
    ppermute x1, starting transfers between devices, local(): left = lax.ppermute(left, 'gy', up_y)  4.17 us
    ppermute x1, starting transfers between devices, extend(): left = lax.ppermute(left, 'gy', up_y)  3.99 us
    ppermute x1, starting transfers between devices, extend(): below = lax.ppermute(lo, 'gx', down_x)  2.96 us
  transfers between devices with their start and end apart: 9, of which 3 were waited for; matrix products, arithmetic and copies ran while one was open for 4% of the time, Pallas kernels for 12%

profile of v9, /device:TPU:1, one launch (start us, length us, event | category | flops | bytes accessed | tf_op | source)
XLA Modules:
  0.0 103.4 jit_solution(4055419619798502127)
XLA Ops:
  0.6 0.0 copy-start.7
  0.6 1.6 %copy.20.owner_ref = s32[4,128,1]{2,1,0:T(8,128)} copy(s32[4,128,1]{1,2,0:T(1,128)} %param.10) | data formatting | bytes 4096 | tf_op args[1]
  2.2 2.4 %shard_map.104 = f32[4,34,256]{2,1,0:T(8,128)} custom-call(f32[4,32,128]{2,1,0:T(8,128)} %adj_ref.1, s32[4,128,1]{2,1,0:T(8,128)} %copy.20.owner_ref, s32[4,128]{1,0:T(4,128)} %col_ref.1, s32[4,128]{1,0:T(4,128)} %lev_ref.1), custom_call_target="tpu_custom_call" | custom-call | tf_op jit(solution)/shard_map/pallas_call | solution.py:50
  4.7 0.0 copy-start.3
  4.7 1.2 %copy.21 = f32[4,34,256]{1,0,2:T(4,128)S(1)} copy(f32[4,34,256]{2,1,0:T(8,128)} %shard_map.104) | data formatting | bytes 278528 | tf_op jit(solution)/shard_map/pallas_call | solution.py:50
  5.8 1.3 %reshape.78 = f32[128,1,272]{2,1,0:T(1,128)} reshape(f32[256,4,34]{2,1,0:T(4,128)S(1)} %bitcast.4) | data formatting | bytes 278528
  7.1 11.5 %all-to-all-start = ((f32[128,1,272]{2,1,0:T(1,128)}), f32[128,1,272]{2,1,0:T(1,128)S(1)}, u32[]{:S(2)}, u32[]{:S(2)}) async-start(f32[128,1,272]{2,1,0:T(1,128)} %reshape.78), calls=%async_computation | async-start | bytes 393216 | tf_op jit(solution)/shard_map/all_to_all | solution.py:447
  18.6 0.1 pad.3.clone
  18.7 0.0 copy-done.7
  18.7 1.6 %maximum_maximum_fusion.chans_ref.st_own = f32[64,8,128]{2,1,0:T(8,128)} fusion(f32[39,8,128]{2,1,0:T(8,128)S(1)} %copy-done.7, f32[4,8,128]{2,1,0:T(8,128)} %param.14, f32[4,8,128]{2,1,0:T(8,128)} %param.13, f32[64]{0:T(128)S(1)} %pad.3.clone), kind=kLoop, calls=%fused_computation.4 | loop fusion | flops 196608 | bytes 454912 | tf_op jit(solution)/shard_map/concatenate | solution.py:460
  20.3 0.0 copy-start
  20.3 1.8 %shard_map.106 = (f32[32,8,128]{2,1,0:T(8,128)}, f32[32,8,128]{2,1,0:T(8,128)}) custom-call(f32[64,8,128]{2,1,0:T(8,128)} %maximum_maximum_fusion.chans_ref.st_own), custom_call_target="tpu_custom_call" | custom-call | tf_op jit(solution)/shard_map/pallas_call | solution.py:413
  22.0 3.0 %collective-permute-start.4 = (f32[32,8,128]{2,1,0:T(8,128)}, f32[32,8,128]{2,1,0:T(8,128)S(1)}, u32[]{:S(2)}, u32[]{:S(2)}) collective-permute-start(f32[32,8,128]{2,1,0:T(8,128)} %get-tuple-element.14), channel_id=1, source_target_pairs={{16,0},{32,16},{48,32},{64,48},{80,64},{96,80},{112,96},{17,1},{33... | collective-permute-start | bytes 393224 | tf_op jit(solution)/shard_map/ppermute | solution.py:416
  25.0 2.6 %collective-permute-start.5 = (f32[32,8,128]{2,1,0:T(8,128)}, f32[32,8,128]{2,1,0:T(8,128)S(1)}, u32[]{:S(2)}, u32[]{:S(2)}) collective-permute-start(f32[32,8,128]{2,1,0:T(8,128)} %get-tuple-element.15), channel_id=1, source_target_pairs={{0,16},{16,32},{32,48},{48,64},{64,80},{80,96},{96,112},{1,17},{17... | collective-permute-start | bytes 393224 | tf_op jit(solution)/shard_map/ppermute | solution.py:417
  27.7 1.5 %all-to-all-done = f32[128,1,272]{2,1,0:T(1,128)S(1)} async-done(((f32[128,1,272]{2,1,0:T(1,128)}), f32[128,1,272]{2,1,0:T(1,128)S(1)}, u32[]{:S(2)}, u32[]{:S(2)}) %all-to-all-start) | async-done | bytes 139296 | tf_op jit(solution)/shard_map/all_to_all | solution.py:447
  29.2 0.5 broadcast.123
  29.7 1.1 %reduce = f32[128,272]{1,0:T(8,128)S(1)} reduce(f32[128,1,272]{2,1,0:T(1,128)S(1)} %all-to-all-done, f32[]{:T(128)} %broadcast.123), dimensions={1}, to_apply=%all_to_all.6.reduce_sub_computation | reduce | bytes 278532 | tf_op jit(solution)/shard_map/all_to_all | solution.py:447
  30.8 0.4 reshape.79
  31.3 0.0 copy-start.10
  31.3 0.2 copy.24.own_ref
  31.5 0.0 copy-start.4
  31.5 2.6 %collective-permute-start = (f32[4,34,256]{2,1,0:T(8,128)S(1)}, f32[4,34,256]{2,1,0:T(8,128)S(1)}, u32[]{:S(2)}, u32[]{:S(2)}) collective-permute-start(f32[4,34,256]{2,1,0:T(8,128)S(1)} %copy.24.own_ref), channel_id=1, source_target_pairs={{16,0},{32,16},{48,32},{64,48},{80,64},{96,80},{112,96},{17,1},{33... | collective-permute-start | bytes 417800 | tf_op jit(solution)/shard_map/ppermute | solution.py:450
  34.1 3.0 %collective-permute-start.1 = (f32[4,34,256]{2,1,0:T(8,128)S(1)}, f32[4,34,256]{2,1,0:T(8,128)S(1)}, u32[]{:S(2)}, u32[]{:S(2)}) collective-permute-start(f32[4,34,256]{2,1,0:T(8,128)S(1)} %copy.24.own_ref), channel_id=1, source_target_pairs={{0,16},{16,32},{32,48},{48,64},{64,80},{80,96},{96,112},{1,17},{17... | collective-permute-start | bytes 417800 | tf_op jit(solution)/shard_map/ppermute | solution.py:451
  37.1 0.1 and_convert_fusion.mask_ref
  37.2 0.0 collective-permute-done.4.below_ref
  37.2 0.0 copy-start.8
  37.2 0.0 collective-permute-done.5.above_ref
  37.2 0.6 copy-done.8
  37.8 0.0 copy-start.9
  37.8 0.7 copy-done.9
  38.5 2.1 %shard_map.107 = (f32[64,8,128]{2,1,0:T(8,128)}, f32[2,16,128]{2,1,0:T(8,128)}, f32[2,16,128]{2,1,0:T(8,128)}) custom-call(f32[64,8,128]{2,1,0:T(8,128)} %maximum_maximum_fusion.chans_ref.st_own, f32[32,8,128]{2,1,0:T(8,128)} %copy-done.8, f32[32,8,128]{2,1,0:T(8,128)} %copy-done.9), custom_call_target="tpu_custom_call" | custom-call | tf_op jit(solution)/shard_map/pallas_call | solution.py:419
  40.6 1.3 %collective-permute-start.6 = (f32[2,16,128]{2,1,0:T(8,128)}, f32[2,16,128]{2,1,0:T(8,128)S(1)}, u32[]{:S(2)}, u32[]{:S(2)}) collective-permute-start(f32[2,16,128]{2,1,0:T(8,128)} %get-tuple-element.16), channel_id=1, source_target_pairs={{1,0},{2,1},{3,2},{4,3},{5,4},{6,5},{7,6},{8,7},{9,8},{10,9},{11,1... | collective-permute-start | bytes 49160 | tf_op jit(solution)/shard_map/ppermute | solution.py:423
  41.9 4.0 %collective-permute-start.7 = (f32[2,16,128]{2,1,0:T(8,128)}, f32[2,16,128]{2,1,0:T(8,128)S(1)}, u32[]{:S(2)}, u32[]{:S(2)}) collective-permute-start(f32[2,16,128]{2,1,0:T(8,128)} %get-tuple-element.17), channel_id=1, source_target_pairs={{0,1},{1,2},{2,3},{3,4},{4,5},{5,6},{6,7},{7,8},{8,9},{9,10},{10,1... | collective-permute-start | bytes 49160 | tf_op jit(solution)/shard_map/ppermute | solution.py:424
  45.9 0.0 collective-permute-done.below_ref
  45.9 0.0 copy-start.5
  45.9 0.0 collective-permute-done.1.above_ref
  45.9 0.0 copy-done.4
  45.9 0.6 copy-done.5
  46.5 0.0 copy-start.6
  46.5 0.7 copy-done.6
  47.2 8.9 %shard_map.105 = (f32[4,80,16,128]{3,2,1,0:T(8,128)}, f32[10,16,128]{2,1,0:T(8,128)}, f32[10,16,128]{2,1,0:T(8,128)}) custom-call(f32[4,34,256]{2,1,0:T(8,128)} %copy-done.4, f32[4,34,256]{2,1,0:T(8,128)} %copy-done.5, f32[4,34,256]{2,1,0:T(8,128)} %copy-done.6), custom_call_target="tpu_custom_call" | custom-call | tf_op jit(solution)/shard_map/pallas_call | solution.py:131
  56.1 1.3 %collective-permute-start.2 = (f32[10,16,128]{2,1,0:T(8,128)}, f32[10,16,128]{2,1,0:T(8,128)S(1)}, u32[]{:S(2)}, u32[]{:S(2)}) collective-permute-start(f32[10,16,128]{2,1,0:T(8,128)} %get-tuple-element.12), channel_id=1, source_target_pairs={{1,0},{2,1},{3,2},{4,3},{5,4},{6,5},{7,6},{8,7},{9,8},{10,9},{11,1... | collective-permute-start | bytes 245768 | tf_op jit(solution)/shard_map/ppermute | solution.py:454
  57.4 4.2 %collective-permute-start.3 = (f32[10,16,128]{2,1,0:T(8,128)}, f32[10,16,128]{2,1,0:T(8,128)S(1)}, u32[]{:S(2)}, u32[]{:S(2)}) collective-permute-start(f32[10,16,128]{2,1,0:T(8,128)} %get-tuple-element.13), channel_id=1, source_target_pairs={{0,1},{1,2},{2,3},{3,4},{4,5},{5,6},{6,7},{7,8},{8,9},{9,10},{10,1... | collective-permute-start | bytes 245768 | tf_op jit(solution)/shard_map/ppermute | solution.py:455
  61.5 0.0 collective-permute-done.6.sright_ref
  61.6 0.0 collective-permute-done.7.sleft_ref
  61.6 0.6 collective-permute-done.2.right_ref
  62.2 0.9 collective-permute-done.3.left_ref
  63.1 0.0 copy-done.3
  63.1 0.0 copy-done
  63.1 0.0 copy-start.1
  63.1 1.7 %copy-done.1 = f32[4,80,16,128]{3,2,1,0:T(8,128)S(1)} copy-done((f32[4,80,16,128]{3,2,1,0:T(8,128)S(1)}, f32[4,80,16,128]{3,2,1,0:T(8,128)}, u32[]{:S(2)}) %copy-start.1) | copy-done | bytes 2621464
  64.9 0.0 copy-start.2
  64.9 0.9 copy-done.2
  65.8 10.9 %shard_map.108 = (f32[2,40,8,128]{3,2,1,0:T(8,128)}, f32[2,8,128]{2,1,0:T(8,128)S(1)}) custom-call(f32[10,16,128]{2,1,0:T(8,128)S(1)} %collective-permute-done.2.right_ref, f32[10,16,128]{2,1,0:T(8,128)S(1)} %collective-permute-done.3.left_ref, f32[2,16,128]{2,1,0:T(8,128)S(1)} %collective-permute-done.6.sright_ref, ...), custom_call_target="tpu_custom_call" | custom-call | tf_op jit(solution)/shard_map/pallas_call | solution.py:326
  76.7 0.0 copy-done.10
  76.7 1.9 %fusion = f32[2,128,8]{1,0,2:T(2,128)S(1)} fusion(f32[2,1024,1]{1,0,2:T(2,128)S(1)} %reshape.76, s32[128,8]{0,1:T(8,128)S(1)} %multiply_add_fusion, s32[1024]{0:T(1024)S(1)} %bitcast.6), kind=kOutput, calls=%fused_computation | convolution fusion | flops 26214400 | bytes 24576 | tf_op jit(solution)/shard_map/dot_general | solution.py:480
  78.6 0.2 copy.25
  78.8 23.9 %all_to_all.10 = f32[2,128,8]{2,0,1:T(2,128)S(1)} all-to-all(f32[2,128,8]{2,0,1:T(2,128)S(1)} %copy.25), channel_id=1, replica_groups=mesh['gx'=8,'gy'=16] {'gx','gy'}, dimensions={1} | all-to-all | bytes 16384 | tf_op jit(solution)/shard_map/all_to_all | solution.py:481
  102.7 0.7 reduce_sum.9
  (6 shorter events, 0.0 us)
Async XLA Ops:
  0.6 18.1 %copy-start.7 = (f32[39,8,128]{2,1,0:T(8,128)S(1)}, f32[39,8,128]{2,1,0:T(8,128)}, u32[]{:S(2)}) copy-start(f32[39,8,128]{2,1,0:T(8,128)} %param.15) | copy-start | bytes 479236
  4.7 58.5 %copy-start.3 = (f32[2,8,128]{2,1,0:T(8,128)S(1)}, f32[2,8,128]{2,1,0:T(8,128)}, u32[]{:S(2)}) copy-start(f32[2,8,128]{2,1,0:T(8,128)} %prior_ref.1) | copy-start | bytes 24580
  7.1 22.1 %all-to-all-start = ((f32[128,1,272]{2,1,0:T(1,128)}), f32[128,1,272]{2,1,0:T(1,128)S(1)}, u32[]{:S(2)}, u32[]{:S(2)}) async-start(f32[128,1,272]{2,1,0:T(1,128)} %reshape.78), calls=%async_computation | async-start | bytes 393216 | tf_op jit(solution)/shard_map/all_to_all | solution.py:447
  20.3 42.9 %copy-start = (f32[64,8,128]{2,1,0:T(8,128)S(1)}, f32[64,8,128]{2,1,0:T(8,128)}, u32[]{:S(2)}) copy-start(f32[64,8,128]{2,1,0:T(8,128)} %maximum_maximum_fusion.chans_ref.st_own) | copy-start | bytes 786436
  22.0 15.1 %collective-permute-start.4 = (f32[32,8,128]{2,1,0:T(8,128)}, f32[32,8,128]{2,1,0:T(8,128)S(1)}, u32[]{:S(2)}, u32[]{:S(2)}) collective-permute-start(f32[32,8,128]{2,1,0:T(8,128)} %get-tuple-element.14), channel_id=1, source_target_pairs={{16,0},{32,16},{48,32},{64,48},{80,64},{96,80},{112,96},{17,1},{33... | collective-permute-start | bytes 393224 | tf_op jit(solution)/shard_map/ppermute | solution.py:416
  25.0 12.2 %collective-permute-start.5 = (f32[32,8,128]{2,1,0:T(8,128)}, f32[32,8,128]{2,1,0:T(8,128)S(1)}, u32[]{:S(2)}, u32[]{:S(2)}) collective-permute-start(f32[32,8,128]{2,1,0:T(8,128)} %get-tuple-element.15), channel_id=1, source_target_pairs={{0,16},{16,32},{32,48},{48,64},{64,80},{80,96},{96,112},{1,17},{17... | collective-permute-start | bytes 393224 | tf_op jit(solution)/shard_map/ppermute | solution.py:417
  31.3 45.4 %copy-start.10 = (s32[8,128]{1,0:T(8,128)S(1)}, s32[8,128]{1,0:T(8,128)}, u32[]{:S(2)}) copy-start(s32[8,128]{1,0:T(8,128)} %param.17) | copy-start | bytes 12292
  31.5 14.4 %copy-start.4 = (f32[4,34,256]{2,1,0:T(8,128)}, f32[4,34,256]{2,1,0:T(8,128)S(1)}, u32[]{:S(2)}) copy-start(f32[4,34,256]{2,1,0:T(8,128)S(1)} %copy.24.own_ref) | copy-start | bytes 417796
  31.5 14.3 %collective-permute-start = (f32[4,34,256]{2,1,0:T(8,128)S(1)}, f32[4,34,256]{2,1,0:T(8,128)S(1)}, u32[]{:S(2)}, u32[]{:S(2)}) collective-permute-start(f32[4,34,256]{2,1,0:T(8,128)S(1)} %copy.24.own_ref), channel_id=1, source_target_pairs={{16,0},{32,16},{48,32},{64,48},{80,64},{96,80},{112,96},{17,1},{33... | collective-permute-start | bytes 417800 | tf_op jit(solution)/shard_map/ppermute | solution.py:450
  34.1 11.8 %collective-permute-start.1 = (f32[4,34,256]{2,1,0:T(8,128)S(1)}, f32[4,34,256]{2,1,0:T(8,128)S(1)}, u32[]{:S(2)}, u32[]{:S(2)}) collective-permute-start(f32[4,34,256]{2,1,0:T(8,128)S(1)} %copy.24.own_ref), channel_id=1, source_target_pairs={{0,16},{16,32},{32,48},{48,64},{64,80},{80,96},{96,112},{1,17},{17... | collective-permute-start | bytes 417800 | tf_op jit(solution)/shard_map/ppermute | solution.py:451
  37.2 0.6 copy-start.8
  37.8 0.7 copy-start.9
  40.6 21.0 %collective-permute-start.6 = (f32[2,16,128]{2,1,0:T(8,128)}, f32[2,16,128]{2,1,0:T(8,128)S(1)}, u32[]{:S(2)}, u32[]{:S(2)}) collective-permute-start(f32[2,16,128]{2,1,0:T(8,128)} %get-tuple-element.16), channel_id=1, source_target_pairs={{1,0},{2,1},{3,2},{4,3},{5,4},{6,5},{7,6},{8,7},{9,8},{10,9},{11,1... | collective-permute-start | bytes 49160 | tf_op jit(solution)/shard_map/ppermute | solution.py:423
  41.9 19.7 %collective-permute-start.7 = (f32[2,16,128]{2,1,0:T(8,128)}, f32[2,16,128]{2,1,0:T(8,128)S(1)}, u32[]{:S(2)}, u32[]{:S(2)}) collective-permute-start(f32[2,16,128]{2,1,0:T(8,128)} %get-tuple-element.17), channel_id=1, source_target_pairs={{0,1},{1,2},{2,3},{3,4},{4,5},{5,6},{6,7},{7,8},{8,9},{9,10},{10,1... | collective-permute-start | bytes 49160 | tf_op jit(solution)/shard_map/ppermute | solution.py:424
  45.9 0.7 copy-start.5
  46.5 0.7 copy-start.6
  56.1 6.1 %collective-permute-start.2 = (f32[10,16,128]{2,1,0:T(8,128)}, f32[10,16,128]{2,1,0:T(8,128)S(1)}, u32[]{:S(2)}, u32[]{:S(2)}) collective-permute-start(f32[10,16,128]{2,1,0:T(8,128)} %get-tuple-element.12), channel_id=1, source_target_pairs={{1,0},{2,1},{3,2},{4,3},{5,4},{6,5},{7,6},{8,7},{9,8},{10,9},{11,1... | collective-permute-start | bytes 245768 | tf_op jit(solution)/shard_map/ppermute | solution.py:454
  57.4 5.8 %collective-permute-start.3 = (f32[10,16,128]{2,1,0:T(8,128)}, f32[10,16,128]{2,1,0:T(8,128)S(1)}, u32[]{:S(2)}, u32[]{:S(2)}) collective-permute-start(f32[10,16,128]{2,1,0:T(8,128)} %get-tuple-element.13), channel_id=1, source_target_pairs={{0,1},{1,2},{2,3},{3,4},{4,5},{5,6},{6,7},{7,8},{8,9},{9,10},{10,1... | collective-permute-start | bytes 245768 | tf_op jit(solution)/shard_map/ppermute | solution.py:455
  63.1 1.7 %copy-start.1 = (f32[4,80,16,128]{3,2,1,0:T(8,128)S(1)}, f32[4,80,16,128]{3,2,1,0:T(8,128)}, u32[]{:S(2)}) copy-start(f32[4,80,16,128]{3,2,1,0:T(8,128)} %get-tuple-element.19.tall_hbm) | copy-start | bytes 7864324
  64.9 0.9 copy-start.2

commit v10 on v9

--- a/solution.py
+++ b/solution.py
@@ -24,7 +24,16 @@
                      jnp.where(lane >= cols - half, pltpu.roll(l, ls, 1) if ls else l, 0.0))
 
 
-def _pack_kernel(capacity, adj_ref, owner_ref, col_ref, lev_ref, out_ref, rows_ref):
+def _static_plane(c, refs):
+    for ref in refs:
+        if c < ref.shape[0]:
+            return ref[c]
+        c -= ref.shape[0]
+    return jnp.zeros(refs[0].shape[1:], jnp.float32)
+
+
+def _pack_kernel(capacity, adj_ref, owner_ref, col_ref, lev_ref, wx_ref, wy_ref, diff_ref,
+                 out_ref, lo_ref, hi_ref, rows_ref):
     steps, n_pay, pixels = adj_ref.shape
     slots = out_ref.shape[2]
     row = lax.broadcasted_iota(jnp.int32, (pixels, pixels), 0)
@@ -42,18 +51,30 @@
         out_ref[k] = lax.dot_general(rows_ref[...], place, (((1,), (0,)), ((), ())),
                                      precision=lax.Precision.HIGHEST,
                                      preferred_element_type=jnp.float32)
-
-
-def pack_call(capacity, slots, pixel_adjoint, pixel_owner, pixel_column, pixel_level):
+    statics = (wx_ref, wy_ref, diff_ref)
+    tr = wx_ref.shape[1]
+    half = tr // 2
+    trow = lax.broadcasted_iota(jnp.int32, wx_ref.shape[1:], 0)
+    for i in range(lo_ref.shape[0]):
+        a = _static_plane(2 * i, statics)
+        b = _static_plane(2 * i + 1, statics)
+        lo_ref[i] = jnp.where(trow < half, a, pltpu.roll(b, half, 0))
+        hi_ref[i] = jnp.where(trow < half, pltpu.roll(a, half, 0), b)
+
+
+def pack_call(capacity, slots, n_pad, pixel_adjoint, pixel_owner, pixel_column, pixel_level,
+              wind_x, wind_y, diffusivity):
     steps, n_pay, pixels = pixel_adjoint.shape
+    rows, cols = wind_x.shape[1:]
+    pairs = jax.ShapeDtypeStruct((n_pad // 2, rows, cols), jnp.float32)
     vmem = pl.BlockSpec(memory_space=pltpu.VMEM)
     return pl.pallas_call(
         functools.partial(_pack_kernel, capacity),
-        in_specs=[vmem] * 4,
-        out_specs=vmem,
-        out_shape=jax.ShapeDtypeStruct((steps, n_pay + 2, slots), jnp.float32),
+        in_specs=[vmem] * 7,
+        out_specs=[vmem] * 3,
+        out_shape=[jax.ShapeDtypeStruct((steps, n_pay + 2, slots), jnp.float32), pairs, pairs],
         scratch_shapes=[pltpu.VMEM((n_pay + 2, pixels), jnp.float32)],
-    )(pixel_adjoint, pixel_owner, pixel_column, pixel_level)
+    )(pixel_adjoint, pixel_owner, pixel_column, pixel_level, wind_x, wind_y, diffusivity)
 
 
 def _exact_dot(a, b):
@@ -67,8 +88,9 @@
     return out + lax.dot_general(lo, b, dims, preferred_element_type=jnp.float32)
 
 
-def _forcing_kernel(species, kernel, levels, own_ref, below_ref, above_ref,
-                    tall_ref, right_ref, left_ref, lown_ref, lnb_ref):
+def _forcing_kernel(species, kernel, levels, n_statics, own_ref, below_ref, above_ref, wx_ref,
+                    wy_ref, diff_ref, sb_ref, sa_ref,
+                    tall_ref, right_ref, left_ref, st_xh_ref, lown_ref, lnb_ref):
     steps, _, slots = own_ref.shape
     tr2, tc = tall_ref.shape[2:]
     tr = tr2 // 2
@@ -119,28 +141,54 @@
             ls = (half * q + half) % tc
             right_ref[g] = jnp.where(sel, pltpu.roll(plane, rs, 1) if rs else plane, right_ref[g])
             left_ref[g] = jnp.where(sel, pltpu.roll(plane, ls, 1) if ls else plane, left_ref[g])
-
-
-def forcing_call(species, kernel, levels, own, below, above, cols):
+    statics = (wx_ref, wy_ref, diff_ref)
+    trow = lax.broadcasted_iota(jnp.int32, (tr, tc), 0)
+    base = steps * species * levels
+    for i in range(sb_ref.shape[0]):
+        b = sb_ref[i]
+        a = sa_ref[i]
+        xhs = (jnp.where(trow < half, b, pltpu.roll(a, half, 0)),
+               jnp.where(trow < half, pltpu.roll(b, half, 0), a))
+        for off in range(2):
+            c = 2 * i + off
+            st_xh_ref[c] = xhs[off]
+            if c >= n_statics:
+                continue
+            g, q = divmod(base + c, group)
+            sel = (lane16 >= half * q) & (lane16 < half * q + half)
+            rs = (half * q) % tc
+            ls = (half * q + half) % tc
+            for part, plane in ((slice(0, tr), _static_plane(c, statics)),
+                                (slice(tr, tr2), xhs[off])):
+                selp = sel[part]
+                right_ref[g, part] = jnp.where(
+                    selp, pltpu.roll(plane, rs, 1) if rs else plane, right_ref[g, part])
+                left_ref[g, part] = jnp.where(
+                    selp, pltpu.roll(plane, ls, 1) if ls else plane, left_ref[g, part])
+
+
+def forcing_call(species, kernel, levels, n_statics, own, below, above, wind_x, wind_y,
+                 diffusivity, st_below, st_above):
     steps, _, slots = own.shape
-    tr = 8
+    tr, cols = wind_x.shape[1:]
     planes = species * levels
     group = cols // (tr // 2)
-    packed = jax.ShapeDtypeStruct((steps * planes // group, 2 * tr, cols), jnp.float32)
+    n_groups = -(-(steps * planes + n_statics) // group)
+    packed = jax.ShapeDtypeStruct((n_groups, 2 * tr, cols), jnp.float32)
     vmem = pl.BlockSpec(memory_space=pltpu.VMEM)
     return pl.pallas_call(
-        functools.partial(_forcing_kernel, species, kernel, levels),
-        in_specs=[vmem, vmem, vmem],
-        out_specs=[vmem, vmem, vmem],
+        functools.partial(_forcing_kernel, species, kernel, levels, n_statics),
+        in_specs=[vmem] * 8,
+        out_specs=[vmem] * 4,
         out_shape=[jax.ShapeDtypeStruct((steps, planes, 2 * tr, cols), jnp.float32), packed,
-                   packed],
+                   packed, jax.ShapeDtypeStruct((2 * st_below.shape[0], tr, cols), jnp.float32)],
         scratch_shapes=[pltpu.VMEM((planes * tr, slots), jnp.float32),
                         pltpu.VMEM((planes * tr, 2 * slots), jnp.float32)],
-    )(own, below, above)
+    )(own, below, above, wind_x, wind_y, diffusivity, st_below, st_above)
 
 
 def _steps_kernel(steps, species, levels, n_statics,
-                  right_ref, left_ref, sright_ref, sleft_ref, st_own, st_xh, mask_ref, prior_ref,
+                  right_ref, left_ref, wx_ref, wy_ref, diff_ref, st_xh, mask_ref, prior_ref,
                   tall_hbm, adj_ref, ss_ref,
                   tall_buf, yh_buf, se_ref, state_ref, red_ref, ratio_ref, inv_ref, sems):
     planes = species * levels
@@ -156,7 +204,7 @@
         copy.start()
         loads[k] = copy
 
-    n_fgroups = right_ref.shape[0]
+    n_fgroups = steps * planes // group
 
     def unpack_group(g, carry):
         r = right_ref[g]
@@ -167,15 +215,12 @@
 
     lax.fori_loop(0, n_fgroups, unpack_group, 0)
     for c in range(n_statics):
-        se_ref[c, :, tc:] = _unpack(sright_ref[c // group], sleft_ref[c // group], c % group,
-                                    tc, half)
-
-    def assemble_static(c, carry):
-        se_ref[c, :tr, :tc] = st_own[c]
+        g, q = divmod(n_fgroups * group + c, group)
+        se_ref[c, :, tc:] = _unpack(right_ref[g], left_ref[g], q, tc, half)
+
+    for c in range(n_statics):
+        se_ref[c, :tr, :tc] = _static_plane(c, (wx_ref, wy_ref, diff_ref))
         se_ref[c, tr:, :tc] = st_xh[c]
-        return carry
-
-    lax.fori_loop(0, n_statics, assemble_static, 0)
 
     zero = jnp.zeros((rows, lanes), jnp.float32)
     inside = mask_ref[...] > 0.5
@@ -316,8 +361,8 @@
         ss_ref[s] = ss_ref[s] + prior_ref[s] * surface[s]
 
 
-def steps_call(steps, species, levels, n_statics, right, left, sright, sleft, st_own, st_xh,
-               mask, prior, tall):
+def steps_call(steps, species, levels, n_statics, right, left, wind_x, wind_y, diffusivity,
+               st_xh, mask, prior, tall):
     _, planes, rows, tc = tall.shape
     tr = rows // 2
     lanes = mask.shape[1]
@@ -340,89 +385,12 @@
             pltpu.SemaphoreType.DMA((steps,)),
         ],
         compiler_params=pltpu.CompilerParams(vmem_limit_bytes=48 * 1024 * 1024),
-    )(right, left, sright, sleft, st_own, st_xh, mask, prior, tall)
+    )(right, left, wind_x, wind_y, diffusivity, st_xh, mask, prior, tall)
 
 
 def _pairs(axis):
     n = lax.axis_size(axis)
     return [(i, i + 1) for i in range(n - 1)], [(i + 1, i) for i in range(n - 1)]
-
-
-def _whole(shapes):
-    return [pl.BlockSpec(memory_space=pltpu.VMEM) for _ in shapes]
-
-
-def _xpack_kernel(chans_ref, lo_ref, hi_ref):
-    rows = chans_ref.shape[1]
-    half = rows // 2
-    row = lax.broadcasted_iota(jnp.int32, chans_ref.shape[1:], 0)
-
-    def body(i, carry):
-        a = chans_ref[2 * i]
-        b = chans_ref[2 * i + 1]
-        lo_ref[i] = jnp.where(row < half, a, pltpu.roll(b, half, 0))
-        hi_ref[i] = jnp.where(row < half, pltpu.roll(a, half, 0), b)
-        return carry
-
-    lax.fori_loop(0, lo_ref.shape[0], body, 0, unroll=4)
-
-
-def _ypack_kernel(chans_ref, below_ref, above_ref, xh_ref, right_ref, left_ref):
-    rows, cols = chans_ref.shape[1:]
-    half = rows // 2
-    group = cols // half
-    row = lax.broadcasted_iota(jnp.int32, (rows, cols), 0)
-    lane = lax.broadcasted_iota(jnp.int32, (rows, cols), 1)
-    zero = jnp.zeros((rows, cols), jnp.float32)
-
-    def body(g, carry):
-        acc = [zero, zero, zero, zero]
-        for q2 in range(group // 2):
-            i = g * (group // 2) + q2
-            b = below_ref[i]
-            a = above_ref[i]
-            xh0 = jnp.where(row < half, b, pltpu.roll(a, half, 0))
-            xh1 = jnp.where(row < half, pltpu.roll(b, half, 0), a)
-            xh_ref[2 * i] = xh0
-            xh_ref[2 * i + 1] = xh1
-            for off, top, bot in ((0, chans_ref[2 * i], xh0), (1, chans_ref[2 * i + 1], xh1)):
-                q = 2 * q2 + off
-                sel = (lane >= half * q) & (lane < half * q + half)
-                rs = (half * q) % cols
-                ls = (half * q + half) % cols
-                acc[0] = jnp.where(sel, pltpu.roll(top, rs, 1) if rs else top, acc[0])
-                acc[1] = jnp.where(sel, pltpu.roll(bot, rs, 1) if rs else bot, acc[1])
-                acc[2] = jnp.where(sel, pltpu.roll(top, ls, 1) if ls else top, acc[2])
-                acc[3] = jnp.where(sel, pltpu.roll(bot, ls, 1) if ls else bot, acc[3])
-        right_ref[g, :rows] = acc[0]
-        right_ref[g, rows:] = acc[1]
-        left_ref[g, :rows] = acc[2]
-        left_ref[g, rows:] = acc[3]
-        return carry
-
-    lax.fori_loop(0, right_ref.shape[0], body, 0)
-
-
-def extend(chans, first_static, n_statics):
-    up_x, down_x = _pairs("gx")
-    up_y, down_y = _pairs("gy")
-    channels, rows, cols = chans.shape
-    halo = rows // 2
-    group = cols // halo
-    pairs = jax.ShapeDtypeStruct((channels // 2, rows, cols), jnp.float32)
-    lo, hi = pl.pallas_call(
-        _xpack_kernel, out_shape=[pairs, pairs],
-        in_specs=_whole([chans]), out_specs=_whole([0, 0]))(chans)
-    below = lax.ppermute(lo, "gx", down_x)
-    above = lax.ppermute(hi, "gx", up_x)
-    packed = jax.ShapeDtypeStruct((channels // group, 2 * rows, cols), jnp.float32)
-    xh, right, left = pl.pallas_call(
-        _ypack_kernel,
-        out_shape=[jax.ShapeDtypeStruct(chans.shape, jnp.float32), packed, packed],
-        in_specs=_whole([0, 0, 0]), out_specs=_whole([0, 0, 0]))(chans, below, above)
-    right = lax.ppermute(right, "gy", down_y)
-    left = lax.ppermute(left, "gy", up_y)
-    return xh, right, left
 
 
 def local(pixel_adjoint, pixel_owner, pixel_column, pixel_level, wind_x, wind_y,
@@ -443,23 +411,23 @@
     lanes = 2 * cols
     ext_rows = 2 * rows
 
-    placed = pack_call(capacity, slots, pixel_adjoint, pixel_owner, pixel_column, pixel_level)
-    received = lax.all_to_all(placed, ("gx", "gy"), 2, 2, tiled=True)
-
-    up_x, down_x = _pairs("gx")
-    below = lax.ppermute(received, "gx", down_x)
-    above = lax.ppermute(received, "gx", up_x)
-    tall, right, left = forcing_call(species, kernel, levels, received, below, above, cols)
-    up_y, down_y = _pairs("gy")
-    right = lax.ppermute(right, "gy", down_y)
-    left = lax.ppermute(left, "gy", up_y)
-
     n_s = 2 * steps + levels - 1
     group = cols // halo
     n_pad = -(-n_s // group) * group
-    statics = jnp.concatenate(
-        [wind_x, wind_y, diffusivity, jnp.zeros((n_pad - n_s, rows, cols), jnp.float32)], axis=0)
-    st_xh, sright, sleft = extend(statics, 0, n_s)
+    placed, st_lo, st_hi = pack_call(capacity, slots, n_pad, pixel_adjoint, pixel_owner,
+                                     pixel_column, pixel_level, wind_x, wind_y, diffusivity)
+    up_x, down_x = _pairs("gx")
+    up_y, down_y = _pairs("gy")
+    st_below = lax.ppermute(st_lo, "gx", down_x)
+    st_above = lax.ppermute(st_hi, "gx", up_x)
+    received = lax.all_to_all(placed, ("gx", "gy"), 2, 2, tiled=True)
+
+    below = lax.ppermute(received, "gx", down_x)
+    above = lax.ppermute(received, "gx", up_x)
+    tall, right, left, st_xh = forcing_call(species, kernel, levels, n_s, received, below, above,
+                                            wind_x, wind_y, diffusivity, st_below, st_above)
+    right = lax.ppermute(right, "gy", down_y)
+    left = lax.ppermute(left, "gy", up_y)
 
     gxi = lax.axis_index("gx")
     gyi = lax.axis_index("gy")
@@ -472,8 +440,8 @@
               & ((c < cols + halo) | (c >= lanes - halo)))
     mask = inside.astype(jnp.float32)
 
-    adjoint, surface_sum = steps_call(steps, species, levels, n_s, right, left, sright, sleft,
-                                      statics, st_xh, mask, prior_emission, tall)
+    adjoint, surface_sum = steps_call(steps, species, levels, n_s, right, left, wind_x, wind_y,
+                                      diffusivity, st_xh, mask, prior_emission, tall)
 
     nreg = REG_DEV * devices
     member = (region_map.reshape(-1)[:, None] == jnp.arange(nreg, dtype=jnp.int32)).astype(jnp.float32)

time: 104 us -> 93.3 us (0.90)
  waiting for transfers between devices: 3.08 us -> 8.8 us
  starting transfers between devices: 33.3 us -> 28.1 us
  Pallas kernels: 26 us -> 22.3 us
  blocking collectives: 23.9 us -> 20.3 us
  local copies, waits for them, and re-layouts: 10.8 us -> 8.71 us
  other arithmetic: 3.51 us -> 1.93 us
    ppermute x4 -> x2, starting transfers between devices: 10.8 us -> 5.58 us  [the longest x1 2.98 us: local(): st_below = lax.ppermute(st_lo, 'gx', down_x)]
    pallas_call x2 -> x0, Pallas kernels: 3.86 us -> none  [the longest x1 2.09 us: extend(): pl.pallas_call(_ypack_kernel, out_shape=[jax.ShapeDtypeStruct(chans.shape...]
    all_to_all x1, blocking collectives: 23.9 us -> 20.3 us  [local(): lax.all_to_all(partial.reshape(species, devices, nreg // devices), ('gx',...]
    all_to_all x1, waiting for transfers between devices: 1.5 us -> 4.92 us  [local(): received = lax.all_to_all(placed, ('gx', 'gy'), 2, 2, tiled=True)]
    unnamed x25 -> x27, local copies, waits for them, and re-layouts: 8.6 us -> 6.65 us
    concatenate x1 -> x0, other arithmetic: 1.57 us -> none  [local(): jnp.concatenate([wind_x, wind_y, diffusivity, jnp.zeros((n_pad - n_s, row...]
    ppermute x1, waiting for transfers between devices: 0.01 us -> 1.18 us  [local(): above = lax.ppermute(received, 'gx', up_x)]
  transfers between devices with their start and end apart: 9 -> 7, of which waited for: 3 -> 5; matrix products, arithmetic and copies ran while one was open for 4% -> 3% of each run, Pallas kernels for 12% -> 0%
where the time goes in v10:
time: 93.3 us; the launch traced here: 92.8 us
  starting transfers between devices  28.1 us (30%)
  Pallas kernels  22.3 us (24%)
  blocking collectives  20.3 us (22%)
  waiting for transfers between devices  8.8 us (9%)
  local copies, waits for them, and re-layouts  8.71 us (9%)
  other arithmetic  1.93 us (2%)
  matrix products  1.87 us (2%)
    all_to_all x1, blocking collectives, local(): lax.all_to_all(partial.reshape(species, devices, nreg // devices), ('gx',...  20.3 us
    all_to_all x1, starting transfers between devices, local(): received = lax.all_to_all(placed, ('gx', 'gy'), 2, 2, tiled=True)  11.5 us
    pallas_call x1, Pallas kernels, steps_call(): pl.pallas_call(functools.partial(_steps_kernel, steps, species, levels, n...  10.4 us
    pallas_call x1, Pallas kernels, forcing_call(): pl.pallas_call(functools.partial(_forcing_kernel, species, kernel, levels...  9.3 us
    unnamed x27, local copies, waits for them, and re-layouts  6.65 us
    all_to_all x1, waiting for transfers between devices, local(): received = lax.all_to_all(placed, ('gx', 'gy'), 2, 2, tiled=True)  4.92 us
    ppermute x1, starting transfers between devices, local(): left = lax.ppermute(left, 'gy', up_y)  4.17 us
    ppermute x1, starting transfers between devices, local(): st_below = lax.ppermute(st_lo, 'gx', down_x)  2.98 us
  transfers between devices with their start and end apart: 7, of which 5 were waited for; matrix products, arithmetic and copies ran while one was open for 3% of the time, Pallas kernels for 0%

profile of v10, /device:TPU:1, one launch (start us, length us, event | category | flops | bytes accessed | tf_op | source)
XLA Modules:
  0.0 92.8 jit_solution(8892171843469567867)
XLA Ops:
  0.6 1.5 %copy.20.owner_ref = s32[4,128,1]{2,1,0:T(8,128)} copy(s32[4,128,1]{1,2,0:T(1,128)} %param.10) | data formatting | bytes 4096 | tf_op args[1]
  2.2 0.0 copy-start.1
  2.2 0.0 copy-start.3
  2.2 0.0 copy-start.4
  2.2 0.0 copy-start.5
  2.2 2.6 %shard_map.104 = (f32[4,34,256]{2,1,0:T(8,128)}, f32[32,8,128]{2,1,0:T(8,128)}, f32[32,8,128]{2,1,0:T(8,128)}) custom-call(f32[4,32,128]{2,1,0:T(8,128)} %adj_ref.1, s32[4,128,1]{2,1,0:T(8,128)} %copy.20.owner_ref, s32[4,128]{1,0:T(4,128)} %col_ref.1, s32[4,128]{1,0:T(4,128)} %lev_ref.1, f32[4,8,128]{2,1,0:T(8,128)} %wx_ref.5, f32[4,8,128]{2,1,0:T(8,128)} %wy_ref.5, ...), custom_call_target="tpu_custom_call" | custom-call | tf_op jit(solution)/shard_map/pallas_call | solution.py:71
  4.8 1.2 %copy.21 = f32[4,34,256]{1,0,2:T(4,128)S(1)} copy(f32[4,34,256]{2,1,0:T(8,128)} %get-tuple-element.11) | data formatting | bytes 278528 | tf_op jit(solution)/shard_map/pallas_call | solution.py:71
  6.0 1.3 %reshape.78 = f32[128,1,272]{2,1,0:T(1,128)} reshape(f32[256,4,34]{2,1,0:T(4,128)S(1)} %bitcast.4) | data formatting | bytes 278528
  7.3 11.5 %all-to-all-start = ((f32[128,1,272]{2,1,0:T(1,128)}), f32[128,1,272]{2,1,0:T(1,128)S(1)}, u32[]{:S(2)}, u32[]{:S(2)}) async-start(f32[128,1,272]{2,1,0:T(1,128)} %reshape.78), calls=%async_computation | async-start | bytes 393216 | tf_op jit(solution)/shard_map/all_to_all | solution.py:423
  18.8 3.0 %collective-permute-start.2 = (f32[32,8,128]{2,1,0:T(8,128)}, f32[32,8,128]{2,1,0:T(8,128)S(1)}, u32[]{:S(2)}, u32[]{:S(2)}) collective-permute-start(f32[32,8,128]{2,1,0:T(8,128)} %get-tuple-element.12), channel_id=1, source_target_pairs={{16,0},{32,16},{48,32},{64,48},{80,64},{96,80},{112,96},{17,1},{33... | collective-permute-start | bytes 393224 | tf_op jit(solution)/shard_map/ppermute | solution.py:421
  21.7 2.6 %collective-permute-start.3 = (f32[32,8,128]{2,1,0:T(8,128)}, f32[32,8,128]{2,1,0:T(8,128)S(1)}, u32[]{:S(2)}, u32[]{:S(2)}) collective-permute-start(f32[32,8,128]{2,1,0:T(8,128)} %get-tuple-element.13), channel_id=1, source_target_pairs={{0,16},{16,32},{32,48},{48,64},{64,80},{80,96},{96,112},{1,17},{17... | collective-permute-start | bytes 393224 | tf_op jit(solution)/shard_map/ppermute | solution.py:422
  24.4 4.9 %all-to-all-done = f32[128,1,272]{2,1,0:T(1,128)S(1)} async-done(((f32[128,1,272]{2,1,0:T(1,128)}), f32[128,1,272]{2,1,0:T(1,128)S(1)}, u32[]{:S(2)}, u32[]{:S(2)}) %all-to-all-start) | async-done | bytes 139296 | tf_op jit(solution)/shard_map/all_to_all | solution.py:423
  29.3 0.5 broadcast.121
  29.9 1.1 %reduce = f32[128,272]{1,0:T(8,128)S(1)} reduce(f32[128,1,272]{2,1,0:T(1,128)S(1)} %all-to-all-done, f32[]{:T(128)} %broadcast.121), dimensions={1}, to_apply=%all_to_all.6.reduce_sub_computation | reduce | bytes 278532 | tf_op jit(solution)/shard_map/all_to_all | solution.py:423
  31.0 0.4 reshape.79
  31.4 0.0 copy-start.11
  31.4 0.2 copy.24.own_ref
  31.7 0.0 copy-start.6
  31.7 2.6 %collective-permute-start = (f32[4,34,256]{2,1,0:T(8,128)S(1)}, f32[4,34,256]{2,1,0:T(8,128)S(1)}, u32[]{:S(2)}, u32[]{:S(2)}) collective-permute-start(f32[4,34,256]{2,1,0:T(8,128)S(1)} %copy.24.own_ref), channel_id=1, source_target_pairs={{16,0},{32,16},{48,32},{64,48},{80,64},{96,80},{112,96},{17,1},{33... | collective-permute-start | bytes 417800 | tf_op jit(solution)/shard_map/ppermute | solution.py:425
  34.3 3.0 %collective-permute-start.1 = (f32[4,34,256]{2,1,0:T(8,128)S(1)}, f32[4,34,256]{2,1,0:T(8,128)S(1)}, u32[]{:S(2)}, u32[]{:S(2)}) collective-permute-start(f32[4,34,256]{2,1,0:T(8,128)S(1)} %copy.24.own_ref), channel_id=1, source_target_pairs={{0,16},{16,32},{32,48},{48,64},{64,80},{80,96},{96,112},{1,17},{17... | collective-permute-start | bytes 417800 | tf_op jit(solution)/shard_map/ppermute | solution.py:426
  37.2 0.1 and_convert_fusion.mask_ref
  37.3 0.0 collective-permute-done.2.sb_ref
  37.3 0.0 copy-start.9
  37.3 0.0 collective-permute-done.3.sa_ref
  37.3 0.0 copy-start.10
  37.3 1.0 %collective-permute-done.below_ref = f32[4,34,256]{2,1,0:T(8,128)S(1)} collective-permute-done((f32[4,34,256]{2,1,0:T(8,128)S(1)}, f32[4,34,256]{2,1,0:T(8,128)S(1)}, u32[]{:S(2)}, u32[]{:S(2)}) %collective-permute-start) | collective-permute-done | bytes 139296 | tf_op jit(solution)/shard_map/ppermute | solution.py:425
  38.3 0.0 copy-start.7
  38.3 1.2 %collective-permute-done.1.above_ref = f32[4,34,256]{2,1,0:T(8,128)S(1)} collective-permute-done((f32[4,34,256]{2,1,0:T(8,128)S(1)}, f32[4,34,256]{2,1,0:T(8,128)S(1)}, u32[]{:S(2)}, u32[]{:S(2)}) %collective-permute-start.1) | collective-permute-done | bytes 139296 | tf_op jit(solution)/shard_map/ppermute | solution.py:426
  39.5 0.0 copy-done.6
  39.5 0.0 copy-done.9
  39.5 0.0 copy-done.10
  39.5 0.0 copy-done.7
  39.5 0.0 copy-start.8
  39.5 0.7 copy-done.8
  40.2 9.3 %shard_map.105 = (f32[4,80,16,128]{3,2,1,0:T(8,128)}, f32[12,16,128]{2,1,0:T(8,128)}, f32[12,16,128]{2,1,0:T(8,128)}, f32[64,8,128]{2,1,0:T(8,128)}) custom-call(f32[4,34,256]{2,1,0:T(8,128)} %copy-done.6, f32[4,34,256]{2,1,0:T(8,128)} %copy-done.7, f32[4,34,256]{2,1,0:T(8,128)} %copy-done.8, f32[4,8,128]{2,1,0:T(8,128)} %wx_ref.5, f32[4,8,128]{2,1,0:T(8,128)} %wy_ref.5, ...), custom_call_target="tpu_custom_call" | custom-call | tf_op jit(solution)/shard_map/pallas_call | solution.py:179
  49.5 1.3 %collective-permute-start.4 = (f32[12,16,128]{2,1,0:T(8,128)}, f32[12,16,128]{2,1,0:T(8,128)S(1)}, u32[]{:S(2)}, u32[]{:S(2)}) collective-permute-start(f32[12,16,128]{2,1,0:T(8,128)} %get-tuple-element.14), channel_id=1, source_target_pairs={{1,0},{2,1},{3,2},{4,3},{5,4},{6,5},{7,6},{8,7},{9,8},{10,9},{11,1... | collective-permute-start | bytes 294920 | tf_op jit(solution)/shard_map/ppermute | solution.py:429
  50.8 4.2 %collective-permute-start.5 = (f32[12,16,128]{2,1,0:T(8,128)}, f32[12,16,128]{2,1,0:T(8,128)S(1)}, u32[]{:S(2)}, u32[]{:S(2)}) collective-permute-start(f32[12,16,128]{2,1,0:T(8,128)} %get-tuple-element.15), channel_id=1, source_target_pairs={{0,1},{1,2},{2,3},{3,4},{4,5},{5,6},{6,7},{7,8},{8,9},{9,10},{10,1... | collective-permute-start | bytes 294920 | tf_op jit(solution)/shard_map/ppermute | solution.py:430
  54.9 0.1 collective-permute-done.4.right_ref
  55.0 1.7 %collective-permute-done.5.left_ref = f32[12,16,128]{2,1,0:T(8,128)S(1)} collective-permute-done((f32[12,16,128]{2,1,0:T(8,128)}, f32[12,16,128]{2,1,0:T(8,128)S(1)}, u32[]{:S(2)}, u32[]{:S(2)}) %collective-permute-start.5) | collective-permute-done | bytes 98336 | tf_op jit(solution)/shard_map/ppermute | solution.py:430
  56.7 0.0 copy-done.1
  56.7 0.0 copy-done.3
  56.7 0.0 copy-done.4
  56.7 0.0 copy-done.5
  56.7 0.0 copy-start
  56.7 1.7 %copy-done = f32[4,80,16,128]{3,2,1,0:T(8,128)S(1)} copy-done((f32[4,80,16,128]{3,2,1,0:T(8,128)S(1)}, f32[4,80,16,128]{3,2,1,0:T(8,128)}, u32[]{:S(2)}) %copy-start) | copy-done | bytes 2621464
  58.4 0.0 copy-start.2
  58.4 0.9 %copy-done.2 = f32[64,8,128]{2,1,0:T(8,128)S(1)} copy-done((f32[64,8,128]{2,1,0:T(8,128)S(1)}, f32[64,8,128]{2,1,0:T(8,128)}, u32[]{:S(2)}) %copy-start.2) | copy-done | bytes 262168
  59.4 10.4 %shard_map.106 = (f32[2,40,8,128]{3,2,1,0:T(8,128)}, f32[2,8,128]{2,1,0:T(8,128)S(1)}) custom-call(f32[12,16,128]{2,1,0:T(8,128)S(1)} %collective-permute-done.4.right_ref, f32[12,16,128]{2,1,0:T(8,128)S(1)} %collective-permute-done.5.left_ref, f32[4,8,128]{2,1,0:T(8,128)S(1)} %copy-done.3, f32[4,8,128]{2,1,0:T(8,128)S(1)} %copy-done.4, ...), custom_call_target="tpu_custom_call" | custom-call | tf_op jit(solution)/shard_map/pallas_call | solution.py:371
  69.8 0.0 copy-done.11
  69.8 1.9 %fusion = f32[2,128,8]{1,0,2:T(2,128)S(1)} fusion(f32[2,1024,1]{1,0,2:T(2,128)S(1)} %reshape.76, s32[128,8]{0,1:T(8,128)S(1)} %multiply_add_fusion, s32[1024]{0:T(1024)S(1)} %bitcast.6), kind=kOutput, calls=%fused_computation | convolution fusion | flops 26214400 | bytes 24576 | tf_op jit(solution)/shard_map/dot_general | solution.py:448
  71.7 0.2 copy.25
  71.8 20.3 %all_to_all.10 = f32[2,128,8]{2,0,1:T(2,128)S(1)} all-to-all(f32[2,128,8]{2,0,1:T(2,128)S(1)} %copy.25), channel_id=1, replica_groups=mesh['gx'=8,'gy'=16] {'gx','gy'}, dimensions={1} | all-to-all | bytes 16384 | tf_op jit(solution)/shard_map/all_to_all | solution.py:449
  92.1 0.7 reduce_sum.9
  (5 shorter events, 0.0 us)
Async XLA Ops:
  2.2 54.5 %copy-start.1 = (f32[39,8,128]{2,1,0:T(8,128)S(1)}, f32[39,8,128]{2,1,0:T(8,128)}, u32[]{:S(2)}) copy-start(f32[39,8,128]{2,1,0:T(8,128)} %diff_ref.5) | copy-start | bytes 479236
  2.2 54.5 %copy-start.3 = (f32[4,8,128]{2,1,0:T(8,128)S(1)}, f32[4,8,128]{2,1,0:T(8,128)}, u32[]{:S(2)}) copy-start(f32[4,8,128]{2,1,0:T(8,128)} %wx_ref.5) | copy-start | bytes 49156
  2.2 54.5 %copy-start.4 = (f32[4,8,128]{2,1,0:T(8,128)S(1)}, f32[4,8,128]{2,1,0:T(8,128)}, u32[]{:S(2)}) copy-start(f32[4,8,128]{2,1,0:T(8,128)} %wy_ref.5) | copy-start | bytes 49156
  2.2 54.5 %copy-start.5 = (f32[2,8,128]{2,1,0:T(8,128)S(1)}, f32[2,8,128]{2,1,0:T(8,128)}, u32[]{:S(2)}) copy-start(f32[2,8,128]{2,1,0:T(8,128)} %prior_ref.1) | copy-start | bytes 24580
  7.3 22.1 %all-to-all-start = ((f32[128,1,272]{2,1,0:T(1,128)}), f32[128,1,272]{2,1,0:T(1,128)S(1)}, u32[]{:S(2)}, u32[]{:S(2)}) async-start(f32[128,1,272]{2,1,0:T(1,128)} %reshape.78), calls=%async_computation | async-start | bytes 393216 | tf_op jit(solution)/shard_map/all_to_all | solution.py:423
  18.8 18.6 %collective-permute-start.2 = (f32[32,8,128]{2,1,0:T(8,128)}, f32[32,8,128]{2,1,0:T(8,128)S(1)}, u32[]{:S(2)}, u32[]{:S(2)}) collective-permute-start(f32[32,8,128]{2,1,0:T(8,128)} %get-tuple-element.12), channel_id=1, source_target_pairs={{16,0},{32,16},{48,32},{64,48},{80,64},{96,80},{112,96},{17,1},{33... | collective-permute-start | bytes 393224 | tf_op jit(solution)/shard_map/ppermute | solution.py:421
  21.7 15.6 %collective-permute-start.3 = (f32[32,8,128]{2,1,0:T(8,128)}, f32[32,8,128]{2,1,0:T(8,128)S(1)}, u32[]{:S(2)}, u32[]{:S(2)}) collective-permute-start(f32[32,8,128]{2,1,0:T(8,128)} %get-tuple-element.13), channel_id=1, source_target_pairs={{0,16},{16,32},{32,48},{48,64},{64,80},{80,96},{96,112},{1,17},{17... | collective-permute-start | bytes 393224 | tf_op jit(solution)/shard_map/ppermute | solution.py:422
  31.4 38.4 %copy-start.11 = (s32[8,128]{1,0:T(8,128)S(1)}, s32[8,128]{1,0:T(8,128)}, u32[]{:S(2)}) copy-start(s32[8,128]{1,0:T(8,128)} %param.17) | copy-start | bytes 12292
  31.7 7.8 %copy-start.6 = (f32[4,34,256]{2,1,0:T(8,128)}, f32[4,34,256]{2,1,0:T(8,128)S(1)}, u32[]{:S(2)}) copy-start(f32[4,34,256]{2,1,0:T(8,128)S(1)} %copy.24.own_ref) | copy-start | bytes 417796
  31.7 6.6 %collective-permute-start = (f32[4,34,256]{2,1,0:T(8,128)S(1)}, f32[4,34,256]{2,1,0:T(8,128)S(1)}, u32[]{:S(2)}, u32[]{:S(2)}) collective-permute-start(f32[4,34,256]{2,1,0:T(8,128)S(1)} %copy.24.own_ref), channel_id=1, source_target_pairs={{16,0},{32,16},{48,32},{64,48},{80,64},{96,80},{112,96},{17,1},{33... | collective-permute-start | bytes 417800 | tf_op jit(solution)/shard_map/ppermute | solution.py:425
  34.3 5.2 %collective-permute-start.1 = (f32[4,34,256]{2,1,0:T(8,128)S(1)}, f32[4,34,256]{2,1,0:T(8,128)S(1)}, u32[]{:S(2)}, u32[]{:S(2)}) collective-permute-start(f32[4,34,256]{2,1,0:T(8,128)S(1)} %copy.24.own_ref), channel_id=1, source_target_pairs={{0,16},{16,32},{32,48},{48,64},{64,80},{80,96},{96,112},{1,17},{17... | collective-permute-start | bytes 417800 | tf_op jit(solution)/shard_map/ppermute | solution.py:426
  37.3 2.2 %copy-start.9 = (f32[32,8,128]{2,1,0:T(8,128)}, f32[32,8,128]{2,1,0:T(8,128)S(1)}, u32[]{:S(2)}) copy-start(f32[32,8,128]{2,1,0:T(8,128)S(1)} %collective-permute-done.2.sb_ref) | copy-start | bytes 393220
  37.3 2.2 %copy-start.10 = (f32[32,8,128]{2,1,0:T(8,128)}, f32[32,8,128]{2,1,0:T(8,128)S(1)}, u32[]{:S(2)}) copy-start(f32[32,8,128]{2,1,0:T(8,128)S(1)} %collective-permute-done.3.sa_ref) | copy-start | bytes 393220
  38.3 1.2 %copy-start.7 = (f32[4,34,256]{2,1,0:T(8,128)}, f32[4,34,256]{2,1,0:T(8,128)S(1)}, u32[]{:S(2)}) copy-start(f32[4,34,256]{2,1,0:T(8,128)S(1)} %collective-permute-done.below_ref) | copy-start | bytes 417796
  39.5 0.7 copy-start.8
  49.5 5.6 %collective-permute-start.4 = (f32[12,16,128]{2,1,0:T(8,128)}, f32[12,16,128]{2,1,0:T(8,128)S(1)}, u32[]{:S(2)}, u32[]{:S(2)}) collective-permute-start(f32[12,16,128]{2,1,0:T(8,128)} %get-tuple-element.14), channel_id=1, source_target_pairs={{1,0},{2,1},{3,2},{4,3},{5,4},{6,5},{7,6},{8,7},{9,8},{10,9},{11,1... | collective-permute-start | bytes 294920 | tf_op jit(solution)/shard_map/ppermute | solution.py:429
  50.8 5.9 %collective-permute-start.5 = (f32[12,16,128]{2,1,0:T(8,128)}, f32[12,16,128]{2,1,0:T(8,128)S(1)}, u32[]{:S(2)}, u32[]{:S(2)}) collective-permute-start(f32[12,16,128]{2,1,0:T(8,128)} %get-tuple-element.15), channel_id=1, source_target_pairs={{0,1},{1,2},{2,3},{3,4},{4,5},{5,6},{6,7},{7,8},{8,9},{9,10},{10,1... | collective-permute-start | bytes 294920 | tf_op jit(solution)/shard_map/ppermute | solution.py:430
  56.7 1.7 %copy-start = (f32[4,80,16,128]{3,2,1,0:T(8,128)S(1)}, f32[4,80,16,128]{3,2,1,0:T(8,128)}, u32[]{:S(2)}) copy-start(f32[4,80,16,128]{3,2,1,0:T(8,128)} %get-tuple-element.17.tall_hbm) | copy-start | bytes 7864324
  58.4 0.9 %copy-start.2 = (f32[64,8,128]{2,1,0:T(8,128)S(1)}, f32[64,8,128]{2,1,0:T(8,128)}, u32[]{:S(2)}) copy-start(f32[64,8,128]{2,1,0:T(8,128)} %get-tuple-element.16.st_xh) | copy-start | bytes 786436

commit v11 on v10

--- a/solution.py
+++ b/solution.py
@@ -33,24 +33,30 @@
 
 
 def _pack_kernel(capacity, adj_ref, owner_ref, col_ref, lev_ref, wx_ref, wy_ref, diff_ref,
-                 out_ref, lo_ref, hi_ref, rows_ref):
+                 out_ref, lo_ref, hi_ref, rows_ref, tbuf_ref):
     steps, n_pay, pixels = adj_ref.shape
-    slots = out_ref.shape[2]
+    devices, width = out_ref.shape
+    block = width // (steps * capacity)
     row = lax.broadcasted_iota(jnp.int32, (pixels, pixels), 0)
     lane = lax.broadcasted_iota(jnp.int32, (pixels, pixels), 1)
-    slot = lax.broadcasted_iota(jnp.int32, (pixels, slots), 1).astype(jnp.float32)
+    dest = lax.broadcasted_iota(jnp.int32, (pixels, devices), 1).astype(jnp.float32)
+    tbuf_ref[...] = jnp.zeros(tbuf_ref.shape, jnp.float32)
     for k in range(steps):
-        owner = jnp.broadcast_to(owner_ref[k].astype(jnp.float32), (pixels, pixels))
-        same = (owner == jnp.transpose(owner)) & (lane < row)
+        across = jnp.broadcast_to(owner_ref[k:k + 1].astype(jnp.float32), (pixels, pixels))
+        down = jnp.transpose(across)
+        same = (down == across) & (lane < row)
         rank = jnp.sum(jnp.where(same, 1.0, 0.0), axis=1, keepdims=True)
-        position = owner[:, :1] * capacity + rank
-        place = jnp.where(position == slot, 1.0, 0.0)
+        owner = down[:, :devices]
         rows_ref[:n_pay] = adj_ref[k]
         rows_ref[n_pay:n_pay + 1] = col_ref[k:k + 1].astype(jnp.float32)
         rows_ref[n_pay + 1:n_pay + 2] = lev_ref[k:k + 1].astype(jnp.float32)
-        out_ref[k] = lax.dot_general(rows_ref[...], place, (((1,), (0,)), ((), ())),
-                                     precision=lax.Precision.HIGHEST,
-                                     preferred_element_type=jnp.float32)
+        for j in range(capacity):
+            pick = jnp.where((owner == dest) & (rank[:, :1] == j), 1.0, 0.0)
+            at = (k * capacity + j) * block
+            tbuf_ref[at:at + n_pay + 2] = lax.dot_general(
+                rows_ref[...], pick, (((1,), (0,)), ((), ())),
+                precision=lax.Precision.HIGHEST, preferred_element_type=jnp.float32)
+    out_ref[...] = jnp.transpose(tbuf_ref[...])
     statics = (wx_ref, wy_ref, diff_ref)
     tr = wx_ref.shape[1]
     half = tr // 2
@@ -62,19 +68,23 @@
         hi_ref[i] = jnp.where(trow < half, pltpu.roll(a, half, 0), b)
 
 
-def pack_call(capacity, slots, n_pad, pixel_adjoint, pixel_owner, pixel_column, pixel_level,
+def pack_call(capacity, devices, n_pad, pixel_adjoint, pixel_owner, pixel_column, pixel_level,
               wind_x, wind_y, diffusivity):
     steps, n_pay, pixels = pixel_adjoint.shape
     rows, cols = wind_x.shape[1:]
+    block = -(-(n_pay + 2) // 16) * 16
+    width = steps * capacity * block
     pairs = jax.ShapeDtypeStruct((n_pad // 2, rows, cols), jnp.float32)
     vmem = pl.BlockSpec(memory_space=pltpu.VMEM)
     return pl.pallas_call(
         functools.partial(_pack_kernel, capacity),
         in_specs=[vmem] * 7,
         out_specs=[vmem] * 3,
-        out_shape=[jax.ShapeDtypeStruct((steps, n_pay + 2, slots), jnp.float32), pairs, pairs],
-        scratch_shapes=[pltpu.VMEM((n_pay + 2, pixels), jnp.float32)],
-    )(pixel_adjoint, pixel_owner, pixel_column, pixel_level, wind_x, wind_y, diffusivity)
+        out_shape=[jax.ShapeDtypeStruct((devices, width), jnp.float32), pairs, pairs],
+        scratch_shapes=[pltpu.VMEM((n_pay + 2, pixels), jnp.float32),
+                        pltpu.VMEM((width, devices), jnp.float32)],
+    )(pixel_adjoint, pixel_owner.reshape(steps, pixels), pixel_column, pixel_level, wind_x,
+      wind_y, diffusivity)
 
 
 def _exact_dot(a, b):
@@ -90,8 +100,12 @@
 
 def _forcing_kernel(species, kernel, levels, n_statics, own_ref, below_ref, above_ref, wx_ref,
                     wy_ref, diff_ref, sb_ref, sa_ref,
-                    tall_ref, right_ref, left_ref, st_xh_ref, lown_ref, lnb_ref):
-    steps, _, slots = own_ref.shape
+                    tall_ref, right_ref, left_ref, st_xh_ref, lown_ref, lnb_ref, *trans):
+    steps = tall_ref.shape[0]
+    devices, width = own_ref.shape
+    capacity = 2
+    block = width // (steps * capacity)
+    slots = devices * capacity
     tr2, tc = tall_ref.shape[2:]
     tr = tr2 // 2
     half = tr // 2
@@ -103,10 +117,14 @@
     lane16 = lax.broadcasted_iota(jnp.int32, (tr2, tc), 1)
     right_ref[...] = jnp.zeros(right_ref.shape, jnp.float32)
     left_ref[...] = jnp.zeros(left_ref.shape, jnp.float32)
+    for tref, ref in zip(trans, (own_ref, below_ref, above_ref)):
+        tref[...] = jnp.transpose(ref[...])
     for k in range(steps):
         hts = []
-        for src, ref in enumerate((own_ref, below_ref, above_ref)):
-            blk = ref[k]
+        for src, tref in enumerate(trans):
+            at = k * capacity * block
+            blk = jnp.concatenate(
+                [tref[at + j * block:at + j * block + n_pay + 2] for j in range(capacity)], axis=1)
             col = blk[n_pay:n_pay + 1].astype(jnp.int32)
             lev = blk[n_pay + 1:n_pay + 2].astype(jnp.int32)
             row_q = col // tc
@@ -169,7 +187,9 @@
 
 def forcing_call(species, kernel, levels, n_statics, own, below, above, wind_x, wind_y,
                  diffusivity, st_below, st_above):
-    steps, _, slots = own.shape
+    steps = wind_x.shape[0]
+    devices, width = own.shape
+    slots = 2 * devices
     tr, cols = wind_x.shape[1:]
     planes = species * levels
     group = cols // (tr // 2)
@@ -183,7 +203,8 @@
         out_shape=[jax.ShapeDtypeStruct((steps, planes, 2 * tr, cols), jnp.float32), packed,
                    packed, jax.ShapeDtypeStruct((2 * st_below.shape[0], tr, cols), jnp.float32)],
         scratch_shapes=[pltpu.VMEM((planes * tr, slots), jnp.float32),
-                        pltpu.VMEM((planes * tr, 2 * slots), jnp.float32)],
+                        pltpu.VMEM((planes * tr, 2 * slots), jnp.float32)]
+        + [pltpu.VMEM((width, devices), jnp.float32)] * 3,
     )(own, below, above, wind_x, wind_y, diffusivity, st_below, st_above)
 
 
@@ -414,13 +435,13 @@
     n_s = 2 * steps + levels - 1
     group = cols // halo
     n_pad = -(-n_s // group) * group
-    placed, st_lo, st_hi = pack_call(capacity, slots, n_pad, pixel_adjoint, pixel_owner,
+    placed, st_lo, st_hi = pack_call(capacity, devices, n_pad, pixel_adjoint, pixel_owner,
                                      pixel_column, pixel_level, wind_x, wind_y, diffusivity)
     up_x, down_x = _pairs("gx")
     up_y, down_y = _pairs("gy")
     st_below = lax.ppermute(st_lo, "gx", down_x)
     st_above = lax.ppermute(st_hi, "gx", up_x)
-    received = lax.all_to_all(placed, ("gx", "gy"), 2, 2, tiled=True)
+    received = lax.all_to_all(placed, ("gx", "gy"), 0, 0, tiled=True)
 
     below = lax.ppermute(received, "gx", down_x)
     above = lax.ppermute(received, "gx", up_x)

time: 93.3 us -> 90.8 us (0.973)
  local copies, waits for them, and re-layouts: 8.71 us -> 7.5 us
  other arithmetic: 1.93 us -> 0.81 us
    pallas_call x1 -> x0, local copies, waits for them, and re-layouts: 1.16 us -> none  [pack_call(): pl.pallas_call(functools.partial(_pack_kernel, capacity), in_specs=[vmem]...]
    all_to_all x1 -> x0, other arithmetic: 1.12 us -> none  [local(): received = lax.all_to_all(placed, ('gx', 'gy'), 2, 2, tiled=True)]
    unnamed x27 -> x25, local copies, waits for them, and re-layouts: 6.65 us -> 5.54 us
    all_to_all x2 -> x1, local copies, waits for them, and re-layouts: 0.73 us -> 1.79 us  [local(): received = lax.all_to_all(placed, ('gx', 'gy'), 0, 0, tiled=True)]
  transfers between devices with their start and end apart: 7 -> 7, of which waited for: 5 -> 5; matrix products, arithmetic and copies ran while one was open for 3% -> 0% of each run, Pallas kernels for 0% -> 0%
where the time goes in v11:
time: 90.8 us; the launch traced here: 90.2 us
  starting transfers between devices  27.9 us (31%)
  Pallas kernels  21.7 us (24%)
  blocking collectives  20.3 us (22%)
  waiting for transfers between devices  9.33 us (10%)
  local copies, waits for them, and re-layouts  7.5 us (8%)
  matrix products  1.87 us (2%)
    all_to_all x1, blocking collectives, local(): lax.all_to_all(partial.reshape(species, devices, nreg // devices), ('gx',...  20.3 us
    all_to_all x1, starting transfers between devices, local(): received = lax.all_to_all(placed, ('gx', 'gy'), 0, 0, tiled=True)  11.5 us
    pallas_call x1, Pallas kernels, steps_call(): pl.pallas_call(functools.partial(_steps_kernel, steps, species, levels, n...  10.4 us
    pallas_call x1, Pallas kernels, forcing_call(): pl.pallas_call(functools.partial(_forcing_kernel, species, kernel, levels...  8.72 us
    unnamed x25, local copies, waits for them, and re-layouts  5.54 us
    all_to_all x1, waiting for transfers between devices, local(): received = lax.all_to_all(placed, ('gx', 'gy'), 0, 0, tiled=True)  4.92 us
    ppermute x1, starting transfers between devices, local(): left = lax.ppermute(left, 'gy', up_y)  3.99 us
    ppermute x1, starting transfers between devices, local(): st_below = lax.ppermute(st_lo, 'gx', down_x)  2.98 us
  transfers between devices with their start and end apart: 7, of which 5 were waited for; matrix products, arithmetic and copies ran while one was open for 0% of the time, Pallas kernels for 0%

profile of v11, /device:TPU:1, one launch (start us, length us, event | category | flops | bytes accessed | tf_op | source)
XLA Modules:
  0.0 90.2 jit_solution(732304826736895781)
XLA Ops:
  0.6 0.0 copy-start.1
  0.6 2.6 %shard_map.104 = (f32[128,384]{1,0:T(8,128)}, f32[32,8,128]{2,1,0:T(8,128)}, f32[32,8,128]{2,1,0:T(8,128)}) custom-call(f32[4,32,128]{2,1,0:T(8,128)} %adj_ref.1, s32[4,128]{1,0:T(4,128)} %bitcast.11, s32[4,128]{1,0:T(4,128)} %col_ref.1, s32[4,128]{1,0:T(4,128)} %lev_ref.1, f32[4,8,128]{2,1,0:T(8,128)} %wx_ref.5, f32[4,8,128]{2,1,0:T(8,128)} %wy_ref.5, ...), custom_call_target="tpu_custom_call" | custom-call | tf_op jit(solution)/shard_map/pallas_call | solution.py:79
  3.2 1.8 %copy.15 = f32[128,1,384]{2,1,0:T(1,128)} copy(f32[128,1,384]{2,0,1:T(8,128)} %bitcast.10) | data formatting | bytes 393216 | tf_op jit(solution)/shard_map/all_to_all | solution.py:444
  5.0 0.0 copy-start.11
  5.0 11.5 %all-to-all-start = ((f32[128,1,384]{2,1,0:T(1,128)}), f32[128,1,384]{2,1,0:T(1,128)S(1)}, u32[]{:S(2)}, u32[]{:S(2)}) async-start(f32[128,1,384]{2,1,0:T(1,128)} %copy.15), calls=%async_computation | async-start | bytes 393216 | tf_op jit(solution)/shard_map/all_to_all | solution.py:444
  16.5 3.0 %collective-permute-start.2 = (f32[32,8,128]{2,1,0:T(8,128)}, f32[32,8,128]{2,1,0:T(8,128)S(1)}, u32[]{:S(2)}, u32[]{:S(2)}) collective-permute-start(f32[32,8,128]{2,1,0:T(8,128)} %get-tuple-element.12), channel_id=1, source_target_pairs={{16,0},{32,16},{48,32},{64,48},{80,64},{96,80},{112,96},{17,1},{33... | collective-permute-start | bytes 393224 | tf_op jit(solution)/shard_map/ppermute | solution.py:442
  19.5 2.6 %collective-permute-start.3 = (f32[32,8,128]{2,1,0:T(8,128)}, f32[32,8,128]{2,1,0:T(8,128)S(1)}, u32[]{:S(2)}, u32[]{:S(2)}) collective-permute-start(f32[32,8,128]{2,1,0:T(8,128)} %get-tuple-element.13), channel_id=1, source_target_pairs={{0,16},{16,32},{32,48},{48,64},{64,80},{80,96},{96,112},{1,17},{17... | collective-permute-start | bytes 393224 | tf_op jit(solution)/shard_map/ppermute | solution.py:443
  22.2 4.9 %all-to-all-done = f32[128,1,384]{2,1,0:T(1,128)S(1)} async-done(((f32[128,1,384]{2,1,0:T(1,128)}), f32[128,1,384]{2,1,0:T(1,128)S(1)}, u32[]{:S(2)}, u32[]{:S(2)}) %all-to-all-start) | async-done | bytes 196640 | tf_op jit(solution)/shard_map/all_to_all | solution.py:444
  27.1 0.0 copy-start.6
  27.1 2.6 %collective-permute-start = (f32[128,384]{1,0:T(8,128)S(1)}, f32[128,384]{1,0:T(8,128)S(1)}, u32[]{:S(2)}, u32[]{:S(2)}) collective-permute-start(f32[128,384]{1,0:T(8,128)S(1)} %bitcast.7), channel_id=1, source_target_pairs={{16,0},{32,16},{48,32},{64,48},{80,64},{96,80},{112,96},{17,1},{33... | collective-permute-start | bytes 589832 | tf_op jit(solution)/shard_map/ppermute | solution.py:446
  29.8 3.0 %collective-permute-start.1 = (f32[128,384]{1,0:T(8,128)S(1)}, f32[128,384]{1,0:T(8,128)S(1)}, u32[]{:S(2)}, u32[]{:S(2)}) collective-permute-start(f32[128,384]{1,0:T(8,128)S(1)} %bitcast.8), channel_id=1, source_target_pairs={{0,16},{16,32},{32,48},{48,64},{64,80},{80,96},{96,112},{1,17},{17... | collective-permute-start | bytes 589832 | tf_op jit(solution)/shard_map/ppermute | solution.py:447
  32.7 0.1 and_convert_fusion.mask_ref
  32.8 0.0 collective-permute-done.2.sb_ref
  32.8 0.0 copy-start.9
  32.8 0.0 collective-permute-done.3.sa_ref
  32.8 0.0 copy-start.10
  32.8 1.3 %collective-permute-done.below_ref = f32[128,384]{1,0:T(8,128)S(1)} collective-permute-done((f32[128,384]{1,0:T(8,128)S(1)}, f32[128,384]{1,0:T(8,128)S(1)}, u32[]{:S(2)}, u32[]{:S(2)}) %collective-permute-start) | collective-permute-done | bytes 196640 | tf_op jit(solution)/shard_map/ppermute | solution.py:446
  34.1 0.0 copy-start.7
  34.1 1.2 %collective-permute-done.1.above_ref = f32[128,384]{1,0:T(8,128)S(1)} collective-permute-done((f32[128,384]{1,0:T(8,128)S(1)}, f32[128,384]{1,0:T(8,128)S(1)}, u32[]{:S(2)}, u32[]{:S(2)}) %collective-permute-start.1) | collective-permute-done | bytes 196640 | tf_op jit(solution)/shard_map/ppermute | solution.py:447
  35.3 0.0 copy-done.6
  35.3 0.0 copy-done.9
  35.3 0.0 copy-done.10
  35.3 0.0 copy-done.7
  35.3 0.0 copy-start.8
  35.3 0.7 copy-done.8
  36.0 8.7 %shard_map.105 = (f32[4,80,16,128]{3,2,1,0:T(8,128)}, f32[12,16,128]{2,1,0:T(8,128)}, f32[12,16,128]{2,1,0:T(8,128)}, f32[64,8,128]{2,1,0:T(8,128)}) custom-call(f32[128,384]{1,0:T(8,128)} %bitcast.9, f32[128,384]{1,0:T(8,128)} %copy-done.7, f32[128,384]{1,0:T(8,128)} %copy-done.8, f32[4,8,128]{2,1,0:T(8,128)} %wx_ref.5, f32[4,8,128]{2,1,0:T(8,128)} %wy_ref.5, ...), custom_call_target="tpu_custom_call" | custom-call | tf_op jit(solution)/shard_map/pallas_call | solution.py:199
  44.7 1.3 %collective-permute-start.4 = (f32[12,16,128]{2,1,0:T(8,128)}, f32[12,16,128]{2,1,0:T(8,128)S(1)}, u32[]{:S(2)}, u32[]{:S(2)}) collective-permute-start(f32[12,16,128]{2,1,0:T(8,128)} %get-tuple-element.14), channel_id=1, source_target_pairs={{1,0},{2,1},{3,2},{4,3},{5,4},{6,5},{7,6},{8,7},{9,8},{10,9},{11,1... | collective-permute-start | bytes 294920 | tf_op jit(solution)/shard_map/ppermute | solution.py:450
  46.0 4.0 %collective-permute-start.5 = (f32[12,16,128]{2,1,0:T(8,128)}, f32[12,16,128]{2,1,0:T(8,128)S(1)}, u32[]{:S(2)}, u32[]{:S(2)}) collective-permute-start(f32[12,16,128]{2,1,0:T(8,128)} %get-tuple-element.15), channel_id=1, source_target_pairs={{0,1},{1,2},{2,3},{3,4},{4,5},{5,6},{6,7},{7,8},{8,9},{9,10},{10,1... | collective-permute-start | bytes 294920 | tf_op jit(solution)/shard_map/ppermute | solution.py:451
  50.0 0.3 collective-permute-done.4.right_ref
  50.3 1.7 %collective-permute-done.5.left_ref = f32[12,16,128]{2,1,0:T(8,128)S(1)} collective-permute-done((f32[12,16,128]{2,1,0:T(8,128)}, f32[12,16,128]{2,1,0:T(8,128)S(1)}, u32[]{:S(2)}, u32[]{:S(2)}) %collective-permute-start.5) | collective-permute-done | bytes 98336 | tf_op jit(solution)/shard_map/ppermute | solution.py:451
  51.9 0.0 copy-done.1
  51.9 0.0 copy-start
  51.9 1.7 %copy-done = f32[4,80,16,128]{3,2,1,0:T(8,128)S(1)} copy-done((f32[4,80,16,128]{3,2,1,0:T(8,128)S(1)}, f32[4,80,16,128]{3,2,1,0:T(8,128)}, u32[]{:S(2)}) %copy-start) | copy-done | bytes 2621464
  53.7 0.0 copy-start.2
  53.7 0.9 %copy-done.2 = f32[64,8,128]{2,1,0:T(8,128)S(1)} copy-done((f32[64,8,128]{2,1,0:T(8,128)S(1)}, f32[64,8,128]{2,1,0:T(8,128)}, u32[]{:S(2)}) %copy-start.2) | copy-done | bytes 262168
  54.6 0.0 copy-start.3
  54.6 0.7 copy-done.3
  55.4 0.0 copy-start.4
  55.4 0.7 copy-done.4
  56.1 0.0 copy-start.5
  56.1 0.7 copy-done.5
  56.8 10.4 %shard_map.106 = (f32[2,40,8,128]{3,2,1,0:T(8,128)}, f32[2,8,128]{2,1,0:T(8,128)S(1)}) custom-call(f32[12,16,128]{2,1,0:T(8,128)S(1)} %collective-permute-done.4.right_ref, f32[12,16,128]{2,1,0:T(8,128)S(1)} %collective-permute-done.5.left_ref, f32[4,8,128]{2,1,0:T(8,128)S(1)} %copy-done.3, f32[4,8,128]{2,1,0:T(8,128)S(1)} %copy-done.4, ...), custom_call_target="tpu_custom_call" | custom-call | tf_op jit(solution)/shard_map/pallas_call | solution.py:392
  67.2 0.0 copy-done.11
  67.2 1.9 %fusion = f32[2,128,8]{1,0,2:T(2,128)S(1)} fusion(f32[2,1024,1]{1,0,2:T(2,128)S(1)} %reshape.82, s32[128,8]{0,1:T(8,128)S(1)} %multiply_add_fusion, s32[1024]{0:T(1024)S(1)} %bitcast.12), kind=kOutput, calls=%fused_computation | convolution fusion | flops 26214400 | bytes 24576 | tf_op jit(solution)/shard_map/dot_general | solution.py:469
  69.0 0.2 copy.16
  69.2 20.3 %all_to_all.16 = f32[2,128,8]{2,0,1:T(2,128)S(1)} all-to-all(f32[2,128,8]{2,0,1:T(2,128)S(1)} %copy.16), channel_id=1, replica_groups=mesh['gx'=8,'gy'=16] {'gx','gy'}, dimensions={1} | all-to-all | bytes 16384 | tf_op jit(solution)/shard_map/all_to_all | solution.py:470
  89.5 0.7 reduce_sum.9
  (6 shorter events, 0.1 us)
Async XLA Ops:
  0.6 51.3 %copy-start.1 = (f32[39,8,128]{2,1,0:T(8,128)S(1)}, f32[39,8,128]{2,1,0:T(8,128)}, u32[]{:S(2)}) copy-start(f32[39,8,128]{2,1,0:T(8,128)} %diff_ref.5) | copy-start | bytes 479236
  5.0 62.1 %copy-start.11 = (s32[8,128]{1,0:T(8,128)S(1)}, s32[8,128]{1,0:T(8,128)}, u32[]{:S(2)}) copy-start(s32[8,128]{1,0:T(8,128)} %param.17) | copy-start | bytes 12292
  5.0 22.1 %all-to-all-start = ((f32[128,1,384]{2,1,0:T(1,128)}), f32[128,1,384]{2,1,0:T(1,128)S(1)}, u32[]{:S(2)}, u32[]{:S(2)}) async-start(f32[128,1,384]{2,1,0:T(1,128)} %copy.15), calls=%async_computation | async-start | bytes 393216 | tf_op jit(solution)/shard_map/all_to_all | solution.py:444
  16.5 16.3 %collective-permute-start.2 = (f32[32,8,128]{2,1,0:T(8,128)}, f32[32,8,128]{2,1,0:T(8,128)S(1)}, u32[]{:S(2)}, u32[]{:S(2)}) collective-permute-start(f32[32,8,128]{2,1,0:T(8,128)} %get-tuple-element.12), channel_id=1, source_target_pairs={{16,0},{32,16},{48,32},{64,48},{80,64},{96,80},{112,96},{17,1},{33... | collective-permute-start | bytes 393224 | tf_op jit(solution)/shard_map/ppermute | solution.py:442
  19.5 13.3 %collective-permute-start.3 = (f32[32,8,128]{2,1,0:T(8,128)}, f32[32,8,128]{2,1,0:T(8,128)S(1)}, u32[]{:S(2)}, u32[]{:S(2)}) collective-permute-start(f32[32,8,128]{2,1,0:T(8,128)} %get-tuple-element.13), channel_id=1, source_target_pairs={{0,16},{16,32},{32,48},{48,64},{64,80},{80,96},{96,112},{1,17},{17... | collective-permute-start | bytes 393224 | tf_op jit(solution)/shard_map/ppermute | solution.py:443
  27.1 8.2 %copy-start.6 = (f32[128,1,384]{2,0,1:T(8,128)}, f32[128,1,384]{2,0,1:T(8,128)S(1)}, u32[]{:S(2)}) copy-start(f32[128,1,384]{2,0,1:T(8,128)S(1)} %copy.22) | copy-start | bytes 589828
  27.1 7.0 %collective-permute-start = (f32[128,384]{1,0:T(8,128)S(1)}, f32[128,384]{1,0:T(8,128)S(1)}, u32[]{:S(2)}, u32[]{:S(2)}) collective-permute-start(f32[128,384]{1,0:T(8,128)S(1)} %bitcast.7), channel_id=1, source_target_pairs={{16,0},{32,16},{48,32},{64,48},{80,64},{96,80},{112,96},{17,1},{33... | collective-permute-start | bytes 589832 | tf_op jit(solution)/shard_map/ppermute | solution.py:446
  29.8 5.6 %collective-permute-start.1 = (f32[128,384]{1,0:T(8,128)S(1)}, f32[128,384]{1,0:T(8,128)S(1)}, u32[]{:S(2)}, u32[]{:S(2)}) collective-permute-start(f32[128,384]{1,0:T(8,128)S(1)} %bitcast.8), channel_id=1, source_target_pairs={{0,16},{16,32},{32,48},{48,64},{64,80},{80,96},{96,112},{1,17},{17... | collective-permute-start | bytes 589832 | tf_op jit(solution)/shard_map/ppermute | solution.py:447
  32.8 2.5 %copy-start.9 = (f32[32,8,128]{2,1,0:T(8,128)}, f32[32,8,128]{2,1,0:T(8,128)S(1)}, u32[]{:S(2)}) copy-start(f32[32,8,128]{2,1,0:T(8,128)S(1)} %collective-permute-done.2.sb_ref) | copy-start | bytes 393220
  32.8 2.5 %copy-start.10 = (f32[32,8,128]{2,1,0:T(8,128)}, f32[32,8,128]{2,1,0:T(8,128)S(1)}, u32[]{:S(2)}) copy-start(f32[32,8,128]{2,1,0:T(8,128)S(1)} %collective-permute-done.3.sa_ref) | copy-start | bytes 393220
  34.1 1.2 %copy-start.7 = (f32[128,384]{1,0:T(8,128)}, f32[128,384]{1,0:T(8,128)S(1)}, u32[]{:S(2)}) copy-start(f32[128,384]{1,0:T(8,128)S(1)} %collective-permute-done.below_ref) | copy-start | bytes 589828
  35.3 0.7 copy-start.8
  44.7 5.6 %collective-permute-start.4 = (f32[12,16,128]{2,1,0:T(8,128)}, f32[12,16,128]{2,1,0:T(8,128)S(1)}, u32[]{:S(2)}, u32[]{:S(2)}) collective-permute-start(f32[12,16,128]{2,1,0:T(8,128)} %get-tuple-element.14), channel_id=1, source_target_pairs={{1,0},{2,1},{3,2},{4,3},{5,4},{6,5},{7,6},{8,7},{9,8},{10,9},{11,1... | collective-permute-start | bytes 294920 | tf_op jit(solution)/shard_map/ppermute | solution.py:450
  46.0 5.9 %collective-permute-start.5 = (f32[12,16,128]{2,1,0:T(8,128)}, f32[12,16,128]{2,1,0:T(8,128)S(1)}, u32[]{:S(2)}, u32[]{:S(2)}) collective-permute-start(f32[12,16,128]{2,1,0:T(8,128)} %get-tuple-element.15), channel_id=1, source_target_pairs={{0,1},{1,2},{2,3},{3,4},{4,5},{5,6},{6,7},{7,8},{8,9},{9,10},{10,1... | collective-permute-start | bytes 294920 | tf_op jit(solution)/shard_map/ppermute | solution.py:451
  51.9 1.7 %copy-start = (f32[4,80,16,128]{3,2,1,0:T(8,128)S(1)}, f32[4,80,16,128]{3,2,1,0:T(8,128)}, u32[]{:S(2)}) copy-start(f32[4,80,16,128]{3,2,1,0:T(8,128)} %get-tuple-element.17.tall_hbm) | copy-start | bytes 7864324
  53.7 0.9 %copy-start.2 = (f32[64,8,128]{2,1,0:T(8,128)S(1)}, f32[64,8,128]{2,1,0:T(8,128)}, u32[]{:S(2)}) copy-start(f32[64,8,128]{2,1,0:T(8,128)} %get-tuple-element.16.st_xh) | copy-start | bytes 786436
  54.6 0.7 copy-start.3
  55.4 0.7 copy-start.4
  56.1 0.7 copy-start.5

commit v12 on v11

--- a/solution.py
+++ b/solution.py
@@ -208,10 +208,20 @@
     )(own, below, above, wind_x, wind_y, diffusivity, st_below, st_above)
 
 
-def _steps_kernel(steps, species, levels, n_statics,
-                  right_ref, left_ref, wx_ref, wy_ref, diff_ref, st_xh, mask_ref, prior_ref,
-                  tall_hbm, adj_ref, ss_ref,
-                  tall_buf, yh_buf, se_ref, state_ref, red_ref, ratio_ref, inv_ref, sems):
+def _steps_kernel(steps, species, levels, n_statics, *refs):
+    n_in = 8
+    hbm = refs[:n_in]
+    tall_hbm, adj_ref, ss_ref = refs[n_in:n_in + 3]
+    (tall_buf, yh_buf, se_ref, state_ref, red_ref, ratio_ref, inv_ref,
+     sems) = refs[n_in + 3:n_in + 11]
+    vbufs = refs[n_in + 11:n_in + 11 + n_in]
+    in_sems = refs[n_in + 11 + n_in]
+    fetch = []
+    for i in range(n_in):
+        copy = pltpu.make_async_copy(hbm[i], vbufs[i], in_sems.at[i])
+        copy.start()
+        fetch.append(copy)
+    right_ref, left_ref, wx_ref, wy_ref, diff_ref, st_xh, mask_ref, prior_ref = vbufs
     planes = species * levels
     rows, lanes = mask_ref.shape
     tr, tc = adj_ref.shape[2:]
@@ -234,15 +244,21 @@
             yh_buf[g * group + q] = _unpack(r, l, q, tc, half)
         return carry
 
+    fetch[0].wait()
+    fetch[1].wait()
     lax.fori_loop(0, n_fgroups, unpack_group, 0)
     for c in range(n_statics):
         g, q = divmod(n_fgroups * group + c, group)
         se_ref[c, :, tc:] = _unpack(right_ref[g], left_ref[g], q, tc, half)
 
+    for i in range(2, 6):
+        fetch[i].wait()
     for c in range(n_statics):
         se_ref[c, :tr, :tc] = _static_plane(c, (wx_ref, wy_ref, diff_ref))
         se_ref[c, tr:, :tc] = st_xh[c]
 
+    fetch[6].wait()
+    fetch[7].wait()
     zero = jnp.zeros((rows, lanes), jnp.float32)
     inside = mask_ref[...] > 0.5
     carried = zero
@@ -389,9 +405,10 @@
     lanes = mask.shape[1]
     vmem = pl.BlockSpec(memory_space=pltpu.VMEM)
     anyspace = pl.BlockSpec(memory_space=pl.ANY)
+    ins = (right, left, wind_x, wind_y, diffusivity, st_xh, mask, prior)
     return pl.pallas_call(
         functools.partial(_steps_kernel, steps, species, levels, n_statics),
-        in_specs=[vmem] * 8 + [anyspace],
+        in_specs=[anyspace] * (len(ins) + 1),
         out_specs=[vmem, vmem],
         out_shape=[jax.ShapeDtypeStruct((species, levels, tr, tc), jnp.float32),
                    jax.ShapeDtypeStruct(prior.shape, jnp.float32)],
@@ -404,9 +421,11 @@
             pltpu.VMEM((levels, rows, lanes), jnp.float32),
             pltpu.VMEM((levels, rows, lanes), jnp.float32),
             pltpu.SemaphoreType.DMA((steps,)),
+        ] + [pltpu.VMEM(a.shape, a.dtype) for a in ins] + [
+            pltpu.SemaphoreType.DMA((len(ins),)),
         ],
         compiler_params=pltpu.CompilerParams(vmem_limit_bytes=48 * 1024 * 1024),
-    )(right, left, wind_x, wind_y, diffusivity, st_xh, mask, prior, tall)
+    )(*ins, tall)
 
 
 def _pairs(axis):

time: 90.8 us -> 91.6 us (level)
  no operation moved by 1% of the time
where the time goes in v12:
time: 91.6 us; the launch traced here: 91 us
  starting transfers between devices  27.9 us (30%)
  Pallas kernels  22.5 us (25%)
  blocking collectives  20.3 us (22%)
  waiting for transfers between devices  9.33 us (10%)
  local copies, waits for them, and re-layouts  7.5 us (8%)
  matrix products  1.87 us (2%)
    all_to_all x1, blocking collectives, local(): lax.all_to_all(partial.reshape(species, devices, nreg // devices), ('gx',...  20.3 us
    all_to_all x1, starting transfers between devices, local(): received = lax.all_to_all(placed, ('gx', 'gy'), 0, 0, tiled=True)  11.5 us
    pallas_call x1, Pallas kernels, steps_call(): pl.pallas_call(functools.partial(_steps_kernel, steps, species, levels, n...  11.2 us
    pallas_call x1, Pallas kernels, forcing_call(): pl.pallas_call(functools.partial(_forcing_kernel, species, kernel, levels...  8.72 us
    unnamed x25, local copies, waits for them, and re-layouts  5.54 us
    all_to_all x1, waiting for transfers between devices, local(): received = lax.all_to_all(placed, ('gx', 'gy'), 0, 0, tiled=True)  4.92 us
    ppermute x1, starting transfers between devices, local(): left = lax.ppermute(left, 'gy', up_y)  3.99 us
    ppermute x1, starting transfers between devices, local(): st_below = lax.ppermute(st_lo, 'gx', down_x)  2.98 us
  transfers between devices with their start and end apart: 7, of which 5 were waited for; matrix products, arithmetic and copies ran while one was open for 0% of the time, Pallas kernels for 0%

profile of v12, /device:TPU:1, one launch (start us, length us, event | category | flops | bytes accessed | tf_op | source)
XLA Modules:
  0.0 91.0 jit_solution(16144505258139972400)
XLA Ops:
  0.6 0.0 copy-start.1
  0.6 2.6 %shard_map.104 = (f32[128,384]{1,0:T(8,128)}, f32[32,8,128]{2,1,0:T(8,128)}, f32[32,8,128]{2,1,0:T(8,128)}) custom-call(f32[4,32,128]{2,1,0:T(8,128)} %adj_ref.1, s32[4,128]{1,0:T(4,128)} %bitcast.11, s32[4,128]{1,0:T(4,128)} %col_ref.1, s32[4,128]{1,0:T(4,128)} %lev_ref.1, f32[4,8,128]{2,1,0:T(8,128)} %refs_2_.1, f32[4,8,128]{2,1,0:T(8,128)} %refs_3_.1, ...), custom_call_target="tpu_custom_call" | custom-call | tf_op jit(solution)/shard_map/pallas_call | solution.py:79
  3.2 1.8 %copy.15 = f32[128,1,384]{2,1,0:T(1,128)} copy(f32[128,1,384]{2,0,1:T(8,128)} %bitcast.10) | data formatting | bytes 393216 | tf_op jit(solution)/shard_map/all_to_all | solution.py:463
  5.0 0.0 copy-start.11
  5.0 11.5 %all-to-all-start = ((f32[128,1,384]{2,1,0:T(1,128)}), f32[128,1,384]{2,1,0:T(1,128)S(1)}, u32[]{:S(2)}, u32[]{:S(2)}) async-start(f32[128,1,384]{2,1,0:T(1,128)} %copy.15), calls=%async_computation | async-start | bytes 393216 | tf_op jit(solution)/shard_map/all_to_all | solution.py:463
  16.5 3.0 %collective-permute-start.2 = (f32[32,8,128]{2,1,0:T(8,128)}, f32[32,8,128]{2,1,0:T(8,128)S(1)}, u32[]{:S(2)}, u32[]{:S(2)}) collective-permute-start(f32[32,8,128]{2,1,0:T(8,128)} %get-tuple-element.12), channel_id=1, source_target_pairs={{16,0},{32,16},{48,32},{64,48},{80,64},{96,80},{112,96},{17,1},{33... | collective-permute-start | bytes 393224 | tf_op jit(solution)/shard_map/ppermute | solution.py:461
  19.5 2.6 %collective-permute-start.3 = (f32[32,8,128]{2,1,0:T(8,128)}, f32[32,8,128]{2,1,0:T(8,128)S(1)}, u32[]{:S(2)}, u32[]{:S(2)}) collective-permute-start(f32[32,8,128]{2,1,0:T(8,128)} %get-tuple-element.13), channel_id=1, source_target_pairs={{0,16},{16,32},{32,48},{48,64},{64,80},{80,96},{96,112},{1,17},{17... | collective-permute-start | bytes 393224 | tf_op jit(solution)/shard_map/ppermute | solution.py:462
  22.2 4.9 %all-to-all-done = f32[128,1,384]{2,1,0:T(1,128)S(1)} async-done(((f32[128,1,384]{2,1,0:T(1,128)}), f32[128,1,384]{2,1,0:T(1,128)S(1)}, u32[]{:S(2)}, u32[]{:S(2)}) %all-to-all-start) | async-done | bytes 196640 | tf_op jit(solution)/shard_map/all_to_all | solution.py:463
  27.1 0.0 copy-start.6
  27.1 2.6 %collective-permute-start = (f32[128,384]{1,0:T(8,128)S(1)}, f32[128,384]{1,0:T(8,128)S(1)}, u32[]{:S(2)}, u32[]{:S(2)}) collective-permute-start(f32[128,384]{1,0:T(8,128)S(1)} %bitcast.7), channel_id=1, source_target_pairs={{16,0},{32,16},{48,32},{64,48},{80,64},{96,80},{112,96},{17,1},{33... | collective-permute-start | bytes 589832 | tf_op jit(solution)/shard_map/ppermute | solution.py:465
  29.8 3.0 %collective-permute-start.1 = (f32[128,384]{1,0:T(8,128)S(1)}, f32[128,384]{1,0:T(8,128)S(1)}, u32[]{:S(2)}, u32[]{:S(2)}) collective-permute-start(f32[128,384]{1,0:T(8,128)S(1)} %bitcast.8), channel_id=1, source_target_pairs={{0,16},{16,32},{32,48},{48,64},{64,80},{80,96},{96,112},{1,17},{17... | collective-permute-start | bytes 589832 | tf_op jit(solution)/shard_map/ppermute | solution.py:466
  32.7 0.1 and_convert_fusion.refs_6_
  32.8 0.0 collective-permute-done.2.sb_ref
  32.8 0.0 copy-start.9
  32.8 0.0 collective-permute-done.3.sa_ref
  32.8 0.0 copy-start.10
  32.8 1.3 %collective-permute-done.below_ref = f32[128,384]{1,0:T(8,128)S(1)} collective-permute-done((f32[128,384]{1,0:T(8,128)S(1)}, f32[128,384]{1,0:T(8,128)S(1)}, u32[]{:S(2)}, u32[]{:S(2)}) %collective-permute-start) | collective-permute-done | bytes 196640 | tf_op jit(solution)/shard_map/ppermute | solution.py:465
  34.1 0.0 copy-start.7
  34.1 1.2 %collective-permute-done.1.above_ref = f32[128,384]{1,0:T(8,128)S(1)} collective-permute-done((f32[128,384]{1,0:T(8,128)S(1)}, f32[128,384]{1,0:T(8,128)S(1)}, u32[]{:S(2)}, u32[]{:S(2)}) %collective-permute-start.1) | collective-permute-done | bytes 196640 | tf_op jit(solution)/shard_map/ppermute | solution.py:466
  35.3 0.0 copy-done.6
  35.3 0.0 copy-done.9
  35.3 0.0 copy-done.10
  35.3 0.0 copy-done.7
  35.3 0.0 copy-start.8
  35.3 0.7 copy-done.8
  36.0 8.7 %shard_map.105 = (f32[4,80,16,128]{3,2,1,0:T(8,128)}, f32[12,16,128]{2,1,0:T(8,128)}, f32[12,16,128]{2,1,0:T(8,128)}, f32[64,8,128]{2,1,0:T(8,128)}) custom-call(f32[128,384]{1,0:T(8,128)} %bitcast.9, f32[128,384]{1,0:T(8,128)} %copy-done.7, f32[128,384]{1,0:T(8,128)} %copy-done.8, f32[4,8,128]{2,1,0:T(8,128)} %refs_2_.1, f32[4,8,128]{2,1,0:T(8,128)} %refs_3_.1, ...), custom_call_target="tpu_custom_call" | custom-call | tf_op jit(solution)/shard_map/pallas_call | solution.py:199
  44.7 1.3 %collective-permute-start.4 = (f32[12,16,128]{2,1,0:T(8,128)}, f32[12,16,128]{2,1,0:T(8,128)S(1)}, u32[]{:S(2)}, u32[]{:S(2)}) collective-permute-start(f32[12,16,128]{2,1,0:T(8,128)} %get-tuple-element.14), channel_id=1, source_target_pairs={{1,0},{2,1},{3,2},{4,3},{5,4},{6,5},{7,6},{8,7},{9,8},{10,9},{11,1... | collective-permute-start | bytes 294920 | tf_op jit(solution)/shard_map/ppermute | solution.py:469
  46.0 4.0 %collective-permute-start.5 = (f32[12,16,128]{2,1,0:T(8,128)}, f32[12,16,128]{2,1,0:T(8,128)S(1)}, u32[]{:S(2)}, u32[]{:S(2)}) collective-permute-start(f32[12,16,128]{2,1,0:T(8,128)} %get-tuple-element.15), channel_id=1, source_target_pairs={{0,1},{1,2},{2,3},{3,4},{4,5},{5,6},{6,7},{7,8},{8,9},{9,10},{10,1... | collective-permute-start | bytes 294920 | tf_op jit(solution)/shard_map/ppermute | solution.py:470
  50.0 0.3 collective-permute-done.4.refs_0_
  50.3 1.7 %collective-permute-done.5.refs_1_ = f32[12,16,128]{2,1,0:T(8,128)S(1)} collective-permute-done((f32[12,16,128]{2,1,0:T(8,128)}, f32[12,16,128]{2,1,0:T(8,128)S(1)}, u32[]{:S(2)}, u32[]{:S(2)}) %collective-permute-start.5) | collective-permute-done | bytes 98336 | tf_op jit(solution)/shard_map/ppermute | solution.py:470
  51.9 0.0 copy-done.1
  51.9 0.0 copy-start
  51.9 1.7 %copy-done = f32[4,80,16,128]{3,2,1,0:T(8,128)S(1)} copy-done((f32[4,80,16,128]{3,2,1,0:T(8,128)S(1)}, f32[4,80,16,128]{3,2,1,0:T(8,128)}, u32[]{:S(2)}) %copy-start) | copy-done | bytes 2621464
  53.7 0.0 copy-start.2
  53.7 0.9 %copy-done.2 = f32[64,8,128]{2,1,0:T(8,128)S(1)} copy-done((f32[64,8,128]{2,1,0:T(8,128)S(1)}, f32[64,8,128]{2,1,0:T(8,128)}, u32[]{:S(2)}) %copy-start.2) | copy-done | bytes 262168
  54.6 0.0 copy-start.3
  54.6 0.7 copy-done.3
  55.4 0.0 copy-start.4
  55.4 0.7 copy-done.4
  56.1 0.0 copy-start.5
  56.1 0.7 copy-done.5
  56.8 11.2 %shard_map.106 = (f32[2,40,8,128]{3,2,1,0:T(8,128)}, f32[2,8,128]{2,1,0:T(8,128)S(1)}) custom-call(f32[12,16,128]{2,1,0:T(8,128)S(1)} %collective-permute-done.4.refs_0_, f32[12,16,128]{2,1,0:T(8,128)S(1)} %collective-permute-done.5.refs_1_, f32[4,8,128]{2,1,0:T(8,128)S(1)} %copy-done.3, f32[4,8,128]{2,1,0:T(8,128)S(1)} %copy-done.4, ...), custom_call_target="tpu_custom_call" | custom-call | tf_op jit(solution)/shard_map/pallas_call | solution.py:409
  68.0 0.0 copy-done.11
  68.0 1.9 %fusion = f32[2,128,8]{1,0,2:T(2,128)S(1)} fusion(f32[2,1024,1]{1,0,2:T(2,128)S(1)} %reshape.82, s32[128,8]{0,1:T(8,128)S(1)} %multiply_add_fusion, s32[1024]{0:T(1024)S(1)} %bitcast.12), kind=kOutput, calls=%fused_computation | convolution fusion | flops 26214400 | bytes 24576 | tf_op jit(solution)/shard_map/dot_general | solution.py:488
  69.8 0.2 copy.16
  70.0 20.3 %all_to_all.16 = f32[2,128,8]{2,0,1:T(2,128)S(1)} all-to-all(f32[2,128,8]{2,0,1:T(2,128)S(1)} %copy.16), channel_id=1, replica_groups=mesh['gx'=8,'gy'=16] {'gx','gy'}, dimensions={1} | all-to-all | bytes 16384 | tf_op jit(solution)/shard_map/all_to_all | solution.py:489
  90.3 0.7 reduce_sum.9
  (6 shorter events, 0.1 us)
Async XLA Ops:
  0.6 51.3 %copy-start.1 = (f32[39,8,128]{2,1,0:T(8,128)S(1)}, f32[39,8,128]{2,1,0:T(8,128)}, u32[]{:S(2)}) copy-start(f32[39,8,128]{2,1,0:T(8,128)} %refs_4_.1) | copy-start | bytes 479236
  5.0 62.9 %copy-start.11 = (s32[8,128]{1,0:T(8,128)S(1)}, s32[8,128]{1,0:T(8,128)}, u32[]{:S(2)}) copy-start(s32[8,128]{1,0:T(8,128)} %param.17) | copy-start | bytes 12292
  5.0 22.1 %all-to-all-start = ((f32[128,1,384]{2,1,0:T(1,128)}), f32[128,1,384]{2,1,0:T(1,128)S(1)}, u32[]{:S(2)}, u32[]{:S(2)}) async-start(f32[128,1,384]{2,1,0:T(1,128)} %copy.15), calls=%async_computation | async-start | bytes 393216 | tf_op jit(solution)/shard_map/all_to_all | solution.py:463
  16.5 16.3 %collective-permute-start.2 = (f32[32,8,128]{2,1,0:T(8,128)}, f32[32,8,128]{2,1,0:T(8,128)S(1)}, u32[]{:S(2)}, u32[]{:S(2)}) collective-permute-start(f32[32,8,128]{2,1,0:T(8,128)} %get-tuple-element.12), channel_id=1, source_target_pairs={{16,0},{32,16},{48,32},{64,48},{80,64},{96,80},{112,96},{17,1},{33... | collective-permute-start | bytes 393224 | tf_op jit(solution)/shard_map/ppermute | solution.py:461
  19.5 13.3 %collective-permute-start.3 = (f32[32,8,128]{2,1,0:T(8,128)}, f32[32,8,128]{2,1,0:T(8,128)S(1)}, u32[]{:S(2)}, u32[]{:S(2)}) collective-permute-start(f32[32,8,128]{2,1,0:T(8,128)} %get-tuple-element.13), channel_id=1, source_target_pairs={{0,16},{16,32},{32,48},{48,64},{64,80},{80,96},{96,112},{1,17},{17... | collective-permute-start | bytes 393224 | tf_op jit(solution)/shard_map/ppermute | solution.py:462
  27.1 8.2 %copy-start.6 = (f32[128,1,384]{2,0,1:T(8,128)}, f32[128,1,384]{2,0,1:T(8,128)S(1)}, u32[]{:S(2)}) copy-start(f32[128,1,384]{2,0,1:T(8,128)S(1)} %copy.22) | copy-start | bytes 589828
  27.1 7.0 %collective-permute-start = (f32[128,384]{1,0:T(8,128)S(1)}, f32[128,384]{1,0:T(8,128)S(1)}, u32[]{:S(2)}, u32[]{:S(2)}) collective-permute-start(f32[128,384]{1,0:T(8,128)S(1)} %bitcast.7), channel_id=1, source_target_pairs={{16,0},{32,16},{48,32},{64,48},{80,64},{96,80},{112,96},{17,1},{33... | collective-permute-start | bytes 589832 | tf_op jit(solution)/shard_map/ppermute | solution.py:465
  29.8 5.6 %collective-permute-start.1 = (f32[128,384]{1,0:T(8,128)S(1)}, f32[128,384]{1,0:T(8,128)S(1)}, u32[]{:S(2)}, u32[]{:S(2)}) collective-permute-start(f32[128,384]{1,0:T(8,128)S(1)} %bitcast.8), channel_id=1, source_target_pairs={{0,16},{16,32},{32,48},{48,64},{64,80},{80,96},{96,112},{1,17},{17... | collective-permute-start | bytes 589832 | tf_op jit(solution)/shard_map/ppermute | solution.py:466
  32.8 2.5 %copy-start.9 = (f32[32,8,128]{2,1,0:T(8,128)}, f32[32,8,128]{2,1,0:T(8,128)S(1)}, u32[]{:S(2)}) copy-start(f32[32,8,128]{2,1,0:T(8,128)S(1)} %collective-permute-done.2.sb_ref) | copy-start | bytes 393220
  32.8 2.5 %copy-start.10 = (f32[32,8,128]{2,1,0:T(8,128)}, f32[32,8,128]{2,1,0:T(8,128)S(1)}, u32[]{:S(2)}) copy-start(f32[32,8,128]{2,1,0:T(8,128)S(1)} %collective-permute-done.3.sa_ref) | copy-start | bytes 393220
  34.1 1.2 %copy-start.7 = (f32[128,384]{1,0:T(8,128)}, f32[128,384]{1,0:T(8,128)S(1)}, u32[]{:S(2)}) copy-start(f32[128,384]{1,0:T(8,128)S(1)} %collective-permute-done.below_ref) | copy-start | bytes 589828
  35.3 0.7 copy-start.8
  44.7 5.6 %collective-permute-start.4 = (f32[12,16,128]{2,1,0:T(8,128)}, f32[12,16,128]{2,1,0:T(8,128)S(1)}, u32[]{:S(2)}, u32[]{:S(2)}) collective-permute-start(f32[12,16,128]{2,1,0:T(8,128)} %get-tuple-element.14), channel_id=1, source_target_pairs={{1,0},{2,1},{3,2},{4,3},{5,4},{6,5},{7,6},{8,7},{9,8},{10,9},{11,1... | collective-permute-start | bytes 294920 | tf_op jit(solution)/shard_map/ppermute | solution.py:469
  46.0 5.9 %collective-permute-start.5 = (f32[12,16,128]{2,1,0:T(8,128)}, f32[12,16,128]{2,1,0:T(8,128)S(1)}, u32[]{:S(2)}, u32[]{:S(2)}) collective-permute-start(f32[12,16,128]{2,1,0:T(8,128)} %get-tuple-element.15), channel_id=1, source_target_pairs={{0,1},{1,2},{2,3},{3,4},{4,5},{5,6},{6,7},{7,8},{8,9},{9,10},{10,1... | collective-permute-start | bytes 294920 | tf_op jit(solution)/shard_map/ppermute | solution.py:470
  51.9 1.7 %copy-start = (f32[4,80,16,128]{3,2,1,0:T(8,128)S(1)}, f32[4,80,16,128]{3,2,1,0:T(8,128)}, u32[]{:S(2)}) copy-start(f32[4,80,16,128]{3,2,1,0:T(8,128)} %get-tuple-element.17.refs_8_) | copy-start | bytes 7864324
  53.7 0.9 %copy-start.2 = (f32[64,8,128]{2,1,0:T(8,128)S(1)}, f32[64,8,128]{2,1,0:T(8,128)}, u32[]{:S(2)}) copy-start(f32[64,8,128]{2,1,0:T(8,128)} %get-tuple-element.16.refs_5_) | copy-start | bytes 786436
  54.6 0.7 copy-start.3
  55.4 0.7 copy-start.4
  56.1 0.7 copy-start.5

commit v13 on v12

--- a/solution.py
+++ b/solution.py
@@ -99,8 +99,9 @@
 
 
 def _forcing_kernel(species, kernel, levels, n_statics, own_ref, below_ref, above_ref, wx_ref,
-                    wy_ref, diff_ref, sb_ref, sa_ref,
-                    tall_ref, right_ref, left_ref, st_xh_ref, lown_ref, lnb_ref, *trans):
+                    wy_ref, diff_ref, sb_ref, sa_ref, prior_ref,
+                    tall_hbm, right_ref, left_ref, comb_hbm, lown_ref, lnb_ref, tall_ref, comb_ref,
+                    sems, *trans):
     steps = tall_ref.shape[0]
     devices, width = own_ref.shape
     capacity = 2
@@ -117,6 +118,7 @@
     lane16 = lax.broadcasted_iota(jnp.int32, (tr2, tc), 1)
     right_ref[...] = jnp.zeros(right_ref.shape, jnp.float32)
     left_ref[...] = jnp.zeros(left_ref.shape, jnp.float32)
+    out_copies = []
     for tref, ref in zip(trans, (own_ref, below_ref, above_ref)):
         tref[...] = jnp.transpose(ref[...])
     for k in range(steps):
@@ -151,6 +153,9 @@
         planes = own.shape[0] // tr
         tall_ref[k, :, :tr, :] = own.reshape(planes, tr, tc)
         tall_ref[k, :, tr:, :] = xh.reshape(planes, tr, tc)
+        out_copy = pltpu.make_async_copy(tall_ref.at[k], tall_hbm.at[k], sems.at[k])
+        out_copy.start()
+        out_copies.append(out_copy)
         for c in range(planes):
             g, q = divmod(k * planes + c, group)
             plane = tall_ref[k, c]
@@ -169,9 +174,10 @@
                jnp.where(trow < half, pltpu.roll(b, half, 0), a))
         for off in range(2):
             c = 2 * i + off
-            st_xh_ref[c] = xhs[off]
             if c >= n_statics:
                 continue
+            comb_ref[c, :tr] = _static_plane(c, statics)
+            comb_ref[c, tr:] = xhs[off]
             g, q = divmod(base + c, group)
             sel = (lane16 >= half * q) & (lane16 < half * q + half)
             rs = (half * q) % tc
@@ -183,10 +189,18 @@
                     selp, pltpu.roll(plane, rs, 1) if rs else plane, right_ref[g, part])
                 left_ref[g, part] = jnp.where(
                     selp, pltpu.roll(plane, ls, 1) if ls else plane, left_ref[g, part])
+    for s in range(prior_ref.shape[0]):
+        comb_ref[n_statics + s, :tr] = prior_ref[s]
+        comb_ref[n_statics + s, tr:] = jnp.zeros((tr, tc), jnp.float32)
+    comb_copy = pltpu.make_async_copy(comb_ref, comb_hbm, sems.at[steps])
+    comb_copy.start()
+    comb_copy.wait()
+    for out_copy in out_copies:
+        out_copy.wait()
 
 
 def forcing_call(species, kernel, levels, n_statics, own, below, above, wind_x, wind_y,
-                 diffusivity, st_below, st_above):
+                 diffusivity, st_below, st_above, prior):
     steps = wind_x.shape[0]
     devices, width = own.shape
     slots = 2 * devices
@@ -195,21 +209,26 @@
     group = cols // (tr // 2)
     n_groups = -(-(steps * planes + n_statics) // group)
     packed = jax.ShapeDtypeStruct((n_groups, 2 * tr, cols), jnp.float32)
+    tall = jax.ShapeDtypeStruct((steps, planes, 2 * tr, cols), jnp.float32)
+    comb = jax.ShapeDtypeStruct((n_statics + prior.shape[0], 2 * tr, cols), jnp.float32)
     vmem = pl.BlockSpec(memory_space=pltpu.VMEM)
+    anyspace = pl.BlockSpec(memory_space=pl.ANY)
     return pl.pallas_call(
         functools.partial(_forcing_kernel, species, kernel, levels, n_statics),
-        in_specs=[vmem] * 8,
-        out_specs=[vmem] * 4,
-        out_shape=[jax.ShapeDtypeStruct((steps, planes, 2 * tr, cols), jnp.float32), packed,
-                   packed, jax.ShapeDtypeStruct((2 * st_below.shape[0], tr, cols), jnp.float32)],
+        in_specs=[vmem] * 9,
+        out_specs=[anyspace, vmem, vmem, anyspace],
+        out_shape=[tall, packed, packed, comb],
         scratch_shapes=[pltpu.VMEM((planes * tr, slots), jnp.float32),
-                        pltpu.VMEM((planes * tr, 2 * slots), jnp.float32)]
+                        pltpu.VMEM((planes * tr, 2 * slots), jnp.float32),
+                        pltpu.VMEM(tall.shape, jnp.float32),
+                        pltpu.VMEM(comb.shape, jnp.float32),
+                        pltpu.SemaphoreType.DMA((steps + 1,))]
         + [pltpu.VMEM((width, devices), jnp.float32)] * 3,
-    )(own, below, above, wind_x, wind_y, diffusivity, st_below, st_above)
-
-
-def _steps_kernel(steps, species, levels, n_statics, *refs):
-    n_in = 8
+    )(own, below, above, wind_x, wind_y, diffusivity, st_below, st_above, prior)
+
+
+def _steps_kernel(steps, species, levels, n_statics, grid_rows, grid_cols, *refs):
+    n_in = 3
     hbm = refs[:n_in]
     tall_hbm, adj_ref, ss_ref = refs[n_in:n_in + 3]
     (tall_buf, yh_buf, se_ref, state_ref, red_ref, ratio_ref, inv_ref,
@@ -221,10 +240,10 @@
         copy = pltpu.make_async_copy(hbm[i], vbufs[i], in_sems.at[i])
         copy.start()
         fetch.append(copy)
-    right_ref, left_ref, wx_ref, wy_ref, diff_ref, st_xh, mask_ref, prior_ref = vbufs
+    right_ref, left_ref, comb_ref = vbufs
     planes = species * levels
-    rows, lanes = mask_ref.shape
     tr, tc = adj_ref.shape[2:]
+    rows, lanes = 2 * tr, 2 * tc
     half = tr // 2
     group = tc // half
     d0 = 2 * steps
@@ -251,16 +270,23 @@
         g, q = divmod(n_fgroups * group + c, group)
         se_ref[c, :, tc:] = _unpack(right_ref[g], left_ref[g], q, tc, half)
 
-    for i in range(2, 6):
-        fetch[i].wait()
-    for c in range(n_statics):
-        se_ref[c, :tr, :tc] = _static_plane(c, (wx_ref, wy_ref, diff_ref))
-        se_ref[c, tr:, :tc] = st_xh[c]
-
-    fetch[6].wait()
-    fetch[7].wait()
+    fetch[2].wait()
+
+    def assemble_static(c, carry):
+        se_ref[c, :, :tc] = comb_ref[c]
+        return carry
+
+    lax.fori_loop(0, n_statics, assemble_static, 0)
+    prior_ref = comb_ref.at[pl.ds(n_statics, species), pl.ds(0, tr)]
+
     zero = jnp.zeros((rows, lanes), jnp.float32)
-    inside = mask_ref[...] > 0.5
+    half_rows = tr // 2
+    r = lax.broadcasted_iota(jnp.int32, (rows, lanes), 0)
+    c = lax.broadcasted_iota(jnp.int32, (rows, lanes), 1)
+    grow = lax.axis_index("gx") * tr + jnp.where(r < tr + half_rows, r, r - rows)
+    gcol = lax.axis_index("gy") * tc + jnp.where(c < tc + half_rows, c, c - lanes)
+    inside = ((grow >= 0) & (grow < grid_rows) & (gcol >= 0) & (gcol < grid_cols)
+              & ((c < tc + half_rows) | (c >= lanes - half_rows)))
     carried = zero
     for l in range(levels):
         below = se_ref[d0 + l - 1] if l > 0 else zero
@@ -398,20 +424,20 @@
         ss_ref[s] = ss_ref[s] + prior_ref[s] * surface[s]
 
 
-def steps_call(steps, species, levels, n_statics, right, left, wind_x, wind_y, diffusivity,
-               st_xh, mask, prior, tall):
+def steps_call(steps, species, levels, n_statics, grid_rows, grid_cols, right, left, comb,
+               tall):
     _, planes, rows, tc = tall.shape
     tr = rows // 2
-    lanes = mask.shape[1]
+    lanes = 2 * tc
     vmem = pl.BlockSpec(memory_space=pltpu.VMEM)
     anyspace = pl.BlockSpec(memory_space=pl.ANY)
-    ins = (right, left, wind_x, wind_y, diffusivity, st_xh, mask, prior)
+    ins = (right, left, comb)
     return pl.pallas_call(
-        functools.partial(_steps_kernel, steps, species, levels, n_statics),
+        functools.partial(_steps_kernel, steps, species, levels, n_statics, grid_rows, grid_cols),
         in_specs=[anyspace] * (len(ins) + 1),
         out_specs=[vmem, vmem],
         out_shape=[jax.ShapeDtypeStruct((species, levels, tr, tc), jnp.float32),
-                   jax.ShapeDtypeStruct(prior.shape, jnp.float32)],
+                   jax.ShapeDtypeStruct((species, tr, tc), jnp.float32)],
         scratch_shapes=[
             pltpu.VMEM((steps, planes, rows, tc), jnp.float32),
             pltpu.VMEM((steps * planes, rows, tc), jnp.float32),
@@ -464,24 +490,14 @@
 
     below = lax.ppermute(received, "gx", down_x)
     above = lax.ppermute(received, "gx", up_x)
-    tall, right, left, st_xh = forcing_call(species, kernel, levels, n_s, received, below, above,
-                                            wind_x, wind_y, diffusivity, st_below, st_above)
+    tall, right, left, comb = forcing_call(species, kernel, levels, n_s, received, below, above,
+                                           wind_x, wind_y, diffusivity, st_below, st_above,
+                                           prior_emission)
     right = lax.ppermute(right, "gy", down_y)
     left = lax.ppermute(left, "gy", up_y)
 
-    gxi = lax.axis_index("gx")
-    gyi = lax.axis_index("gy")
-    r = jnp.arange(ext_rows, dtype=jnp.int32)[:, None]
-    c = jnp.arange(lanes, dtype=jnp.int32)[None, :]
-    grow = gxi * rows + jnp.where(r < rows + halo, r, r - ext_rows)
-    ccol = jnp.where(c < cols + halo, c, c - lanes)
-    gcol = gyi * cols + ccol
-    inside = ((grow >= 0) & (grow < gx_n * rows) & (gcol >= 0) & (gcol < gy_n * cols)
-              & ((c < cols + halo) | (c >= lanes - halo)))
-    mask = inside.astype(jnp.float32)
-
-    adjoint, surface_sum = steps_call(steps, species, levels, n_s, right, left, wind_x, wind_y,
-                                      diffusivity, st_xh, mask, prior_emission, tall)
+    adjoint, surface_sum = steps_call(steps, species, levels, n_s, gx_n * rows, gy_n * cols,
+                                      right, left, comb, tall)
 
     nreg = REG_DEV * devices
     member = (region_map.reshape(-1)[:, None] == jnp.arange(nreg, dtype=jnp.int32)).astype(jnp.float32)

time: 91.6 us -> 94.5 us (1.032)
  blocking collectives: 20.3 us -> 42 us
  starting transfers between devices: 27.9 us -> 16.4 us
  waiting for transfers between devices: 9.33 us -> 4.16 us
  local copies, waits for them, and re-layouts: 7.5 us -> 5.43 us
    all_to_all x0 -> x1, blocking collectives: none -> 21.9 us  [local(): received = lax.all_to_all(placed, ('gx', 'gy'), 0, 0, tiled=True)]
    all_to_all x1 -> x0, starting transfers between devices: 11.5 us -> none  [local(): received = lax.all_to_all(placed, ('gx', 'gy'), 0, 0, tiled=True)]
    all_to_all x1 -> x0, waiting for transfers between devices: 4.92 us -> none  [local(): received = lax.all_to_all(placed, ('gx', 'gy'), 0, 0, tiled=True)]
    unnamed x25 -> x17, local copies, waits for them, and re-layouts: 5.54 us -> 4.13 us
    ppermute x1, waiting for transfers between devices: 0.01 us -> 1.32 us  [local(): st_above = lax.ppermute(st_hi, 'gx', up_x)]
    ppermute x1, waiting for transfers between devices: 1.31 us -> 0.01 us  [local(): below = lax.ppermute(received, 'gx', down_x)]
    ppermute x1, waiting for transfers between devices: 1.18 us -> 0.01 us  [local(): above = lax.ppermute(received, 'gx', up_x)]
    ppermute x1, starting transfers between devices: 2.98 us -> 1.92 us  [local(): st_below = lax.ppermute(st_lo, 'gx', down_x)]
  transfers between devices with their start and end apart: 7 -> 6, of which waited for: 5 -> 4; matrix products, arithmetic and copies ran while one was open for 0% -> 0% of each run, Pallas kernels for 0% -> 0%
where the time goes in v13:
time: 94.5 us; the launch traced here: 94.1 us
  blocking collectives  42 us (44%)
  Pallas kernels  22.7 us (24%)
  starting transfers between devices  16.4 us (17%)
  local copies, waits for them, and re-layouts  5.43 us (6%)
  waiting for transfers between devices  4.16 us (4%)
  matrix products  1.87 us (2%)
    all_to_all x1, blocking collectives, local(): received = lax.all_to_all(placed, ('gx', 'gy'), 0, 0, tiled=True)  21.9 us
    all_to_all x1, blocking collectives, local(): lax.all_to_all(partial.reshape(species, devices, nreg // devices), ('gx',...  20.1 us
    pallas_call x1, Pallas kernels, steps_call(): pl.pallas_call(functools.partial(_steps_kernel, steps, species, levels, n...  11.3 us
    pallas_call x1, Pallas kernels, forcing_call(): pl.pallas_call(functools.partial(_forcing_kernel, species, kernel, levels...  8.87 us
    unnamed x17, local copies, waits for them, and re-layouts  4.13 us
    ppermute x1, starting transfers between devices, local(): left = lax.ppermute(left, 'gy', up_y)  3.99 us
    ppermute x1, starting transfers between devices, local(): st_above = lax.ppermute(st_hi, 'gx', up_x)  3.64 us
    ppermute x1, starting transfers between devices, local(): above = lax.ppermute(received, 'gx', up_x)  2.96 us
  transfers between devices with their start and end apart: 6, of which 4 were waited for; matrix products, arithmetic and copies ran while one was open for 0% of the time, Pallas kernels for 0%

profile of v13, /device:TPU:1, one launch (start us, length us, event | category | flops | bytes accessed | tf_op | source)
XLA Modules:
  0.0 94.1 jit_solution(18076698018566670203)
XLA Ops:
  0.6 2.6 %shard_map.104 = (f32[128,384]{1,0:T(8,128)}, f32[32,8,128]{2,1,0:T(8,128)}, f32[32,8,128]{2,1,0:T(8,128)}) custom-call(f32[4,32,128]{2,1,0:T(8,128)} %adj_ref.1, s32[4,128]{1,0:T(4,128)} %bitcast.11, s32[4,128]{1,0:T(4,128)} %col_ref.1, s32[4,128]{1,0:T(4,128)} %lev_ref.1, f32[4,8,128]{2,1,0:T(8,128)} %wx_ref.3, f32[4,8,128]{2,1,0:T(8,128)} %wy_ref.3, ...), custom_call_target="tpu_custom_call" | custom-call | tf_op jit(solution)/shard_map/pallas_call | solution.py:79
  3.2 1.1 %copy.15 = f32[128,1,384]{2,1,0:T(1,128)S(1)} copy(f32[128,1,384]{2,0,1:T(8,128)} %bitcast.10) | data formatting | bytes 393216 | tf_op jit(solution)/shard_map/all_to_all | solution.py:489
  4.3 0.0 copy-start.7
  4.3 21.9 %all_to_all.16 = f32[128,1,384]{2,1,0:T(1,128)S(1)} all-to-all(f32[128,1,384]{2,1,0:T(1,128)S(1)} %copy.15), channel_id=1, replica_groups=mesh['gx'=8,'gy'=16] {'gx','gy'}, dimensions={0} | all-to-all | bytes 393216 | tf_op jit(solution)/shard_map/all_to_all | solution.py:489
  26.2 0.0 copy-start.2
  26.3 2.6 %collective-permute-start = (f32[128,384]{1,0:T(8,128)S(1)}, f32[128,384]{1,0:T(8,128)S(1)}, u32[]{:S(2)}, u32[]{:S(2)}) collective-permute-start(f32[128,384]{1,0:T(8,128)S(1)} %bitcast.7), channel_id=1, source_target_pairs={{16,0},{32,16},{48,32},{64,48},{80,64},{96,80},{112,96},{17,1},{33... | collective-permute-start | bytes 589832 | tf_op jit(solution)/shard_map/ppermute | solution.py:491
  28.9 3.0 %collective-permute-start.1 = (f32[128,384]{1,0:T(8,128)S(1)}, f32[128,384]{1,0:T(8,128)S(1)}, u32[]{:S(2)}, u32[]{:S(2)}) collective-permute-start(f32[128,384]{1,0:T(8,128)S(1)} %bitcast.8), channel_id=1, source_target_pairs={{0,16},{16,32},{32,48},{48,64},{64,80},{80,96},{96,112},{1,17},{17... | collective-permute-start | bytes 589832 | tf_op jit(solution)/shard_map/ppermute | solution.py:492
  31.8 1.9 %collective-permute-start.2 = (f32[32,8,128]{2,1,0:T(8,128)}, f32[32,8,128]{2,1,0:T(8,128)S(1)}, u32[]{:S(2)}, u32[]{:S(2)}) collective-permute-start(f32[32,8,128]{2,1,0:T(8,128)} %get-tuple-element.12), channel_id=1, source_target_pairs={{16,0},{32,16},{48,32},{64,48},{80,64},{96,80},{112,96},{17,1},{33... | collective-permute-start | bytes 393224 | tf_op jit(solution)/shard_map/ppermute | solution.py:487
  33.8 3.6 %collective-permute-start.3 = (f32[32,8,128]{2,1,0:T(8,128)}, f32[32,8,128]{2,1,0:T(8,128)S(1)}, u32[]{:S(2)}, u32[]{:S(2)}) collective-permute-start(f32[32,8,128]{2,1,0:T(8,128)} %get-tuple-element.13), channel_id=1, source_target_pairs={{0,16},{16,32},{32,48},{48,64},{64,80},{80,96},{96,112},{1,17},{17... | collective-permute-start | bytes 393224 | tf_op jit(solution)/shard_map/ppermute | solution.py:488
  37.4 0.9 collective-permute-done.2.sb_ref
  38.3 0.0 copy-start.5
  38.3 1.3 %collective-permute-done.3.sa_ref = f32[32,8,128]{2,1,0:T(8,128)S(1)} collective-permute-done((f32[32,8,128]{2,1,0:T(8,128)}, f32[32,8,128]{2,1,0:T(8,128)S(1)}, u32[]{:S(2)}, u32[]{:S(2)}) %collective-permute-start.3) | collective-permute-done | bytes 131104 | tf_op jit(solution)/shard_map/ppermute | solution.py:488
  39.6 0.0 copy-start.6
  39.7 0.0 collective-permute-done.below_ref
  39.7 0.0 copy-start.3
  39.7 0.0 collective-permute-done.1.above_ref
  39.7 0.0 copy-done.2
  39.7 0.0 copy-done.5
  39.7 0.6 copy-done.6
  40.3 0.1 copy-done.3
  40.4 0.0 copy-start.4
  40.4 0.7 copy-done.4
  41.0 8.9 %shard_map.105 = (f32[4,80,16,128]{3,2,1,0:T(8,128)}, f32[12,16,128]{2,1,0:T(8,128)}, f32[12,16,128]{2,1,0:T(8,128)}, f32[49,16,128]{2,1,0:T(8,128)}) custom-call(f32[128,384]{1,0:T(8,128)} %bitcast.9, f32[128,384]{1,0:T(8,128)} %copy-done.3, f32[128,384]{1,0:T(8,128)} %copy-done.4, f32[4,8,128]{2,1,0:T(8,128)} %wx_ref.3, f32[4,8,128]{2,1,0:T(8,128)} %wy_ref.3, ...), custom_call_target="tpu_custom_call" | custom-call | tf_op jit(solution)/shard_map/pallas_call | solution.py:216
  49.9 1.3 %collective-permute-start.4 = (f32[12,16,128]{2,1,0:T(8,128)}, f32[12,16,128]{2,1,0:T(8,128)S(1)}, u32[]{:S(2)}, u32[]{:S(2)}) collective-permute-start(f32[12,16,128]{2,1,0:T(8,128)} %get-tuple-element.14), channel_id=1, source_target_pairs={{1,0},{2,1},{3,2},{4,3},{5,4},{6,5},{7,6},{8,7},{9,8},{10,9},{11,1... | collective-permute-start | bytes 294920 | tf_op jit(solution)/shard_map/ppermute | solution.py:496
  51.2 4.0 %collective-permute-start.5 = (f32[12,16,128]{2,1,0:T(8,128)}, f32[12,16,128]{2,1,0:T(8,128)S(1)}, u32[]{:S(2)}, u32[]{:S(2)}) collective-permute-start(f32[12,16,128]{2,1,0:T(8,128)} %get-tuple-element.15), channel_id=1, source_target_pairs={{0,1},{1,2},{2,3},{3,4},{4,5},{5,6},{6,7},{7,8},{8,9},{9,10},{10,1... | collective-permute-start | bytes 294920 | tf_op jit(solution)/shard_map/ppermute | solution.py:497
  55.2 0.3 collective-permute-done.4.refs_0_
  55.5 1.7 %collective-permute-done.5.refs_1_ = f32[12,16,128]{2,1,0:T(8,128)S(1)} collective-permute-done((f32[12,16,128]{2,1,0:T(8,128)}, f32[12,16,128]{2,1,0:T(8,128)S(1)}, u32[]{:S(2)}, u32[]{:S(2)}) %collective-permute-start.5) | collective-permute-done | bytes 98336 | tf_op jit(solution)/shard_map/ppermute | solution.py:497
  57.2 0.0 copy-start
  57.2 1.7 %copy-done = f32[4,80,16,128]{3,2,1,0:T(8,128)S(1)} copy-done((f32[4,80,16,128]{3,2,1,0:T(8,128)S(1)}, f32[4,80,16,128]{3,2,1,0:T(8,128)}, u32[]{:S(2)}) %copy-start) | copy-done | bytes 2621464
  58.9 0.0 copy-start.1
  58.9 1.0 %copy-done.1 = f32[49,16,128]{2,1,0:T(8,128)S(1)} copy-done((f32[49,16,128]{2,1,0:T(8,128)S(1)}, f32[49,16,128]{2,1,0:T(8,128)}, u32[]{:S(2)}) %copy-start.1) | copy-done | bytes 401432
  59.9 11.3 %shard_map.106 = (f32[2,40,8,128]{3,2,1,0:T(8,128)}, f32[2,8,128]{2,1,0:T(8,128)S(1)}) custom-call(f32[12,16,128]{2,1,0:T(8,128)S(1)} %collective-permute-done.4.refs_0_, f32[12,16,128]{2,1,0:T(8,128)S(1)} %collective-permute-done.5.refs_1_, f32[49,16,128]{2,1,0:T(8,128)S(1)} %copy-done.1, f32[4,80,16,128]{3,2,1,0:T(8,128)S(1)} %copy-done), custom_call_target="tpu_custom_call" | custom-call | tf_op jit(solution)/shard_map/pallas_call | solution.py:435
  71.2 0.0 copy-done.7
  71.2 1.9 %fusion = f32[2,128,8]{1,0,2:T(2,128)S(1)} fusion(f32[2,1024,1]{1,0,2:T(2,128)S(1)} %reshape.34, s32[128,8]{0,1:T(8,128)S(1)} %multiply_add_fusion, s32[1024]{0:T(1024)S(1)} %bitcast.12), kind=kOutput, calls=%fused_computation | convolution fusion | flops 26214400 | bytes 24576 | tf_op jit(solution)/shard_map/dot_general | solution.py:504
  73.1 0.2 copy.16
  73.3 20.1 %all_to_all.17 = f32[2,128,8]{2,0,1:T(2,128)S(1)} all-to-all(f32[2,128,8]{2,0,1:T(2,128)S(1)} %copy.16), channel_id=1, replica_groups=mesh['gx'=8,'gy'=16] {'gx','gy'}, dimensions={1} | all-to-all | bytes 16384 | tf_op jit(solution)/shard_map/all_to_all | solution.py:505
  93.4 0.7 reduce_sum.9
  (3 shorter events, 0.0 us)
Async XLA Ops:
  4.3 66.9 %copy-start.7 = (s32[8,128]{1,0:T(8,128)S(1)}, s32[8,128]{1,0:T(8,128)}, u32[]{:S(2)}) copy-start(s32[8,128]{1,0:T(8,128)} %param.17) | copy-start | bytes 12292
  26.2 13.4 %copy-start.2 = (f32[128,1,384]{2,0,1:T(8,128)}, f32[128,1,384]{2,0,1:T(8,128)S(1)}, u32[]{:S(2)}) copy-start(f32[128,1,384]{2,0,1:T(8,128)S(1)} %copy.22) | copy-start | bytes 589828
  26.3 13.4 %collective-permute-start = (f32[128,384]{1,0:T(8,128)S(1)}, f32[128,384]{1,0:T(8,128)S(1)}, u32[]{:S(2)}, u32[]{:S(2)}) collective-permute-start(f32[128,384]{1,0:T(8,128)S(1)} %bitcast.7), channel_id=1, source_target_pairs={{16,0},{32,16},{48,32},{64,48},{80,64},{96,80},{112,96},{17,1},{33... | collective-permute-start | bytes 589832 | tf_op jit(solution)/shard_map/ppermute | solution.py:491
  28.9 10.8 %collective-permute-start.1 = (f32[128,384]{1,0:T(8,128)S(1)}, f32[128,384]{1,0:T(8,128)S(1)}, u32[]{:S(2)}, u32[]{:S(2)}) collective-permute-start(f32[128,384]{1,0:T(8,128)S(1)} %bitcast.8), channel_id=1, source_target_pairs={{0,16},{16,32},{32,48},{48,64},{64,80},{80,96},{96,112},{1,17},{17... | collective-permute-start | bytes 589832 | tf_op jit(solution)/shard_map/ppermute | solution.py:492
  31.8 6.5 %collective-permute-start.2 = (f32[32,8,128]{2,1,0:T(8,128)}, f32[32,8,128]{2,1,0:T(8,128)S(1)}, u32[]{:S(2)}, u32[]{:S(2)}) collective-permute-start(f32[32,8,128]{2,1,0:T(8,128)} %get-tuple-element.12), channel_id=1, source_target_pairs={{16,0},{32,16},{48,32},{64,48},{80,64},{96,80},{112,96},{17,1},{33... | collective-permute-start | bytes 393224 | tf_op jit(solution)/shard_map/ppermute | solution.py:487
  33.8 5.9 %collective-permute-start.3 = (f32[32,8,128]{2,1,0:T(8,128)}, f32[32,8,128]{2,1,0:T(8,128)S(1)}, u32[]{:S(2)}, u32[]{:S(2)}) collective-permute-start(f32[32,8,128]{2,1,0:T(8,128)} %get-tuple-element.13), channel_id=1, source_target_pairs={{0,16},{16,32},{32,48},{48,64},{64,80},{80,96},{96,112},{1,17},{17... | collective-permute-start | bytes 393224 | tf_op jit(solution)/shard_map/ppermute | solution.py:488
  38.3 1.3 %copy-start.5 = (f32[32,8,128]{2,1,0:T(8,128)}, f32[32,8,128]{2,1,0:T(8,128)S(1)}, u32[]{:S(2)}) copy-start(f32[32,8,128]{2,1,0:T(8,128)S(1)} %collective-permute-done.2.sb_ref) | copy-start | bytes 393220
  39.6 0.6 copy-start.6
  39.7 0.7 copy-start.3
  40.4 0.7 copy-start.4
  49.9 5.6 %collective-permute-start.4 = (f32[12,16,128]{2,1,0:T(8,128)}, f32[12,16,128]{2,1,0:T(8,128)S(1)}, u32[]{:S(2)}, u32[]{:S(2)}) collective-permute-start(f32[12,16,128]{2,1,0:T(8,128)} %get-tuple-element.14), channel_id=1, source_target_pairs={{1,0},{2,1},{3,2},{4,3},{5,4},{6,5},{7,6},{8,7},{9,8},{10,9},{11,1... | collective-permute-start | bytes 294920 | tf_op jit(solution)/shard_map/ppermute | solution.py:496
  51.2 5.9 %collective-permute-start.5 = (f32[12,16,128]{2,1,0:T(8,128)}, f32[12,16,128]{2,1,0:T(8,128)S(1)}, u32[]{:S(2)}, u32[]{:S(2)}) collective-permute-start(f32[12,16,128]{2,1,0:T(8,128)} %get-tuple-element.15), channel_id=1, source_target_pairs={{0,1},{1,2},{2,3},{3,4},{4,5},{5,6},{6,7},{7,8},{8,9},{9,10},{10,1... | collective-permute-start | bytes 294920 | tf_op jit(solution)/shard_map/ppermute | solution.py:497
  57.2 1.7 %copy-start = (f32[4,80,16,128]{3,2,1,0:T(8,128)S(1)}, f32[4,80,16,128]{3,2,1,0:T(8,128)}, u32[]{:S(2)}) copy-start(f32[4,80,16,128]{3,2,1,0:T(8,128)} %get-tuple-element.17.refs_3_) | copy-start | bytes 7864324
  58.9 1.0 %copy-start.1 = (f32[49,16,128]{2,1,0:T(8,128)S(1)}, f32[49,16,128]{2,1,0:T(8,128)}, u32[]{:S(2)}) copy-start(f32[49,16,128]{2,1,0:T(8,128)} %get-tuple-element.16.refs_2_) | copy-start | bytes 1204228

commit v14 on v11

--- a/solution.py
+++ b/solution.py
@@ -303,7 +303,7 @@
                 out.append(r)
             return tuple(out)
 
-        lax.fori_loop(0, levels, forward, (zero,) * species, unroll=4)
+        lax.fori_loop(0, levels, forward, (zero,) * species, unroll=8)
 
         def backward(i, result, k=k):
             l = levels - 1 - i
@@ -319,7 +319,7 @@
                 out.append(r)
             return tuple(out)
 
-        surface = lax.fori_loop(0, levels, backward, (zero,) * species, unroll=4)
+        surface = lax.fori_loop(0, levels, backward, (zero,) * species, unroll=8)
         for s in range(species):
             if first:
                 ss_ref[s] = prior_ref[s] * surface[s][:tr, :tc]

time: 90.8 us -> 89.9 us (0.990)
  Pallas kernels: 21.7 us -> 20.7 us
    pallas_call x1, Pallas kernels: 10.4 us -> 9.39 us  [steps_call(): pl.pallas_call(functools.partial(_steps_kernel, steps, species, levels, n...]
where the time goes in v14:
time: 89.9 us; the launch traced here: 89.2 us
  starting transfers between devices  27.9 us (31%)
  Pallas kernels  20.7 us (23%)
  blocking collectives  20.3 us (23%)
  waiting for transfers between devices  9.33 us (10%)
  local copies, waits for them, and re-layouts  7.5 us (8%)
  matrix products  1.87 us (2%)
    all_to_all x1, blocking collectives, local(): lax.all_to_all(partial.reshape(species, devices, nreg // devices), ('gx',...  20.3 us
    all_to_all x1, starting transfers between devices, local(): received = lax.all_to_all(placed, ('gx', 'gy'), 0, 0, tiled=True)  11.5 us
    pallas_call x1, Pallas kernels, steps_call(): pl.pallas_call(functools.partial(_steps_kernel, steps, species, levels, n...  9.39 us
    pallas_call x1, Pallas kernels, forcing_call(): pl.pallas_call(functools.partial(_forcing_kernel, species, kernel, levels...  8.72 us
    unnamed x25, local copies, waits for them, and re-layouts  5.54 us
    all_to_all x1, waiting for transfers between devices, local(): received = lax.all_to_all(placed, ('gx', 'gy'), 0, 0, tiled=True)  4.92 us
    ppermute x1, starting transfers between devices, local(): left = lax.ppermute(left, 'gy', up_y)  3.99 us
    ppermute x1, starting transfers between devices, local(): st_below = lax.ppermute(st_lo, 'gx', down_x)  2.98 us
  transfers between devices with their start and end apart: 7, of which 5 were waited for; matrix products, arithmetic and copies ran while one was open for 0% of the time, Pallas kernels for 0%

profile of v14, /device:TPU:1, one launch (start us, length us, event | category | flops | bytes accessed | tf_op | source)
XLA Modules:
  0.0 89.2 jit_solution(17897361392861765885)
XLA Ops:
  0.6 0.0 copy-start.1
  0.6 2.6 %shard_map.104 = (f32[128,384]{1,0:T(8,128)}, f32[32,8,128]{2,1,0:T(8,128)}, f32[32,8,128]{2,1,0:T(8,128)}) custom-call(f32[4,32,128]{2,1,0:T(8,128)} %adj_ref.1, s32[4,128]{1,0:T(4,128)} %bitcast.11, s32[4,128]{1,0:T(4,128)} %col_ref.1, s32[4,128]{1,0:T(4,128)} %lev_ref.1, f32[4,8,128]{2,1,0:T(8,128)} %wx_ref.5, f32[4,8,128]{2,1,0:T(8,128)} %wy_ref.5, ...), custom_call_target="tpu_custom_call" | custom-call | tf_op jit(solution)/shard_map/pallas_call | solution.py:79
  3.2 1.8 %copy.15 = f32[128,1,384]{2,1,0:T(1,128)} copy(f32[128,1,384]{2,0,1:T(8,128)} %bitcast.10) | data formatting | bytes 393216 | tf_op jit(solution)/shard_map/all_to_all | solution.py:444
  5.0 0.0 copy-start.11
  5.0 11.5 %all-to-all-start = ((f32[128,1,384]{2,1,0:T(1,128)}), f32[128,1,384]{2,1,0:T(1,128)S(1)}, u32[]{:S(2)}, u32[]{:S(2)}) async-start(f32[128,1,384]{2,1,0:T(1,128)} %copy.15), calls=%async_computation | async-start | bytes 393216 | tf_op jit(solution)/shard_map/all_to_all | solution.py:444
  16.5 3.0 %collective-permute-start.2 = (f32[32,8,128]{2,1,0:T(8,128)}, f32[32,8,128]{2,1,0:T(8,128)S(1)}, u32[]{:S(2)}, u32[]{:S(2)}) collective-permute-start(f32[32,8,128]{2,1,0:T(8,128)} %get-tuple-element.12), channel_id=1, source_target_pairs={{16,0},{32,16},{48,32},{64,48},{80,64},{96,80},{112,96},{17,1},{33... | collective-permute-start | bytes 393224 | tf_op jit(solution)/shard_map/ppermute | solution.py:442
  19.5 2.6 %collective-permute-start.3 = (f32[32,8,128]{2,1,0:T(8,128)}, f32[32,8,128]{2,1,0:T(8,128)S(1)}, u32[]{:S(2)}, u32[]{:S(2)}) collective-permute-start(f32[32,8,128]{2,1,0:T(8,128)} %get-tuple-element.13), channel_id=1, source_target_pairs={{0,16},{16,32},{32,48},{48,64},{64,80},{80,96},{96,112},{1,17},{17... | collective-permute-start | bytes 393224 | tf_op jit(solution)/shard_map/ppermute | solution.py:443
  22.2 4.9 %all-to-all-done = f32[128,1,384]{2,1,0:T(1,128)S(1)} async-done(((f32[128,1,384]{2,1,0:T(1,128)}), f32[128,1,384]{2,1,0:T(1,128)S(1)}, u32[]{:S(2)}, u32[]{:S(2)}) %all-to-all-start) | async-done | bytes 196640 | tf_op jit(solution)/shard_map/all_to_all | solution.py:444
  27.1 0.0 copy-start.6
  27.1 2.6 %collective-permute-start = (f32[128,384]{1,0:T(8,128)S(1)}, f32[128,384]{1,0:T(8,128)S(1)}, u32[]{:S(2)}, u32[]{:S(2)}) collective-permute-start(f32[128,384]{1,0:T(8,128)S(1)} %bitcast.7), channel_id=1, source_target_pairs={{16,0},{32,16},{48,32},{64,48},{80,64},{96,80},{112,96},{17,1},{33... | collective-permute-start | bytes 589832 | tf_op jit(solution)/shard_map/ppermute | solution.py:446
  29.8 3.0 %collective-permute-start.1 = (f32[128,384]{1,0:T(8,128)S(1)}, f32[128,384]{1,0:T(8,128)S(1)}, u32[]{:S(2)}, u32[]{:S(2)}) collective-permute-start(f32[128,384]{1,0:T(8,128)S(1)} %bitcast.8), channel_id=1, source_target_pairs={{0,16},{16,32},{32,48},{48,64},{64,80},{80,96},{96,112},{1,17},{17... | collective-permute-start | bytes 589832 | tf_op jit(solution)/shard_map/ppermute | solution.py:447
  32.7 0.1 and_convert_fusion.mask_ref
  32.8 0.0 collective-permute-done.2.sb_ref
  32.8 0.0 copy-start.9
  32.8 0.0 collective-permute-done.3.sa_ref
  32.8 0.0 copy-start.10
  32.8 1.3 %collective-permute-done.below_ref = f32[128,384]{1,0:T(8,128)S(1)} collective-permute-done((f32[128,384]{1,0:T(8,128)S(1)}, f32[128,384]{1,0:T(8,128)S(1)}, u32[]{:S(2)}, u32[]{:S(2)}) %collective-permute-start) | collective-permute-done | bytes 196640 | tf_op jit(solution)/shard_map/ppermute | solution.py:446
  34.1 0.0 copy-start.7
  34.1 1.2 %collective-permute-done.1.above_ref = f32[128,384]{1,0:T(8,128)S(1)} collective-permute-done((f32[128,384]{1,0:T(8,128)S(1)}, f32[128,384]{1,0:T(8,128)S(1)}, u32[]{:S(2)}, u32[]{:S(2)}) %collective-permute-start.1) | collective-permute-done | bytes 196640 | tf_op jit(solution)/shard_map/ppermute | solution.py:447
  35.3 0.0 copy-done.6
  35.3 0.0 copy-done.9
  35.3 0.0 copy-done.10
  35.3 0.0 copy-done.7
  35.3 0.0 copy-start.8
  35.3 0.7 copy-done.8
  36.0 8.7 %shard_map.105 = (f32[4,80,16,128]{3,2,1,0:T(8,128)}, f32[12,16,128]{2,1,0:T(8,128)}, f32[12,16,128]{2,1,0:T(8,128)}, f32[64,8,128]{2,1,0:T(8,128)}) custom-call(f32[128,384]{1,0:T(8,128)} %bitcast.9, f32[128,384]{1,0:T(8,128)} %copy-done.7, f32[128,384]{1,0:T(8,128)} %copy-done.8, f32[4,8,128]{2,1,0:T(8,128)} %wx_ref.5, f32[4,8,128]{2,1,0:T(8,128)} %wy_ref.5, ...), custom_call_target="tpu_custom_call" | custom-call | tf_op jit(solution)/shard_map/pallas_call | solution.py:199
  44.7 1.3 %collective-permute-start.4 = (f32[12,16,128]{2,1,0:T(8,128)}, f32[12,16,128]{2,1,0:T(8,128)S(1)}, u32[]{:S(2)}, u32[]{:S(2)}) collective-permute-start(f32[12,16,128]{2,1,0:T(8,128)} %get-tuple-element.14), channel_id=1, source_target_pairs={{1,0},{2,1},{3,2},{4,3},{5,4},{6,5},{7,6},{8,7},{9,8},{10,9},{11,1... | collective-permute-start | bytes 294920 | tf_op jit(solution)/shard_map/ppermute | solution.py:450
  46.0 4.0 %collective-permute-start.5 = (f32[12,16,128]{2,1,0:T(8,128)}, f32[12,16,128]{2,1,0:T(8,128)S(1)}, u32[]{:S(2)}, u32[]{:S(2)}) collective-permute-start(f32[12,16,128]{2,1,0:T(8,128)} %get-tuple-element.15), channel_id=1, source_target_pairs={{0,1},{1,2},{2,3},{3,4},{4,5},{5,6},{6,7},{7,8},{8,9},{9,10},{10,1... | collective-permute-start | bytes 294920 | tf_op jit(solution)/shard_map/ppermute | solution.py:451
  50.0 0.3 collective-permute-done.4.right_ref
  50.3 1.7 %collective-permute-done.5.left_ref = f32[12,16,128]{2,1,0:T(8,128)S(1)} collective-permute-done((f32[12,16,128]{2,1,0:T(8,128)}, f32[12,16,128]{2,1,0:T(8,128)S(1)}, u32[]{:S(2)}, u32[]{:S(2)}) %collective-permute-start.5) | collective-permute-done | bytes 98336 | tf_op jit(solution)/shard_map/ppermute | solution.py:451
  51.9 0.0 copy-done.1
  51.9 0.0 copy-start
  51.9 1.7 %copy-done = f32[4,80,16,128]{3,2,1,0:T(8,128)S(1)} copy-done((f32[4,80,16,128]{3,2,1,0:T(8,128)S(1)}, f32[4,80,16,128]{3,2,1,0:T(8,128)}, u32[]{:S(2)}) %copy-start) | copy-done | bytes 2621464
  53.7 0.0 copy-start.2
  53.7 0.9 %copy-done.2 = f32[64,8,128]{2,1,0:T(8,128)S(1)} copy-done((f32[64,8,128]{2,1,0:T(8,128)S(1)}, f32[64,8,128]{2,1,0:T(8,128)}, u32[]{:S(2)}) %copy-start.2) | copy-done | bytes 262168
  54.6 0.0 copy-start.3
  54.6 0.7 copy-done.3
  55.4 0.0 copy-start.4
  55.4 0.7 copy-done.4
  56.1 0.0 copy-start.5
  56.1 0.7 copy-done.5
  56.8 9.4 %shard_map.106 = (f32[2,40,8,128]{3,2,1,0:T(8,128)}, f32[2,8,128]{2,1,0:T(8,128)S(1)}) custom-call(f32[12,16,128]{2,1,0:T(8,128)S(1)} %collective-permute-done.4.right_ref, f32[12,16,128]{2,1,0:T(8,128)S(1)} %collective-permute-done.5.left_ref, f32[4,8,128]{2,1,0:T(8,128)S(1)} %copy-done.3, f32[4,8,128]{2,1,0:T(8,128)S(1)} %copy-done.4, ...), custom_call_target="tpu_custom_call" | custom-call | tf_op jit(solution)/shard_map/pallas_call | solution.py:392
  66.2 0.0 copy-done.11
  66.2 1.9 %fusion = f32[2,128,8]{1,0,2:T(2,128)S(1)} fusion(f32[2,1024,1]{1,0,2:T(2,128)S(1)} %reshape.82, s32[128,8]{0,1:T(8,128)S(1)} %multiply_add_fusion, s32[1024]{0:T(1024)S(1)} %bitcast.12), kind=kOutput, calls=%fused_computation | convolution fusion | flops 26214400 | bytes 24576 | tf_op jit(solution)/shard_map/dot_general | solution.py:469
  68.1 0.2 copy.16
  68.2 20.3 %all_to_all.16 = f32[2,128,8]{2,0,1:T(2,128)S(1)} all-to-all(f32[2,128,8]{2,0,1:T(2,128)S(1)} %copy.16), channel_id=1, replica_groups=mesh['gx'=8,'gy'=16] {'gx','gy'}, dimensions={1} | all-to-all | bytes 16384 | tf_op jit(solution)/shard_map/all_to_all | solution.py:470
  88.5 0.7 reduce_sum.9
  (6 shorter events, 0.1 us)
Async XLA Ops:
  0.6 51.3 %copy-start.1 = (f32[39,8,128]{2,1,0:T(8,128)S(1)}, f32[39,8,128]{2,1,0:T(8,128)}, u32[]{:S(2)}) copy-start(f32[39,8,128]{2,1,0:T(8,128)} %diff_ref.5) | copy-start | bytes 479236
  5.0 61.2 %copy-start.11 = (s32[8,128]{1,0:T(8,128)S(1)}, s32[8,128]{1,0:T(8,128)}, u32[]{:S(2)}) copy-start(s32[8,128]{1,0:T(8,128)} %param.17) | copy-start | bytes 12292
  5.0 22.1 %all-to-all-start = ((f32[128,1,384]{2,1,0:T(1,128)}), f32[128,1,384]{2,1,0:T(1,128)S(1)}, u32[]{:S(2)}, u32[]{:S(2)}) async-start(f32[128,1,384]{2,1,0:T(1,128)} %copy.15), calls=%async_computation | async-start | bytes 393216 | tf_op jit(solution)/shard_map/all_to_all | solution.py:444
  16.5 16.3 %collective-permute-start.2 = (f32[32,8,128]{2,1,0:T(8,128)}, f32[32,8,128]{2,1,0:T(8,128)S(1)}, u32[]{:S(2)}, u32[]{:S(2)}) collective-permute-start(f32[32,8,128]{2,1,0:T(8,128)} %get-tuple-element.12), channel_id=1, source_target_pairs={{16,0},{32,16},{48,32},{64,48},{80,64},{96,80},{112,96},{17,1},{33... | collective-permute-start | bytes 393224 | tf_op jit(solution)/shard_map/ppermute | solution.py:442
  19.5 13.3 %collective-permute-start.3 = (f32[32,8,128]{2,1,0:T(8,128)}, f32[32,8,128]{2,1,0:T(8,128)S(1)}, u32[]{:S(2)}, u32[]{:S(2)}) collective-permute-start(f32[32,8,128]{2,1,0:T(8,128)} %get-tuple-element.13), channel_id=1, source_target_pairs={{0,16},{16,32},{32,48},{48,64},{64,80},{80,96},{96,112},{1,17},{17... | collective-permute-start | bytes 393224 | tf_op jit(solution)/shard_map/ppermute | solution.py:443
  27.1 8.2 %copy-start.6 = (f32[128,1,384]{2,0,1:T(8,128)}, f32[128,1,384]{2,0,1:T(8,128)S(1)}, u32[]{:S(2)}) copy-start(f32[128,1,384]{2,0,1:T(8,128)S(1)} %copy.22) | copy-start | bytes 589828
  27.1 7.0 %collective-permute-start = (f32[128,384]{1,0:T(8,128)S(1)}, f32[128,384]{1,0:T(8,128)S(1)}, u32[]{:S(2)}, u32[]{:S(2)}) collective-permute-start(f32[128,384]{1,0:T(8,128)S(1)} %bitcast.7), channel_id=1, source_target_pairs={{16,0},{32,16},{48,32},{64,48},{80,64},{96,80},{112,96},{17,1},{33... | collective-permute-start | bytes 589832 | tf_op jit(solution)/shard_map/ppermute | solution.py:446
  29.8 5.6 %collective-permute-start.1 = (f32[128,384]{1,0:T(8,128)S(1)}, f32[128,384]{1,0:T(8,128)S(1)}, u32[]{:S(2)}, u32[]{:S(2)}) collective-permute-start(f32[128,384]{1,0:T(8,128)S(1)} %bitcast.8), channel_id=1, source_target_pairs={{0,16},{16,32},{32,48},{48,64},{64,80},{80,96},{96,112},{1,17},{17... | collective-permute-start | bytes 589832 | tf_op jit(solution)/shard_map/ppermute | solution.py:447
  32.8 2.5 %copy-start.9 = (f32[32,8,128]{2,1,0:T(8,128)}, f32[32,8,128]{2,1,0:T(8,128)S(1)}, u32[]{:S(2)}) copy-start(f32[32,8,128]{2,1,0:T(8,128)S(1)} %collective-permute-done.2.sb_ref) | copy-start | bytes 393220
  32.8 2.5 %copy-start.10 = (f32[32,8,128]{2,1,0:T(8,128)}, f32[32,8,128]{2,1,0:T(8,128)S(1)}, u32[]{:S(2)}) copy-start(f32[32,8,128]{2,1,0:T(8,128)S(1)} %collective-permute-done.3.sa_ref) | copy-start | bytes 393220
  34.1 1.2 %copy-start.7 = (f32[128,384]{1,0:T(8,128)}, f32[128,384]{1,0:T(8,128)S(1)}, u32[]{:S(2)}) copy-start(f32[128,384]{1,0:T(8,128)S(1)} %collective-permute-done.below_ref) | copy-start | bytes 589828
  35.3 0.7 copy-start.8
  44.7 5.6 %collective-permute-start.4 = (f32[12,16,128]{2,1,0:T(8,128)}, f32[12,16,128]{2,1,0:T(8,128)S(1)}, u32[]{:S(2)}, u32[]{:S(2)}) collective-permute-start(f32[12,16,128]{2,1,0:T(8,128)} %get-tuple-element.14), channel_id=1, source_target_pairs={{1,0},{2,1},{3,2},{4,3},{5,4},{6,5},{7,6},{8,7},{9,8},{10,9},{11,1... | collective-permute-start | bytes 294920 | tf_op jit(solution)/shard_map/ppermute | solution.py:450
  46.0 5.9 %collective-permute-start.5 = (f32[12,16,128]{2,1,0:T(8,128)}, f32[12,16,128]{2,1,0:T(8,128)S(1)}, u32[]{:S(2)}, u32[]{:S(2)}) collective-permute-start(f32[12,16,128]{2,1,0:T(8,128)} %get-tuple-element.15), channel_id=1, source_target_pairs={{0,1},{1,2},{2,3},{3,4},{4,5},{5,6},{6,7},{7,8},{8,9},{9,10},{10,1... | collective-permute-start | bytes 294920 | tf_op jit(solution)/shard_map/ppermute | solution.py:451
  51.9 1.7 %copy-start = (f32[4,80,16,128]{3,2,1,0:T(8,128)S(1)}, f32[4,80,16,128]{3,2,1,0:T(8,128)}, u32[]{:S(2)}) copy-start(f32[4,80,16,128]{3,2,1,0:T(8,128)} %get-tuple-element.17.tall_hbm) | copy-start | bytes 7864324
  53.7 0.9 %copy-start.2 = (f32[64,8,128]{2,1,0:T(8,128)S(1)}, f32[64,8,128]{2,1,0:T(8,128)}, u32[]{:S(2)}) copy-start(f32[64,8,128]{2,1,0:T(8,128)} %get-tuple-element.16.st_xh) | copy-start | bytes 786436
  54.6 0.7 copy-start.3
  55.4 0.7 copy-start.4
  56.1 0.7 copy-start.5

commit v15 on v14

--- a/solution.py
+++ b/solution.py
@@ -465,8 +465,10 @@
                                       diffusivity, st_xh, mask, prior_emission, tall)
 
     nreg = REG_DEV * devices
-    member = (region_map.reshape(-1)[:, None] == jnp.arange(nreg, dtype=jnp.int32)).astype(jnp.float32)
-    partial = jnp.dot(surface_sum.reshape(species, cells), member, precision=HI)
+    blocks = surface_sum.reshape(species, rows // 2, 2, cols // 4, 4).sum(axis=(2, 4))
+    block_region = region_map[::2, ::4].reshape(-1)
+    member = (block_region[:, None] == jnp.arange(nreg, dtype=jnp.int32)).astype(jnp.float32)
+    partial = jnp.dot(blocks.reshape(species, -1), member, precision=HI)
     pieces = lax.all_to_all(partial.reshape(species, devices, nreg // devices), ("gx", "gy"), 1, 1,
                             tiled=True)
     gradient = jnp.sum(pieces, axis=1)

time: 89.9 us -> 89.2 us (level)
  matrix products: 1.87 us -> 0.45 us
  local copies, waits for them, and re-layouts: 7.5 us -> 8.7 us
    dot_general x1, matrix products: 1.87 us -> 0.45 us  [local(): partial = jnp.dot(blocks.reshape(species, -1), member, precision=HI)]
    unnamed x25 -> x23, local copies, waits for them, and re-layouts: 5.54 us -> 5.52 us
  transfers between devices with their start and end apart: 7 -> 7, of which waited for: 5 -> 5; matrix products, arithmetic and copies ran while one was open for 0% -> 1% of each run, Pallas kernels for 0% -> 0%
where the time goes in v15:
time: 89.2 us; the launch traced here: 88.6 us
  starting transfers between devices  27.9 us (31%)
  Pallas kernels  20.7 us (23%)
  blocking collectives  20.6 us (23%)
  local copies, waits for them, and re-layouts  8.7 us (10%)
  waiting for transfers between devices  8.46 us (9%)
  other arithmetic  0.93 us (1%)
    all_to_all x1, blocking collectives, local(): lax.all_to_all(partial.reshape(species, devices, nreg // devices), ('gx',...  20.6 us
    all_to_all x1, starting transfers between devices, local(): received = lax.all_to_all(placed, ('gx', 'gy'), 0, 0, tiled=True)  11.5 us
    pallas_call x1, Pallas kernels, steps_call(): pl.pallas_call(functools.partial(_steps_kernel, steps, species, levels, n...  9.39 us
    pallas_call x1, Pallas kernels, forcing_call(): pl.pallas_call(functools.partial(_forcing_kernel, species, kernel, levels...  8.74 us
    unnamed x23, local copies, waits for them, and re-layouts  5.52 us
    all_to_all x1, waiting for transfers between devices, local(): received = lax.all_to_all(placed, ('gx', 'gy'), 0, 0, tiled=True)  4.05 us
    ppermute x1, starting transfers between devices, local(): left = lax.ppermute(left, 'gy', up_y)  3.99 us
    ppermute x1, starting transfers between devices, local(): st_below = lax.ppermute(st_lo, 'gx', down_x)  2.98 us
  transfers between devices with their start and end apart: 7, of which 5 were waited for; matrix products, arithmetic and copies ran while one was open for 1% of the time, Pallas kernels for 0%

profile of v15, /device:TPU:1, one launch (start us, length us, event | category | flops | bytes accessed | tf_op | source)
XLA Modules:
  0.0 88.6 jit_solution(1720006274444768133)
XLA Ops:
  0.6 0.0 copy-start.1
  0.6 2.6 %shard_map.104 = (f32[128,384]{1,0:T(8,128)}, f32[32,8,128]{2,1,0:T(8,128)}, f32[32,8,128]{2,1,0:T(8,128)}) custom-call(f32[4,32,128]{2,1,0:T(8,128)} %adj_ref.1, s32[4,128]{1,0:T(4,128)} %bitcast.10, s32[4,128]{1,0:T(4,128)} %col_ref.1, s32[4,128]{1,0:T(4,128)} %lev_ref.1, f32[4,8,128]{2,1,0:T(8,128)} %wx_ref.5, f32[4,8,128]{2,1,0:T(8,128)} %wy_ref.5, ...), custom_call_target="tpu_custom_call" | custom-call | tf_op jit(solution)/shard_map/pallas_call | solution.py:79
  3.2 1.8 %copy.15 = f32[128,1,384]{2,1,0:T(1,128)} copy(f32[128,1,384]{2,0,1:T(8,128)} %bitcast.9) | data formatting | bytes 393216 | tf_op jit(solution)/shard_map/all_to_all | solution.py:444
  5.0 11.5 %all-to-all-start = ((f32[128,1,384]{2,1,0:T(1,128)}), f32[128,1,384]{2,1,0:T(1,128)S(1)}, u32[]{:S(2)}, u32[]{:S(2)}) async-start(f32[128,1,384]{2,1,0:T(1,128)} %copy.15), calls=%async_computation | async-start | bytes 393216 | tf_op jit(solution)/shard_map/all_to_all | solution.py:444
  16.5 3.0 %collective-permute-start.2 = (f32[32,8,128]{2,1,0:T(8,128)}, f32[32,8,128]{2,1,0:T(8,128)S(1)}, u32[]{:S(2)}, u32[]{:S(2)}) collective-permute-start(f32[32,8,128]{2,1,0:T(8,128)} %get-tuple-element.12), channel_id=1, source_target_pairs={{16,0},{32,16},{48,32},{64,48},{80,64},{96,80},{112,96},{17,1},{33... | collective-permute-start | bytes 393224 | tf_op jit(solution)/shard_map/ppermute | solution.py:442
  19.5 2.6 %collective-permute-start.3 = (f32[32,8,128]{2,1,0:T(8,128)}, f32[32,8,128]{2,1,0:T(8,128)S(1)}, u32[]{:S(2)}, u32[]{:S(2)}) collective-permute-start(f32[32,8,128]{2,1,0:T(8,128)} %get-tuple-element.13), channel_id=1, source_target_pairs={{0,16},{16,32},{32,48},{48,64},{64,80},{80,96},{96,112},{1,17},{17... | collective-permute-start | bytes 393224 | tf_op jit(solution)/shard_map/ppermute | solution.py:443
  22.2 0.8 slice.3
  23.0 0.1 eq.31
  23.1 4.0 %all-to-all-done = f32[128,1,384]{2,1,0:T(1,128)S(1)} async-done(((f32[128,1,384]{2,1,0:T(1,128)}), f32[128,1,384]{2,1,0:T(1,128)S(1)}, u32[]{:S(2)}, u32[]{:S(2)}) %all-to-all-start) | async-done | bytes 196640 | tf_op jit(solution)/shard_map/all_to_all | solution.py:444
  27.1 0.0 copy-start.6
  27.1 2.6 %collective-permute-start = (f32[128,384]{1,0:T(8,128)S(1)}, f32[128,384]{1,0:T(8,128)S(1)}, u32[]{:S(2)}, u32[]{:S(2)}) collective-permute-start(f32[128,384]{1,0:T(8,128)S(1)} %bitcast.6), channel_id=1, source_target_pairs={{16,0},{32,16},{48,32},{64,48},{80,64},{96,80},{112,96},{17,1},{33... | collective-permute-start | bytes 589832 | tf_op jit(solution)/shard_map/ppermute | solution.py:446
  29.8 3.0 %collective-permute-start.1 = (f32[128,384]{1,0:T(8,128)S(1)}, f32[128,384]{1,0:T(8,128)S(1)}, u32[]{:S(2)}, u32[]{:S(2)}) collective-permute-start(f32[128,384]{1,0:T(8,128)S(1)} %bitcast.7), channel_id=1, source_target_pairs={{0,16},{16,32},{32,48},{48,64},{64,80},{80,96},{96,112},{1,17},{17... | collective-permute-start | bytes 589832 | tf_op jit(solution)/shard_map/ppermute | solution.py:447
  32.7 0.1 and_convert_fusion.mask_ref
  32.8 0.0 collective-permute-done.2.sb_ref
  32.8 0.0 copy-start.9
  32.8 0.0 collective-permute-done.3.sa_ref
  32.8 0.0 copy-start.10
  32.8 1.3 %collective-permute-done.below_ref = f32[128,384]{1,0:T(8,128)S(1)} collective-permute-done((f32[128,384]{1,0:T(8,128)S(1)}, f32[128,384]{1,0:T(8,128)S(1)}, u32[]{:S(2)}, u32[]{:S(2)}) %collective-permute-start) | collective-permute-done | bytes 196640 | tf_op jit(solution)/shard_map/ppermute | solution.py:446
  34.1 0.0 copy-start.7
  34.1 1.2 %collective-permute-done.1.above_ref = f32[128,384]{1,0:T(8,128)S(1)} collective-permute-done((f32[128,384]{1,0:T(8,128)S(1)}, f32[128,384]{1,0:T(8,128)S(1)}, u32[]{:S(2)}, u32[]{:S(2)}) %collective-permute-start.1) | collective-permute-done | bytes 196640 | tf_op jit(solution)/shard_map/ppermute | solution.py:447
  35.3 0.0 copy-done.6
  35.3 0.0 copy-done.9
  35.3 0.0 copy-done.10
  35.3 0.0 copy-done.7
  35.3 0.0 copy-start.8
  35.3 0.7 copy-done.8
  36.0 8.7 %shard_map.105 = (f32[4,80,16,128]{3,2,1,0:T(8,128)}, f32[12,16,128]{2,1,0:T(8,128)}, f32[12,16,128]{2,1,0:T(8,128)}, f32[64,8,128]{2,1,0:T(8,128)}) custom-call(f32[128,384]{1,0:T(8,128)} %bitcast.8, f32[128,384]{1,0:T(8,128)} %copy-done.7, f32[128,384]{1,0:T(8,128)} %copy-done.8, f32[4,8,128]{2,1,0:T(8,128)} %wx_ref.5, f32[4,8,128]{2,1,0:T(8,128)} %wy_ref.5, ...), custom_call_target="tpu_custom_call" | custom-call | tf_op jit(solution)/shard_map/pallas_call | solution.py:199
  44.7 1.3 %collective-permute-start.4 = (f32[12,16,128]{2,1,0:T(8,128)}, f32[12,16,128]{2,1,0:T(8,128)S(1)}, u32[]{:S(2)}, u32[]{:S(2)}) collective-permute-start(f32[12,16,128]{2,1,0:T(8,128)} %get-tuple-element.14), channel_id=1, source_target_pairs={{1,0},{2,1},{3,2},{4,3},{5,4},{6,5},{7,6},{8,7},{9,8},{10,9},{11,1... | collective-permute-start | bytes 294920 | tf_op jit(solution)/shard_map/ppermute | solution.py:450
  46.0 4.0 %collective-permute-start.5 = (f32[12,16,128]{2,1,0:T(8,128)}, f32[12,16,128]{2,1,0:T(8,128)S(1)}, u32[]{:S(2)}, u32[]{:S(2)}) collective-permute-start(f32[12,16,128]{2,1,0:T(8,128)} %get-tuple-element.15), channel_id=1, source_target_pairs={{0,1},{1,2},{2,3},{3,4},{4,5},{5,6},{6,7},{7,8},{8,9},{9,10},{10,1... | collective-permute-start | bytes 294920 | tf_op jit(solution)/shard_map/ppermute | solution.py:451
  50.0 0.3 collective-permute-done.4.right_ref
  50.3 1.7 %collective-permute-done.5.left_ref = f32[12,16,128]{2,1,0:T(8,128)S(1)} collective-permute-done((f32[12,16,128]{2,1,0:T(8,128)}, f32[12,16,128]{2,1,0:T(8,128)S(1)}, u32[]{:S(2)}, u32[]{:S(2)}) %collective-permute-start.5) | collective-permute-done | bytes 98336 | tf_op jit(solution)/shard_map/ppermute | solution.py:451
  52.0 0.0 copy-done.1
  52.0 0.0 copy-start
  52.0 1.7 %copy-done = f32[4,80,16,128]{3,2,1,0:T(8,128)S(1)} copy-done((f32[4,80,16,128]{3,2,1,0:T(8,128)S(1)}, f32[4,80,16,128]{3,2,1,0:T(8,128)}, u32[]{:S(2)}) %copy-start) | copy-done | bytes 2621464
  53.7 0.0 copy-start.2
  53.7 0.9 %copy-done.2 = f32[64,8,128]{2,1,0:T(8,128)S(1)} copy-done((f32[64,8,128]{2,1,0:T(8,128)S(1)}, f32[64,8,128]{2,1,0:T(8,128)}, u32[]{:S(2)}) %copy-start.2) | copy-done | bytes 262168
  54.7 0.0 copy-start.3
  54.7 0.7 copy-done.3
  55.4 0.0 copy-start.4
  55.4 0.7 copy-done.4
  56.1 0.0 copy-start.5
  56.1 0.7 copy-done.5
  56.8 9.4 %shard_map.106 = (f32[2,40,8,128]{3,2,1,0:T(8,128)}, f32[2,8,128]{2,1,0:T(8,128)S(1)}) custom-call(f32[12,16,128]{2,1,0:T(8,128)S(1)} %collective-permute-done.4.right_ref, f32[12,16,128]{2,1,0:T(8,128)S(1)} %collective-permute-done.5.left_ref, f32[4,8,128]{2,1,0:T(8,128)S(1)} %copy-done.3, f32[4,8,128]{2,1,0:T(8,128)S(1)} %copy-done.4, ...), custom_call_target="tpu_custom_call" | custom-call | tf_op jit(solution)/shard_map/pallas_call | solution.py:392
  66.2 0.3 reshape.84
  66.4 0.1 reduce_sum.18
  66.6 0.1 reshape.86
  66.7 0.5 fusion
  67.1 0.2 copy.16
  67.3 20.6 %all_to_all.16 = f32[2,128,8]{2,0,1:T(2,128)S(1)} all-to-all(f32[2,128,8]{2,0,1:T(2,128)S(1)} %copy.16), channel_id=1, replica_groups=mesh['gx'=8,'gy'=16] {'gx','gy'}, dimensions={1} | all-to-all | bytes 16384 | tf_op jit(solution)/shard_map/all_to_all | solution.py:472
  87.9 0.7 reduce_sum.19
  (5 shorter events, 0.0 us)
Async XLA Ops:
  0.6 51.3 %copy-start.1 = (f32[39,8,128]{2,1,0:T(8,128)S(1)}, f32[39,8,128]{2,1,0:T(8,128)}, u32[]{:S(2)}) copy-start(f32[39,8,128]{2,1,0:T(8,128)} %diff_ref.5) | copy-start | bytes 479236
  5.0 22.1 %all-to-all-start = ((f32[128,1,384]{2,1,0:T(1,128)}), f32[128,1,384]{2,1,0:T(1,128)S(1)}, u32[]{:S(2)}, u32[]{:S(2)}) async-start(f32[128,1,384]{2,1,0:T(1,128)} %copy.15), calls=%async_computation | async-start | bytes 393216 | tf_op jit(solution)/shard_map/all_to_all | solution.py:444
  16.5 16.3 %collective-permute-start.2 = (f32[32,8,128]{2,1,0:T(8,128)}, f32[32,8,128]{2,1,0:T(8,128)S(1)}, u32[]{:S(2)}, u32[]{:S(2)}) collective-permute-start(f32[32,8,128]{2,1,0:T(8,128)} %get-tuple-element.12), channel_id=1, source_target_pairs={{16,0},{32,16},{48,32},{64,48},{80,64},{96,80},{112,96},{17,1},{33... | collective-permute-start | bytes 393224 | tf_op jit(solution)/shard_map/ppermute | solution.py:442
  19.5 13.3 %collective-permute-start.3 = (f32[32,8,128]{2,1,0:T(8,128)}, f32[32,8,128]{2,1,0:T(8,128)S(1)}, u32[]{:S(2)}, u32[]{:S(2)}) collective-permute-start(f32[32,8,128]{2,1,0:T(8,128)} %get-tuple-element.13), channel_id=1, source_target_pairs={{0,16},{16,32},{32,48},{48,64},{64,80},{80,96},{96,112},{1,17},{17... | collective-permute-start | bytes 393224 | tf_op jit(solution)/shard_map/ppermute | solution.py:443
  27.1 8.2 %copy-start.6 = (f32[128,1,384]{2,0,1:T(8,128)}, f32[128,1,384]{2,0,1:T(8,128)S(1)}, u32[]{:S(2)}) copy-start(f32[128,1,384]{2,0,1:T(8,128)S(1)} %copy.22) | copy-start | bytes 589828
  27.1 7.0 %collective-permute-start = (f32[128,384]{1,0:T(8,128)S(1)}, f32[128,384]{1,0:T(8,128)S(1)}, u32[]{:S(2)}, u32[]{:S(2)}) collective-permute-start(f32[128,384]{1,0:T(8,128)S(1)} %bitcast.6), channel_id=1, source_target_pairs={{16,0},{32,16},{48,32},{64,48},{80,64},{96,80},{112,96},{17,1},{33... | collective-permute-start | bytes 589832 | tf_op jit(solution)/shard_map/ppermute | solution.py:446
  29.8 5.6 %collective-permute-start.1 = (f32[128,384]{1,0:T(8,128)S(1)}, f32[128,384]{1,0:T(8,128)S(1)}, u32[]{:S(2)}, u32[]{:S(2)}) collective-permute-start(f32[128,384]{1,0:T(8,128)S(1)} %bitcast.7), channel_id=1, source_target_pairs={{0,16},{16,32},{32,48},{48,64},{64,80},{80,96},{96,112},{1,17},{17... | collective-permute-start | bytes 589832 | tf_op jit(solution)/shard_map/ppermute | solution.py:447
  32.8 2.5 %copy-start.9 = (f32[32,8,128]{2,1,0:T(8,128)}, f32[32,8,128]{2,1,0:T(8,128)S(1)}, u32[]{:S(2)}) copy-start(f32[32,8,128]{2,1,0:T(8,128)S(1)} %collective-permute-done.2.sb_ref) | copy-start | bytes 393220
  32.8 2.5 %copy-start.10 = (f32[32,8,128]{2,1,0:T(8,128)}, f32[32,8,128]{2,1,0:T(8,128)S(1)}, u32[]{:S(2)}) copy-start(f32[32,8,128]{2,1,0:T(8,128)S(1)} %collective-permute-done.3.sa_ref) | copy-start | bytes 393220
  34.1 1.2 %copy-start.7 = (f32[128,384]{1,0:T(8,128)}, f32[128,384]{1,0:T(8,128)S(1)}, u32[]{:S(2)}) copy-start(f32[128,384]{1,0:T(8,128)S(1)} %collective-permute-done.below_ref) | copy-start | bytes 589828
  35.3 0.7 copy-start.8
  44.7 5.6 %collective-permute-start.4 = (f32[12,16,128]{2,1,0:T(8,128)}, f32[12,16,128]{2,1,0:T(8,128)S(1)}, u32[]{:S(2)}, u32[]{:S(2)}) collective-permute-start(f32[12,16,128]{2,1,0:T(8,128)} %get-tuple-element.14), channel_id=1, source_target_pairs={{1,0},{2,1},{3,2},{4,3},{5,4},{6,5},{7,6},{8,7},{9,8},{10,9},{11,1... | collective-permute-start | bytes 294920 | tf_op jit(solution)/shard_map/ppermute | solution.py:450
  46.0 5.9 %collective-permute-start.5 = (f32[12,16,128]{2,1,0:T(8,128)}, f32[12,16,128]{2,1,0:T(8,128)S(1)}, u32[]{:S(2)}, u32[]{:S(2)}) collective-permute-start(f32[12,16,128]{2,1,0:T(8,128)} %get-tuple-element.15), channel_id=1, source_target_pairs={{0,1},{1,2},{2,3},{3,4},{4,5},{5,6},{6,7},{7,8},{8,9},{9,10},{10,1... | collective-permute-start | bytes 294920 | tf_op jit(solution)/shard_map/ppermute | solution.py:451
  52.0 1.7 %copy-start = (f32[4,80,16,128]{3,2,1,0:T(8,128)S(1)}, f32[4,80,16,128]{3,2,1,0:T(8,128)}, u32[]{:S(2)}) copy-start(f32[4,80,16,128]{3,2,1,0:T(8,128)} %get-tuple-element.17.tall_hbm) | copy-start | bytes 7864324
  53.7 0.9 %copy-start.2 = (f32[64,8,128]{2,1,0:T(8,128)S(1)}, f32[64,8,128]{2,1,0:T(8,128)}, u32[]{:S(2)}) copy-start(f32[64,8,128]{2,1,0:T(8,128)} %get-tuple-element.16.st_xh) | copy-start | bytes 786436
  54.7 0.7 copy-start.3
  55.4 0.7 copy-start.4
  56.1 0.7 copy-start.5

commit v16 on v15

--- a/solution.py
+++ b/solution.py
@@ -53,9 +53,8 @@
         for j in range(capacity):
             pick = jnp.where((owner == dest) & (rank[:, :1] == j), 1.0, 0.0)
             at = (k * capacity + j) * block
-            tbuf_ref[at:at + n_pay + 2] = lax.dot_general(
-                rows_ref[...], pick, (((1,), (0,)), ((), ())),
-                precision=lax.Precision.HIGHEST, preferred_element_type=jnp.float32)
+            tbuf_ref[at:at + n_pay + 2] = _exact_dot(
+                rows_ref[...], pick.astype(jnp.bfloat16), (((1,), (0,)), ((), ())))
     out_ref[...] = jnp.transpose(tbuf_ref[...])
     statics = (wx_ref, wy_ref, diff_ref)
     tr = wx_ref.shape[1]
@@ -87,8 +86,7 @@
       wind_y, diffusivity)
 
 
-def _exact_dot(a, b):
-    dims = (((1,), (1,)), ((), ()))
+def _exact_dot(a, b, dims=(((1,), (1,)), ((), ()))):
     hi = a.astype(jnp.bfloat16)
     rest = a - hi.astype(jnp.float32)
     mid = rest.astype(jnp.bfloat16)

time: 89.2 us -> 89 us (level)
  no operation moved by 1% of the time
where the time goes in v16:
time: 89 us; the launch traced here: 88.3 us
  starting transfers between devices  27.9 us (31%)
  blocking collectives  20.6 us (23%)
  Pallas kernels  20.5 us (23%)
  local copies, waits for them, and re-layouts  8.7 us (10%)
  waiting for transfers between devices  8.46 us (10%)
  other arithmetic  0.93 us (1%)
    all_to_all x1, blocking collectives, local(): lax.all_to_all(partial.reshape(species, devices, nreg // devices), ('gx',...  20.6 us
    all_to_all x1, starting transfers between devices, local(): received = lax.all_to_all(placed, ('gx', 'gy'), 0, 0, tiled=True)  11.5 us
    pallas_call x1, Pallas kernels, steps_call(): pl.pallas_call(functools.partial(_steps_kernel, steps, species, levels, n...  9.39 us
    pallas_call x1, Pallas kernels, forcing_call(): pl.pallas_call(functools.partial(_forcing_kernel, species, kernel, levels...  8.72 us
    unnamed x23, local copies, waits for them, and re-layouts  5.52 us
    all_to_all x1, waiting for transfers between devices, local(): received = lax.all_to_all(placed, ('gx', 'gy'), 0, 0, tiled=True)  4.05 us
    ppermute x1, starting transfers between devices, local(): left = lax.ppermute(left, 'gy', up_y)  3.99 us
    ppermute x1, starting transfers between devices, local(): st_below = lax.ppermute(st_lo, 'gx', down_x)  2.98 us
  transfers between devices with their start and end apart: 7, of which 5 were waited for; matrix products, arithmetic and copies ran while one was open for 1% of the time, Pallas kernels for 0%

profile of v16, /device:TPU:1, one launch (start us, length us, event | category | flops | bytes accessed | tf_op | source)
XLA Modules:
  0.0 88.3 jit_solution(16585344372456505)
XLA Ops:
  0.6 0.0 copy-start.1
  0.6 2.4 %shard_map.104 = (f32[128,384]{1,0:T(8,128)}, f32[32,8,128]{2,1,0:T(8,128)}, f32[32,8,128]{2,1,0:T(8,128)}) custom-call(f32[4,32,128]{2,1,0:T(8,128)} %adj_ref.1, s32[4,128]{1,0:T(4,128)} %bitcast.10, s32[4,128]{1,0:T(4,128)} %col_ref.1, s32[4,128]{1,0:T(4,128)} %lev_ref.1, f32[4,8,128]{2,1,0:T(8,128)} %wx_ref.5, f32[4,8,128]{2,1,0:T(8,128)} %wy_ref.5, ...), custom_call_target="tpu_custom_call" | custom-call | tf_op jit(solution)/shard_map/pallas_call | solution.py:78
  3.0 1.8 %copy.15 = f32[128,1,384]{2,1,0:T(1,128)} copy(f32[128,1,384]{2,0,1:T(8,128)} %bitcast.9) | data formatting | bytes 393216 | tf_op jit(solution)/shard_map/all_to_all | solution.py:442
  4.8 11.5 %all-to-all-start = ((f32[128,1,384]{2,1,0:T(1,128)}), f32[128,1,384]{2,1,0:T(1,128)S(1)}, u32[]{:S(2)}, u32[]{:S(2)}) async-start(f32[128,1,384]{2,1,0:T(1,128)} %copy.15), calls=%async_computation | async-start | bytes 393216 | tf_op jit(solution)/shard_map/all_to_all | solution.py:442
  16.3 3.0 %collective-permute-start.2 = (f32[32,8,128]{2,1,0:T(8,128)}, f32[32,8,128]{2,1,0:T(8,128)S(1)}, u32[]{:S(2)}, u32[]{:S(2)}) collective-permute-start(f32[32,8,128]{2,1,0:T(8,128)} %get-tuple-element.12), channel_id=1, source_target_pairs={{16,0},{32,16},{48,32},{64,48},{80,64},{96,80},{112,96},{17,1},{33... | collective-permute-start | bytes 393224 | tf_op jit(solution)/shard_map/ppermute | solution.py:440
  19.3 2.6 %collective-permute-start.3 = (f32[32,8,128]{2,1,0:T(8,128)}, f32[32,8,128]{2,1,0:T(8,128)S(1)}, u32[]{:S(2)}, u32[]{:S(2)}) collective-permute-start(f32[32,8,128]{2,1,0:T(8,128)} %get-tuple-element.13), channel_id=1, source_target_pairs={{0,16},{16,32},{32,48},{48,64},{64,80},{80,96},{96,112},{1,17},{17... | collective-permute-start | bytes 393224 | tf_op jit(solution)/shard_map/ppermute | solution.py:441
  21.9 0.8 slice.3
  22.7 0.1 eq.31
  22.8 4.0 %all-to-all-done = f32[128,1,384]{2,1,0:T(1,128)S(1)} async-done(((f32[128,1,384]{2,1,0:T(1,128)}), f32[128,1,384]{2,1,0:T(1,128)S(1)}, u32[]{:S(2)}, u32[]{:S(2)}) %all-to-all-start) | async-done | bytes 196640 | tf_op jit(solution)/shard_map/all_to_all | solution.py:442
  26.9 0.0 copy-start.6
  26.9 2.6 %collective-permute-start = (f32[128,384]{1,0:T(8,128)S(1)}, f32[128,384]{1,0:T(8,128)S(1)}, u32[]{:S(2)}, u32[]{:S(2)}) collective-permute-start(f32[128,384]{1,0:T(8,128)S(1)} %bitcast.6), channel_id=1, source_target_pairs={{16,0},{32,16},{48,32},{64,48},{80,64},{96,80},{112,96},{17,1},{33... | collective-permute-start | bytes 589832 | tf_op jit(solution)/shard_map/ppermute | solution.py:444
  29.5 3.0 %collective-permute-start.1 = (f32[128,384]{1,0:T(8,128)S(1)}, f32[128,384]{1,0:T(8,128)S(1)}, u32[]{:S(2)}, u32[]{:S(2)}) collective-permute-start(f32[128,384]{1,0:T(8,128)S(1)} %bitcast.7), channel_id=1, source_target_pairs={{0,16},{16,32},{32,48},{48,64},{64,80},{80,96},{96,112},{1,17},{17... | collective-permute-start | bytes 589832 | tf_op jit(solution)/shard_map/ppermute | solution.py:445
  32.5 0.1 and_convert_fusion.mask_ref
  32.6 0.0 collective-permute-done.2.sb_ref
  32.6 0.0 copy-start.9
  32.6 0.0 collective-permute-done.3.sa_ref
  32.6 0.0 copy-start.10
  32.6 1.3 %collective-permute-done.below_ref = f32[128,384]{1,0:T(8,128)S(1)} collective-permute-done((f32[128,384]{1,0:T(8,128)S(1)}, f32[128,384]{1,0:T(8,128)S(1)}, u32[]{:S(2)}, u32[]{:S(2)}) %collective-permute-start) | collective-permute-done | bytes 196640 | tf_op jit(solution)/shard_map/ppermute | solution.py:444
  33.9 0.0 copy-start.7
  33.9 1.2 %collective-permute-done.1.above_ref = f32[128,384]{1,0:T(8,128)S(1)} collective-permute-done((f32[128,384]{1,0:T(8,128)S(1)}, f32[128,384]{1,0:T(8,128)S(1)}, u32[]{:S(2)}, u32[]{:S(2)}) %collective-permute-start.1) | collective-permute-done | bytes 196640 | tf_op jit(solution)/shard_map/ppermute | solution.py:445
  35.1 0.0 copy-done.6
  35.1 0.0 copy-done.9
  35.1 0.0 copy-done.10
  35.1 0.0 copy-done.7
  35.1 0.0 copy-start.8
  35.1 0.7 copy-done.8
  35.8 8.7 %shard_map.105 = (f32[4,80,16,128]{3,2,1,0:T(8,128)}, f32[12,16,128]{2,1,0:T(8,128)}, f32[12,16,128]{2,1,0:T(8,128)}, f32[64,8,128]{2,1,0:T(8,128)}) custom-call(f32[128,384]{1,0:T(8,128)} %bitcast.8, f32[128,384]{1,0:T(8,128)} %copy-done.7, f32[128,384]{1,0:T(8,128)} %copy-done.8, f32[4,8,128]{2,1,0:T(8,128)} %wx_ref.5, f32[4,8,128]{2,1,0:T(8,128)} %wy_ref.5, ...), custom_call_target="tpu_custom_call" | custom-call | tf_op jit(solution)/shard_map/pallas_call | solution.py:197
  44.5 1.3 %collective-permute-start.4 = (f32[12,16,128]{2,1,0:T(8,128)}, f32[12,16,128]{2,1,0:T(8,128)S(1)}, u32[]{:S(2)}, u32[]{:S(2)}) collective-permute-start(f32[12,16,128]{2,1,0:T(8,128)} %get-tuple-element.14), channel_id=1, source_target_pairs={{1,0},{2,1},{3,2},{4,3},{5,4},{6,5},{7,6},{8,7},{9,8},{10,9},{11,1... | collective-permute-start | bytes 294920 | tf_op jit(solution)/shard_map/ppermute | solution.py:448
  45.8 4.0 %collective-permute-start.5 = (f32[12,16,128]{2,1,0:T(8,128)}, f32[12,16,128]{2,1,0:T(8,128)S(1)}, u32[]{:S(2)}, u32[]{:S(2)}) collective-permute-start(f32[12,16,128]{2,1,0:T(8,128)} %get-tuple-element.15), channel_id=1, source_target_pairs={{0,1},{1,2},{2,3},{3,4},{4,5},{5,6},{6,7},{7,8},{8,9},{9,10},{10,1... | collective-permute-start | bytes 294920 | tf_op jit(solution)/shard_map/ppermute | solution.py:449
  49.8 0.3 collective-permute-done.4.right_ref
  50.1 1.7 %collective-permute-done.5.left_ref = f32[12,16,128]{2,1,0:T(8,128)S(1)} collective-permute-done((f32[12,16,128]{2,1,0:T(8,128)}, f32[12,16,128]{2,1,0:T(8,128)S(1)}, u32[]{:S(2)}, u32[]{:S(2)}) %collective-permute-start.5) | collective-permute-done | bytes 98336 | tf_op jit(solution)/shard_map/ppermute | solution.py:449
  51.7 0.0 copy-done.1
  51.7 0.0 copy-start
  51.7 1.7 %copy-done = f32[4,80,16,128]{3,2,1,0:T(8,128)S(1)} copy-done((f32[4,80,16,128]{3,2,1,0:T(8,128)S(1)}, f32[4,80,16,128]{3,2,1,0:T(8,128)}, u32[]{:S(2)}) %copy-start) | copy-done | bytes 2621464
  53.5 0.0 copy-start.2
  53.5 0.9 %copy-done.2 = f32[64,8,128]{2,1,0:T(8,128)S(1)} copy-done((f32[64,8,128]{2,1,0:T(8,128)S(1)}, f32[64,8,128]{2,1,0:T(8,128)}, u32[]{:S(2)}) %copy-start.2) | copy-done | bytes 262168
  54.4 0.0 copy-start.3
  54.4 0.7 copy-done.3
  55.1 0.0 copy-start.4
  55.1 0.7 copy-done.4
  55.9 0.0 copy-start.5
  55.9 0.7 copy-done.5
  56.5 9.4 %shard_map.106 = (f32[2,40,8,128]{3,2,1,0:T(8,128)}, f32[2,8,128]{2,1,0:T(8,128)S(1)}) custom-call(f32[12,16,128]{2,1,0:T(8,128)S(1)} %collective-permute-done.4.right_ref, f32[12,16,128]{2,1,0:T(8,128)S(1)} %collective-permute-done.5.left_ref, f32[4,8,128]{2,1,0:T(8,128)S(1)} %copy-done.3, f32[4,8,128]{2,1,0:T(8,128)S(1)} %copy-done.4, ...), custom_call_target="tpu_custom_call" | custom-call | tf_op jit(solution)/shard_map/pallas_call | solution.py:390
  65.9 0.3 reshape.84
  66.2 0.1 reduce_sum.18
  66.3 0.1 reshape.86
  66.4 0.5 fusion
  66.9 0.2 copy.16
  67.0 20.6 %all_to_all.16 = f32[2,128,8]{2,0,1:T(2,128)S(1)} all-to-all(f32[2,128,8]{2,0,1:T(2,128)S(1)} %copy.16), channel_id=1, replica_groups=mesh['gx'=8,'gy'=16] {'gx','gy'}, dimensions={1} | all-to-all | bytes 16384 | tf_op jit(solution)/shard_map/all_to_all | solution.py:470
  87.6 0.7 reduce_sum.19
  (5 shorter events, 0.0 us)
Async XLA Ops:
  0.6 51.1 %copy-start.1 = (f32[39,8,128]{2,1,0:T(8,128)S(1)}, f32[39,8,128]{2,1,0:T(8,128)}, u32[]{:S(2)}) copy-start(f32[39,8,128]{2,1,0:T(8,128)} %diff_ref.5) | copy-start | bytes 479236
  4.8 22.1 %all-to-all-start = ((f32[128,1,384]{2,1,0:T(1,128)}), f32[128,1,384]{2,1,0:T(1,128)S(1)}, u32[]{:S(2)}, u32[]{:S(2)}) async-start(f32[128,1,384]{2,1,0:T(1,128)} %copy.15), calls=%async_computation | async-start | bytes 393216 | tf_op jit(solution)/shard_map/all_to_all | solution.py:442
  16.3 16.3 %collective-permute-start.2 = (f32[32,8,128]{2,1,0:T(8,128)}, f32[32,8,128]{2,1,0:T(8,128)S(1)}, u32[]{:S(2)}, u32[]{:S(2)}) collective-permute-start(f32[32,8,128]{2,1,0:T(8,128)} %get-tuple-element.12), channel_id=1, source_target_pairs={{16,0},{32,16},{48,32},{64,48},{80,64},{96,80},{112,96},{17,1},{33... | collective-permute-start | bytes 393224 | tf_op jit(solution)/shard_map/ppermute | solution.py:440
  19.3 13.3 %collective-permute-start.3 = (f32[32,8,128]{2,1,0:T(8,128)}, f32[32,8,128]{2,1,0:T(8,128)S(1)}, u32[]{:S(2)}, u32[]{:S(2)}) collective-permute-start(f32[32,8,128]{2,1,0:T(8,128)} %get-tuple-element.13), channel_id=1, source_target_pairs={{0,16},{16,32},{32,48},{48,64},{64,80},{80,96},{96,112},{1,17},{17... | collective-permute-start | bytes 393224 | tf_op jit(solution)/shard_map/ppermute | solution.py:441
  26.9 8.2 %copy-start.6 = (f32[128,1,384]{2,0,1:T(8,128)}, f32[128,1,384]{2,0,1:T(8,128)S(1)}, u32[]{:S(2)}) copy-start(f32[128,1,384]{2,0,1:T(8,128)S(1)} %copy.22) | copy-start | bytes 589828
  26.9 7.0 %collective-permute-start = (f32[128,384]{1,0:T(8,128)S(1)}, f32[128,384]{1,0:T(8,128)S(1)}, u32[]{:S(2)}, u32[]{:S(2)}) collective-permute-start(f32[128,384]{1,0:T(8,128)S(1)} %bitcast.6), channel_id=1, source_target_pairs={{16,0},{32,16},{48,32},{64,48},{80,64},{96,80},{112,96},{17,1},{33... | collective-permute-start | bytes 589832 | tf_op jit(solution)/shard_map/ppermute | solution.py:444
  29.5 5.6 %collective-permute-start.1 = (f32[128,384]{1,0:T(8,128)S(1)}, f32[128,384]{1,0:T(8,128)S(1)}, u32[]{:S(2)}, u32[]{:S(2)}) collective-permute-start(f32[128,384]{1,0:T(8,128)S(1)} %bitcast.7), channel_id=1, source_target_pairs={{0,16},{16,32},{32,48},{48,64},{64,80},{80,96},{96,112},{1,17},{17... | collective-permute-start | bytes 589832 | tf_op jit(solution)/shard_map/ppermute | solution.py:445
  32.6 2.5 %copy-start.9 = (f32[32,8,128]{2,1,0:T(8,128)}, f32[32,8,128]{2,1,0:T(8,128)S(1)}, u32[]{:S(2)}) copy-start(f32[32,8,128]{2,1,0:T(8,128)S(1)} %collective-permute-done.2.sb_ref) | copy-start | bytes 393220
  32.6 2.5 %copy-start.10 = (f32[32,8,128]{2,1,0:T(8,128)}, f32[32,8,128]{2,1,0:T(8,128)S(1)}, u32[]{:S(2)}) copy-start(f32[32,8,128]{2,1,0:T(8,128)S(1)} %collective-permute-done.3.sa_ref) | copy-start | bytes 393220
  33.9 1.2 %copy-start.7 = (f32[128,384]{1,0:T(8,128)}, f32[128,384]{1,0:T(8,128)S(1)}, u32[]{:S(2)}) copy-start(f32[128,384]{1,0:T(8,128)S(1)} %collective-permute-done.below_ref) | copy-start | bytes 589828
  35.1 0.7 copy-start.8
  44.5 5.6 %collective-permute-start.4 = (f32[12,16,128]{2,1,0:T(8,128)}, f32[12,16,128]{2,1,0:T(8,128)S(1)}, u32[]{:S(2)}, u32[]{:S(2)}) collective-permute-start(f32[12,16,128]{2,1,0:T(8,128)} %get-tuple-element.14), channel_id=1, source_target_pairs={{1,0},{2,1},{3,2},{4,3},{5,4},{6,5},{7,6},{8,7},{9,8},{10,9},{11,1... | collective-permute-start | bytes 294920 | tf_op jit(solution)/shard_map/ppermute | solution.py:448
  45.8 5.9 %collective-permute-start.5 = (f32[12,16,128]{2,1,0:T(8,128)}, f32[12,16,128]{2,1,0:T(8,128)S(1)}, u32[]{:S(2)}, u32[]{:S(2)}) collective-permute-start(f32[12,16,128]{2,1,0:T(8,128)} %get-tuple-element.15), channel_id=1, source_target_pairs={{0,1},{1,2},{2,3},{3,4},{4,5},{5,6},{6,7},{7,8},{8,9},{9,10},{10,1... | collective-permute-start | bytes 294920 | tf_op jit(solution)/shard_map/ppermute | solution.py:449
  51.7 1.7 %copy-start = (f32[4,80,16,128]{3,2,1,0:T(8,128)S(1)}, f32[4,80,16,128]{3,2,1,0:T(8,128)}, u32[]{:S(2)}) copy-start(f32[4,80,16,128]{3,2,1,0:T(8,128)} %get-tuple-element.17.tall_hbm) | copy-start | bytes 7864324
  53.5 0.9 %copy-start.2 = (f32[64,8,128]{2,1,0:T(8,128)S(1)}, f32[64,8,128]{2,1,0:T(8,128)}, u32[]{:S(2)}) copy-start(f32[64,8,128]{2,1,0:T(8,128)} %get-tuple-element.16.st_xh) | copy-start | bytes 786436
  54.4 0.7 copy-start.3
  55.1 0.7 copy-start.4
  55.9 0.7 copy-start.5

commit v17 on v16

--- a/solution.py
+++ b/solution.py
@@ -301,7 +301,7 @@
                 out.append(r)
             return tuple(out)
 
-        lax.fori_loop(0, levels, forward, (zero,) * species, unroll=8)
+        lax.fori_loop(0, levels, forward, (zero,) * species, unroll=True)
 
         def backward(i, result, k=k):
             l = levels - 1 - i
@@ -317,7 +317,7 @@
                 out.append(r)
             return tuple(out)
 
-        surface = lax.fori_loop(0, levels, backward, (zero,) * species, unroll=8)
+        surface = lax.fori_loop(0, levels, backward, (zero,) * species, unroll=True)
         for s in range(species):
             if first:
                 ss_ref[s] = prior_ref[s] * surface[s][:tr, :tc]

time: 89 us -> 88 us (0.989)
  Pallas kernels: 20.5 us -> 19.5 us
    pallas_call x1, Pallas kernels: 9.39 us -> 8.43 us  [steps_call(): pl.pallas_call(functools.partial(_steps_kernel, steps, species, levels, n...]
where the time goes in v17:
time: 88 us; the launch traced here: 87.4 us
  starting transfers between devices  28.1 us (32%)
  blocking collectives  20.6 us (23%)
  Pallas kernels  19.5 us (22%)
  local copies, waits for them, and re-layouts  8.7 us (10%)
  waiting for transfers between devices  8.28 us (9%)
  other arithmetic  0.93 us (1%)
    all_to_all x1, blocking collectives, local(): lax.all_to_all(partial.reshape(species, devices, nreg // devices), ('gx',...  20.6 us
    all_to_all x1, starting transfers between devices, local(): received = lax.all_to_all(placed, ('gx', 'gy'), 0, 0, tiled=True)  11.5 us
    pallas_call x1, Pallas kernels, forcing_call(): pl.pallas_call(functools.partial(_forcing_kernel, species, kernel, levels...  8.73 us
    pallas_call x1, Pallas kernels, steps_call(): pl.pallas_call(functools.partial(_steps_kernel, steps, species, levels, n...  8.43 us
    unnamed x23, local copies, waits for them, and re-layouts  5.52 us
    ppermute x1, starting transfers between devices, local(): left = lax.ppermute(left, 'gy', up_y)  4.17 us
    all_to_all x1, waiting for transfers between devices, local(): received = lax.all_to_all(placed, ('gx', 'gy'), 0, 0, tiled=True)  4.05 us
    ppermute x1, starting transfers between devices, local(): st_below = lax.ppermute(st_lo, 'gx', down_x)  2.98 us
  transfers between devices with their start and end apart: 7, of which 5 were waited for; matrix products, arithmetic and copies ran while one was open for 1% of the time, Pallas kernels for 0%

profile of v17, /device:TPU:1, one launch (start us, length us, event | category | flops | bytes accessed | tf_op | source)
XLA Modules:
  0.0 87.4 jit_solution(3467782769331528674)
XLA Ops:
  0.6 0.0 copy-start.1
  0.6 2.4 %shard_map.104 = (f32[128,384]{1,0:T(8,128)}, f32[32,8,128]{2,1,0:T(8,128)}, f32[32,8,128]{2,1,0:T(8,128)}) custom-call(f32[4,32,128]{2,1,0:T(8,128)} %adj_ref.1, s32[4,128]{1,0:T(4,128)} %bitcast.10, s32[4,128]{1,0:T(4,128)} %col_ref.1, s32[4,128]{1,0:T(4,128)} %lev_ref.1, f32[4,8,128]{2,1,0:T(8,128)} %wx_ref.5, f32[4,8,128]{2,1,0:T(8,128)} %wy_ref.5, ...), custom_call_target="tpu_custom_call" | custom-call | tf_op jit(solution)/shard_map/pallas_call | solution.py:78
  3.0 1.8 %copy.15 = f32[128,1,384]{2,1,0:T(1,128)} copy(f32[128,1,384]{2,0,1:T(8,128)} %bitcast.9) | data formatting | bytes 393216 | tf_op jit(solution)/shard_map/all_to_all | solution.py:442
  4.8 11.5 %all-to-all-start = ((f32[128,1,384]{2,1,0:T(1,128)}), f32[128,1,384]{2,1,0:T(1,128)S(1)}, u32[]{:S(2)}, u32[]{:S(2)}) async-start(f32[128,1,384]{2,1,0:T(1,128)} %copy.15), calls=%async_computation | async-start | bytes 393216 | tf_op jit(solution)/shard_map/all_to_all | solution.py:442
  16.3 3.0 %collective-permute-start.2 = (f32[32,8,128]{2,1,0:T(8,128)}, f32[32,8,128]{2,1,0:T(8,128)S(1)}, u32[]{:S(2)}, u32[]{:S(2)}) collective-permute-start(f32[32,8,128]{2,1,0:T(8,128)} %get-tuple-element.12), channel_id=1, source_target_pairs={{16,0},{32,16},{48,32},{64,48},{80,64},{96,80},{112,96},{17,1},{33... | collective-permute-start | bytes 393224 | tf_op jit(solution)/shard_map/ppermute | solution.py:440
  19.3 2.6 %collective-permute-start.3 = (f32[32,8,128]{2,1,0:T(8,128)}, f32[32,8,128]{2,1,0:T(8,128)S(1)}, u32[]{:S(2)}, u32[]{:S(2)}) collective-permute-start(f32[32,8,128]{2,1,0:T(8,128)} %get-tuple-element.13), channel_id=1, source_target_pairs={{0,16},{16,32},{32,48},{48,64},{64,80},{80,96},{96,112},{1,17},{17... | collective-permute-start | bytes 393224 | tf_op jit(solution)/shard_map/ppermute | solution.py:441
  21.9 0.8 slice.3
  22.7 0.1 eq.31
  22.8 4.0 %all-to-all-done = f32[128,1,384]{2,1,0:T(1,128)S(1)} async-done(((f32[128,1,384]{2,1,0:T(1,128)}), f32[128,1,384]{2,1,0:T(1,128)S(1)}, u32[]{:S(2)}, u32[]{:S(2)}) %all-to-all-start) | async-done | bytes 196640 | tf_op jit(solution)/shard_map/all_to_all | solution.py:442
  26.9 0.0 copy-start.6
  26.9 2.6 %collective-permute-start = (f32[128,384]{1,0:T(8,128)S(1)}, f32[128,384]{1,0:T(8,128)S(1)}, u32[]{:S(2)}, u32[]{:S(2)}) collective-permute-start(f32[128,384]{1,0:T(8,128)S(1)} %bitcast.6), channel_id=1, source_target_pairs={{16,0},{32,16},{48,32},{64,48},{80,64},{96,80},{112,96},{17,1},{33... | collective-permute-start | bytes 589832 | tf_op jit(solution)/shard_map/ppermute | solution.py:444
  29.5 3.0 %collective-permute-start.1 = (f32[128,384]{1,0:T(8,128)S(1)}, f32[128,384]{1,0:T(8,128)S(1)}, u32[]{:S(2)}, u32[]{:S(2)}) collective-permute-start(f32[128,384]{1,0:T(8,128)S(1)} %bitcast.7), channel_id=1, source_target_pairs={{0,16},{16,32},{32,48},{48,64},{64,80},{80,96},{96,112},{1,17},{17... | collective-permute-start | bytes 589832 | tf_op jit(solution)/shard_map/ppermute | solution.py:445
  32.5 0.1 and_convert_fusion.mask_ref
  32.6 0.0 collective-permute-done.2.sb_ref
  32.6 0.0 copy-start.9
  32.6 0.0 collective-permute-done.3.sa_ref
  32.6 0.0 copy-start.10
  32.6 1.3 %collective-permute-done.below_ref = f32[128,384]{1,0:T(8,128)S(1)} collective-permute-done((f32[128,384]{1,0:T(8,128)S(1)}, f32[128,384]{1,0:T(8,128)S(1)}, u32[]{:S(2)}, u32[]{:S(2)}) %collective-permute-start) | collective-permute-done | bytes 196640 | tf_op jit(solution)/shard_map/ppermute | solution.py:444
  33.9 0.0 copy-start.7
  33.9 1.2 %collective-permute-done.1.above_ref = f32[128,384]{1,0:T(8,128)S(1)} collective-permute-done((f32[128,384]{1,0:T(8,128)S(1)}, f32[128,384]{1,0:T(8,128)S(1)}, u32[]{:S(2)}, u32[]{:S(2)}) %collective-permute-start.1) | collective-permute-done | bytes 196640 | tf_op jit(solution)/shard_map/ppermute | solution.py:445
  35.1 0.0 copy-done.6
  35.1 0.0 copy-done.9
  35.1 0.0 copy-done.10
  35.1 0.0 copy-done.7
  35.1 0.0 copy-start.8
  35.1 0.7 copy-done.8
  35.8 8.7 %shard_map.105 = (f32[4,80,16,128]{3,2,1,0:T(8,128)}, f32[12,16,128]{2,1,0:T(8,128)}, f32[12,16,128]{2,1,0:T(8,128)}, f32[64,8,128]{2,1,0:T(8,128)}) custom-call(f32[128,384]{1,0:T(8,128)} %bitcast.8, f32[128,384]{1,0:T(8,128)} %copy-done.7, f32[128,384]{1,0:T(8,128)} %copy-done.8, f32[4,8,128]{2,1,0:T(8,128)} %wx_ref.5, f32[4,8,128]{2,1,0:T(8,128)} %wy_ref.5, ...), custom_call_target="tpu_custom_call" | custom-call | tf_op jit(solution)/shard_map/pallas_call | solution.py:197
  44.5 1.3 %collective-permute-start.4 = (f32[12,16,128]{2,1,0:T(8,128)}, f32[12,16,128]{2,1,0:T(8,128)S(1)}, u32[]{:S(2)}, u32[]{:S(2)}) collective-permute-start(f32[12,16,128]{2,1,0:T(8,128)} %get-tuple-element.14), channel_id=1, source_target_pairs={{1,0},{2,1},{3,2},{4,3},{5,4},{6,5},{7,6},{8,7},{9,8},{10,9},{11,1... | collective-permute-start | bytes 294920 | tf_op jit(solution)/shard_map/ppermute | solution.py:448
  45.8 4.2 %collective-permute-start.5 = (f32[12,16,128]{2,1,0:T(8,128)}, f32[12,16,128]{2,1,0:T(8,128)S(1)}, u32[]{:S(2)}, u32[]{:S(2)}) collective-permute-start(f32[12,16,128]{2,1,0:T(8,128)} %get-tuple-element.15), channel_id=1, source_target_pairs={{0,1},{1,2},{2,3},{3,4},{4,5},{5,6},{6,7},{7,8},{8,9},{9,10},{10,1... | collective-permute-start | bytes 294920 | tf_op jit(solution)/shard_map/ppermute | solution.py:449
  50.0 0.1 collective-permute-done.4.right_ref
  50.1 1.7 %collective-permute-done.5.left_ref = f32[12,16,128]{2,1,0:T(8,128)S(1)} collective-permute-done((f32[12,16,128]{2,1,0:T(8,128)}, f32[12,16,128]{2,1,0:T(8,128)S(1)}, u32[]{:S(2)}, u32[]{:S(2)}) %collective-permute-start.5) | collective-permute-done | bytes 98336 | tf_op jit(solution)/shard_map/ppermute | solution.py:449
  51.7 0.0 copy-done.1
  51.7 0.0 copy-start
  51.7 1.7 %copy-done = f32[4,80,16,128]{3,2,1,0:T(8,128)S(1)} copy-done((f32[4,80,16,128]{3,2,1,0:T(8,128)S(1)}, f32[4,80,16,128]{3,2,1,0:T(8,128)}, u32[]{:S(2)}) %copy-start) | copy-done | bytes 2621464
  53.5 0.0 copy-start.2
  53.5 0.9 %copy-done.2 = f32[64,8,128]{2,1,0:T(8,128)S(1)} copy-done((f32[64,8,128]{2,1,0:T(8,128)S(1)}, f32[64,8,128]{2,1,0:T(8,128)}, u32[]{:S(2)}) %copy-start.2) | copy-done | bytes 262168
  54.4 0.0 copy-start.3
  54.4 0.7 copy-done.3
  55.1 0.0 copy-start.4
  55.1 0.7 copy-done.4
  55.9 0.0 copy-start.5
  55.9 0.7 copy-done.5
  56.6 8.4 %shard_map.106 = (f32[2,40,8,128]{3,2,1,0:T(8,128)}, f32[2,8,128]{2,1,0:T(8,128)S(1)}) custom-call(f32[12,16,128]{2,1,0:T(8,128)S(1)} %collective-permute-done.4.right_ref, f32[12,16,128]{2,1,0:T(8,128)S(1)} %collective-permute-done.5.left_ref, f32[4,8,128]{2,1,0:T(8,128)S(1)} %copy-done.3, f32[4,8,128]{2,1,0:T(8,128)S(1)} %copy-done.4, ...), custom_call_target="tpu_custom_call" | custom-call | tf_op jit(solution)/shard_map/pallas_call | solution.py:390
  65.0 0.3 reshape.84
  65.3 0.1 reduce_sum.18
  65.4 0.1 reshape.86
  65.5 0.5 fusion
  65.9 0.2 copy.16
  66.1 20.6 %all_to_all.16 = f32[2,128,8]{2,0,1:T(2,128)S(1)} all-to-all(f32[2,128,8]{2,0,1:T(2,128)S(1)} %copy.16), channel_id=1, replica_groups=mesh['gx'=8,'gy'=16] {'gx','gy'}, dimensions={1} | all-to-all | bytes 16384 | tf_op jit(solution)/shard_map/all_to_all | solution.py:470
  86.7 0.7 reduce_sum.19
  (5 shorter events, 0.0 us)
Async XLA Ops:
  0.6 51.1 %copy-start.1 = (f32[39,8,128]{2,1,0:T(8,128)S(1)}, f32[39,8,128]{2,1,0:T(8,128)}, u32[]{:S(2)}) copy-start(f32[39,8,128]{2,1,0:T(8,128)} %diff_ref.5) | copy-start | bytes 479236
  4.8 22.1 %all-to-all-start = ((f32[128,1,384]{2,1,0:T(1,128)}), f32[128,1,384]{2,1,0:T(1,128)S(1)}, u32[]{:S(2)}, u32[]{:S(2)}) async-start(f32[128,1,384]{2,1,0:T(1,128)} %copy.15), calls=%async_computation | async-start | bytes 393216 | tf_op jit(solution)/shard_map/all_to_all | solution.py:442
  16.3 16.3 %collective-permute-start.2 = (f32[32,8,128]{2,1,0:T(8,128)}, f32[32,8,128]{2,1,0:T(8,128)S(1)}, u32[]{:S(2)}, u32[]{:S(2)}) collective-permute-start(f32[32,8,128]{2,1,0:T(8,128)} %get-tuple-element.12), channel_id=1, source_target_pairs={{16,0},{32,16},{48,32},{64,48},{80,64},{96,80},{112,96},{17,1},{33... | collective-permute-start | bytes 393224 | tf_op jit(solution)/shard_map/ppermute | solution.py:440
  19.3 13.3 %collective-permute-start.3 = (f32[32,8,128]{2,1,0:T(8,128)}, f32[32,8,128]{2,1,0:T(8,128)S(1)}, u32[]{:S(2)}, u32[]{:S(2)}) collective-permute-start(f32[32,8,128]{2,1,0:T(8,128)} %get-tuple-element.13), channel_id=1, source_target_pairs={{0,16},{16,32},{32,48},{48,64},{64,80},{80,96},{96,112},{1,17},{17... | collective-permute-start | bytes 393224 | tf_op jit(solution)/shard_map/ppermute | solution.py:441
  26.9 8.2 %copy-start.6 = (f32[128,1,384]{2,0,1:T(8,128)}, f32[128,1,384]{2,0,1:T(8,128)S(1)}, u32[]{:S(2)}) copy-start(f32[128,1,384]{2,0,1:T(8,128)S(1)} %copy.22) | copy-start | bytes 589828
  26.9 7.0 %collective-permute-start = (f32[128,384]{1,0:T(8,128)S(1)}, f32[128,384]{1,0:T(8,128)S(1)}, u32[]{:S(2)}, u32[]{:S(2)}) collective-permute-start(f32[128,384]{1,0:T(8,128)S(1)} %bitcast.6), channel_id=1, source_target_pairs={{16,0},{32,16},{48,32},{64,48},{80,64},{96,80},{112,96},{17,1},{33... | collective-permute-start | bytes 589832 | tf_op jit(solution)/shard_map/ppermute | solution.py:444
  29.5 5.6 %collective-permute-start.1 = (f32[128,384]{1,0:T(8,128)S(1)}, f32[128,384]{1,0:T(8,128)S(1)}, u32[]{:S(2)}, u32[]{:S(2)}) collective-permute-start(f32[128,384]{1,0:T(8,128)S(1)} %bitcast.7), channel_id=1, source_target_pairs={{0,16},{16,32},{32,48},{48,64},{64,80},{80,96},{96,112},{1,17},{17... | collective-permute-start | bytes 589832 | tf_op jit(solution)/shard_map/ppermute | solution.py:445
  32.6 2.5 %copy-start.9 = (f32[32,8,128]{2,1,0:T(8,128)}, f32[32,8,128]{2,1,0:T(8,128)S(1)}, u32[]{:S(2)}) copy-start(f32[32,8,128]{2,1,0:T(8,128)S(1)} %collective-permute-done.2.sb_ref) | copy-start | bytes 393220
  32.6 2.5 %copy-start.10 = (f32[32,8,128]{2,1,0:T(8,128)}, f32[32,8,128]{2,1,0:T(8,128)S(1)}, u32[]{:S(2)}) copy-start(f32[32,8,128]{2,1,0:T(8,128)S(1)} %collective-permute-done.3.sa_ref) | copy-start | bytes 393220
  33.9 1.2 %copy-start.7 = (f32[128,384]{1,0:T(8,128)}, f32[128,384]{1,0:T(8,128)S(1)}, u32[]{:S(2)}) copy-start(f32[128,384]{1,0:T(8,128)S(1)} %collective-permute-done.below_ref) | copy-start | bytes 589828
  35.1 0.7 copy-start.8
  44.5 5.6 %collective-permute-start.4 = (f32[12,16,128]{2,1,0:T(8,128)}, f32[12,16,128]{2,1,0:T(8,128)S(1)}, u32[]{:S(2)}, u32[]{:S(2)}) collective-permute-start(f32[12,16,128]{2,1,0:T(8,128)} %get-tuple-element.14), channel_id=1, source_target_pairs={{1,0},{2,1},{3,2},{4,3},{5,4},{6,5},{7,6},{8,7},{9,8},{10,9},{11,1... | collective-permute-start | bytes 294920 | tf_op jit(solution)/shard_map/ppermute | solution.py:448
  45.8 5.9 %collective-permute-start.5 = (f32[12,16,128]{2,1,0:T(8,128)}, f32[12,16,128]{2,1,0:T(8,128)S(1)}, u32[]{:S(2)}, u32[]{:S(2)}) collective-permute-start(f32[12,16,128]{2,1,0:T(8,128)} %get-tuple-element.15), channel_id=1, source_target_pairs={{0,1},{1,2},{2,3},{3,4},{4,5},{5,6},{6,7},{7,8},{8,9},{9,10},{10,1... | collective-permute-start | bytes 294920 | tf_op jit(solution)/shard_map/ppermute | solution.py:449
  51.7 1.7 %copy-start = (f32[4,80,16,128]{3,2,1,0:T(8,128)S(1)}, f32[4,80,16,128]{3,2,1,0:T(8,128)}, u32[]{:S(2)}) copy-start(f32[4,80,16,128]{3,2,1,0:T(8,128)} %get-tuple-element.17.tall_hbm) | copy-start | bytes 7864324
  53.5 0.9 %copy-start.2 = (f32[64,8,128]{2,1,0:T(8,128)S(1)}, f32[64,8,128]{2,1,0:T(8,128)}, u32[]{:S(2)}) copy-start(f32[64,8,128]{2,1,0:T(8,128)} %get-tuple-element.16.st_xh) | copy-start | bytes 786436
  54.4 0.7 copy-start.3
  55.1 0.7 copy-start.4
  55.9 0.7 copy-start.5

commit v18 on v17

--- a/solution.py
+++ b/solution.py
@@ -363,7 +363,7 @@
             out.append(r)
         return tuple(out)
 
-    lax.fori_loop(0, levels, forward, (zero,) * species, unroll=4)
+    lax.fori_loop(0, levels, forward, (zero,) * species, unroll=True)
 
     def backward(i, result):
         l = levels - 1 - i
@@ -375,7 +375,7 @@
             out.append(r)
         return tuple(out)
 
-    surface = lax.fori_loop(0, levels, backward, (zero,) * species, unroll=4)
+    surface = lax.fori_loop(0, levels, backward, (zero,) * species, unroll=True)
     for s in range(species):
         ss_ref[s] = ss_ref[s] + prior_ref[s] * surface[s]
 

time: 88 us -> 87.2 us (level)
  no operation moved by 1% of the time
where the time goes in v18:
time: 87.2 us; the launch traced here: 86.6 us
  starting transfers between devices  28.1 us (32%)
  blocking collectives  20.6 us (24%)
  Pallas kernels  18.7 us (21%)
  local copies, waits for them, and re-layouts  8.7 us (10%)
  waiting for transfers between devices  8.28 us (9%)
  other arithmetic  0.93 us (1%)
    all_to_all x1, blocking collectives, local(): lax.all_to_all(partial.reshape(species, devices, nreg // devices), ('gx',...  20.6 us
    all_to_all x1, starting transfers between devices, local(): received = lax.all_to_all(placed, ('gx', 'gy'), 0, 0, tiled=True)  11.5 us
    pallas_call x1, Pallas kernels, forcing_call(): pl.pallas_call(functools.partial(_forcing_kernel, species, kernel, levels...  8.73 us
    pallas_call x1, Pallas kernels, steps_call(): pl.pallas_call(functools.partial(_steps_kernel, steps, species, levels, n...  7.64 us
    unnamed x23, local copies, waits for them, and re-layouts  5.52 us
    ppermute x1, starting transfers between devices, local(): left = lax.ppermute(left, 'gy', up_y)  4.17 us
    all_to_all x1, waiting for transfers between devices, local(): received = lax.all_to_all(placed, ('gx', 'gy'), 0, 0, tiled=True)  4.05 us
    ppermute x1, starting transfers between devices, local(): st_below = lax.ppermute(st_lo, 'gx', down_x)  2.98 us
  transfers between devices with their start and end apart: 7, of which 5 were waited for; matrix products, arithmetic and copies ran while one was open for 1% of the time, Pallas kernels for 0%

profile of v18, /device:TPU:1, one launch (start us, length us, event | category | flops | bytes accessed | tf_op | source)
XLA Modules:
  0.0 86.6 jit_solution(7232402842747332196)
XLA Ops:
  0.6 0.0 copy-start.1
  0.6 2.4 %shard_map.104 = (f32[128,384]{1,0:T(8,128)}, f32[32,8,128]{2,1,0:T(8,128)}, f32[32,8,128]{2,1,0:T(8,128)}) custom-call(f32[4,32,128]{2,1,0:T(8,128)} %adj_ref.1, s32[4,128]{1,0:T(4,128)} %bitcast.10, s32[4,128]{1,0:T(4,128)} %col_ref.1, s32[4,128]{1,0:T(4,128)} %lev_ref.1, f32[4,8,128]{2,1,0:T(8,128)} %wx_ref.5, f32[4,8,128]{2,1,0:T(8,128)} %wy_ref.5, ...), custom_call_target="tpu_custom_call" | custom-call | tf_op jit(solution)/shard_map/pallas_call | solution.py:78
  3.0 1.8 %copy.15 = f32[128,1,384]{2,1,0:T(1,128)} copy(f32[128,1,384]{2,0,1:T(8,128)} %bitcast.9) | data formatting | bytes 393216 | tf_op jit(solution)/shard_map/all_to_all | solution.py:442
  4.8 11.5 %all-to-all-start = ((f32[128,1,384]{2,1,0:T(1,128)}), f32[128,1,384]{2,1,0:T(1,128)S(1)}, u32[]{:S(2)}, u32[]{:S(2)}) async-start(f32[128,1,384]{2,1,0:T(1,128)} %copy.15), calls=%async_computation | async-start | bytes 393216 | tf_op jit(solution)/shard_map/all_to_all | solution.py:442
  16.3 3.0 %collective-permute-start.2 = (f32[32,8,128]{2,1,0:T(8,128)}, f32[32,8,128]{2,1,0:T(8,128)S(1)}, u32[]{:S(2)}, u32[]{:S(2)}) collective-permute-start(f32[32,8,128]{2,1,0:T(8,128)} %get-tuple-element.12), channel_id=1, source_target_pairs={{16,0},{32,16},{48,32},{64,48},{80,64},{96,80},{112,96},{17,1},{33... | collective-permute-start | bytes 393224 | tf_op jit(solution)/shard_map/ppermute | solution.py:440
  19.3 2.6 %collective-permute-start.3 = (f32[32,8,128]{2,1,0:T(8,128)}, f32[32,8,128]{2,1,0:T(8,128)S(1)}, u32[]{:S(2)}, u32[]{:S(2)}) collective-permute-start(f32[32,8,128]{2,1,0:T(8,128)} %get-tuple-element.13), channel_id=1, source_target_pairs={{0,16},{16,32},{32,48},{48,64},{64,80},{80,96},{96,112},{1,17},{17... | collective-permute-start | bytes 393224 | tf_op jit(solution)/shard_map/ppermute | solution.py:441
  21.9 0.8 slice.3
  22.7 0.1 eq.31
  22.8 4.0 %all-to-all-done = f32[128,1,384]{2,1,0:T(1,128)S(1)} async-done(((f32[128,1,384]{2,1,0:T(1,128)}), f32[128,1,384]{2,1,0:T(1,128)S(1)}, u32[]{:S(2)}, u32[]{:S(2)}) %all-to-all-start) | async-done | bytes 196640 | tf_op jit(solution)/shard_map/all_to_all | solution.py:442
  26.9 0.0 copy-start.6
  26.9 2.6 %collective-permute-start = (f32[128,384]{1,0:T(8,128)S(1)}, f32[128,384]{1,0:T(8,128)S(1)}, u32[]{:S(2)}, u32[]{:S(2)}) collective-permute-start(f32[128,384]{1,0:T(8,128)S(1)} %bitcast.6), channel_id=1, source_target_pairs={{16,0},{32,16},{48,32},{64,48},{80,64},{96,80},{112,96},{17,1},{33... | collective-permute-start | bytes 589832 | tf_op jit(solution)/shard_map/ppermute | solution.py:444
  29.5 3.0 %collective-permute-start.1 = (f32[128,384]{1,0:T(8,128)S(1)}, f32[128,384]{1,0:T(8,128)S(1)}, u32[]{:S(2)}, u32[]{:S(2)}) collective-permute-start(f32[128,384]{1,0:T(8,128)S(1)} %bitcast.7), channel_id=1, source_target_pairs={{0,16},{16,32},{32,48},{48,64},{64,80},{80,96},{96,112},{1,17},{17... | collective-permute-start | bytes 589832 | tf_op jit(solution)/shard_map/ppermute | solution.py:445
  32.5 0.1 and_convert_fusion.mask_ref
  32.6 0.0 collective-permute-done.2.sb_ref
  32.6 0.0 copy-start.9
  32.6 0.0 collective-permute-done.3.sa_ref
  32.6 0.0 copy-start.10
  32.6 1.3 %collective-permute-done.below_ref = f32[128,384]{1,0:T(8,128)S(1)} collective-permute-done((f32[128,384]{1,0:T(8,128)S(1)}, f32[128,384]{1,0:T(8,128)S(1)}, u32[]{:S(2)}, u32[]{:S(2)}) %collective-permute-start) | collective-permute-done | bytes 196640 | tf_op jit(solution)/shard_map/ppermute | solution.py:444
  33.9 0.0 copy-start.7
  33.9 1.2 %collective-permute-done.1.above_ref = f32[128,384]{1,0:T(8,128)S(1)} collective-permute-done((f32[128,384]{1,0:T(8,128)S(1)}, f32[128,384]{1,0:T(8,128)S(1)}, u32[]{:S(2)}, u32[]{:S(2)}) %collective-permute-start.1) | collective-permute-done | bytes 196640 | tf_op jit(solution)/shard_map/ppermute | solution.py:445
  35.1 0.0 copy-done.6
  35.1 0.0 copy-done.9
  35.1 0.0 copy-done.10
  35.1 0.0 copy-done.7
  35.1 0.0 copy-start.8
  35.1 0.7 copy-done.8
  35.8 8.7 %shard_map.105 = (f32[4,80,16,128]{3,2,1,0:T(8,128)}, f32[12,16,128]{2,1,0:T(8,128)}, f32[12,16,128]{2,1,0:T(8,128)}, f32[64,8,128]{2,1,0:T(8,128)}) custom-call(f32[128,384]{1,0:T(8,128)} %bitcast.8, f32[128,384]{1,0:T(8,128)} %copy-done.7, f32[128,384]{1,0:T(8,128)} %copy-done.8, f32[4,8,128]{2,1,0:T(8,128)} %wx_ref.5, f32[4,8,128]{2,1,0:T(8,128)} %wy_ref.5, ...), custom_call_target="tpu_custom_call" | custom-call | tf_op jit(solution)/shard_map/pallas_call | solution.py:197
  44.5 1.3 %collective-permute-start.4 = (f32[12,16,128]{2,1,0:T(8,128)}, f32[12,16,128]{2,1,0:T(8,128)S(1)}, u32[]{:S(2)}, u32[]{:S(2)}) collective-permute-start(f32[12,16,128]{2,1,0:T(8,128)} %get-tuple-element.14), channel_id=1, source_target_pairs={{1,0},{2,1},{3,2},{4,3},{5,4},{6,5},{7,6},{8,7},{9,8},{10,9},{11,1... | collective-permute-start | bytes 294920 | tf_op jit(solution)/shard_map/ppermute | solution.py:448
  45.8 4.2 %collective-permute-start.5 = (f32[12,16,128]{2,1,0:T(8,128)}, f32[12,16,128]{2,1,0:T(8,128)S(1)}, u32[]{:S(2)}, u32[]{:S(2)}) collective-permute-start(f32[12,16,128]{2,1,0:T(8,128)} %get-tuple-element.15), channel_id=1, source_target_pairs={{0,1},{1,2},{2,3},{3,4},{4,5},{5,6},{6,7},{7,8},{8,9},{9,10},{10,1... | collective-permute-start | bytes 294920 | tf_op jit(solution)/shard_map/ppermute | solution.py:449
  50.0 0.1 collective-permute-done.4.right_ref
  50.1 1.7 %collective-permute-done.5.left_ref = f32[12,16,128]{2,1,0:T(8,128)S(1)} collective-permute-done((f32[12,16,128]{2,1,0:T(8,128)}, f32[12,16,128]{2,1,0:T(8,128)S(1)}, u32[]{:S(2)}, u32[]{:S(2)}) %collective-permute-start.5) | collective-permute-done | bytes 98336 | tf_op jit(solution)/shard_map/ppermute | solution.py:449
  51.7 0.0 copy-done.1
  51.7 0.0 copy-start
  51.7 1.7 %copy-done = f32[4,80,16,128]{3,2,1,0:T(8,128)S(1)} copy-done((f32[4,80,16,128]{3,2,1,0:T(8,128)S(1)}, f32[4,80,16,128]{3,2,1,0:T(8,128)}, u32[]{:S(2)}) %copy-start) | copy-done | bytes 2621464
  53.5 0.0 copy-start.2
  53.5 0.9 %copy-done.2 = f32[64,8,128]{2,1,0:T(8,128)S(1)} copy-done((f32[64,8,128]{2,1,0:T(8,128)S(1)}, f32[64,8,128]{2,1,0:T(8,128)}, u32[]{:S(2)}) %copy-start.2) | copy-done | bytes 262168
  54.4 0.0 copy-start.3
  54.4 0.7 copy-done.3
  55.1 0.0 copy-start.4
  55.1 0.7 copy-done.4
  55.9 0.0 copy-start.5
  55.9 0.7 copy-done.5
  56.6 7.6 %shard_map.106 = (f32[2,40,8,128]{3,2,1,0:T(8,128)}, f32[2,8,128]{2,1,0:T(8,128)S(1)}) custom-call(f32[12,16,128]{2,1,0:T(8,128)S(1)} %collective-permute-done.4.right_ref, f32[12,16,128]{2,1,0:T(8,128)S(1)} %collective-permute-done.5.left_ref, f32[4,8,128]{2,1,0:T(8,128)S(1)} %copy-done.3, f32[4,8,128]{2,1,0:T(8,128)S(1)} %copy-done.4, ...), custom_call_target="tpu_custom_call" | custom-call | tf_op jit(solution)/shard_map/pallas_call | solution.py:390
  64.2 0.3 reshape.84
  64.5 0.1 reduce_sum.18
  64.6 0.1 reshape.86
  64.7 0.5 fusion
  65.1 0.2 copy.16
  65.3 20.6 %all_to_all.16 = f32[2,128,8]{2,0,1:T(2,128)S(1)} all-to-all(f32[2,128,8]{2,0,1:T(2,128)S(1)} %copy.16), channel_id=1, replica_groups=mesh['gx'=8,'gy'=16] {'gx','gy'}, dimensions={1} | all-to-all | bytes 16384 | tf_op jit(solution)/shard_map/all_to_all | solution.py:470
  85.9 0.7 reduce_sum.19
  (5 shorter events, 0.0 us)
Async XLA Ops:
  0.6 51.1 %copy-start.1 = (f32[39,8,128]{2,1,0:T(8,128)S(1)}, f32[39,8,128]{2,1,0:T(8,128)}, u32[]{:S(2)}) copy-start(f32[39,8,128]{2,1,0:T(8,128)} %diff_ref.5) | copy-start | bytes 479236
  4.8 22.1 %all-to-all-start = ((f32[128,1,384]{2,1,0:T(1,128)}), f32[128,1,384]{2,1,0:T(1,128)S(1)}, u32[]{:S(2)}, u32[]{:S(2)}) async-start(f32[128,1,384]{2,1,0:T(1,128)} %copy.15), calls=%async_computation | async-start | bytes 393216 | tf_op jit(solution)/shard_map/all_to_all | solution.py:442
  16.3 16.3 %collective-permute-start.2 = (f32[32,8,128]{2,1,0:T(8,128)}, f32[32,8,128]{2,1,0:T(8,128)S(1)}, u32[]{:S(2)}, u32[]{:S(2)}) collective-permute-start(f32[32,8,128]{2,1,0:T(8,128)} %get-tuple-element.12), channel_id=1, source_target_pairs={{16,0},{32,16},{48,32},{64,48},{80,64},{96,80},{112,96},{17,1},{33... | collective-permute-start | bytes 393224 | tf_op jit(solution)/shard_map/ppermute | solution.py:440
  19.3 13.3 %collective-permute-start.3 = (f32[32,8,128]{2,1,0:T(8,128)}, f32[32,8,128]{2,1,0:T(8,128)S(1)}, u32[]{:S(2)}, u32[]{:S(2)}) collective-permute-start(f32[32,8,128]{2,1,0:T(8,128)} %get-tuple-element.13), channel_id=1, source_target_pairs={{0,16},{16,32},{32,48},{48,64},{64,80},{80,96},{96,112},{1,17},{17... | collective-permute-start | bytes 393224 | tf_op jit(solution)/shard_map/ppermute | solution.py:441
  26.9 8.2 %copy-start.6 = (f32[128,1,384]{2,0,1:T(8,128)}, f32[128,1,384]{2,0,1:T(8,128)S(1)}, u32[]{:S(2)}) copy-start(f32[128,1,384]{2,0,1:T(8,128)S(1)} %copy.22) | copy-start | bytes 589828
  26.9 7.0 %collective-permute-start = (f32[128,384]{1,0:T(8,128)S(1)}, f32[128,384]{1,0:T(8,128)S(1)}, u32[]{:S(2)}, u32[]{:S(2)}) collective-permute-start(f32[128,384]{1,0:T(8,128)S(1)} %bitcast.6), channel_id=1, source_target_pairs={{16,0},{32,16},{48,32},{64,48},{80,64},{96,80},{112,96},{17,1},{33... | collective-permute-start | bytes 589832 | tf_op jit(solution)/shard_map/ppermute | solution.py:444
  29.5 5.6 %collective-permute-start.1 = (f32[128,384]{1,0:T(8,128)S(1)}, f32[128,384]{1,0:T(8,128)S(1)}, u32[]{:S(2)}, u32[]{:S(2)}) collective-permute-start(f32[128,384]{1,0:T(8,128)S(1)} %bitcast.7), channel_id=1, source_target_pairs={{0,16},{16,32},{32,48},{48,64},{64,80},{80,96},{96,112},{1,17},{17... | collective-permute-start | bytes 589832 | tf_op jit(solution)/shard_map/ppermute | solution.py:445
  32.6 2.5 %copy-start.9 = (f32[32,8,128]{2,1,0:T(8,128)}, f32[32,8,128]{2,1,0:T(8,128)S(1)}, u32[]{:S(2)}) copy-start(f32[32,8,128]{2,1,0:T(8,128)S(1)} %collective-permute-done.2.sb_ref) | copy-start | bytes 393220
  32.6 2.5 %copy-start.10 = (f32[32,8,128]{2,1,0:T(8,128)}, f32[32,8,128]{2,1,0:T(8,128)S(1)}, u32[]{:S(2)}) copy-start(f32[32,8,128]{2,1,0:T(8,128)S(1)} %collective-permute-done.3.sa_ref) | copy-start | bytes 393220
  33.9 1.2 %copy-start.7 = (f32[128,384]{1,0:T(8,128)}, f32[128,384]{1,0:T(8,128)S(1)}, u32[]{:S(2)}) copy-start(f32[128,384]{1,0:T(8,128)S(1)} %collective-permute-done.below_ref) | copy-start | bytes 589828
  35.1 0.7 copy-start.8
  44.5 5.6 %collective-permute-start.4 = (f32[12,16,128]{2,1,0:T(8,128)}, f32[12,16,128]{2,1,0:T(8,128)S(1)}, u32[]{:S(2)}, u32[]{:S(2)}) collective-permute-start(f32[12,16,128]{2,1,0:T(8,128)} %get-tuple-element.14), channel_id=1, source_target_pairs={{1,0},{2,1},{3,2},{4,3},{5,4},{6,5},{7,6},{8,7},{9,8},{10,9},{11,1... | collective-permute-start | bytes 294920 | tf_op jit(solution)/shard_map/ppermute | solution.py:448
  45.8 5.9 %collective-permute-start.5 = (f32[12,16,128]{2,1,0:T(8,128)}, f32[12,16,128]{2,1,0:T(8,128)S(1)}, u32[]{:S(2)}, u32[]{:S(2)}) collective-permute-start(f32[12,16,128]{2,1,0:T(8,128)} %get-tuple-element.15), channel_id=1, source_target_pairs={{0,1},{1,2},{2,3},{3,4},{4,5},{5,6},{6,7},{7,8},{8,9},{9,10},{10,1... | collective-permute-start | bytes 294920 | tf_op jit(solution)/shard_map/ppermute | solution.py:449
  51.7 1.7 %copy-start = (f32[4,80,16,128]{3,2,1,0:T(8,128)S(1)}, f32[4,80,16,128]{3,2,1,0:T(8,128)}, u32[]{:S(2)}) copy-start(f32[4,80,16,128]{3,2,1,0:T(8,128)} %get-tuple-element.17.tall_hbm) | copy-start | bytes 7864324
  53.5 0.9 %copy-start.2 = (f32[64,8,128]{2,1,0:T(8,128)S(1)}, f32[64,8,128]{2,1,0:T(8,128)}, u32[]{:S(2)}) copy-start(f32[64,8,128]{2,1,0:T(8,128)} %get-tuple-element.16.st_xh) | copy-start | bytes 786436
  54.4 0.7 copy-start.3
  55.1 0.7 copy-start.4
  55.9 0.7 copy-start.5

commit v19 on v18

--- a/solution.py
+++ b/solution.py
@@ -267,7 +267,7 @@
                     state_ref[s, l] = jnp.where(inside, state_ref[s, l], 0.0)
                     return carry
 
-                lax.fori_loop(0, levels, assemble, 0, unroll=4)
+                lax.fori_loop(0, levels, assemble, 0, unroll=True)
         if not last:
             loads[k - 1].wait()
 

time: 87.2 us -> 87 us (level)
  no operation moved by 1% of the time
where the time goes in v19:
time: 87 us; the launch traced here: 86.4 us
  starting transfers between devices  28.1 us (32%)
  blocking collectives  20.6 us (24%)
  Pallas kernels  18.5 us (21%)
  local copies, waits for them, and re-layouts  8.7 us (10%)
  waiting for transfers between devices  8.28 us (10%)
  other arithmetic  0.93 us (1%)
    all_to_all x1, blocking collectives, local(): lax.all_to_all(partial.reshape(species, devices, nreg // devices), ('gx',...  20.6 us
    all_to_all x1, starting transfers between devices, local(): received = lax.all_to_all(placed, ('gx', 'gy'), 0, 0, tiled=True)  11.5 us
    pallas_call x1, Pallas kernels, forcing_call(): pl.pallas_call(functools.partial(_forcing_kernel, species, kernel, levels...  8.73 us
    pallas_call x1, Pallas kernels, steps_call(): pl.pallas_call(functools.partial(_steps_kernel, steps, species, levels, n...  7.44 us
    unnamed x23, local copies, waits for them, and re-layouts  5.52 us
    ppermute x1, starting transfers between devices, local(): left = lax.ppermute(left, 'gy', up_y)  4.17 us
    all_to_all x1, waiting for transfers between devices, local(): received = lax.all_to_all(placed, ('gx', 'gy'), 0, 0, tiled=True)  4.05 us
    ppermute x1, starting transfers between devices, local(): st_below = lax.ppermute(st_lo, 'gx', down_x)  2.98 us
  transfers between devices with their start and end apart: 7, of which 5 were waited for; matrix products, arithmetic and copies ran while one was open for 1% of the time, Pallas kernels for 0%

profile of v19, /device:TPU:1, one launch (start us, length us, event | category | flops | bytes accessed | tf_op | source)
XLA Modules:
  0.0 86.4 jit_solution(17042910202053774454)
XLA Ops:
  0.6 0.0 copy-start.1
  0.6 2.4 %shard_map.104 = (f32[128,384]{1,0:T(8,128)}, f32[32,8,128]{2,1,0:T(8,128)}, f32[32,8,128]{2,1,0:T(8,128)}) custom-call(f32[4,32,128]{2,1,0:T(8,128)} %adj_ref.1, s32[4,128]{1,0:T(4,128)} %bitcast.10, s32[4,128]{1,0:T(4,128)} %col_ref.1, s32[4,128]{1,0:T(4,128)} %lev_ref.1, f32[4,8,128]{2,1,0:T(8,128)} %wx_ref.5, f32[4,8,128]{2,1,0:T(8,128)} %wy_ref.5, ...), custom_call_target="tpu_custom_call" | custom-call | tf_op jit(solution)/shard_map/pallas_call | solution.py:78
  3.0 1.8 %copy.15 = f32[128,1,384]{2,1,0:T(1,128)} copy(f32[128,1,384]{2,0,1:T(8,128)} %bitcast.9) | data formatting | bytes 393216 | tf_op jit(solution)/shard_map/all_to_all | solution.py:442
  4.8 11.5 %all-to-all-start = ((f32[128,1,384]{2,1,0:T(1,128)}), f32[128,1,384]{2,1,0:T(1,128)S(1)}, u32[]{:S(2)}, u32[]{:S(2)}) async-start(f32[128,1,384]{2,1,0:T(1,128)} %copy.15), calls=%async_computation | async-start | bytes 393216 | tf_op jit(solution)/shard_map/all_to_all | solution.py:442
  16.3 3.0 %collective-permute-start.2 = (f32[32,8,128]{2,1,0:T(8,128)}, f32[32,8,128]{2,1,0:T(8,128)S(1)}, u32[]{:S(2)}, u32[]{:S(2)}) collective-permute-start(f32[32,8,128]{2,1,0:T(8,128)} %get-tuple-element.12), channel_id=1, source_target_pairs={{16,0},{32,16},{48,32},{64,48},{80,64},{96,80},{112,96},{17,1},{33... | collective-permute-start | bytes 393224 | tf_op jit(solution)/shard_map/ppermute | solution.py:440
  19.3 2.6 %collective-permute-start.3 = (f32[32,8,128]{2,1,0:T(8,128)}, f32[32,8,128]{2,1,0:T(8,128)S(1)}, u32[]{:S(2)}, u32[]{:S(2)}) collective-permute-start(f32[32,8,128]{2,1,0:T(8,128)} %get-tuple-element.13), channel_id=1, source_target_pairs={{0,16},{16,32},{32,48},{48,64},{64,80},{80,96},{96,112},{1,17},{17... | collective-permute-start | bytes 393224 | tf_op jit(solution)/shard_map/ppermute | solution.py:441
  21.9 0.8 slice.3
  22.7 0.1 eq.31
  22.8 4.0 %all-to-all-done = f32[128,1,384]{2,1,0:T(1,128)S(1)} async-done(((f32[128,1,384]{2,1,0:T(1,128)}), f32[128,1,384]{2,1,0:T(1,128)S(1)}, u32[]{:S(2)}, u32[]{:S(2)}) %all-to-all-start) | async-done | bytes 196640 | tf_op jit(solution)/shard_map/all_to_all | solution.py:442
  26.9 0.0 copy-start.6
  26.9 2.6 %collective-permute-start = (f32[128,384]{1,0:T(8,128)S(1)}, f32[128,384]{1,0:T(8,128)S(1)}, u32[]{:S(2)}, u32[]{:S(2)}) collective-permute-start(f32[128,384]{1,0:T(8,128)S(1)} %bitcast.6), channel_id=1, source_target_pairs={{16,0},{32,16},{48,32},{64,48},{80,64},{96,80},{112,96},{17,1},{33... | collective-permute-start | bytes 589832 | tf_op jit(solution)/shard_map/ppermute | solution.py:444
  29.5 3.0 %collective-permute-start.1 = (f32[128,384]{1,0:T(8,128)S(1)}, f32[128,384]{1,0:T(8,128)S(1)}, u32[]{:S(2)}, u32[]{:S(2)}) collective-permute-start(f32[128,384]{1,0:T(8,128)S(1)} %bitcast.7), channel_id=1, source_target_pairs={{0,16},{16,32},{32,48},{48,64},{64,80},{80,96},{96,112},{1,17},{17... | collective-permute-start | bytes 589832 | tf_op jit(solution)/shard_map/ppermute | solution.py:445
  32.5 0.1 and_convert_fusion.mask_ref
  32.6 0.0 collective-permute-done.2.sb_ref
  32.6 0.0 copy-start.9
  32.6 0.0 collective-permute-done.3.sa_ref
  32.6 0.0 copy-start.10
  32.6 1.3 %collective-permute-done.below_ref = f32[128,384]{1,0:T(8,128)S(1)} collective-permute-done((f32[128,384]{1,0:T(8,128)S(1)}, f32[128,384]{1,0:T(8,128)S(1)}, u32[]{:S(2)}, u32[]{:S(2)}) %collective-permute-start) | collective-permute-done | bytes 196640 | tf_op jit(solution)/shard_map/ppermute | solution.py:444
  33.9 0.0 copy-start.7
  33.9 1.2 %collective-permute-done.1.above_ref = f32[128,384]{1,0:T(8,128)S(1)} collective-permute-done((f32[128,384]{1,0:T(8,128)S(1)}, f32[128,384]{1,0:T(8,128)S(1)}, u32[]{:S(2)}, u32[]{:S(2)}) %collective-permute-start.1) | collective-permute-done | bytes 196640 | tf_op jit(solution)/shard_map/ppermute | solution.py:445
  35.1 0.0 copy-done.6
  35.1 0.0 copy-done.9
  35.1 0.0 copy-done.10
  35.1 0.0 copy-done.7
  35.1 0.0 copy-start.8
  35.1 0.7 copy-done.8
  35.8 8.7 %shard_map.105 = (f32[4,80,16,128]{3,2,1,0:T(8,128)}, f32[12,16,128]{2,1,0:T(8,128)}, f32[12,16,128]{2,1,0:T(8,128)}, f32[64,8,128]{2,1,0:T(8,128)}) custom-call(f32[128,384]{1,0:T(8,128)} %bitcast.8, f32[128,384]{1,0:T(8,128)} %copy-done.7, f32[128,384]{1,0:T(8,128)} %copy-done.8, f32[4,8,128]{2,1,0:T(8,128)} %wx_ref.5, f32[4,8,128]{2,1,0:T(8,128)} %wy_ref.5, ...), custom_call_target="tpu_custom_call" | custom-call | tf_op jit(solution)/shard_map/pallas_call | solution.py:197
  44.5 1.3 %collective-permute-start.4 = (f32[12,16,128]{2,1,0:T(8,128)}, f32[12,16,128]{2,1,0:T(8,128)S(1)}, u32[]{:S(2)}, u32[]{:S(2)}) collective-permute-start(f32[12,16,128]{2,1,0:T(8,128)} %get-tuple-element.14), channel_id=1, source_target_pairs={{1,0},{2,1},{3,2},{4,3},{5,4},{6,5},{7,6},{8,7},{9,8},{10,9},{11,1... | collective-permute-start | bytes 294920 | tf_op jit(solution)/shard_map/ppermute | solution.py:448
  45.8 4.2 %collective-permute-start.5 = (f32[12,16,128]{2,1,0:T(8,128)}, f32[12,16,128]{2,1,0:T(8,128)S(1)}, u32[]{:S(2)}, u32[]{:S(2)}) collective-permute-start(f32[12,16,128]{2,1,0:T(8,128)} %get-tuple-element.15), channel_id=1, source_target_pairs={{0,1},{1,2},{2,3},{3,4},{4,5},{5,6},{6,7},{7,8},{8,9},{9,10},{10,1... | collective-permute-start | bytes 294920 | tf_op jit(solution)/shard_map/ppermute | solution.py:449
  50.0 0.1 collective-permute-done.4.right_ref
  50.1 1.7 %collective-permute-done.5.left_ref = f32[12,16,128]{2,1,0:T(8,128)S(1)} collective-permute-done((f32[12,16,128]{2,1,0:T(8,128)}, f32[12,16,128]{2,1,0:T(8,128)S(1)}, u32[]{:S(2)}, u32[]{:S(2)}) %collective-permute-start.5) | collective-permute-done | bytes 98336 | tf_op jit(solution)/shard_map/ppermute | solution.py:449
  51.7 0.0 copy-done.1
  51.7 0.0 copy-start
  51.7 1.7 %copy-done = f32[4,80,16,128]{3,2,1,0:T(8,128)S(1)} copy-done((f32[4,80,16,128]{3,2,1,0:T(8,128)S(1)}, f32[4,80,16,128]{3,2,1,0:T(8,128)}, u32[]{:S(2)}) %copy-start) | copy-done | bytes 2621464
  53.5 0.0 copy-start.2
  53.5 0.9 %copy-done.2 = f32[64,8,128]{2,1,0:T(8,128)S(1)} copy-done((f32[64,8,128]{2,1,0:T(8,128)S(1)}, f32[64,8,128]{2,1,0:T(8,128)}, u32[]{:S(2)}) %copy-start.2) | copy-done | bytes 262168
  54.4 0.0 copy-start.3
  54.4 0.7 copy-done.3
  55.1 0.0 copy-start.4
  55.1 0.7 copy-done.4
  55.9 0.0 copy-start.5
  55.9 0.7 copy-done.5
  56.6 7.4 %shard_map.106 = (f32[2,40,8,128]{3,2,1,0:T(8,128)}, f32[2,8,128]{2,1,0:T(8,128)S(1)}) custom-call(f32[12,16,128]{2,1,0:T(8,128)S(1)} %collective-permute-done.4.right_ref, f32[12,16,128]{2,1,0:T(8,128)S(1)} %collective-permute-done.5.left_ref, f32[4,8,128]{2,1,0:T(8,128)S(1)} %copy-done.3, f32[4,8,128]{2,1,0:T(8,128)S(1)} %copy-done.4, ...), custom_call_target="tpu_custom_call" | custom-call | tf_op jit(solution)/shard_map/pallas_call | solution.py:390
  64.0 0.3 reshape.84
  64.3 0.1 reduce_sum.18
  64.4 0.1 reshape.86
  64.5 0.5 fusion
  64.9 0.2 copy.16
  65.1 20.6 %all_to_all.16 = f32[2,128,8]{2,0,1:T(2,128)S(1)} all-to-all(f32[2,128,8]{2,0,1:T(2,128)S(1)} %copy.16), channel_id=1, replica_groups=mesh['gx'=8,'gy'=16] {'gx','gy'}, dimensions={1} | all-to-all | bytes 16384 | tf_op jit(solution)/shard_map/all_to_all | solution.py:470
  85.7 0.7 reduce_sum.19
  (5 shorter events, 0.0 us)
Async XLA Ops:
  0.6 51.1 %copy-start.1 = (f32[39,8,128]{2,1,0:T(8,128)S(1)}, f32[39,8,128]{2,1,0:T(8,128)}, u32[]{:S(2)}) copy-start(f32[39,8,128]{2,1,0:T(8,128)} %diff_ref.5) | copy-start | bytes 479236
  4.8 22.1 %all-to-all-start = ((f32[128,1,384]{2,1,0:T(1,128)}), f32[128,1,384]{2,1,0:T(1,128)S(1)}, u32[]{:S(2)}, u32[]{:S(2)}) async-start(f32[128,1,384]{2,1,0:T(1,128)} %copy.15), calls=%async_computation | async-start | bytes 393216 | tf_op jit(solution)/shard_map/all_to_all | solution.py:442
  16.3 16.3 %collective-permute-start.2 = (f32[32,8,128]{2,1,0:T(8,128)}, f32[32,8,128]{2,1,0:T(8,128)S(1)}, u32[]{:S(2)}, u32[]{:S(2)}) collective-permute-start(f32[32,8,128]{2,1,0:T(8,128)} %get-tuple-element.12), channel_id=1, source_target_pairs={{16,0},{32,16},{48,32},{64,48},{80,64},{96,80},{112,96},{17,1},{33... | collective-permute-start | bytes 393224 | tf_op jit(solution)/shard_map/ppermute | solution.py:440
  19.3 13.3 %collective-permute-start.3 = (f32[32,8,128]{2,1,0:T(8,128)}, f32[32,8,128]{2,1,0:T(8,128)S(1)}, u32[]{:S(2)}, u32[]{:S(2)}) collective-permute-start(f32[32,8,128]{2,1,0:T(8,128)} %get-tuple-element.13), channel_id=1, source_target_pairs={{0,16},{16,32},{32,48},{48,64},{64,80},{80,96},{96,112},{1,17},{17... | collective-permute-start | bytes 393224 | tf_op jit(solution)/shard_map/ppermute | solution.py:441
  26.9 8.2 %copy-start.6 = (f32[128,1,384]{2,0,1:T(8,128)}, f32[128,1,384]{2,0,1:T(8,128)S(1)}, u32[]{:S(2)}) copy-start(f32[128,1,384]{2,0,1:T(8,128)S(1)} %copy.22) | copy-start | bytes 589828
  26.9 7.0 %collective-permute-start = (f32[128,384]{1,0:T(8,128)S(1)}, f32[128,384]{1,0:T(8,128)S(1)}, u32[]{:S(2)}, u32[]{:S(2)}) collective-permute-start(f32[128,384]{1,0:T(8,128)S(1)} %bitcast.6), channel_id=1, source_target_pairs={{16,0},{32,16},{48,32},{64,48},{80,64},{96,80},{112,96},{17,1},{33... | collective-permute-start | bytes 589832 | tf_op jit(solution)/shard_map/ppermute | solution.py:444
  29.5 5.6 %collective-permute-start.1 = (f32[128,384]{1,0:T(8,128)S(1)}, f32[128,384]{1,0:T(8,128)S(1)}, u32[]{:S(2)}, u32[]{:S(2)}) collective-permute-start(f32[128,384]{1,0:T(8,128)S(1)} %bitcast.7), channel_id=1, source_target_pairs={{0,16},{16,32},{32,48},{48,64},{64,80},{80,96},{96,112},{1,17},{17... | collective-permute-start | bytes 589832 | tf_op jit(solution)/shard_map/ppermute | solution.py:445
  32.6 2.5 %copy-start.9 = (f32[32,8,128]{2,1,0:T(8,128)}, f32[32,8,128]{2,1,0:T(8,128)S(1)}, u32[]{:S(2)}) copy-start(f32[32,8,128]{2,1,0:T(8,128)S(1)} %collective-permute-done.2.sb_ref) | copy-start | bytes 393220
  32.6 2.5 %copy-start.10 = (f32[32,8,128]{2,1,0:T(8,128)}, f32[32,8,128]{2,1,0:T(8,128)S(1)}, u32[]{:S(2)}) copy-start(f32[32,8,128]{2,1,0:T(8,128)S(1)} %collective-permute-done.3.sa_ref) | copy-start | bytes 393220
  33.9 1.2 %copy-start.7 = (f32[128,384]{1,0:T(8,128)}, f32[128,384]{1,0:T(8,128)S(1)}, u32[]{:S(2)}) copy-start(f32[128,384]{1,0:T(8,128)S(1)} %collective-permute-done.below_ref) | copy-start | bytes 589828
  35.1 0.7 copy-start.8
  44.5 5.6 %collective-permute-start.4 = (f32[12,16,128]{2,1,0:T(8,128)}, f32[12,16,128]{2,1,0:T(8,128)S(1)}, u32[]{:S(2)}, u32[]{:S(2)}) collective-permute-start(f32[12,16,128]{2,1,0:T(8,128)} %get-tuple-element.14), channel_id=1, source_target_pairs={{1,0},{2,1},{3,2},{4,3},{5,4},{6,5},{7,6},{8,7},{9,8},{10,9},{11,1... | collective-permute-start | bytes 294920 | tf_op jit(solution)/shard_map/ppermute | solution.py:448
  45.8 5.9 %collective-permute-start.5 = (f32[12,16,128]{2,1,0:T(8,128)}, f32[12,16,128]{2,1,0:T(8,128)S(1)}, u32[]{:S(2)}, u32[]{:S(2)}) collective-permute-start(f32[12,16,128]{2,1,0:T(8,128)} %get-tuple-element.15), channel_id=1, source_target_pairs={{0,1},{1,2},{2,3},{3,4},{4,5},{5,6},{6,7},{7,8},{8,9},{9,10},{10,1... | collective-permute-start | bytes 294920 | tf_op jit(solution)/shard_map/ppermute | solution.py:449
  51.7 1.7 %copy-start = (f32[4,80,16,128]{3,2,1,0:T(8,128)S(1)}, f32[4,80,16,128]{3,2,1,0:T(8,128)}, u32[]{:S(2)}) copy-start(f32[4,80,16,128]{3,2,1,0:T(8,128)} %get-tuple-element.17.tall_hbm) | copy-start | bytes 7864324
  53.5 0.9 %copy-start.2 = (f32[64,8,128]{2,1,0:T(8,128)S(1)}, f32[64,8,128]{2,1,0:T(8,128)}, u32[]{:S(2)}) copy-start(f32[64,8,128]{2,1,0:T(8,128)} %get-tuple-element.16.st_xh) | copy-start | bytes 786436
  54.4 0.7 copy-start.3
  55.1 0.7 copy-start.4
  55.9 0.7 copy-start.5
